TPU v7x, 256 devices: a whole 4x4x8 slice. The times are simulated.
256 devices in a mesh: req: 32 (over y, z), vocab: 8 (over x, core).
Axes of the slice: x: 4, y: 4, z: 8, core: 2. Of those that a mesh axis runs over, the one named last changes fastest.
Arguments:
- draft_states: bfloat16 [64, 64, 1536], P('req')
- parents: int32 [64, 64], P('req'), may hold values from -1 to 62, as said below
- live_draft_count: int32 [64], replicated, may hold values from 32 to 64, as said below
- path_index: int32 [64, 8], P('req'), may hold values from 0 to 63, as said below
- cached_length_list: int32 [64], P('req'), may hold values from 256 to 1792, as said below
- cached_key_rows: bfloat16 [65536, 768], P('req', 'vocab')
- cached_value_rows: bfloat16 [65536, 768], P('req', 'vocab'), may hold values from -6 to 6
- attend_gain: bfloat16 [1536], replicated, may hold values from 0.099609375 to 1.8984375
- hidden_gain: bfloat16 [1536], replicated, may hold values from 0.099609375 to 1.8984375
- final_gain: bfloat16 [1536], replicated, may hold values from 0.099609375 to 1.8984375
- query_weight: bfloat16 [1536, 1536], P(None, 'vocab')
- key_matrix: bfloat16 [1536, 768], P(None, 'vocab')
- value_matrix: bfloat16 [1536, 768], P(None, 'vocab'), may hold values from -0.15625 to 0.15625
- out_weight: bfloat16 [1536, 1536], P('vocab'), may hold values from -0.15625 to 0.15625
- gate_weight: bfloat16 [1536, 4096], P(None, 'vocab'), may hold values from -0.15625 to 0.15625
- up_weight: bfloat16 [1536, 4096], P(None, 'vocab'), may hold values from -0.15625 to 0.15625
- down_weight: bfloat16 [4096, 1536], P('vocab'), may hold values from -0.09375 to 0.09375
- head_weight: bfloat16 [1536, 32000], P(None, 'req'), may hold values from -0.4375 to 0.4375
Outputs:
- layer_output_rows: bfloat16 [64, 64, 1536], P('req', None, 'vocab')
- accepted_keys: bfloat16 [64, 8, 768], P('req', None, 'vocab')
- accepted_values: bfloat16 [64, 8, 768], P('req', None, 'vocab')
- norm_values: float32 [64, 8], P('req', 'vocab')
- maxima: float32 [64, 8], P(None, 'vocab')
Inputs may be any that keep to these rules, and one draw needn't show every extreme that they name: `live_draft_count`: the counts of all requests sum to exactly 3072. `parents`: each draft token's parent lies below its own index; the first token's is -1. `path_index`: each row lists 8 live draft tokens of its request, each the parent of the next. `cached_length_list`: the lengths of the 2 requests of one index of req sum to at most 2048, and to exactly 2048 on a quarter of the indices of req (at least one); on such an index one request is long and the others hold 256 each.
All inputs are finite; a program needn't handle non-finite values.
Results may differ from a plain program's by a relative error of at most 0.012.
Values may be sent and summed in bfloat16 or wider, within the bound.
No kernel may reach another device: no remote copies, remote signals or barrier semaphores. Data moves between devices by JAX's collectives and lax.ppermute only.
A program may use at most 64 MiB of HBM per device.

v0:
```python
import jax
import jax.numpy as jnp
from jax import lax
from jax.sharding import PartitionSpec as P

HEAD_SIZE = 96


eps_norm = 1e-05
rope_base = 100000.0
masked_score = -1e30


def apply_rotation(values, token_positions):
    half_dim = values.shape[-1] // 2
    inverse = rope_base ** (-jnp.arange(half_dim, dtype=jnp.float32) * 2.0 / values.shape[-1])
    angles = token_positions.astype(jnp.float32)[:, None] * inverse[None, :]
    cosine = jnp.cos(angles)[:, None, :]
    sine_of = jnp.sin(angles)[:, None, :]
    first_half = values[..., :half_dim]
    second_half = values[..., half_dim:]
    return jnp.concatenate(
        [first_half * cosine - second_half * sine_of, second_half * cosine + first_half * sine_of],
        axis=-1,
    )


def ancestors(parents):
    draft_length = parents.shape[-1]
    columns = jnp.arange(draft_length, dtype=jnp.int32)
    reached = jnp.eye(draft_length, dtype=jnp.float32) + (parents[..., :, None] == columns).astype(
        jnp.float32
    )
    for sweep_number in range((draft_length - 1).bit_length()):
        reached = jnp.minimum(
            jnp.einsum("bij,bjk->bik", reached, reached, precision=lax.Precision.HIGHEST), 1.0
        )
    return reached


def lookup(entries, indices):
    matches = indices[:, None] == jnp.arange(entries.shape[0], dtype=jnp.int32)[None, :]
    return jnp.sum(jnp.where(matches, entries[None, :], 0), axis=1)


def span_scores(query_block, first, last, number, joined_keys, block_len):
    pool_rows = joined_keys.shape[0]
    nominal = first + number * block_len
    actual = jnp.minimum(nominal, pool_rows - block_len)
    keys_block = lax.dynamic_slice_in_dim(joined_keys, actual, block_len, 0)
    scores = jnp.einsum(
        "kqd,pkd->kqp", query_block, keys_block, preferred_element_type=jnp.float32
    ) * query_block.shape[-1] ** (-0.5)
    slots = actual + jnp.arange(block_len, dtype=jnp.int32)
    allowed = (slots >= nominal) & (slots < jnp.minimum(last, nominal + block_len))
    return (scores, allowed[None, None, :], actual)


def span_max(query_block, first, last, joined_keys, block_len):
    block_count = (last - first + block_len - 1) // block_len

    def step(number, running):
        scores, allowed, actual = span_scores(
            query_block, first, last, number, joined_keys, block_len
        )
        return jnp.maximum(running, jnp.max(jnp.where(allowed, scores, masked_score), axis=2))

    start_max = jnp.full(query_block.shape[:2], masked_score, jnp.float32)
    return lax.fori_loop(0, block_count, step, start_max)


def span_sums(query_block, first, last, top, joined_keys, joined_values, block_len):
    block_count = (last - first + block_len - 1) // block_len

    def step(number, running):
        totals_now, weighted_now = running
        scores, allowed, actual = span_scores(
            query_block, first, last, number, joined_keys, block_len
        )
        weights = jnp.where(allowed, jnp.exp(scores - top[:, :, None]), 0.0).astype(jnp.bfloat16)
        values_block = lax.dynamic_slice_in_dim(joined_values, actual, block_len, 0)
        return (
            totals_now + jnp.sum(weights.astype(jnp.float32), axis=2),
            weighted_now
            + jnp.einsum("kqp,pkd->kqd", weights, values_block, preferred_element_type=jnp.float32),
        )

    start_sums = (
        jnp.zeros(query_block.shape[:2], jnp.float32),
        jnp.zeros(query_block.shape, jnp.float32),
    )
    return lax.fori_loop(0, block_count, step, start_sums)


def maxima_over(query_sets, firsts, lasts, joined_keys, block_len):
    return lax.map(
        lambda item: span_max(item[0], item[1], item[2], joined_keys, block_len),
        (query_sets, firsts, lasts),
    )


def sums_over(query_sets, firsts, lasts, tops, joined_keys, joined_values, block_len):
    return lax.map(
        lambda item: span_sums(
            item[0], item[1], item[2], item[3], joined_keys, joined_values, block_len
        ),
        (query_sets, firsts, lasts, tops),
    )


def feed_forward(hidden_in, gate_weight, up_weight, down_weight):
    gate_out = jnp.dot(hidden_in, gate_weight, preferred_element_type=jnp.float32)
    up_out = jnp.dot(hidden_in, up_weight, preferred_element_type=jnp.float32)
    hidden = (jax.nn.silu(gate_out) * up_out).astype(jnp.bfloat16)
    partial_sum = jnp.dot(hidden, down_weight, preferred_element_type=jnp.float32)
    summed = lax.psum(partial_sum.astype(jnp.bfloat16), "vocab")
    return summed


def per_device(
    draft_states,
    parents,
    live_draft_count,
    path_index,
    cached_length_list,
    cached_key_rows,
    cached_value_rows,
    attend_gain,
    hidden_gain,
    final_gain,
    query_weight,
    key_matrix,
    value_matrix,
    out_weight,
    gate_weight,
    up_weight,
    down_weight,
    head_weight,
):
    local_requests, draft_length, model_width = draft_states.shape
    token_rows = local_requests * draft_length
    request_shards = lax.axis_size("req")
    request_shard = lax.axis_index("req")
    vocab_shards = lax.axis_size("vocab")
    vocab_shard = lax.axis_index("vocab")
    head_dim = HEAD_SIZE
    key_local = key_matrix.shape[1] // head_dim
    query_local = query_weight.shape[1] // head_dim
    group_factor = query_local // key_local
    pool_rows = cached_key_rows.shape[0]
    rows_per_request = draft_length * group_factor
    states = draft_states.reshape(token_rows, model_width).astype(jnp.float32)
    normalized_states = (
        states
        * lax.rsqrt(jnp.mean(states * states, axis=1, keepdims=True) + eps_norm)
        * attend_gain.astype(jnp.float32)
    ).astype(jnp.bfloat16)
    reached = ancestors(parents)
    token_positions = (
        cached_length_list[:, None] + (jnp.sum(reached, axis=2) - 1.0).astype(jnp.int32)
    ).reshape(token_rows)
    query_vectors = apply_rotation(
        jnp.dot(normalized_states, query_weight, preferred_element_type=jnp.float32).reshape(
            token_rows, query_local, head_dim
        ),
        token_positions,
    ).astype(jnp.bfloat16)
    fresh_keys = apply_rotation(
        jnp.dot(normalized_states, key_matrix, preferred_element_type=jnp.float32).reshape(
            token_rows, key_local, head_dim
        ),
        token_positions,
    ).astype(jnp.bfloat16)
    fresh_values = (
        jnp.dot(normalized_states, value_matrix, preferred_element_type=jnp.float32)
        .astype(jnp.bfloat16)
        .reshape(token_rows, key_local, head_dim)
    )
    query_rows = (
        query_vectors.reshape(token_rows, key_local, group_factor, head_dim)
        .transpose(1, 0, 2, 3)
        .reshape(key_local, token_rows * group_factor, head_dim)
    )
    score_scale = head_dim ** (-0.5)
    same_request = jnp.eye(local_requests, dtype=jnp.float32)
    tree_mask = (
        jnp.einsum("jk,jim->jikm", same_request, reached).reshape(token_rows, token_rows) > 0.5
    )
    tree_mask = jnp.repeat(tree_mask, group_factor, axis=0)[None]
    tree_scores = (
        jnp.einsum("kqd,rkd->kqr", query_rows, fresh_keys, preferred_element_type=jnp.float32)
        * score_scale
    )
    tree_max = jnp.max(jnp.where(tree_mask, tree_scores, masked_score), axis=2)
    tree_top = tree_max.reshape(key_local, local_requests, rows_per_request).transpose(1, 0, 2)
    cache_end = jnp.cumsum(cached_length_list)
    cache_start = cache_end - cached_length_list
    block_len = min(512, pool_rows)
    pool_keys = cached_key_rows.reshape(pool_rows, key_local, head_dim)
    pool_values = cached_value_rows.reshape(pool_rows, key_local, head_dim)
    by_request = query_rows.reshape(
        key_local, local_requests, rows_per_request, head_dim
    ).transpose(1, 0, 2, 3)
    pool_max = maxima_over(by_request, cache_start, cache_end, pool_keys, block_len)
    top = jnp.maximum(tree_top, pool_max)
    pool_totals, pool_weighted = sums_over(
        by_request, cache_start, cache_end, top, pool_keys, pool_values, block_len
    )
    top_rows = top.transpose(1, 0, 2).reshape(key_local, token_rows * group_factor)
    tree_weights = jnp.where(tree_mask, jnp.exp(tree_scores - top_rows[:, :, None]), 0.0).astype(
        jnp.bfloat16
    )
    totals = jnp.sum(tree_weights.astype(jnp.float32), axis=2) + pool_totals.transpose(
        1, 0, 2
    ).reshape(key_local, token_rows * group_factor)
    weighted_values = jnp.einsum(
        "kqr,rkd->kqd", tree_weights, fresh_values, preferred_element_type=jnp.float32
    )
    weighted_values = weighted_values + pool_weighted.transpose(1, 0, 2, 3).reshape(
        key_local, token_rows * group_factor, head_dim
    )
    attended = (
        (weighted_values / totals[:, :, None])
        .reshape(key_local, token_rows, group_factor, head_dim)
        .transpose(1, 0, 2, 3)
    )
    attended = attended.reshape(token_rows, query_local * head_dim).astype(jnp.bfloat16)
    attend_part = jnp.dot(attended, out_weight, preferred_element_type=jnp.float32)
    share_width = model_width // vocab_shards
    share_start = vocab_shard * share_width
    residual = states + lax.psum(attend_part, "vocab")
    hidden_in = (
        residual
        * lax.rsqrt(jnp.mean(residual * residual, axis=1, keepdims=True) + eps_norm)
        * hidden_gain.astype(jnp.float32)
    ).astype(jnp.bfloat16)
    local_counts = lax.dynamic_slice_in_dim(
        live_draft_count, request_shard * local_requests, local_requests
    )
    device_totals = jnp.sum(live_draft_count.reshape(request_shards, local_requests), axis=1)
    device_ends = jnp.cumsum(device_totals)
    device_starts = device_ends - device_totals
    own_start = lax.dynamic_index_in_dim(device_starts, request_shard, keepdims=False)
    own_total = jnp.sum(local_counts)
    local_ends = jnp.cumsum(local_counts)
    local_starts = local_ends - local_counts
    token_number = jnp.arange(token_rows, dtype=jnp.int32)
    token_request = token_number // draft_length
    token_place = token_number % draft_length
    live_rows = token_place < lookup(local_counts, token_request)
    slot_count = token_rows // request_shards
    even_rows = 3 * token_rows // 4
    slot_index = jnp.arange(request_shards * slot_count, dtype=jnp.int32)
    slot_target = slot_index // slot_count
    slot_order = slot_index % slot_count * request_shards
    send_rank = slot_order + (slot_target - own_start) % request_shards
    send_request = jnp.minimum(
        jnp.sum((local_ends[None, :] <= send_rank[:, None]).astype(jnp.int32), axis=1),
        local_requests - 1,
    )
    send_row = jnp.clip(
        send_request * draft_length + send_rank - lookup(local_starts, send_request),
        0,
        token_rows - 1,
    )
    outgoing = jnp.where(
        (send_rank < own_total)[:, None],
        jnp.take(hidden_in, send_row, axis=0),
        jnp.zeros((), jnp.bfloat16),
    )
    arrived = lax.all_to_all(outgoing, "req", split_axis=0, concat_axis=0, tiled=True)
    global_rank = jnp.arange(even_rows, dtype=jnp.int32) * request_shards + request_shard
    source = jnp.minimum(
        jnp.sum((device_ends[None, :] <= global_rank[:, None]).astype(jnp.int32), axis=1),
        request_shards - 1,
    )
    source_rank = global_rank - lookup(device_starts, source)
    packed = jnp.take(arrived, source * slot_count + source_rank // request_shards, axis=0)
    computed = feed_forward(packed, gate_weight, up_weight, down_weight)
    slot_starts = lookup(device_starts, slot_target)
    return_rank = slot_order + (request_shard - slot_starts) % request_shards
    return_live = return_rank < lookup(device_totals, slot_target)
    return_row = jnp.clip((slot_starts + return_rank) // request_shards, 0, even_rows - 1)
    backward = jnp.where(
        return_live[:, None], jnp.take(computed, return_row, axis=0), jnp.zeros((), jnp.bfloat16)
    )
    returned = lax.all_to_all(backward, "req", split_axis=0, concat_axis=0, tiled=True)
    local_rank = lookup(local_starts, token_request) + token_place
    home_slot = jnp.clip(
        (own_start + local_rank) % request_shards * slot_count + local_rank // request_shards,
        0,
        request_shards * slot_count - 1,
    )
    feed_rows = jnp.take(returned, home_slot, axis=0)
    updated = jnp.where(live_rows[:, None], residual + feed_rows.astype(jnp.float32), 0.0).astype(
        jnp.bfloat16
    )
    layer_part = lax.dynamic_slice_in_dim(updated, share_start, share_width, 1)
    path_length = path_index.shape[1]
    request_picker = (
        path_index[:, :, None] == jnp.arange(draft_length, dtype=jnp.int32)[None, None, :]
    ).astype(jnp.bfloat16)
    accepted_keys = jnp.einsum(
        "ytm,ymu->ytu",
        request_picker,
        fresh_keys.reshape(local_requests, draft_length, key_local * head_dim),
        preferred_element_type=jnp.float32,
    ).astype(jnp.bfloat16)
    accepted_values = jnp.einsum(
        "ytm,ymu->ytu",
        request_picker,
        fresh_values.reshape(local_requests, draft_length, key_local * head_dim),
        preferred_element_type=jnp.float32,
    ).astype(jnp.bfloat16)
    path_states = jnp.einsum(
        "ytm,ymu->ytu",
        request_picker,
        updated.reshape(local_requests, draft_length, updated.shape[1]),
        preferred_element_type=jnp.float32,
    ).astype(jnp.bfloat16)
    per_shard = path_length // vocab_shards
    head_rows = lax.dynamic_slice_in_dim(path_states, vocab_shard * per_shard, per_shard, 1)
    flat_rows = head_rows.reshape(local_requests * per_shard, model_width).astype(jnp.float32)
    mean_square = jnp.mean(flat_rows * flat_rows, axis=1)
    norm_values = jnp.sqrt(mean_square + eps_norm).reshape(local_requests, per_shard)
    head_in = (
        flat_rows * lax.rsqrt(mean_square + eps_norm)[:, None] * final_gain.astype(jnp.float32)
    ).astype(jnp.bfloat16)
    local_max = jnp.max(
        jnp.dot(
            lax.all_gather(head_in, "req", axis=0, tiled=True),
            head_weight,
            preferred_element_type=jnp.float32,
        ),
        axis=1,
    )
    maxima = lax.pmax(local_max, "req").reshape(request_shards * local_requests, per_shard)
    return (
        layer_part.reshape(local_requests, draft_length, share_width),
        accepted_keys,
        accepted_values,
        norm_values,
        maxima,
    )


def solution(mesh):
    in_specs = (
        P("req", None, None),
        P("req", None),
        P(),
        P("req", None),
        P("req"),
        P("req", "vocab"),
        P("req", "vocab"),
        P(),
        P(),
        P(),
        P(None, "vocab"),
        P(None, "vocab"),
        P(None, "vocab"),
        P("vocab", None),
        P(None, "vocab"),
        P(None, "vocab"),
        P("vocab", None),
        P(None, "req"),
    )
    out_specs = (
        P("req", None, "vocab"),
        P("req", None, "vocab"),
        P("req", None, "vocab"),
        P("req", "vocab"),
        P(None, "vocab"),
    )
    return jax.shard_map(
        per_device, mesh=mesh, in_specs=in_specs, out_specs=out_specs, check_vma=False
    )
```

profile of v0, /device:TPU:2, one launch (start us, length us, event | category | flops | bytes accessed | tf_op | source)
XLA Modules:
  0.0 428.3 jit_solution(2715974961499457239)
XLA Ops:
  7.8 1.4 reduce-window.24
  9.2 1.3 bitcast_subtract_fusion.3
  18.8 1.4 copy.72
  21.9 1.4 fusion.105
  25.5 1.6 maximum_bitcast_fusion
  27.1 21.4 %while.104 = (s32[]{:T(128)}, f32[2,1,128]{2,1,0:T(1,128)S(1)}, s32[2]{0:T(128)}, s32[2]{0:T(128)}, bf16[2,1,128,96]{3,2,1,0:T(8,128)(2,1)}, /*index=5*/bf16[204...) while((s32[]{:T(128)}, f32[2,1,128]{2,1,0:T(1,128)S(1)}, ...), condition=%wide.region_9.10_spmd, body=%wide.region_5.9_spmd.sunk | while | flops 12781597 | bytes 177346 | solution.py:96
  27.1 1.2 dynamic_slice.135
  28.4 1.3 dynamic_slice.136
  31.6 2.5 while.107
  32.8 1.2 fusion.151
  35.4 1.3 dynamic_slice.136
  38.6 9.9 %while.107 = (s32[]{:T(128)}, f32[1,128]{1,0:T(1,128)S(1)}, s32[]{:T(128)}, s32[]{:T(128)}, s32[]{:T(128)}, /*index=5*/bf16[2048,1,96]{0,2,1:T(8,128)(2,1)}, bf1...) while((s32[]{:T(128)}, f32[1,128]{1,0:T(1,128)S(1)}, ...), condition=%wide.region_8.8_spmd, body=%wide.region_6.7_spmd.sunk | while | flops 12781578 | bytes 126179 | solution.py:69
  39.8 1.2 fusion.151
  42.3 1.2 fusion.151
  44.8 1.2 fusion.151
  48.8 1.8 convolution_convert_fusion.1
  52.0 41.9 %while.106 = (s32[]{:T(128)}, f32[2,1,128]{2,1,0:T(1,128)S(1)}, f32[2,1,128,96]{2,0,3,1:T(2,128)}, s32[2]{0:T(128)}, s32[2]{0:T(128)}, /*index=5*/bf16[2,1,128,9...) while((s32[]{:T(128)}, f32[2,1,128]{2,1,0:T(1,128)S(1)}, ...), condition=%wide.region_14.15_spmd, body=%wide.region_10.14_spmd.sunk | while | flops 25573404 | bytes 785178 | solution.py:103
  53.3 1.3 dynamic_slice.140
  57.6 4.8 %while.108 = (s32[]{:T(128)}, f32[1,128]{1,0:T(1,128)}, f32[1,128,96]{1,2,0:T(8,128)S(1)}, s32[]{:T(128)}, s32[]{:T(128)}, /*index=5*/s32[]{:T(128)}, bf16[2048,...) while((s32[]{:T(128)}, f32[1,128]{1,0:T(1,128)}, ...), condition=%wide.region_13.13_spmd, body=%wide.region_11.12_spmd.sunk | while | flops 25573384 | bytes 585471 | solution.py:92
  58.8 1.3 convert_reduce_fusion.4
  63.1 2.7 dynamic_update_slice.39
  67.0 1.3 dynamic_slice.140
  71.3 19.2 %while.108 = (s32[]{:T(128)}, f32[1,128]{1,0:T(1,128)}, f32[1,128,96]{1,2,0:T(8,128)S(1)}, s32[]{:T(128)}, s32[]{:T(128)}, /*index=5*/s32[]{:T(128)}, bf16[2048,...) while((s32[]{:T(128)}, f32[1,128]{1,0:T(1,128)}, ...), condition=%wide.region_13.13_spmd, body=%wide.region_11.12_spmd.sunk | while | flops 25573384 | bytes 585471 | solution.py:92
  72.6 1.3 convert_reduce_fusion.4
  77.4 1.3 convert_reduce_fusion.4
  82.2 1.3 convert_reduce_fusion.4
  87.0 1.3 convert_reduce_fusion.4
  91.2 2.7 dynamic_update_slice.39
  97.8 2.2 fusion.106
  103.6 1.3 compare_and_fusion.2
  105.2 61.5 %all-reduce.3.cloned.1.call-done = f32[128,1536]{1,0:T(8,128)} async-done(((f32[128,1536]{1,0:T(8,128)}), f32[128,1536]{1,0:T(8,128)}) %all-reduce.3.cloned.1.call-update) | async-done | bytes 786448 | tf_op jit(solution)/shard_map/psum | solution.py:231
  166.8 1.4 multiply_reduce_fusion
  169.3 1.6 gather_fusion.2
  173.0 10.0 %all-to-all-start = ((bf16[32,4,1536]{2,1,0:T(4,128)(2,1)}), bf16[32,4,1536]{2,1,0:T(4,128)(2,1)}, u32[]{:S(2)}, u32[]{:S(2)}) async-start(bf16[32,4,1536]{2,1,0:T(4,128)(2,1)} %all_to_all.14), calls=%async_computation | async-start | bytes 786432 | tf_op jit(solution)/shard_map/all_to_all | solution.py:271
  183.1 12.7 %all-to-all-done = bf16[32,4,1536]{2,1,0:T(4,128)(2,1)} async-done(((bf16[32,4,1536]{2,1,0:T(4,128)(2,1)}), bf16[32,4,1536]{2,1,0:T(4,128)(2,1)}, u32[]{:S(2)}, u32[]{:S(2)}) %all-to-all-start) | async-done | bytes 393248 | tf_op jit(solution)/shard_map/all_to_all | solution.py:271
  196.8 1.5 gather_fusion
  198.4 2.7 fusion.38
  201.1 3.5 convolution_convert_fusion
  205.6 60.8 %all-reduce.5.cloned.1.call-done = bf16[96,1536]{1,0:T(8,128)(2,1)} async-done(((bf16[96,1536]{1,0:T(8,128)(2,1)}), bf16[96,1536]{1,0:T(8,128)(2,1)}) %all-reduce.5.cloned.1.call-update) | async-done | bytes 294928 | tf_op jit(solution)/shard_map/psum | solution.py:116
  266.4 3.0 gather_fusion.1
  271.7 10.0 %all-to-all-start.1 = ((bf16[32,4,1536]{2,1,0:T(4,128)(2,1)}), bf16[32,4,1536]{2,1,0:T(4,128)(2,1)}, u32[]{:S(2)}, u32[]{:S(2)}) async-start(bf16[32,4,1536]{2,1,0:T(4,128)(2,1)} %select_select_fusion.1), calls=%async_computation.1 | async-start | bytes 786432 | tf_op jit(solution)/shard_map/all_to_all | solution.py:287
  281.7 1.3 compare_and_fusion.1
  283.9 1.5 convolution_convert_fusion.2
  285.4 9.4 %all-to-all-done.1 = bf16[32,4,1536]{2,1,0:T(4,128)(2,1)} async-done(((bf16[32,4,1536]{2,1,0:T(4,128)(2,1)}), bf16[32,4,1536]{2,1,0:T(4,128)(2,1)}, u32[]{:S(2)}, u32[]{:S(2)}) %all-to-all-start.1) | async-done | bytes 393248 | tf_op jit(solution)/shard_map/all_to_all | solution.py:287
  295.9 1.6 gather_fusion.3
  297.6 1.6 select_convert_fusion
  300.9 46.6 %all-gather = bf16[32,2,1536]{2,1,0:T(2,128)(2,1)S(1)} all-gather(bf16[1,2,1536]{2,1,0:T(2,128)(2,1)S(1)} %fusion.76), channel_id=1, replica_groups=mesh['req'=32,'vocab'=8] {'req'}, dimensions={0}, use_global_device_ids=true | all-gather | bytes 202752 | tf_op jit(solution)/shard_map/all_gather | solution.py:331
  348.6 72.8 %pmax.7 = f32[64,1]{0,1:T(1,128)} all-reduce(f32[64,1]{0,1:T(1,128)S(1)} %bitcast.225), channel_id=1, replica_groups=mesh['req'=32,'vocab'=8] {'req'}, use_global_device_ids=true, to_apply=%region_32.34 | all-reduce | flops 64 | bytes 512 | tf_op jit(solution)/shard_map/pmax | solution.py:337
  (187 shorter events, 57.5 us)
Async XLA Ops:
  7.2 340.3 %copy-start = (bf16[1536,1000]{0,1:T(8,128)(2,1)S(1)}, bf16[1536,1000]{0,1:T(8,128)(2,1)}, u32[]{:S(2)}) copy-start(bf16[1536,1000]{0,1:T(8,128)(2,1)} %param.45) | copy-start | bytes 9216004
  7.2 13.1 %copy-start.1 = (bf16[2,64,1536]{2,1,0:T(8,128)(2,1)S(1)}, bf16[2,64,1536]{2,1,0:T(8,128)(2,1)}, u32[]{:S(2)}) copy-start(bf16[2,64,1536]{2,1,0:T(8,128)(2,1)} %param.28) | copy-start | bytes 1179652
  7.2 159.6 %all-reduce.3.cloned.1.call-start = ((), (), s32[]{:S(2)}) async-start(), calls=%async_computation.2 | async-start | bytes 1572864 | tf_op jit(solution)/shard_map/psum | solution.py:231
  11.6 2.9 copy-start.17
  12.9 10.4 %copy-start.14 = (f32[1536]{0:T(1024)}, f32[1536]{0:T(1024)S(1)}, u32[]{:S(2)}) copy-start(f32[1536]{0:T(1024)S(1)} %convert_element_type.141) | copy-start | bytes 18436
  24.8 2.3 copy-start.4
  27.1 21.4 %copy-start.15 = (f32[1536]{0:T(1024)S(1)}, f32[1536]{0:T(1024)}, u32[]{:S(2)}) copy-start(f32[1536]{0:T(1024)} %copy-done.14) | copy-start | bytes 18436
  27.1 21.5 %copy-start.23 = (f32[128]{0:T(128)S(1)}, f32[128]{0:T(128)}, u32[]{:S(2)}) copy-start(f32[128]{0:T(128)} %rsqrt.28) | copy-start | bytes 1540
  48.6 2.1 copy-start.8
  48.6 2.3 copy-start.20
  48.6 2.3 copy-start.21
  48.6 2.5 copy-start.5
  48.6 2.5 copy-start.6
  48.6 2.5 copy-start.7
  51.1 1.0 copy-start.9
  51.1 0.9 copy-start.11
  93.9 6.1 %copy-start.22 = (s32[64]{0:T(128)S(1)}, s32[64]{0:T(128)}, u32[]{:S(2)}) copy-start(s32[64]{0:T(128)} %param.30) | copy-start | bytes 772
  94.9 10.0 %copy-start.18 = (bf16[1536]{0:T(1024)(128)(2,1)S(1)}, bf16[1536]{0:T(1024)(128)(2,1)}, u32[]{:S(2)}) copy-start(bf16[1536]{0:T(1024)(128)(2,1)} %param.36) | copy-start | bytes 9220
  166.7 1.4 copy-start.2
  173.0 22.8 %all-to-all-start = ((bf16[32,4,1536]{2,1,0:T(4,128)(2,1)}), bf16[32,4,1536]{2,1,0:T(4,128)(2,1)}, u32[]{:S(2)}, u32[]{:S(2)}) async-start(bf16[32,4,1536]{2,1,0:T(4,128)(2,1)} %all_to_all.14), calls=%async_computation | async-start | bytes 786432 | tf_op jit(solution)/shard_map/all_to_all | solution.py:271
  182.9 83.5 %all-reduce.5.cloned.1.call-start = ((), (), s32[]{:S(2)}) async-start(), calls=%async_computation.3 | async-start | bytes 589824 | tf_op jit(solution)/shard_map/psum | solution.py:116
  198.4 2.7 copy-start.3
  201.0 3.6 copy-start.13
  201.0 4.3 %copy-start.12 = (bf16[128,1,48]{0,2,1:T(8,128)(2,1)S(1)}, bf16[128,1,48]{0,2,1:T(8,128)(2,1)}, u32[]{:S(2)}) copy-start(bf16[128,1,48]{0,2,1:T(8,128)(2,1)} %copy-done.11) | copy-start | bytes 36868
  201.0 4.4 %copy-start.10 = (bf16[128,1,48]{0,2,1:T(8,128)(2,1)S(1)}, bf16[128,1,48]{0,2,1:T(8,128)(2,1)}, u32[]{:S(2)}) copy-start(bf16[128,1,48]{0,2,1:T(8,128)(2,1)} %copy-done.9) | copy-start | bytes 36868
  201.0 4.6 %copy-start.19 = (bf16[1536]{0:T(1024)(128)(2,1)S(1)}, bf16[1536]{0:T(1024)(128)(2,1)}, u32[]{:S(2)}) copy-start(bf16[1536]{0:T(1024)(128)(2,1)} %param.37) | copy-start | bytes 9220
  269.4 13.6 %copy-start.16 = (s32[2,8]{1,0:T(2,128)S(1)}, s32[2,8]{1,0:T(2,128)}, u32[]{:S(2)}) copy-start(s32[2,8]{1,0:T(2,128)} %param.31) | copy-start | bytes 196
  271.7 23.1 %all-to-all-start.1 = ((bf16[32,4,1536]{2,1,0:T(4,128)(2,1)}), bf16[32,4,1536]{2,1,0:T(4,128)(2,1)}, u32[]{:S(2)}, u32[]{:S(2)}) async-start(bf16[32,4,1536]{2,1,0:T(4,128)(2,1)} %select_select_fusion.1), calls=%async_computation.1 | async-start | bytes 786432 | tf_op jit(solution)/shard_map/all_to_all | solution.py:287
Sparse Core Ops, SparseCore 0:
  100.2 66.5 all-reduce.2
  204.7 61.6 all-reduce.4
where the time goes:
time: 433 us; the launch traced here: 428 us
  waiting for transfers between devices  144 us (33%)
  blocking collectives  119 us (27%)
  local copies, waits for them, and re-layouts  44.3 us (10%)
  matrix products  37.8 us (9%)
  other arithmetic  30.5 us (7%)
  starting transfers between devices  20 us (5%)
  loops' own time  17.2 us (4%)
  between operations  14.6 us (3%)
    pmax x1, blocking collectives, per_device(): lax.pmax(local_max, 'req')  72.8 us
    psum x1, waiting for transfers between devices, per_device(): residual = states + lax.psum(attend_part, 'vocab')  61.5 us
    psum x1, waiting for transfers between devices, feed_forward(): summed = lax.psum(partial_sum.astype(jnp.bfloat16), 'vocab')  60.8 us
    all_gather x1, blocking collectives, per_device(): lax.all_gather(head_in, 'req', axis=0, tiled=True)  46.6 us
    all_to_all x1, waiting for transfers between devices, per_device(): lax.all_to_all(outgoing, 'req', split_axis=0, concat_axis=0, tiled=True)  12.7 us
    dot_general x10, matrix products, span_scores(): jnp.einsum('kqd,pkd->kqp', query_block, keys_block, preferred_element_typ...  12.5 us
    dynamic_slice x8, local copies, waits for them, and re-layouts, maxima_over(): lax.map(lambda item: span_max(item[0], item[1], item[2], joined_keys, blo...  10 us
    all_to_all x1, starting transfers between devices, per_device(): lax.all_to_all(outgoing, 'req', split_axis=0, concat_axis=0, tiled=True)  9.97 us
  transfers between devices with their start and end apart: 4, of which 4 were waited for; matrix products, arithmetic and copies ran while one was open for 2% of the time, Pallas kernels for 0%

commit v1 on v0

v1 whole, which is shorter than its diff:
```python
import jax
import jax.numpy as jnp
from jax import lax
from jax.sharding import PartitionSpec as P

HEAD_SIZE = 96


eps_norm = 1e-05
rope_base = 100000.0
masked_score = -1e30


def apply_rotation(values, token_positions):
    half_dim = values.shape[-1] // 2
    inverse = rope_base ** (-jnp.arange(half_dim, dtype=jnp.float32) * 2.0 / values.shape[-1])
    angles = token_positions.astype(jnp.float32)[:, None] * inverse[None, :]
    cosine = jnp.cos(angles)[:, None, :]
    sine_of = jnp.sin(angles)[:, None, :]
    first_half = values[..., :half_dim]
    second_half = values[..., half_dim:]
    return jnp.concatenate(
        [first_half * cosine - second_half * sine_of, second_half * cosine + first_half * sine_of],
        axis=-1,
    )


def ancestors(parents):
    draft_length = parents.shape[-1]
    columns = jnp.arange(draft_length, dtype=jnp.int32)
    reached = jnp.eye(draft_length, dtype=jnp.float32) + (parents[..., :, None] == columns).astype(
        jnp.float32
    )
    for sweep_number in range((draft_length - 1).bit_length()):
        reached = jnp.minimum(
            jnp.einsum("bij,bjk->bik", reached, reached, precision=lax.Precision.HIGHEST), 1.0
        )
    return reached


def scatter_rows(partial, axis_name, shards):
    rows = partial.shape[0] // shards
    pieces = partial.reshape(shards, rows, *partial.shape[1:])
    arrived = lax.all_to_all(pieces, axis_name, split_axis=0, concat_axis=0, tiled=True)
    return jnp.sum(arrived, axis=0)


def gather_rows(chunk, axis_name, shards):
    copies = jnp.broadcast_to(chunk[None], (shards, *chunk.shape))
    arrived = lax.all_to_all(copies, axis_name, split_axis=0, concat_axis=0, tiled=True)
    return arrived.reshape(shards * chunk.shape[0], *chunk.shape[1:])


def per_device(
    draft_states,
    parents,
    live_draft_count,
    path_index,
    cached_length_list,
    cached_key_rows,
    cached_value_rows,
    attend_gain,
    hidden_gain,
    final_gain,
    query_weight,
    key_matrix,
    value_matrix,
    out_weight,
    gate_weight,
    up_weight,
    down_weight,
    head_weight,
):
    local_requests, draft_length, model_width = draft_states.shape
    token_rows = local_requests * draft_length
    request_shards = lax.axis_size("req")
    request_shard = lax.axis_index("req")
    vocab_shards = lax.axis_size("vocab")
    vocab_shard = lax.axis_index("vocab")
    head_dim = HEAD_SIZE
    key_local = key_matrix.shape[1] // head_dim
    query_local = query_weight.shape[1] // head_dim
    group_factor = query_local // key_local
    pool_rows = cached_key_rows.shape[0]
    states = draft_states.reshape(token_rows, model_width).astype(jnp.float32)
    normalized_states = (
        states
        * lax.rsqrt(jnp.mean(states * states, axis=1, keepdims=True) + eps_norm)
        * attend_gain.astype(jnp.float32)
    ).astype(jnp.bfloat16)
    reached = ancestors(parents)
    token_positions = (
        cached_length_list[:, None] + (jnp.sum(reached, axis=2) - 1.0).astype(jnp.int32)
    ).reshape(token_rows)
    query_vectors = apply_rotation(
        jnp.dot(normalized_states, query_weight, preferred_element_type=jnp.float32).reshape(
            token_rows, query_local, head_dim
        ),
        token_positions,
    ).astype(jnp.bfloat16)
    fresh_keys = apply_rotation(
        jnp.dot(normalized_states, key_matrix, preferred_element_type=jnp.float32).reshape(
            token_rows, key_local, head_dim
        ),
        token_positions,
    ).astype(jnp.bfloat16)
    fresh_values = (
        jnp.dot(normalized_states, value_matrix, preferred_element_type=jnp.float32)
        .astype(jnp.bfloat16)
        .reshape(token_rows, key_local, head_dim)
    )
    score_scale = head_dim ** (-0.5)
    query_rows = query_vectors.reshape(
        local_requests, draft_length, key_local, group_factor, head_dim
    ).transpose(0, 2, 1, 3, 4).reshape(
        local_requests, key_local, draft_length * group_factor, head_dim
    )
    request_keys = fresh_keys.reshape(local_requests, draft_length, key_local, head_dim)
    request_values = fresh_values.reshape(local_requests, draft_length, key_local, head_dim)
    pool_keys = cached_key_rows.reshape(pool_rows, key_local, head_dim)
    pool_values = cached_value_rows.reshape(pool_rows, key_local, head_dim)
    cache_end = jnp.cumsum(cached_length_list)
    cache_start = cache_end - cached_length_list
    slots = jnp.arange(pool_rows, dtype=jnp.int32)
    pool_allowed = (slots[None, :] >= cache_start[:, None]) & (slots[None, :] < cache_end[:, None])
    pool_allowed = pool_allowed[:, None, None, :]
    tree_allowed = jnp.repeat(reached > 0.5, group_factor, axis=1)[:, None, :, :]
    pool_scores = (
        jnp.einsum("rkqd,pkd->rkqp", query_rows, pool_keys, preferred_element_type=jnp.float32)
        * score_scale
    )
    tree_scores = (
        jnp.einsum("rkqd,rmkd->rkqm", query_rows, request_keys, preferred_element_type=jnp.float32)
        * score_scale
    )
    top = jnp.maximum(
        jnp.max(jnp.where(pool_allowed, pool_scores, masked_score), axis=3),
        jnp.max(jnp.where(tree_allowed, tree_scores, masked_score), axis=3),
    )
    pool_weights = jnp.where(pool_allowed, jnp.exp(pool_scores - top[..., None]), 0.0).astype(
        jnp.bfloat16
    )
    tree_weights = jnp.where(tree_allowed, jnp.exp(tree_scores - top[..., None]), 0.0).astype(
        jnp.bfloat16
    )
    totals = jnp.sum(pool_weights.astype(jnp.float32), axis=3) + jnp.sum(
        tree_weights.astype(jnp.float32), axis=3
    )
    weighted_values = jnp.einsum(
        "rkqp,pkd->rkqd", pool_weights, pool_values, preferred_element_type=jnp.float32
    ) + jnp.einsum(
        "rkqm,rmkd->rkqd", tree_weights, request_values, preferred_element_type=jnp.float32
    )
    attended = (
        (weighted_values / totals[..., None])
        .reshape(local_requests, key_local, draft_length, group_factor, head_dim)
        .transpose(0, 2, 1, 3, 4)
        .reshape(token_rows, query_local * head_dim)
        .astype(jnp.bfloat16)
    )
    attend_part = jnp.dot(attended, out_weight, preferred_element_type=jnp.float32)
    chunk_rows = token_rows // vocab_shards
    chunk_start = vocab_shard * chunk_rows
    residual_chunk = lax.dynamic_slice_in_dim(states, chunk_start, chunk_rows, 0) + scatter_rows(
        attend_part, "vocab", vocab_shards
    )
    hidden_chunk = (
        residual_chunk
        * lax.rsqrt(jnp.mean(residual_chunk * residual_chunk, axis=1, keepdims=True) + eps_norm)
        * hidden_gain.astype(jnp.float32)
    ).astype(jnp.bfloat16)
    hidden_in = gather_rows(hidden_chunk, "vocab", vocab_shards)
    gate_out = jnp.dot(hidden_in, gate_weight, preferred_element_type=jnp.float32)
    up_out = jnp.dot(hidden_in, up_weight, preferred_element_type=jnp.float32)
    hidden = (jax.nn.silu(gate_out) * up_out).astype(jnp.bfloat16)
    down_part = jnp.dot(hidden, down_weight, preferred_element_type=jnp.float32)
    feed_chunk = scatter_rows(down_part, "vocab", vocab_shards).astype(jnp.bfloat16)
    local_counts = lax.dynamic_slice_in_dim(
        live_draft_count, request_shard * local_requests, local_requests
    )
    chunk_token = chunk_start + jnp.arange(chunk_rows, dtype=jnp.int32)
    chunk_count = jnp.take(local_counts, chunk_token // draft_length)
    chunk_live = (chunk_token % draft_length) < chunk_count
    layer_chunk = jnp.where(
        chunk_live[:, None], residual_chunk + feed_chunk.astype(jnp.float32), 0.0
    ).astype(jnp.bfloat16)
    updated = gather_rows(layer_chunk, "vocab", vocab_shards)
    share_width = model_width // vocab_shards
    layer_part = lax.dynamic_slice_in_dim(updated, vocab_shard * share_width, share_width, 1)
    path_length = path_index.shape[1]
    request_picker = (
        path_index[:, :, None] == jnp.arange(draft_length, dtype=jnp.int32)[None, None, :]
    ).astype(jnp.bfloat16)
    accepted_keys = jnp.einsum(
        "ytm,ymu->ytu",
        request_picker,
        fresh_keys.reshape(local_requests, draft_length, key_local * head_dim),
        preferred_element_type=jnp.float32,
    ).astype(jnp.bfloat16)
    accepted_values = jnp.einsum(
        "ytm,ymu->ytu",
        request_picker,
        fresh_values.reshape(local_requests, draft_length, key_local * head_dim),
        preferred_element_type=jnp.float32,
    ).astype(jnp.bfloat16)
    per_shard = path_length // vocab_shards
    head_picker = lax.dynamic_slice_in_dim(request_picker, vocab_shard * per_shard, per_shard, 1)
    head_rows = jnp.einsum(
        "ytm,ymu->ytu",
        head_picker,
        updated.reshape(local_requests, draft_length, model_width),
        preferred_element_type=jnp.float32,
    ).astype(jnp.bfloat16)
    flat_rows = head_rows.reshape(local_requests * per_shard, model_width).astype(jnp.float32)
    mean_square = jnp.mean(flat_rows * flat_rows, axis=1)
    norm_values = jnp.sqrt(mean_square + eps_norm).reshape(local_requests, per_shard)
    head_in = (
        flat_rows * lax.rsqrt(mean_square + eps_norm)[:, None] * final_gain.astype(jnp.float32)
    ).astype(jnp.bfloat16)
    local_max = jnp.max(
        jnp.dot(
            gather_rows(head_in, "req", request_shards),
            head_weight,
            preferred_element_type=jnp.float32,
        ),
        axis=1,
    )
    every_max = gather_rows(local_max[None], "req", request_shards)
    maxima = jnp.max(every_max, axis=0).reshape(request_shards * local_requests, per_shard)
    return (
        layer_part.reshape(local_requests, draft_length, share_width),
        accepted_keys,
        accepted_values,
        norm_values,
        maxima,
    )


def solution(mesh):
    in_specs = (
        P("req", None, None),
        P("req", None),
        P(),
        P("req", None),
        P("req"),
        P("req", "vocab"),
        P("req", "vocab"),
        P(),
        P(),
        P(),
        P(None, "vocab"),
        P(None, "vocab"),
        P(None, "vocab"),
        P("vocab", None),
        P(None, "vocab"),
        P(None, "vocab"),
        P("vocab", None),
        P(None, "req"),
    )
    out_specs = (
        P("req", None, "vocab"),
        P("req", None, "vocab"),
        P("req", None, "vocab"),
        P("req", "vocab"),
        P(None, "vocab"),
    )
    return jax.shard_map(
        per_device, mesh=mesh, in_specs=in_specs, out_specs=out_specs, check_vma=False
    )
```

time: 433 us -> 152 us (0.35)
  blocking collectives: 119 us -> 11.3 us
  waiting for transfers between devices: 144 us -> 44.9 us
  local copies, waits for them, and re-layouts: 44.3 us -> 18.3 us
  loops' own time: 17.2 us -> 0 us
  matrix products: 37.8 us -> 23.8 us
  between operations: 14.6 us -> 0.92 us
  starting transfers between devices: 20 us -> 30.9 us
  other arithmetic: 30.5 us -> 20.2 us
    psum x2 -> x0, waiting for transfers between devices: 122 us -> none  [the longest x1 61.5 us: per_device(): residual = states + lax.psum(attend_part, 'vocab')]
    pmax x1 -> x0, blocking collectives: 72.8 us -> none  [per_device(): lax.pmax(local_max, 'req')]
    all_gather x1 -> x0, blocking collectives: 46.6 us -> none  [per_device(): lax.all_gather(head_in, 'req', axis=0, tiled=True)]
    all_to_all x2 -> x5, waiting for transfers between devices: 22.1 us -> 44.9 us  [the longest x3 25 us: gather_rows(): lax.all_to_all(copies, axis_name, split_axis=0, concat_axis=0, tiled=True)]
    another operation x6 -> x0, loops' own time: 17.2 us -> none  [the longest x2 6.2 us: span_sums(): return lax.fori_loop(0, block_count, step, start_sums)]
    dot_general x21 -> x8, matrix products: 27.7 us -> 13.1 us  [the longest x1 3.55 us: per_device(): down_part = jnp.dot(hidden, down_weight, preferred_element_type=jnp.float32)]
    all_to_all x0 -> x1, blocking collectives: none -> 11.3 us  [gather_rows(): lax.all_to_all(copies, axis_name, split_axis=0, concat_axis=0, tiled=True)]
    all_to_all x2 -> x5, starting transfers between devices: 19.9 us -> 30.9 us  [the longest x3 18.9 us: gather_rows(): lax.all_to_all(copies, axis_name, split_axis=0, concat_axis=0, tiled=True)]
  transfers between devices with their start and end apart: 4 -> 5, of which waited for: 4 -> 5; matrix products, arithmetic and copies ran while one was open for 2% -> 5% of each run, Pallas kernels for 0% -> 0%
where the time goes in v1:
time: 152 us; the launch traced here: 150 us
  waiting for transfers between devices  44.9 us (30%)
  starting transfers between devices  30.9 us (20%)
  matrix products  23.8 us (16%)
  other arithmetic  20.2 us (13%)
  local copies, waits for them, and re-layouts  18.3 us (12%)
  blocking collectives  11.3 us (7%)
    all_to_all x3, waiting for transfers between devices, gather_rows(): lax.all_to_all(copies, axis_name, split_axis=0, concat_axis=0, tiled=True)  25 us
    all_to_all x2, waiting for transfers between devices, scatter_rows(): lax.all_to_all(pieces, axis_name, split_axis=0, concat_axis=0, tiled=True)  19.9 us
    all_to_all x3, starting transfers between devices, gather_rows(): lax.all_to_all(copies, axis_name, split_axis=0, concat_axis=0, tiled=True)  18.9 us
    all_to_all x2, starting transfers between devices, scatter_rows(): lax.all_to_all(pieces, axis_name, split_axis=0, concat_axis=0, tiled=True)  12 us
    all_to_all x1, blocking collectives, gather_rows(): lax.all_to_all(copies, axis_name, split_axis=0, concat_axis=0, tiled=True)  11.3 us
    dot_general x1, matrix products, per_device(): down_part = jnp.dot(hidden, down_weight, preferred_element_type=jnp.float32)  3.55 us
    another operation x3, other arithmetic  3.4 us
    convert_element_type x2, local copies, waits for them, and re-layouts, per_device(): attended = (weighted_values / totals[..., None]).reshape(local_requests,...  3.09 us
  transfers between devices with their start and end apart: 5, of which 5 were waited for; matrix products, arithmetic and copies ran while one was open for 5% of the time, Pallas kernels for 0%

profile of v1, /device:TPU:2, one launch (start us, length us, event | category | flops | bytes accessed | tf_op | source)
XLA Modules:
  0.0 150.3 jit_solution(1504727906158168336)
XLA Ops:
  0.7 1.2 convolution_minimum_fusion.5
  2.7 0.8 fusion.46
  5.0 1.2 multiply_reduce_fusion
  6.8 1.2 multiply_convert_fusion.1
  8.1 1.4 fusion.47
  10.3 0.9 copy.64
  11.9 0.9 multiply_convert_fusion
  12.8 0.7 copy-done.2
  13.5 1.2 convolution_bitcast_fusion.2
  14.7 1.5 fusion.27
  16.3 0.8 copy.82
  17.1 0.9 broadcast_compare_fusion
  18.7 1.5 %broadcast_in_dim_reshape.3 = pred[2,128,64]{2,1,0:T(32,128)(4,1)} reshape(pred[2,64,2,64]{3,2,1,0:T(4,128)(4,1)} %broadcast_in_dim.52) | data formatting | bytes 32768 | tf_op jit(solution)/shard_map/broadcast_in_dim;reshape | solution.py:127
  20.2 1.4 copy.69
  21.6 1.3 reduce-window.8
  23.6 0.7 compare_and_fusion
  24.4 1.6 %select_reduce_fusion = (f32[2,128]{1,0:T(2,128)S(1)}, f32[2,1,128,2048]{3,2,0,1:T(8,128)S(1)}) fusion(pred[2,2048]{1,0:T(4,128)(4,1)S(1)} %compare_and_fusion, bf16[2048,96]{0,1:T(8,128)(2,1)} %param.23, bf16[2,128,48]{1,2,0:T(8,128)(2,1)} %copy.66, bf16[2,128,48]{1,2,0:T(8,128)(2,1)S(1)} %copy.65), kind=kOutput, calls=%fused_computation.4 | convolution fusion | flops 102334208 | bytes 2544640 | tf_op jit(solution)/shard_map/rkqd,pkd->rkqp/dot_general | solution.py:129
  27.4 1.2 convolution_bitcast_fusion
  28.6 0.9 convolution_convert_fusion
  29.5 1.4 copy.71
  31.6 1.8 %fusion.5 = bf16[2,1,128,96]{2,3,0,1:T(8,128)(2,1)} fusion(f32[2,1,128,96]{2,3,0,1:T(8,128)} %convolution_bitcast_fusion, bf16[2,64,96]{2,1,0:T(8,128)(2,1)} %bitcast.122, f32[2,128]{1,0:T(2,128)S(1)} %add.187, pred[2,128,64]{1,2,0:T(32,128)(4,1)S(1)} %copy-done.10, f32[2,128,64]{1,2,0:T(8,128)} %copy-done.7, f32[2,128]{1,0:T(2,128)S(1)} %max.9), kind=kOutput, calls=%fused_computation.13 | convolution fusion | flops 3268608 | bytes 256000 | tf_op jit(solution)/shard_map/rkqm,rmkd->rkqd/dot_general | solution.py:151
  33.4 1.5 %copy.72 = bf16[2,1,128,96]{3,2,0,1:T(8,128)(2,1)} copy(bf16[2,1,128,96]{2,3,0,1:T(8,128)(2,1)} %fusion.5) | data formatting | bytes 98304 | tf_op jit(solution)/shard_map/convert_element_type | solution.py:159
  34.9 1.6 %convert_element_type.145 = bf16[8,16,192]{2,1,0:T(8,128)(2,1)} reshape(bf16[2,1,128,96]{3,2,0,1:T(8,128)(2,1)} %copy.72) | data formatting | bytes 98304 | tf_op jit(solution)/shard_map/convert_element_type | solution.py:159
  36.5 2.2 %fusion.7 = f32[8,16,1536]{2,1,0:T(8,128)} fusion(bf16[8,16,192]{2,1,0:T(8,128)(2,1)} %convert_element_type.145, bf16[192,1536]{1,0:T(8,128)(2,1)} %param.31), kind=kOutput, calls=%fused_computation.29 | convolution fusion | flops 75497472 | bytes 1425408 | tf_op jit(solution)/shard_map/dot_general | solution.py:161
  38.7 6.3 %all-to-all-start = ((f32[8,16,1536]{2,1,0:T(8,128)}), f32[8,16,1536]{2,1,0:T(8,128)}, u32[]{:S(2)}, u32[]{:S(2)}) async-start(f32[8,16,1536]{2,1,0:T(8,128)} %fusion.7), calls=%async_computation | async-start | bytes 1572864 | tf_op jit(solution)/shard_map/all_to_all | solution.py:44
  45.7 1.0 bitcast_convert_fusion.1
  46.7 10.1 %all-to-all-done = f32[8,16,1536]{2,1,0:T(8,128)} async-done(((f32[8,16,1536]{2,1,0:T(8,128)}), f32[8,16,1536]{2,1,0:T(8,128)}, u32[]{:S(2)}, u32[]{:S(2)}) %all-to-all-start) | async-done | bytes 786464 | tf_op jit(solution)/shard_map/all_to_all | solution.py:44
  56.8 1.2 reduce_sum.76
  58.0 1.0 multiply_reduce_fusion.1
  59.8 11.3 %all_to_all.30 = bf16[8,16,1536]{2,1,0:T(8,128)(2,1)S(1)} all-to-all(bf16[8,16,1536]{2,1,0:T(8,128)(2,1)S(1)} %broadcast_in_dim.56), channel_id=1, replica_groups=mesh['req'=32,'vocab'=8] {'vocab'}, dimensions={0} | all-to-all | bytes 786432 | tf_op jit(solution)/shard_map/all_to_all | solution.py:50
  71.1 2.5 %fusion.48 = f32[128,512]{1,0:T(8,128)} fusion(bf16[128,1536]{1,0:T(8,128)(2,1)S(1)} %bitcast.109, bf16[1536,512]{1,0:T(8,128)(2,1)} %param.32), kind=kOutput, calls=%fused_computation.116 | convolution fusion | flops 201326592 | bytes 2228224 | tf_op jit(solution)/shard_map/dot_general | solution.py:173
  73.6 3.6 %fusion.2 = f32[128,1536]{1,0:T(8,128)} fusion(bf16[512,1536]{1,0:T(8,128)(2,1)} %param.34, bf16[128,1536]{1,0:T(8,128)(2,1)S(1)} %bitcast.110, bf16[1536,512]{1,0:T(8,128)(2,1)} %param.33, f32[128,512]{1,0:T(8,128)} %fusion.48), kind=kOutput, calls=%fused_computation.8 | convolution fusion | flops 403046400 | bytes 4587520 | tf_op jit(solution)/shard_map/dot_general | solution.py:176
  77.1 5.7 %all-to-all-start.2 = ((f32[8,16,1536]{2,1,0:T(8,128)}), f32[8,16,1536]{2,1,0:T(8,128)}, u32[]{:S(2)}, u32[]{:S(2)}) async-start(f32[8,16,1536]{2,1,0:T(8,128)} %bitcast.111), calls=%async_computation.2 | async-start | bytes 1572864 | tf_op jit(solution)/shard_map/all_to_all | solution.py:44
  83.5 1.3 fusion.37
  84.8 9.8 %all-to-all-done.2 = f32[8,16,1536]{2,1,0:T(8,128)} async-done(((f32[8,16,1536]{2,1,0:T(8,128)}), f32[8,16,1536]{2,1,0:T(8,128)}, u32[]{:S(2)}, u32[]{:S(2)}) %all-to-all-start.2) | async-done | bytes 786464 | tf_op jit(solution)/shard_map/all_to_all | solution.py:44
  94.6 1.2 reduce_sum.78
  95.9 0.8 broadcast_in_dim.58
  96.7 4.8 %all-to-all-start.3 = ((bf16[8,16,1536]{2,1,0:T(8,128)(2,1)}), bf16[8,16,1536]{2,1,0:T(8,128)(2,1)S(1)}, u32[]{:S(2)}, u32[]{:S(2)}) async-start(bf16[8,16,1536]{2,1,0:T(8,128)(2,1)} %broadcast_in_dim.58), calls=%async_computation.3 | async-start | bytes 786432 | tf_op jit(solution)/shard_map/all_to_all | solution.py:50
  101.7 7.3 %all-to-all-done.3 = bf16[8,16,1536]{2,1,0:T(8,128)(2,1)S(1)} async-done(((bf16[8,16,1536]{2,1,0:T(8,128)(2,1)}), bf16[8,16,1536]{2,1,0:T(8,128)(2,1)S(1)}, u32[]{:S(2)}, u32[]{:S(2)}) %all-to-all-start.3) | async-done | bytes 393248 | tf_op jit(solution)/shard_map/all_to_all | solution.py:50
  109.9 0.8 broadcast_in_dim.59
  110.6 10.1 %all-to-all-start.4 = ((bf16[32,2,1536]{2,1,0:T(2,128)(2,1)}), bf16[32,2,1536]{2,1,0:T(2,128)(2,1)}, u32[]{:S(2)}, u32[]{:S(2)}) async-start(bf16[32,2,1536]{2,1,0:T(2,128)(2,1)} %broadcast_in_dim.59), calls=%async_computation.4 | async-start | bytes 393216 | tf_op jit(solution)/shard_map/all_to_all | solution.py:50
  120.7 0.8 convolution_convert_fusion.2
  121.5 1.5 convolution_convert_fusion.1
  123.0 8.6 %all-to-all-done.4 = bf16[32,2,1536]{2,1,0:T(2,128)(2,1)} async-done(((bf16[32,2,1536]{2,1,0:T(2,128)(2,1)}), bf16[32,2,1536]{2,1,0:T(2,128)(2,1)}, u32[]{:S(2)}, u32[]{:S(2)}) %all-to-all-start.4) | async-done | bytes 196640 | tf_op jit(solution)/shard_map/all_to_all | solution.py:50
  131.6 1.7 %reshape.516 = bf16[64,1536]{1,0:T(8,128)(2,1)} reshape(bf16[32,2,1536]{2,1,0:T(2,128)(2,1)} %all-to-all-done.4) | data formatting | bytes 393216 | tf_op jit(solution)/shard_map/reshape | solution.py:51
  133.3 2.1 %convolution_reduce_fusion = f32[64]{0:T(128)S(1)} fusion(bf16[64,1536]{1,0:T(8,128)(2,1)} %reshape.516, bf16[1536,1000]{0,1:T(8,128)(2,1)S(1)} %copy-done), kind=kOutput, calls=%fused_computation.7 | convolution fusion | flops 196671936 | bytes 3268864 | tf_op jit(solution)/shard_map/dot_general | solution.py:221
  136.0 4.0 %all-to-all-start.5 = ((f32[32,1,64]{2,1,0:T(1,128)}), f32[32,1,64]{2,1,0:T(1,128)S(1)}, u32[]{:S(2)}, u32[]{:S(2)}) async-start(f32[32,1,64]{2,1,0:T(1,128)} %broadcast_in_dim.60), calls=%async_computation.5 | async-start | bytes 32768 | tf_op jit(solution)/shard_map/all_to_all | solution.py:50
  140.7 9.1 %all-to-all-done.5 = f32[32,1,64]{2,1,0:T(1,128)S(1)} async-done(((f32[32,1,64]{2,1,0:T(1,128)}), f32[32,1,64]{2,1,0:T(1,128)S(1)}, u32[]{:S(2)}, u32[]{:S(2)}) %all-to-all-start.5) | async-done | bytes 8224 | tf_op jit(solution)/shard_map/all_to_all | solution.py:50
  (77 shorter events, 13.3 us)
Async XLA Ops:
  0.6 132.6 %copy-start = (bf16[1536,1000]{0,1:T(8,128)(2,1)S(1)}, bf16[1536,1000]{0,1:T(8,128)(2,1)}, u32[]{:S(2)}) copy-start(bf16[1536,1000]{0,1:T(8,128)(2,1)} %param.35) | copy-start | bytes 9216004
  0.6 11.2 %copy-start.1 = (bf16[2,64,1536]{2,1,0:T(8,128)(2,1)S(1)}, bf16[2,64,1536]{2,1,0:T(8,128)(2,1)}, u32[]{:S(2)}) copy-start(bf16[2,64,1536]{2,1,0:T(8,128)(2,1)} %param.18) | copy-start | bytes 1179652
  0.7 9.4 %copy-start.13 = (f32[48]{0:T(128)}, f32[48]{0:T(128)S(1)}, u32[]{:S(2)}) copy-start(f32[48]{0:T(128)S(1)} %multiply_power_fusion) | copy-start | bytes 580
  4.3 5.8 %copy-start.14 = (f32[128]{0:T(128)}, f32[128]{0:T(128)S(1)}, u32[]{:S(2)}) copy-start(f32[128]{0:T(128)S(1)} %convert_element_type.137) | copy-start | bytes 1540
  5.0 5.1 %copy-start.11 = (f32[1536]{0:T(1024)}, f32[1536]{0:T(1024)S(1)}, u32[]{:S(2)}) copy-start(f32[1536]{0:T(1024)S(1)} %convert_element_type.130) | copy-start | bytes 18436
  12.8 0.7 copy-start.2
  22.9 3.1 %copy-start.8 = (bf16[2,128,48]{1,2,0:T(8,128)(2,1)S(1)}, bf16[2,128,48]{1,2,0:T(8,128)(2,1)}, u32[]{:S(2)}) copy-start(bf16[2,128,48]{1,2,0:T(8,128)(2,1)} %copy.66) | copy-start | bytes 73732
  23.0 3.1 %copy-start.9 = (pred[2,128,64]{1,2,0:T(32,128)(4,1)S(1)}, pred[2,128,64]{1,2,0:T(32,128)(4,1)}, u32[]{:S(2)}) copy-start(pred[2,128,64]{1,2,0:T(32,128)(4,1)} %copy.69) | copy-start | bytes 49156
  24.4 3.0 %copy-start.16 = (bf16[2048,96]{0,1:T(8,128)(2,1)S(1)}, bf16[2048,96]{0,1:T(8,128)(2,1)}, u32[]{:S(2)}) copy-start(bf16[2048,96]{0,1:T(8,128)(2,1)} %param.24) | copy-start | bytes 1179652
  26.3 0.6 copy-start.7
  26.9 1.7 %copy-start.3 = (bf16[128,1536]{1,0:T(8,128)(2,1)S(1)}, bf16[128,1536]{1,0:T(8,128)(2,1)}, u32[]{:S(2)}) copy-start(bf16[128,1536]{1,0:T(8,128)(2,1)} %copy-done.2) | copy-start | bytes 1179652
  26.9 1.7 %copy-start.6 = (bf16[1536,96]{0,1:T(8,128)(2,1)S(1)}, bf16[1536,96]{0,1:T(8,128)(2,1)}, u32[]{:S(2)}) copy-start(bf16[1536,96]{0,1:T(8,128)(2,1)} %param.30) | copy-start | bytes 884740
  27.4 4.2 %copy-start.10 = (pred[2,128,64]{1,2,0:T(32,128)(4,1)S(1)}, pred[2,128,64]{1,2,0:T(32,128)(4,1)}, u32[]{:S(2)}) copy-start(pred[2,128,64]{1,2,0:T(32,128)(4,1)} %copy.69) | copy-start | bytes 49156
  38.7 18.1 %all-to-all-start = ((f32[8,16,1536]{2,1,0:T(8,128)}), f32[8,16,1536]{2,1,0:T(8,128)}, u32[]{:S(2)}, u32[]{:S(2)}) async-start(f32[8,16,1536]{2,1,0:T(8,128)} %fusion.7), calls=%async_computation | async-start | bytes 1572864 | tf_op jit(solution)/shard_map/all_to_all | solution.py:44
  59.0 0.6 copy-start.4
  73.6 9.2 %copy-start.17 = (s32[64]{0:T(128)S(1)}, s32[64]{0:T(128)}, u32[]{:S(2)}) copy-start(s32[64]{0:T(128)} %param.20) | copy-start | bytes 772
  77.1 18.7 %copy-start.5 = (f32[16,1536]{1,0:T(8,128)S(1)}, f32[16,1536]{1,0:T(8,128)}, u32[]{:S(2)}) copy-start(f32[16,1536]{1,0:T(8,128)} %copy-done.4) | copy-start | bytes 294916
  77.1 24.3 %copy-start.15 = (s32[2,8]{1,0:T(2,128)S(1)}, s32[2,8]{1,0:T(2,128)}, u32[]{:S(2)}) copy-start(s32[2,8]{1,0:T(2,128)} %param.21) | copy-start | bytes 196
  77.1 24.4 %copy-start.12 = (bf16[1536]{0:T(1024)(128)(2,1)S(1)}, bf16[1536]{0:T(1024)(128)(2,1)}, u32[]{:S(2)}) copy-start(bf16[1536]{0:T(1024)(128)(2,1)} %param.27) | copy-start | bytes 9220
  77.1 17.5 %all-to-all-start.2 = ((f32[8,16,1536]{2,1,0:T(8,128)}), f32[8,16,1536]{2,1,0:T(8,128)}, u32[]{:S(2)}, u32[]{:S(2)}) async-start(f32[8,16,1536]{2,1,0:T(8,128)} %bitcast.111), calls=%async_computation.2 | async-start | bytes 1572864 | tf_op jit(solution)/shard_map/all_to_all | solution.py:44
  96.7 12.3 %all-to-all-start.3 = ((bf16[8,16,1536]{2,1,0:T(8,128)(2,1)}), bf16[8,16,1536]{2,1,0:T(8,128)(2,1)S(1)}, u32[]{:S(2)}, u32[]{:S(2)}) async-start(bf16[8,16,1536]{2,1,0:T(8,128)(2,1)} %broadcast_in_dim.58), calls=%async_computation.3 | async-start | bytes 786432 | tf_op jit(solution)/shard_map/all_to_all | solution.py:50
  110.6 20.9 %all-to-all-start.4 = ((bf16[32,2,1536]{2,1,0:T(2,128)(2,1)}), bf16[32,2,1536]{2,1,0:T(2,128)(2,1)}, u32[]{:S(2)}, u32[]{:S(2)}) async-start(bf16[32,2,1536]{2,1,0:T(2,128)(2,1)} %broadcast_in_dim.59), calls=%async_computation.4 | async-start | bytes 393216 | tf_op jit(solution)/shard_map/all_to_all | solution.py:50
  136.0 13.9 %all-to-all-start.5 = ((f32[32,1,64]{2,1,0:T(1,128)}), f32[32,1,64]{2,1,0:T(1,128)S(1)}, u32[]{:S(2)}, u32[]{:S(2)}) async-start(f32[32,1,64]{2,1,0:T(1,128)} %broadcast_in_dim.60), calls=%async_computation.5 | async-start | bytes 32768 | tf_op jit(solution)/shard_map/all_to_all | solution.py:50

commit v2 on v1

--- a/solution.py
+++ b/solution.py
@@ -9,20 +9,6 @@
 eps_norm = 1e-05
 rope_base = 100000.0
 masked_score = -1e30
-
-
-def apply_rotation(values, token_positions):
-    half_dim = values.shape[-1] // 2
-    inverse = rope_base ** (-jnp.arange(half_dim, dtype=jnp.float32) * 2.0 / values.shape[-1])
-    angles = token_positions.astype(jnp.float32)[:, None] * inverse[None, :]
-    cosine = jnp.cos(angles)[:, None, :]
-    sine_of = jnp.sin(angles)[:, None, :]
-    first_half = values[..., :half_dim]
-    second_half = values[..., half_dim:]
-    return jnp.concatenate(
-        [first_half * cosine - second_half * sine_of, second_half * cosine + first_half * sine_of],
-        axis=-1,
-    )
 
 
 def ancestors(parents):
@@ -40,9 +26,9 @@
 
 def scatter_rows(partial, axis_name, shards):
     rows = partial.shape[0] // shards
-    pieces = partial.reshape(shards, rows, *partial.shape[1:])
+    pieces = partial.reshape(shards, rows, *partial.shape[1:]).astype(jnp.bfloat16)
     arrived = lax.all_to_all(pieces, axis_name, split_axis=0, concat_axis=0, tiled=True)
-    return jnp.sum(arrived, axis=0)
+    return jnp.sum(arrived.astype(jnp.float32), axis=0)
 
 
 def gather_rows(chunk, axis_name, shards):
@@ -92,50 +78,71 @@
     token_positions = (
         cached_length_list[:, None] + (jnp.sum(reached, axis=2) - 1.0).astype(jnp.int32)
     ).reshape(token_rows)
-    query_vectors = apply_rotation(
-        jnp.dot(normalized_states, query_weight, preferred_element_type=jnp.float32).reshape(
-            token_rows, query_local, head_dim
-        ),
-        token_positions,
-    ).astype(jnp.bfloat16)
-    fresh_keys = apply_rotation(
-        jnp.dot(normalized_states, key_matrix, preferred_element_type=jnp.float32).reshape(
-            token_rows, key_local, head_dim
-        ),
-        token_positions,
-    ).astype(jnp.bfloat16)
-    fresh_values = (
-        jnp.dot(normalized_states, value_matrix, preferred_element_type=jnp.float32)
-        .astype(jnp.bfloat16)
-        .reshape(token_rows, key_local, head_dim)
-    )
+    request_states = normalized_states.reshape(local_requests, draft_length, model_width)
+    request_positions = token_positions.reshape(local_requests, draft_length)
+    inverse = rope_base ** (-jnp.arange(head_dim // 2, dtype=jnp.float32) * 2.0 / head_dim)
+    angles = request_positions.astype(jnp.float32)[:, :, None] * inverse
+    cosine = jnp.cos(angles)
+    sine_of = jnp.sin(angles)
+
+    def rotate(values):
+        half = head_dim // 2
+        lift = (local_requests,) + (1,) * (values.ndim - 3) + (draft_length, half)
+        cos_b = cosine.reshape(lift)
+        sin_b = sine_of.reshape(lift)
+        first_half = values[..., :half]
+        second_half = values[..., half:]
+        return jnp.concatenate(
+            [first_half * cos_b - second_half * sin_b, second_half * cos_b + first_half * sin_b],
+            axis=-1,
+        )
+
+    query_rows = rotate(
+        jnp.einsum(
+            "rim,mkgd->rkgid",
+            request_states,
+            query_weight.reshape(model_width, key_local, group_factor, head_dim),
+            preferred_element_type=jnp.float32,
+        )
+    ).astype(jnp.bfloat16)
+    fresh_keys = rotate(
+        jnp.einsum(
+            "rim,mkd->rkid",
+            request_states,
+            key_matrix.reshape(model_width, key_local, head_dim),
+            preferred_element_type=jnp.float32,
+        )
+    ).astype(jnp.bfloat16)
+    fresh_values = jnp.einsum(
+        "rim,mkd->rkid",
+        request_states,
+        value_matrix.reshape(model_width, key_local, head_dim),
+        preferred_element_type=jnp.float32,
+    ).astype(jnp.bfloat16)
     score_scale = head_dim ** (-0.5)
-    query_rows = query_vectors.reshape(
-        local_requests, draft_length, key_local, group_factor, head_dim
-    ).transpose(0, 2, 1, 3, 4).reshape(
-        local_requests, key_local, draft_length * group_factor, head_dim
-    )
-    request_keys = fresh_keys.reshape(local_requests, draft_length, key_local, head_dim)
-    request_values = fresh_values.reshape(local_requests, draft_length, key_local, head_dim)
     pool_keys = cached_key_rows.reshape(pool_rows, key_local, head_dim)
     pool_values = cached_value_rows.reshape(pool_rows, key_local, head_dim)
-    cache_end = jnp.cumsum(cached_length_list)
-    cache_start = cache_end - cached_length_list
+    earlier = (
+        jnp.arange(local_requests, dtype=jnp.int32)[None, :]
+        < jnp.arange(local_requests, dtype=jnp.int32)[:, None]
+    )
+    cache_start = jnp.sum(jnp.where(earlier, cached_length_list[None, :], 0), axis=1)
+    cache_end = cache_start + cached_length_list
     slots = jnp.arange(pool_rows, dtype=jnp.int32)
     pool_allowed = (slots[None, :] >= cache_start[:, None]) & (slots[None, :] < cache_end[:, None])
-    pool_allowed = pool_allowed[:, None, None, :]
-    tree_allowed = jnp.repeat(reached > 0.5, group_factor, axis=1)[:, None, :, :]
+    pool_allowed = pool_allowed[:, None, None, None, :]
+    tree_allowed = (reached > 0.5)[:, None, None, :, :]
     pool_scores = (
-        jnp.einsum("rkqd,pkd->rkqp", query_rows, pool_keys, preferred_element_type=jnp.float32)
+        jnp.einsum("rkgid,pkd->rkgip", query_rows, pool_keys, preferred_element_type=jnp.float32)
         * score_scale
     )
     tree_scores = (
-        jnp.einsum("rkqd,rmkd->rkqm", query_rows, request_keys, preferred_element_type=jnp.float32)
+        jnp.einsum("rkgid,rkmd->rkgim", query_rows, fresh_keys, preferred_element_type=jnp.float32)
         * score_scale
     )
     top = jnp.maximum(
-        jnp.max(jnp.where(pool_allowed, pool_scores, masked_score), axis=3),
-        jnp.max(jnp.where(tree_allowed, tree_scores, masked_score), axis=3),
+        jnp.max(jnp.where(pool_allowed, pool_scores, masked_score), axis=4),
+        jnp.max(jnp.where(tree_allowed, tree_scores, masked_score), axis=4),
     )
     pool_weights = jnp.where(pool_allowed, jnp.exp(pool_scores - top[..., None]), 0.0).astype(
         jnp.bfloat16
@@ -143,22 +150,23 @@
     tree_weights = jnp.where(tree_allowed, jnp.exp(tree_scores - top[..., None]), 0.0).astype(
         jnp.bfloat16
     )
-    totals = jnp.sum(pool_weights.astype(jnp.float32), axis=3) + jnp.sum(
-        tree_weights.astype(jnp.float32), axis=3
+    totals = jnp.sum(pool_weights.astype(jnp.float32), axis=4) + jnp.sum(
+        tree_weights.astype(jnp.float32), axis=4
     )
     weighted_values = jnp.einsum(
-        "rkqp,pkd->rkqd", pool_weights, pool_values, preferred_element_type=jnp.float32
+        "rkgip,pkd->rkgid", pool_weights, pool_values, preferred_element_type=jnp.float32
     ) + jnp.einsum(
-        "rkqm,rmkd->rkqd", tree_weights, request_values, preferred_element_type=jnp.float32
-    )
-    attended = (
-        (weighted_values / totals[..., None])
-        .reshape(local_requests, key_local, draft_length, group_factor, head_dim)
-        .transpose(0, 2, 1, 3, 4)
-        .reshape(token_rows, query_local * head_dim)
-        .astype(jnp.bfloat16)
-    )
-    attend_part = jnp.dot(attended, out_weight, preferred_element_type=jnp.float32)
+        "rkgim,rkmd->rkgid", tree_weights, fresh_values, preferred_element_type=jnp.float32
+    )
+    attended = (weighted_values / totals[..., None]).astype(jnp.bfloat16)
+    attend_part = jnp.einsum(
+        "rkgid,kgdn->rin",
+        attended,
+        out_weight.reshape(key_local, group_factor, head_dim, model_width),
+        preferred_element_type=jnp.float32,
+    ).reshape(token_rows, model_width)
+    fresh_keys = fresh_keys.transpose(0, 2, 1, 3)
+    fresh_values = fresh_values.transpose(0, 2, 1, 3)
     chunk_rows = token_rows // vocab_shards
     chunk_start = vocab_shard * chunk_rows
     residual_chunk = lax.dynamic_slice_in_dim(states, chunk_start, chunk_rows, 0) + scatter_rows(

time: 152 us -> 118 us (0.78)
  local copies, waits for them, and re-layouts: 18.3 us -> 6.74 us
  waiting for transfers between devices: 44.9 us -> 37.1 us
  matrix products: 23.8 us -> 16.9 us
  other arithmetic: 20.2 us -> 14 us
    all_to_all x2, waiting for transfers between devices: 19.9 us -> 12.1 us  [scatter_rows(): lax.all_to_all(pieces, axis_name, split_axis=0, concat_axis=0, tiled=True)]
    convert_element_type x4 -> x0, local copies, waits for them, and re-layouts: 4.61 us -> none  [the longest x2 3.09 us: per_device(): attended = (weighted_values / totals[..., None]).reshape(local_requests,...]
    dot_general x8, matrix products: 10.5 us -> 5.89 us  [the longest x1 1.61 us: per_device(): jnp.einsum('rim,mkgd->rkgid', request_states, query_weight.reshape(model_...]
    another operation x5 -> x1, local copies, waits for them, and re-layouts: 3.93 us -> 0.01 us  [the longest x2 2.94 us: per_device(): jnp.repeat(reached > 0.5, group_factor, axis=1)[:, None, :, :]]
    another operation x3 -> x0, other arithmetic: 3.4 us -> none
    convert_element_type x3 -> x1, other arithmetic: 2.74 us -> 0.73 us  [per_device(): angles = request_positions.astype(jnp.float32)[:, :, None] * inverse]
    concatenate x4 -> x0, local copies, waits for them, and re-layouts: 1.72 us -> none  [apply_rotation(): jnp.concatenate([first_half * cosine - second_half * sine_of, second_half...]
    reduce_sum x4 -> x5, other arithmetic: 3.48 us -> 3.38 us  [the longest x2 1.85 us: scatter_rows(): return jnp.sum(arrived.astype(jnp.float32), axis=0)]
where the time goes in v2:
time: 118 us; the launch traced here: 117 us
  waiting for transfers between devices  37.1 us (31%)
  starting transfers between devices  30.2 us (26%)
  matrix products  16.9 us (14%)
  other arithmetic  14 us (12%)
  blocking collectives  11.3 us (10%)
  local copies, waits for them, and re-layouts  6.74 us (6%)
    all_to_all x3, waiting for transfers between devices, gather_rows(): lax.all_to_all(copies, axis_name, split_axis=0, concat_axis=0, tiled=True)  25 us
    all_to_all x3, starting transfers between devices, gather_rows(): lax.all_to_all(copies, axis_name, split_axis=0, concat_axis=0, tiled=True)  19 us
    all_to_all x2, waiting for transfers between devices, scatter_rows(): lax.all_to_all(pieces, axis_name, split_axis=0, concat_axis=0, tiled=True)  12.1 us
    all_to_all x1, blocking collectives, gather_rows(): lax.all_to_all(copies, axis_name, split_axis=0, concat_axis=0, tiled=True)  11.3 us
    all_to_all x2, starting transfers between devices, scatter_rows(): lax.all_to_all(pieces, axis_name, split_axis=0, concat_axis=0, tiled=True)  11.2 us
    dot_general x1, matrix products, per_device(): down_part = jnp.dot(hidden, down_weight, preferred_element_type=jnp.float32)  3.42 us
  transfers between devices with their start and end apart: 5, of which 5 were waited for; matrix products, arithmetic and copies ran while one was open for 5% of the time, Pallas kernels for 0%

profile of v2, /device:TPU:2, one launch (start us, length us, event | category | flops | bytes accessed | tf_op | source)
XLA Modules:
  0.0 117.3 jit_solution(11933971783348984384)
XLA Ops:
  0.7 0.9 fusion.45
  1.6 0.7 add.175
  2.4 0.7 convert_element_type.130
  3.1 1.2 multiply_reduce_fusion
  4.3 1.0 convolution_minimum_fusion.5
  6.4 0.7 add_convert_fusion.1
  7.3 1.6 %convolution_bitcast_fusion.1 = f32[2,1,2,64,96]{4,3,2,0,1:T(8,128)S(1)} fusion(bf16[1536,2,96,1]{0,2,1,3:T(8,128)(2,1)} %bitcast.156, bf16[2,64,1536]{2,1,0:T(8,128)(2,1)} %param.18, f32[1536]{0:T(1024)S(1)} %convert_element_type.130, f32[2,64]{1,0:T(2,128)S(1)} %add_rsqrt_fusion), kind=kOutput, calls=%fused_computation.11 | convolution fusion | flops 76283904 | bytes 1088000 | tf_op jit(solution)/shard_map/rim,mkgd->rkgid/dot_general | solution.py:101
  8.9 1.3 %convolution_bitcast_fusion.4 = f32[2,1,64,96]{3,2,0,1:T(8,128)S(1)} fusion(bf16[1536,96]{0,1:T(8,128)(2,1)} %param.29, bf16[2,64,1536]{2,1,0:T(8,128)(2,1)S(1)} %copy-done.2, f32[1536]{0:T(1024)S(1)} %convert_element_type.130, f32[2,64]{1,0:T(2,128)S(1)} %add_rsqrt_fusion), kind=kOutput, calls=%fused_computation.18 | convolution fusion | flops 38535168 | bytes 743936 | tf_op jit(solution)/shard_map/rim,mkd->rkid/dot_general | solution.py:109
  10.3 0.3 multiply_cosine_fusion.1
  10.6 1.0 fusion.36
  11.7 0.6 select_reduce_fusion
  12.3 0.3 select_reduce_fusion.1
  12.6 0.5 convert_reduce_fusion
  13.2 0.5 convolution_bitcast_fusion.3
  13.8 0.3 convolution_convert_fusion.1
  14.1 0.6 copy-done.6
  15.0 1.1 fusion.1
  16.1 6.2 %all-to-all-start = ((bf16[8,16,1536]{2,1,0:T(8,128)(2,1)}), bf16[8,16,1536]{2,1,0:T(8,128)(2,1)}, u32[]{:S(2)}, u32[]{:S(2)}) async-start(bf16[8,16,1536]{2,1,0:T(8,128)(2,1)} %fusion.1), calls=%async_computation | async-start | bytes 786432 | tf_op jit(solution)/shard_map/all_to_all | solution.py:30
  22.3 1.0 bitcast_convert_fusion.1
  23.3 6.6 %all-to-all-done = bf16[8,16,1536]{2,1,0:T(8,128)(2,1)} async-done(((bf16[8,16,1536]{2,1,0:T(8,128)(2,1)}), bf16[8,16,1536]{2,1,0:T(8,128)(2,1)}, u32[]{:S(2)}, u32[]{:S(2)}) %all-to-all-start) | async-done | bytes 393248 | tf_op jit(solution)/shard_map/all_to_all | solution.py:30
  29.9 1.2 %convert_reduce_fusion.1 = f32[16,1536]{1,0:T(8,128)S(1)} fusion(bf16[8,16,1536]{2,1,0:T(8,128)(2,1)} %all-to-all-done), kind=kLoop, calls=%fused_computation.30 | loop fusion | flops 368640 | bytes 491520 | tf_op jit(solution)/shard_map/reduce_sum | solution.py:31
  31.0 1.0 multiply_reduce_fusion.1
  32.1 0.6 copy-done.3
  32.8 11.3 %all_to_all.30 = bf16[8,16,1536]{2,1,0:T(8,128)(2,1)S(1)} all-to-all(bf16[8,16,1536]{2,1,0:T(8,128)(2,1)S(1)} %broadcast_in_dim.121), channel_id=1, replica_groups=mesh['req'=32,'vocab'=8] {'vocab'}, dimensions={0} | all-to-all | bytes 786432 | tf_op jit(solution)/shard_map/all_to_all | solution.py:36
  44.1 1.1 fusion.57
  45.2 3.4 %convolution_convert_fusion = bf16[128,1536]{1,0:T(8,128)(2,1)} fusion(bf16[512,1536]{1,0:T(8,128)(2,1)} %param.34, bf16[128,1536]{1,0:T(8,128)(2,1)S(1)} %bitcast.149, bf16[1536,512]{1,0:T(8,128)(2,1)} %param.33, f32[128,512]{1,0:T(8,128)} %fusion.57), kind=kOutput, calls=%fused_computation.4 | convolution fusion | flops 403243008 | bytes 4194304 | tf_op jit(solution)/shard_map/dot_general | solution.py:184
  48.6 5.0 %all-to-all-start.2 = ((bf16[8,16,1536]{2,1,0:T(8,128)(2,1)}), bf16[8,16,1536]{2,1,0:T(8,128)(2,1)S(1)}, u32[]{:S(2)}, u32[]{:S(2)}) async-start(bf16[8,16,1536]{2,1,0:T(8,128)(2,1)} %bitcast.151), calls=%async_computation.2 | async-start | bytes 786432 | tf_op jit(solution)/shard_map/all_to_all | solution.py:30
  53.7 0.6 fusion.55
  54.3 1.3 %fusion.46 = pred[16]{0:T(512)(128)(4,1)S(1)} fusion(s32[]{:T(128)} %bitcast.1, s32[]{:T(128)} %bitcast, s32[]{:T(128)S(6)} %mul.182), kind=kLoop, calls=%fused_computation.112 | loop fusion | flops 784 | bytes 28 | tf_op jit(solution)/shard_map/lt | solution.py:191
  55.6 5.5 %all-to-all-done.2 = bf16[8,16,1536]{2,1,0:T(8,128)(2,1)S(1)} async-done(((bf16[8,16,1536]{2,1,0:T(8,128)(2,1)}), bf16[8,16,1536]{2,1,0:T(8,128)(2,1)S(1)}, u32[]{:S(2)}, u32[]{:S(2)}) %all-to-all-start.2) | async-done | bytes 393248 | tf_op jit(solution)/shard_map/all_to_all | solution.py:30
  61.1 0.7 reduce_sum.91
  61.8 1.0 select_convert_fusion.3
  62.7 0.8 broadcast_in_dim.123
  63.5 4.8 %all-to-all-start.3 = ((bf16[8,16,1536]{2,1,0:T(8,128)(2,1)}), bf16[8,16,1536]{2,1,0:T(8,128)(2,1)S(1)}, u32[]{:S(2)}, u32[]{:S(2)}) async-start(bf16[8,16,1536]{2,1,0:T(8,128)(2,1)} %broadcast_in_dim.123), calls=%async_computation.3 | async-start | bytes 786432 | tf_op jit(solution)/shard_map/all_to_all | solution.py:36
  68.5 7.3 %all-to-all-done.3 = bf16[8,16,1536]{2,1,0:T(8,128)(2,1)S(1)} async-done(((bf16[8,16,1536]{2,1,0:T(8,128)(2,1)}), bf16[8,16,1536]{2,1,0:T(8,128)(2,1)S(1)}, u32[]{:S(2)}, u32[]{:S(2)}) %all-to-all-start.3) | async-done | bytes 393248 | tf_op jit(solution)/shard_map/all_to_all | solution.py:36
  76.1 0.5 fusion.48
  76.7 0.8 broadcast_in_dim.124
  77.5 10.2 %all-to-all-start.4 = ((bf16[32,2,1536]{2,1,0:T(2,128)(2,1)}), bf16[32,2,1536]{2,1,0:T(2,128)(2,1)}, u32[]{:S(2)}, u32[]{:S(2)}) async-start(bf16[32,2,1536]{2,1,0:T(2,128)(2,1)} %broadcast_in_dim.124), calls=%async_computation.4 | async-start | bytes 393216 | tf_op jit(solution)/shard_map/all_to_all | solution.py:36
  87.7 0.8 convolution_convert_fusion.3
  88.5 1.5 %convolution_convert_fusion.2 = bf16[2,8,96]{2,1,0:T(8,128)(2,1)} fusion(bf16[2,64,96]{2,1,0:T(8,128)(2,1)} %copy-done.6, pred[2,8,64]{2,0,1:T(4,128)(4,1)S(1)} %iota_compare_fusion.3), kind=kOutput, calls=%fused_computation.27 | convolution fusion | flops 198144 | bytes 28672 | tf_op jit(solution)/shard_map/ytm,ymu->ytu/dot_general | solution.py:208
  89.9 8.6 %all-to-all-done.4 = bf16[32,2,1536]{2,1,0:T(2,128)(2,1)} async-done(((bf16[32,2,1536]{2,1,0:T(2,128)(2,1)}), bf16[32,2,1536]{2,1,0:T(2,128)(2,1)}, u32[]{:S(2)}, u32[]{:S(2)}) %all-to-all-start.4) | async-done | bytes 196640 | tf_op jit(solution)/shard_map/all_to_all | solution.py:36
  98.5 1.7 %reshape.422 = bf16[64,1536]{1,0:T(8,128)(2,1)} reshape(bf16[32,2,1536]{2,1,0:T(2,128)(2,1)} %all-to-all-done.4) | data formatting | bytes 393216 | tf_op jit(solution)/shard_map/reshape | solution.py:37
  100.2 2.1 %convolution_reduce_fusion = f32[64]{0:T(128)S(1)} fusion(bf16[64,1536]{1,0:T(8,128)(2,1)} %reshape.422, bf16[1536,1000]{0,1:T(8,128)(2,1)S(1)} %copy-done), kind=kOutput, calls=%fused_computation.10 | convolution fusion | flops 196671936 | bytes 3268864 | tf_op jit(solution)/shard_map/dot_general | solution.py:229
  102.3 0.6 broadcast_in_dim.125
  102.9 4.0 %all-to-all-start.5 = ((f32[32,1,64]{2,1,0:T(1,128)}), f32[32,1,64]{2,1,0:T(1,128)S(1)}, u32[]{:S(2)}, u32[]{:S(2)}) async-start(f32[32,1,64]{2,1,0:T(1,128)} %broadcast_in_dim.125), calls=%async_computation.5 | async-start | bytes 32768 | tf_op jit(solution)/shard_map/all_to_all | solution.py:36
  106.9 0.7 constant_dynamic-slice_fusion
  107.7 9.1 %all-to-all-done.5 = f32[32,1,64]{2,1,0:T(1,128)S(1)} async-done(((f32[32,1,64]{2,1,0:T(1,128)}), f32[32,1,64]{2,1,0:T(1,128)S(1)}, u32[]{:S(2)}, u32[]{:S(2)}) %all-to-all-start.5) | async-done | bytes 8224 | tf_op jit(solution)/shard_map/all_to_all | solution.py:36
  116.7 0.5 reduce_max.39
  (65 shorter events, 2.5 us)
Async XLA Ops:
  0.6 99.6 %copy-start = (bf16[1536,1000]{0,1:T(8,128)(2,1)S(1)}, bf16[1536,1000]{0,1:T(8,128)(2,1)}, u32[]{:S(2)}) copy-start(bf16[1536,1000]{0,1:T(8,128)(2,1)} %param.35) | copy-start | bytes 9216004
  0.6 8.3 %copy-start.2 = (bf16[2,64,1536]{2,1,0:T(8,128)(2,1)S(1)}, bf16[2,64,1536]{2,1,0:T(8,128)(2,1)}, u32[]{:S(2)}) copy-start(bf16[2,64,1536]{2,1,0:T(8,128)(2,1)} %param.18) | copy-start | bytes 1179652
  0.7 9.5 %copy-start.12 = (f32[48]{0:T(128)}, f32[48]{0:T(128)S(1)}, u32[]{:S(2)}) copy-start(f32[48]{0:T(128)S(1)} %multiply_power_fusion) | copy-start | bytes 580
  3.1 7.1 %copy-start.8 = (f32[1536]{0:T(1024)}, f32[1536]{0:T(1024)S(1)}, u32[]{:S(2)}) copy-start(f32[1536]{0:T(1024)S(1)} %convert_element_type.130) | copy-start | bytes 18436
  4.3 5.9 %copy-start.14 = (f32[2,64]{1,0:T(2,128)}, f32[2,64]{1,0:T(2,128)S(1)}, u32[]{:S(2)}) copy-start(f32[2,64]{1,0:T(2,128)S(1)} %add_rsqrt_fusion) | copy-start | bytes 1540
  7.2 3.1 %copy-start.7 = (f32[2,64]{1,0:T(2,128)}, f32[2,64]{1,0:T(2,128)S(1)}, u32[]{:S(2)}) copy-start(f32[2,64]{1,0:T(2,128)S(1)} %add_convert_fusion.1) | copy-start | bytes 1540
  7.3 4.4 %copy-start.5 = (bf16[2048,96]{0,1:T(8,128)(2,1)S(1)}, bf16[2048,96]{0,1:T(8,128)(2,1)}, u32[]{:S(2)}) copy-start(bf16[2048,96]{0,1:T(8,128)(2,1)} %param.23) | copy-start | bytes 1179652
  11.7 1.5 %copy-start.16 = (bf16[2048,96]{0,1:T(8,128)(2,1)S(1)}, bf16[2048,96]{0,1:T(8,128)(2,1)}, u32[]{:S(2)}) copy-start(bf16[2048,96]{0,1:T(8,128)(2,1)} %param.24) | copy-start | bytes 1179652
  12.6 1.2 copy-start.9
  12.6 1.2 copy-start.15
  12.6 1.2 copy-start.17
  13.2 1.8 %copy-start.4 = (bf16[192,1536]{1,0:T(8,128)(2,1)S(1)}, bf16[192,1536]{1,0:T(8,128)(2,1)}, u32[]{:S(2)}) copy-start(bf16[192,1536]{1,0:T(8,128)(2,1)} %param.31) | copy-start | bytes 1769476
  13.7 8.6 %copy-start.10 = (bf16[1536]{0:T(1024)(128)(2,1)S(1)}, bf16[1536]{0:T(1024)(128)(2,1)}, u32[]{:S(2)}) copy-start(bf16[1536]{0:T(1024)(128)(2,1)} %param.26) | copy-start | bytes 9220
  14.1 0.6 copy-start.6
  16.1 13.8 %all-to-all-start = ((bf16[8,16,1536]{2,1,0:T(8,128)(2,1)}), bf16[8,16,1536]{2,1,0:T(8,128)(2,1)}, u32[]{:S(2)}, u32[]{:S(2)}) async-start(bf16[8,16,1536]{2,1,0:T(8,128)(2,1)} %fusion.1), calls=%async_computation | async-start | bytes 786432 | tf_op jit(solution)/shard_map/all_to_all | solution.py:30
  29.9 14.3 %copy-start.1 = (bf16[1536,512]{1,0:T(8,128)(2,1)S(1)}, bf16[1536,512]{1,0:T(8,128)(2,1)}, u32[]{:S(2)}) copy-start(bf16[1536,512]{1,0:T(8,128)(2,1)} %param.32) | copy-start | bytes 4718596
  32.1 0.6 copy-start.3
  45.2 8.4 %copy-start.18 = (s32[64]{0:T(128)S(1)}, s32[64]{0:T(128)}, u32[]{:S(2)}) copy-start(s32[64]{0:T(128)} %param.20) | copy-start | bytes 772
  48.6 19.7 %copy-start.13 = (s32[2,8]{1,0:T(2,128)S(1)}, s32[2,8]{1,0:T(2,128)}, u32[]{:S(2)}) copy-start(s32[2,8]{1,0:T(2,128)} %param.21) | copy-start | bytes 196
  48.6 19.7 %copy-start.11 = (bf16[1536]{0:T(1024)(128)(2,1)S(1)}, bf16[1536]{0:T(1024)(128)(2,1)}, u32[]{:S(2)}) copy-start(bf16[1536]{0:T(1024)(128)(2,1)} %param.27) | copy-start | bytes 9220
  48.6 12.4 %all-to-all-start.2 = ((bf16[8,16,1536]{2,1,0:T(8,128)(2,1)}), bf16[8,16,1536]{2,1,0:T(8,128)(2,1)S(1)}, u32[]{:S(2)}, u32[]{:S(2)}) async-start(bf16[8,16,1536]{2,1,0:T(8,128)(2,1)} %bitcast.151), calls=%async_computation.2 | async-start | bytes 786432 | tf_op jit(solution)/shard_map/all_to_all | solution.py:30
  63.5 12.3 %all-to-all-start.3 = ((bf16[8,16,1536]{2,1,0:T(8,128)(2,1)}), bf16[8,16,1536]{2,1,0:T(8,128)(2,1)S(1)}, u32[]{:S(2)}, u32[]{:S(2)}) async-start(bf16[8,16,1536]{2,1,0:T(8,128)(2,1)} %broadcast_in_dim.123), calls=%async_computation.3 | async-start | bytes 786432 | tf_op jit(solution)/shard_map/all_to_all | solution.py:36
  77.5 21.1 %all-to-all-start.4 = ((bf16[32,2,1536]{2,1,0:T(2,128)(2,1)}), bf16[32,2,1536]{2,1,0:T(2,128)(2,1)}, u32[]{:S(2)}, u32[]{:S(2)}) async-start(bf16[32,2,1536]{2,1,0:T(2,128)(2,1)} %broadcast_in_dim.124), calls=%async_computation.4 | async-start | bytes 393216 | tf_op jit(solution)/shard_map/all_to_all | solution.py:36
  102.9 13.9 %all-to-all-start.5 = ((f32[32,1,64]{2,1,0:T(1,128)}), f32[32,1,64]{2,1,0:T(1,128)S(1)}, u32[]{:S(2)}, u32[]{:S(2)}) async-start(f32[32,1,64]{2,1,0:T(1,128)} %broadcast_in_dim.125), calls=%async_computation.5 | async-start | bytes 32768 | tf_op jit(solution)/shard_map/all_to_all | solution.py:36

commit v3 on v2

--- a/solution.py
+++ b/solution.py
@@ -169,8 +169,59 @@
     fresh_values = fresh_values.transpose(0, 2, 1, 3)
     chunk_rows = token_rows // vocab_shards
     chunk_start = vocab_shard * chunk_rows
-    residual_chunk = lax.dynamic_slice_in_dim(states, chunk_start, chunk_rows, 0) + scatter_rows(
-        attend_part, "vocab", vocab_shards
+    share_width = model_width // vocab_shards
+    share_start = vocab_shard * share_width
+    path_length = path_index.shape[1]
+    per_shard = path_length // vocab_shards
+    path_count = local_requests * per_shard
+    path_rows_all = (
+        (
+            path_index.reshape(local_requests, vocab_shards, per_shard)
+            + (jnp.arange(local_requests, dtype=jnp.int32) * draft_length)[:, None, None]
+        )
+        .transpose(1, 0, 2)
+        .reshape(vocab_shards, path_count)
+    )
+    own_path_rows = lax.dynamic_index_in_dim(path_rows_all, vocab_shard, keepdims=False)
+
+    def row_pieces(partial):
+        return partial.reshape(vocab_shards, chunk_rows * model_width)
+
+    def column_pieces(partial):
+        return (
+            partial.reshape(token_rows, vocab_shards, share_width)
+            .transpose(1, 0, 2)
+            .reshape(vocab_shards, token_rows * share_width)
+        )
+
+    def path_pieces(partial):
+        return jnp.take(partial, path_rows_all.reshape(-1), axis=0).reshape(
+            vocab_shards, path_count * model_width
+        )
+
+    def exchange(pieces):
+        widths = [piece.shape[1] for piece in pieces]
+        packed = jnp.concatenate([piece.astype(jnp.bfloat16) for piece in pieces], axis=1)
+        arrived = lax.all_to_all(packed, "vocab", split_axis=0, concat_axis=0, tiled=True)
+        summed = jnp.sum(arrived.astype(jnp.float32), axis=0)
+        parts = []
+        at = 0
+        for width in widths:
+            parts.append(summed[at : at + width])
+            at += width
+        return parts
+
+    attn_rows, attn_cols, attn_path = exchange(
+        [row_pieces(attend_part), column_pieces(attend_part), path_pieces(attend_part)]
+    )
+    residual_chunk = lax.dynamic_slice_in_dim(
+        states, chunk_start, chunk_rows, 0
+    ) + attn_rows.reshape(chunk_rows, model_width)
+    residual_cols = lax.dynamic_slice_in_dim(
+        states, share_start, share_width, 1
+    ) + attn_cols.reshape(token_rows, share_width)
+    residual_path = jnp.take(states, own_path_rows, axis=0) + attn_path.reshape(
+        path_count, model_width
     )
     hidden_chunk = (
         residual_chunk
@@ -182,20 +233,23 @@
     up_out = jnp.dot(hidden_in, up_weight, preferred_element_type=jnp.float32)
     hidden = (jax.nn.silu(gate_out) * up_out).astype(jnp.bfloat16)
     down_part = jnp.dot(hidden, down_weight, preferred_element_type=jnp.float32)
-    feed_chunk = scatter_rows(down_part, "vocab", vocab_shards).astype(jnp.bfloat16)
+    feed_cols, feed_path = exchange([column_pieces(down_part), path_pieces(down_part)])
+    feed_cols = feed_cols.reshape(token_rows, share_width).astype(jnp.bfloat16)
+    feed_path = feed_path.reshape(path_count, model_width).astype(jnp.bfloat16)
     local_counts = lax.dynamic_slice_in_dim(
         live_draft_count, request_shard * local_requests, local_requests
     )
-    chunk_token = chunk_start + jnp.arange(chunk_rows, dtype=jnp.int32)
-    chunk_count = jnp.take(local_counts, chunk_token // draft_length)
-    chunk_live = (chunk_token % draft_length) < chunk_count
-    layer_chunk = jnp.where(
-        chunk_live[:, None], residual_chunk + feed_chunk.astype(jnp.float32), 0.0
-    ).astype(jnp.bfloat16)
-    updated = gather_rows(layer_chunk, "vocab", vocab_shards)
-    share_width = model_width // vocab_shards
-    layer_part = lax.dynamic_slice_in_dim(updated, vocab_shard * share_width, share_width, 1)
-    path_length = path_index.shape[1]
+    token_number = jnp.arange(token_rows, dtype=jnp.int32)
+    live_rows = (token_number % draft_length) < jnp.take(local_counts, token_number // draft_length)
+    layer_part = jnp.where(
+        live_rows[:, None], residual_cols + feed_cols.astype(jnp.float32), 0.0
+    ).astype(jnp.bfloat16)
+    path_live = (own_path_rows % draft_length) < jnp.take(
+        local_counts, own_path_rows // draft_length
+    )
+    head_rows = jnp.where(
+        path_live[:, None], residual_path + feed_path.astype(jnp.float32), 0.0
+    ).astype(jnp.bfloat16)
     request_picker = (
         path_index[:, :, None] == jnp.arange(draft_length, dtype=jnp.int32)[None, None, :]
     ).astype(jnp.bfloat16)
@@ -211,15 +265,7 @@
         fresh_values.reshape(local_requests, draft_length, key_local * head_dim),
         preferred_element_type=jnp.float32,
     ).astype(jnp.bfloat16)
-    per_shard = path_length // vocab_shards
-    head_picker = lax.dynamic_slice_in_dim(request_picker, vocab_shard * per_shard, per_shard, 1)
-    head_rows = jnp.einsum(
-        "ytm,ymu->ytu",
-        head_picker,
-        updated.reshape(local_requests, draft_length, model_width),
-        preferred_element_type=jnp.float32,
-    ).astype(jnp.bfloat16)
-    flat_rows = head_rows.reshape(local_requests * per_shard, model_width).astype(jnp.float32)
+    flat_rows = head_rows.astype(jnp.float32)
     mean_square = jnp.mean(flat_rows * flat_rows, axis=1)
     norm_values = jnp.sqrt(mean_square + eps_norm).reshape(local_requests, per_shard)
     head_in = (

time: 118 us -> 158 us (1.34)
  local copies, waits for them, and re-layouts: 6.74 us -> 39.6 us
  other arithmetic: 14 us -> 34.8 us
  blocking collectives: 11.3 us -> 0 us
  waiting for transfers between devices: 37.1 us -> 32.2 us
  matrix products: 16.9 us -> 19.1 us
    convert_element_type x0 -> x11, local copies, waits for them, and re-layouts: none -> 13.2 us  [the longest x9 12.5 us: exchange(): piece.astype(jnp.bfloat16)]
    unnamed x39 -> x51, local copies, waits for them, and re-layouts: 1.37 us -> 14.2 us
    all_to_all x1 -> x0, blocking collectives: 11.3 us -> none  [gather_rows(): lax.all_to_all(copies, axis_name, split_axis=0, concat_axis=0, tiled=True)]
    all_to_all x0 -> x4, other arithmetic: none -> 7.84 us  [exchange(): lax.all_to_all(packed, 'vocab', split_axis=0, concat_axis=0, tiled=True)]
    gather x1 -> x5, local copies, waits for them, and re-layouts: 0.59 us -> 5.23 us  [the longest x2 1.8 us: path_pieces(): jnp.take(partial, path_rows_all.reshape(-1), axis=0)]
    reduce_sum x2, other arithmetic: 1.85 us -> 5.62 us  [exchange(): summed = jnp.sum(arrived.astype(jnp.float32), axis=0)]
    all_to_all x2, waiting for transfers between devices: 12.1 us -> 8.39 us  [exchange(): lax.all_to_all(packed, 'vocab', split_axis=0, concat_axis=0, tiled=True)]
    convert_element_type x1 -> x5, other arithmetic: 0.97 us -> 2.72 us  [the longest x1 1.75 us: per_device(): layer_part = jnp.where(live_rows[:, None], residual_cols + feed_cols.asty...]
  transfers between devices with their start and end apart: 5 -> 5, of which waited for: 5 -> 5; matrix products, arithmetic and copies ran while one was open for 5% -> 10% of each run, Pallas kernels for 0% -> 0%
where the time goes in v3:
time: 158 us; the launch traced here: 157 us
  local copies, waits for them, and re-layouts  39.6 us (25%)
  other arithmetic  34.8 us (22%)
  waiting for transfers between devices  32.2 us (20%)
  starting transfers between devices  30.1 us (19%)
  matrix products  19.1 us (12%)
    all_to_all x3, waiting for transfers between devices, gather_rows(): lax.all_to_all(copies, axis_name, split_axis=0, concat_axis=0, tiled=True)  23.8 us
    all_to_all x3, starting transfers between devices, gather_rows(): lax.all_to_all(copies, axis_name, split_axis=0, concat_axis=0, tiled=True)  18.9 us
    unnamed x51, local copies, waits for them, and re-layouts  14.2 us
    convert_element_type x9, local copies, waits for them, and re-layouts, exchange(): piece.astype(jnp.bfloat16)  12.5 us
    all_to_all x2, starting transfers between devices, exchange(): lax.all_to_all(packed, 'vocab', split_axis=0, concat_axis=0, tiled=True)  11.2 us
    all_to_all x2, waiting for transfers between devices, exchange(): lax.all_to_all(packed, 'vocab', split_axis=0, concat_axis=0, tiled=True)  8.39 us
    all_to_all x4, other arithmetic, exchange(): lax.all_to_all(packed, 'vocab', split_axis=0, concat_axis=0, tiled=True)  7.84 us
    reduce_sum x2, other arithmetic, exchange(): summed = jnp.sum(arrived.astype(jnp.float32), axis=0)  5.62 us
  transfers between devices with their start and end apart: 5, of which 5 were waited for; matrix products, arithmetic and copies ran while one was open for 10% of the time, Pallas kernels for 0%

profile of v3, /device:TPU:2, one launch (start us, length us, event | category | flops | bytes accessed | tf_op | source)
XLA Modules:
  0.0 156.8 jit_solution(795454232716267096)
XLA Ops:
  0.7 1.1 convolution_minimum_fusion.5
  2.9 1.3 fusion.46
  5.6 1.2 multiply_reduce_fusion
  6.8 2.2 %convolution_bitcast_fusion = f32[2,1,2,64,96]{4,3,2,0,1:T(8,128)} fusion(bf16[1536,2,96,1]{0,2,1,3:T(8,128)(2,1)} %bitcast.169, bf16[2,64,1536]{2,1,0:T(8,128)(2,1)} %param.20, f32[1536]{0:T(1024)S(1)} %convert_element_type.172, f32[2,64]{1,0:T(2,128)S(1)} %add_rsqrt_fusion), kind=kOutput, calls=%fused_computation.13 | convolution fusion | flops 76283904 | bytes 1088000 | tf_op jit(solution)/shard_map/rim,mkgd->rkgid/dot_general | solution.py:101
  9.3 1.0 multiply_cosine_fusion.1
  13.5 1.1 fusion.28
  14.6 1.6 %select_reduce_fusion = (f32[2,2,64]{2,1,0:T(2,128)S(1)}, f32[2,1,2,64,2048]{4,3,2,0,1:T(8,128)S(1)}) fusion(pred[2,2048]{1,0:T(4,128)(4,1)S(1)} %compare_and_fusion, bf16[2048,96]{0,1:T(8,128)(2,1)} %param.25, bf16[2,2,64,48]{3,2,1,0:T(8,128)(2,1)S(1)} %get-tuple-element.11, bf16[2,2,64,48]{3,2,1,0:T(8,128)(2,1)S(1)} %get-tuple-element.10), kind=kOutput, calls=%fused_computation.8 | convolution fusion | flops 102334208 | bytes 2544640 | tf_op jit(solution)/shard_map/rkgid,pkd->rkgip/dot_general | solution.py:136
  17.7 1.1 convolution_bitcast_fusion.2
  19.8 1.7 %fusion.8 = bf16[2,64,1536,1]{2,1,3,0:T(8,128)(2,1)S(1)} fusion(bf16[2,96,1536,1]{2,1,0,3:T(8,128)(2,1)} %bitcast.163, f32[2,1,2,64,96]{4,3,2,0,1:T(8,128)} %convolution_bitcast_fusion.2, f32[2,2,64]{2,1,0:T(2,128)S(1)} %add.219, bf16[2,64,96]{2,1,0:T(8,128)(2,1)} %convolution_convert_fusion, f32[2,2,64,64]{2,3,1,0:T(8,128)} %copy-done.4, ...), kind=kOutput, calls=%fused_computation.37 | convolution fusion | flops 78766080 | bytes 1181696 | tf_op jit(solution)/shard_map/rkgid,kgdn->rin/dot_general | solution.py:162
  21.6 1.2 convert_element_type.186
  22.8 0.9 convert_element_type.185
  24.7 1.9 %copy.64 = bf16[8,128,192]{2,1,0:T(8,128)(2,1)} copy(bf16[8,128,192]{2,0,1:T(8,128)(2,1)} %bitcast.159) | data formatting | bytes 786432 | tf_op jit(solution)/shard_map/convert_element_type | solution.py:204
  26.7 2.4 %convert_element_type.188 = bf16[8,24576]{1,0:T(8,128)(2,1)} reshape(bf16[8,128,192]{2,1,0:T(8,128)(2,1)} %copy.64) | data formatting | bytes 786432 | tf_op jit(solution)/shard_map/convert_element_type | solution.py:204
  29.1 1.2 gather_fusion.2
  31.2 2.1 %maximum_bitcast_fusion = bf16[8,1,52224]{2,0,1:T(8,128)(2,1)} fusion(bf16[8,3072]{1,0:T(8,128)(2,1)S(1)} %convert_element_type.190, bf16[8,24576]{1,0:T(8,128)(2,1)} %convert_element_type.188, bf16[8,24576]{1,0:T(8,128)(2,1)} %convert_element_type.185), kind=kLoop, calls=%fused_computation.33 | loop fusion | flops 2506752 | bytes 1671168 | tf_op jit(solution)/shard_map/all_to_all | solution.py:205
  33.8 3.1 %reduce.11 = bf16[8,52224]{1,0:T(8,128)(2,1)} reduce(bf16[8,1,52224]{2,0,1:T(8,128)(2,1)} %maximum_bitcast_fusion, bf16[]{:T(256)} %broadcast.527), dimensions={1}, to_apply=%copy.68.reduce_sub_computation | reduce | bytes 1671170 | tf_op jit(solution)/shard_map/all_to_all | solution.py:205
  36.9 2.8 %reshape.552 = bf16[8,2,26112]{2,1,0:T(2,128)(2,1)} reshape(bf16[8,52224]{1,0:T(8,128)(2,1)} %reduce.11) | data formatting | bytes 1671168
  39.7 6.3 %all-to-all-start = ((bf16[8,2,26112]{2,1,0:T(2,128)(2,1)}), bf16[8,2,26112]{2,1,0:T(2,128)(2,1)}, u32[]{:S(2)}, u32[]{:S(2)}) async-start(bf16[8,2,26112]{2,1,0:T(2,128)(2,1)} %reshape.552), calls=%async_computation | async-start | bytes 1671168 | tf_op jit(solution)/shard_map/all_to_all | solution.py:205
  47.3 1.1 gather_fusion
  48.5 1.2 compare_bitcast_fusion
  49.7 1.0 bitcast_convert_fusion.1
  50.7 7.6 %all-to-all-done = bf16[8,2,26112]{2,1,0:T(2,128)(2,1)} async-done(((bf16[8,2,26112]{2,1,0:T(2,128)(2,1)}), bf16[8,2,26112]{2,1,0:T(2,128)(2,1)}, u32[]{:S(2)}, u32[]{:S(2)}) %all-to-all-start) | async-done | bytes 835616 | tf_op jit(solution)/shard_map/all_to_all | solution.py:205
  58.3 5.5 %reshape.553 = bf16[8,1,52224]{2,1,0:T(2,128)(2,1)} reshape(bf16[8,2,26112]{2,1,0:T(2,128)(2,1)} %all-to-all-done) | data formatting | bytes 1671168
  63.8 3.6 %convert_reduce_fusion.1 = f32[52224]{0:T(1024)S(1)} fusion(bf16[8,1,52224]{2,1,0:T(2,128)(2,1)} %reshape.553), kind=kLoop, calls=%fused_computation.9 | loop fusion | flops 783360 | bytes 1044480 | tf_op jit(solution)/shard_map/reduce_sum | solution.py:206
  68.1 1.0 multiply_reduce_fusion.1
  69.2 1.0 multiply_convert_fusion.4
  70.9 4.8 %all-to-all-start.1 = ((bf16[8,16,1536]{2,1,0:T(8,128)(2,1)}), bf16[8,16,1536]{2,1,0:T(8,128)(2,1)S(1)}, u32[]{:S(2)}, u32[]{:S(2)}) async-start(bf16[8,16,1536]{2,1,0:T(8,128)(2,1)} %broadcast_in_dim.157), calls=%async_computation.1 | async-start | bytes 786432 | tf_op jit(solution)/shard_map/all_to_all | solution.py:36
  77.7 5.5 %all-to-all-done.1 = bf16[8,16,1536]{2,1,0:T(8,128)(2,1)S(1)} async-done(((bf16[8,16,1536]{2,1,0:T(8,128)(2,1)}), bf16[8,16,1536]{2,1,0:T(8,128)(2,1)S(1)}, u32[]{:S(2)}, u32[]{:S(2)}) %all-to-all-start.1) | async-done | bytes 393248 | tf_op jit(solution)/shard_map/all_to_all | solution.py:36
  84.0 2.5 %fusion.61 = f32[128,512]{1,0:T(8,128)} fusion(bf16[128,1536]{1,0:T(8,128)(2,1)S(1)} %bitcast.161, bf16[1536,512]{1,0:T(8,128)(2,1)} %param.34), kind=kOutput, calls=%fused_computation.155 | convolution fusion | flops 201326592 | bytes 2228224 | tf_op jit(solution)/shard_map/dot_general | solution.py:232
  86.5 2.8 %fusion.2 = bf16[128,1536]{1,0:T(8,128)(2,1)S(1)} fusion(bf16[512,1536]{1,0:T(8,128)(2,1)} %param.36, bf16[128,1536]{1,0:T(8,128)(2,1)} %bitcast.162, bf16[1536,512]{1,0:T(8,128)(2,1)} %param.35, f32[128,512]{1,0:T(8,128)} %fusion.61), kind=kOutput, calls=%fused_computation.14 | convolution fusion | flops 403046400 | bytes 4194304 | tf_op jit(solution)/shard_map/dot_general | solution.py:235
  90.8 2.0 %copy.70 = bf16[8,128,192]{2,1,0:T(8,128)(2,1)} copy(bf16[8,128,192]{1,2,0:T(8,128)(2,1)} %bitcast.160) | data formatting | bytes 786432 | tf_op jit(solution)/shard_map/convert_element_type | solution.py:204
  92.7 2.4 %convert_element_type.198 = bf16[8,24576]{1,0:T(8,128)(2,1)} reshape(bf16[8,128,192]{2,1,0:T(8,128)(2,1)} %copy.70) | data formatting | bytes 786432 | tf_op jit(solution)/shard_map/convert_element_type | solution.py:204
  95.9 1.1 maximum_bitcast_fusion.1
  97.0 1.6 %reduce.12 = bf16[8,27648]{1,0:T(8,128)(2,1)} reduce(bf16[8,1,27648]{2,0,1:T(8,128)(2,1)S(1)} %maximum_bitcast_fusion.1, bf16[]{:T(256)} %broadcast.527), dimensions={1}, to_apply=%copy.71.reduce_sub_computation | reduce | bytes 884738 | tf_op jit(solution)/shard_map/all_to_all | solution.py:205
  98.6 2.1 %reshape.554 = bf16[8,2,13824]{2,1,0:T(2,128)(2,1)} reshape(bf16[8,27648]{1,0:T(8,128)(2,1)} %reduce.12) | data formatting | bytes 884736
  100.7 4.8 %all-to-all-start.2 = ((bf16[8,2,13824]{2,1,0:T(2,128)(2,1)}), bf16[8,2,13824]{2,1,0:T(2,128)(2,1)S(1)}, u32[]{:S(2)}, u32[]{:S(2)}) async-start(bf16[8,2,13824]{2,1,0:T(2,128)(2,1)} %reshape.554), calls=%async_computation.2 | async-start | bytes 884736 | tf_op jit(solution)/shard_map/all_to_all | solution.py:205
  105.5 1.7 %gather_fusion.1 = f32[2,1536]{1,0:T(2,128)S(1)} fusion(f32[128,1536]{1,0:T(8,128)} %bitcast_convert_fusion.1, s32[1024]{0:T(1024)S(1)} %pad_clamp_fusion), kind=kCustom, calls=%fused_computation.3 | custom fusion | bytes 24584 | tf_op jit(solution)/shard_map/jit(_take)/gather | solution.py:223
  107.8 1.7 %fusion.47 = pred[128]{0:T(512)(128)(4,1)} fusion(s32[]{:T(128)} %bitcast.1, s32[]{:T(128)} %bitcast), kind=kLoop, calls=%fused_computation.136 | loop fusion | flops 4224 | bytes 136 | tf_op jit(solution)/shard_map/lt | solution.py:243
  109.6 1.5 convolution_convert_fusion.1
  111.1 1.6 %reshape.480 = f32[128,192]{1,0:T(8,128)} reshape(f32[24576]{0:T(1024)} %get-tuple-element.12) | data formatting | bytes 196608 | tf_op jit(solution)/shard_map/reshape | solution.py:222
  113.5 1.6 %reshape.555 = bf16[8,1,27648]{2,1,0:T(2,128)(2,1)} reshape(bf16[8,2,13824]{2,1,0:T(2,128)(2,1)S(1)} %all-to-all-done.2) | data formatting | bytes 884736
  115.1 2.0 %reduce.10 = bf16[27648]{0:T(1024)(128)(2,1)S(1)} reduce(bf16[8,1,27648]{2,1,0:T(2,128)(2,1)} %reshape.555, bf16[]{:T(256)} %constant.167), dimensions={0,1}, to_apply=%region_9.11.clone | reduce | flops 193536 | bytes 497666 | tf_op jit(solution)/shard_map/reduce_sum | solution.py:206
  119.5 10.0 %all-to-all-start.3 = ((bf16[32,2,1536]{2,1,0:T(2,128)(2,1)}), bf16[32,2,1536]{2,1,0:T(2,128)(2,1)S(1)}, u32[]{:S(2)}, u32[]{:S(2)}) async-start(bf16[32,2,1536]{2,1,0:T(2,128)(2,1)} %broadcast_in_dim.164), calls=%async_computation.3 | async-start | bytes 393216 | tf_op jit(solution)/shard_map/all_to_all | solution.py:36
  130.2 10.2 %all-to-all-done.3 = bf16[32,2,1536]{2,1,0:T(2,128)(2,1)S(1)} async-done(((bf16[32,2,1536]{2,1,0:T(2,128)(2,1)}), bf16[32,2,1536]{2,1,0:T(2,128)(2,1)S(1)}, u32[]{:S(2)}, u32[]{:S(2)}) %all-to-all-start.3) | async-done | bytes 196640 | tf_op jit(solution)/shard_map/all_to_all | solution.py:36
  140.5 1.1 convolution_reduce_fusion
  142.3 4.2 %all-to-all-start.4 = ((f32[32,1,64]{2,1,0:T(1,128)}), f32[32,1,64]{2,1,0:T(1,128)S(1)}, u32[]{:S(2)}, u32[]{:S(2)}) async-start(f32[32,1,64]{2,1,0:T(1,128)} %broadcast_in_dim.165), calls=%async_computation.4 | async-start | bytes 32768 | tf_op jit(solution)/shard_map/all_to_all | solution.py:36
  146.5 1.8 %select_convert_fusion.2 = bf16[128,192]{1,0:T(8,128)(2,1)} fusion(f32[128,192]{1,0:T(8,128)} %reshape.486, f32[128,192]{1,0:T(8,128)S(1)} %copy-done.6, f32[128,1536]{1,0:T(8,128)} %bitcast_convert_fusion.1, s32[]{:T(128)S(6)} %select_n.153, pred[128]{0:T(512)(128)(4,1)S(1)} %copy-done.18), kind=kLoop, calls=%fused_computation.49 | loop fusion | flops 98304 | bytes 344196 | tf_op jit(solution)/shard_map/convert_element_type | solution.py:246
  148.2 8.0 %all-to-all-done.4 = f32[32,1,64]{2,1,0:T(1,128)S(1)} async-done(((f32[32,1,64]{2,1,0:T(1,128)}), f32[32,1,64]{2,1,0:T(1,128)S(1)}, u32[]{:S(2)}, u32[]{:S(2)}) %all-to-all-start.4) | async-done | bytes 8224 | tf_op jit(solution)/shard_map/all_to_all | solution.py:36
  (113 shorter events, 24.3 us)
Async XLA Ops:
  0.6 139.9 %copy-start = (bf16[1536,1000]{0,1:T(8,128)(2,1)S(1)}, bf16[1536,1000]{0,1:T(8,128)(2,1)}, u32[]{:S(2)}) copy-start(bf16[1536,1000]{0,1:T(8,128)(2,1)} %param.37) | copy-start | bytes 9216004
  0.6 8.3 %copy-start.1 = (bf16[2,64,1536]{2,1,0:T(8,128)(2,1)S(1)}, bf16[2,64,1536]{2,1,0:T(8,128)(2,1)}, u32[]{:S(2)}) copy-start(bf16[2,64,1536]{2,1,0:T(8,128)(2,1)} %param.20) | copy-start | bytes 1179652
  0.7 8.3 %copy-start.21 = (bf16[1536,96]{0,1:T(8,128)(2,1)S(1)}, bf16[1536,96]{0,1:T(8,128)(2,1)}, u32[]{:S(2)}) copy-start(bf16[1536,96]{0,1:T(8,128)(2,1)} %param.31) | copy-start | bytes 884740
  5.6 5.0 %copy-start.8 = (f32[1536]{0:T(1024)}, f32[1536]{0:T(1024)S(1)}, u32[]{:S(2)}) copy-start(f32[1536]{0:T(1024)S(1)} %convert_element_type.172) | copy-start | bytes 18436
  14.6 3.2 %copy-start.20 = (bf16[2048,96]{0,1:T(8,128)(2,1)S(1)}, bf16[2048,96]{0,1:T(8,128)(2,1)}, u32[]{:S(2)}) copy-start(bf16[2048,96]{0,1:T(8,128)(2,1)} %param.26) | copy-start | bytes 1179652
  16.5 0.6 copy-start.4
  17.2 1.7 %copy-start.9 = (f32[1536]{0:T(1024)S(1)}, f32[1536]{0:T(1024)}, u32[]{:S(2)}) copy-start(f32[1536]{0:T(1024)} %copy-done.8) | copy-start | bytes 18436
  17.2 1.7 %copy-start.22 = (bf16[1536,96]{0,1:T(8,128)(2,1)S(1)}, bf16[1536,96]{0,1:T(8,128)(2,1)}, u32[]{:S(2)}) copy-start(bf16[1536,96]{0,1:T(8,128)(2,1)} %param.32) | copy-start | bytes 884740
  24.7 8.6 %copy-start.13 = (pred[16]{0:T(512)(128)(4,1)}, pred[16]{0:T(512)(128)(4,1)S(1)}, u32[]{:S(2)}) copy-start(pred[16]{0:T(512)(128)(4,1)S(1)} %compare_and_fusion.1) | copy-start | bytes 52
  36.9 9.7 %copy-start.11 = (bf16[1536]{0:T(1024)(128)(2,1)S(1)}, bf16[1536]{0:T(1024)(128)(2,1)}, u32[]{:S(2)}) copy-start(bf16[1536]{0:T(1024)(128)(2,1)} %param.28) | copy-start | bytes 9220
  36.9 12.8 %copy-start.2 = (bf16[2,64,1536]{2,1,0:T(8,128)(2,1)S(1)}, bf16[2,64,1536]{2,1,0:T(8,128)(2,1)}, u32[]{:S(2)}) copy-start(bf16[2,64,1536]{2,1,0:T(8,128)(2,1)} %param.20) | copy-start | bytes 1179652
  39.7 18.7 %all-to-all-start = ((bf16[8,2,26112]{2,1,0:T(2,128)(2,1)}), bf16[8,2,26112]{2,1,0:T(2,128)(2,1)}, u32[]{:S(2)}, u32[]{:S(2)}) async-start(bf16[8,2,26112]{2,1,0:T(2,128)(2,1)} %reshape.552), calls=%async_computation | async-start | bytes 1671168 | tf_op jit(solution)/shard_map/all_to_all | solution.py:205
  46.0 0.6 copy-start.16
  63.8 11.9 %copy-start.17 = (s32[2,1]{0,1:T(1,128)S(1)}, s32[2,1]{0,1:T(1,128)}, u32[]{:S(2)}) copy-start(s32[2,1]{0,1:T(1,128)} %copy-done.16) | copy-start | bytes 28
  63.8 13.1 %copy-start.10 = (s32[2,8]{1,0:T(2,128)S(1)}, s32[2,8]{1,0:T(2,128)}, u32[]{:S(2)}) copy-start(s32[2,8]{1,0:T(2,128)} %param.23) | copy-start | bytes 196
  67.4 0.7 copy-start.5
  70.9 12.3 %all-to-all-start.1 = ((bf16[8,16,1536]{2,1,0:T(8,128)(2,1)}), bf16[8,16,1536]{2,1,0:T(8,128)(2,1)S(1)}, u32[]{:S(2)}, u32[]{:S(2)}) async-start(bf16[8,16,1536]{2,1,0:T(8,128)(2,1)} %broadcast_in_dim.157), calls=%async_computation.1 | async-start | bytes 786432 | tf_op jit(solution)/shard_map/all_to_all | solution.py:36
  83.2 0.7 copy-start.3
  89.2 5.9 %copy-start.14 = (pred[16]{0:T(512)(128)(4,1)S(1)}, pred[16]{0:T(512)(128)(4,1)}, u32[]{:S(2)}) copy-start(pred[16]{0:T(512)(128)(4,1)} %copy-done.13) | copy-start | bytes 52
  95.2 10.3 %copy-start.19 = (s32[2]{0:T(128)S(1)}, s32[2]{0:T(128)}, u32[]{:S(2)}) copy-start(s32[2]{0:T(128)} %fusion.49) | copy-start | bytes 28
  95.2 12.1 %copy-start.12 = (bf16[1536]{0:T(1024)(128)(2,1)S(1)}, bf16[1536]{0:T(1024)(128)(2,1)}, u32[]{:S(2)}) copy-start(bf16[1536]{0:T(1024)(128)(2,1)} %param.29) | copy-start | bytes 9220
  95.2 15.9 %slice-start = ((f32[52224]{0:T(1024)}), f32[3072]{0:T(1024)S(1)}, s32[]{:S(2)}) async-start(f32[52224]{0:T(1024)} %copy-done.5), calls=%async_computation.5 | async-start | bytes 24576 | tf_op jit(solution)/shard_map/slice | solution.py:210
  98.6 18.6 %copy-start.15 = (pred[2]{0:T(512)(128)(4,1)S(1)}, pred[2]{0:T(512)(128)(4,1)}, u32[]{:S(2)}) copy-start(pred[2]{0:T(512)(128)(4,1)} %compare_bitcast_fusion) | copy-start | bytes 10
  100.7 12.8 %all-to-all-start.2 = ((bf16[8,2,13824]{2,1,0:T(2,128)(2,1)}), bf16[8,2,13824]{2,1,0:T(2,128)(2,1)S(1)}, u32[]{:S(2)}, u32[]{:S(2)}) async-start(bf16[8,2,13824]{2,1,0:T(2,128)(2,1)} %reshape.554), calls=%async_computation.2 | async-start | bytes 884736 | tf_op jit(solution)/shard_map/all_to_all | solution.py:205
  111.1 7.5 %copy-start.7 = (f32[1536]{0:T(1024)S(1)}, f32[1536]{0:T(1024)}, u32[]{:S(2)}) copy-start(f32[1536]{0:T(1024)} %convert_element_type.211) | copy-start | bytes 18436
  119.5 21.0 %all-to-all-start.3 = ((bf16[32,2,1536]{2,1,0:T(2,128)(2,1)}), bf16[32,2,1536]{2,1,0:T(2,128)(2,1)S(1)}, u32[]{:S(2)}, u32[]{:S(2)}) async-start(bf16[32,2,1536]{2,1,0:T(2,128)(2,1)} %broadcast_in_dim.164), calls=%async_computation.3 | async-start | bytes 393216 | tf_op jit(solution)/shard_map/all_to_all | solution.py:36
  129.4 17.0 %copy-start.18 = (pred[128]{0:T(512)(128)(4,1)S(1)}, pred[128]{0:T(512)(128)(4,1)}, u32[]{:S(2)}) copy-start(pred[128]{0:T(512)(128)(4,1)} %fusion.47) | copy-start | bytes 388
  140.5 5.9 %copy-start.6 = (f32[128,192]{1,0:T(8,128)S(1)}, f32[128,192]{1,0:T(8,128)}, u32[]{:S(2)}) copy-start(f32[128,192]{1,0:T(8,128)} %reshape.480) | copy-start | bytes 294916
  142.3 14.0 %all-to-all-start.4 = ((f32[32,1,64]{2,1,0:T(1,128)}), f32[32,1,64]{2,1,0:T(1,128)S(1)}, u32[]{:S(2)}, u32[]{:S(2)}) async-start(f32[32,1,64]{2,1,0:T(1,128)} %broadcast_in_dim.165), calls=%async_computation.4 | async-start | bytes 32768 | tf_op jit(solution)/shard_map/all_to_all | solution.py:36

commit v4 on v2

--- a/solution.py
+++ b/solution.py
@@ -192,10 +192,44 @@
     layer_chunk = jnp.where(
         chunk_live[:, None], residual_chunk + feed_chunk.astype(jnp.float32), 0.0
     ).astype(jnp.bfloat16)
-    updated = gather_rows(layer_chunk, "vocab", vocab_shards)
     share_width = model_width // vocab_shards
-    layer_part = lax.dynamic_slice_in_dim(updated, vocab_shard * share_width, share_width, 1)
     path_length = path_index.shape[1]
+    per_shard = path_length // vocab_shards
+    path_count = local_requests * per_shard
+    path_rows_all = (
+        (
+            path_index.reshape(local_requests, vocab_shards, per_shard)
+            + (jnp.arange(local_requests, dtype=jnp.int32) * draft_length)[:, None, None]
+        )
+        .transpose(1, 0, 2)
+        .reshape(vocab_shards, path_count)
+    )
+    column_pieces = (
+        layer_chunk.reshape(chunk_rows, vocab_shards, share_width)
+        .transpose(1, 0, 2)
+        .reshape(vocab_shards, chunk_rows * share_width)
+    )
+    in_chunk = (
+        path_rows_all[:, :, None] == chunk_token[None, None, :]
+    ).astype(jnp.bfloat16)
+    path_pieces = (
+        jnp.einsum("vjt,tf->vjf", in_chunk, layer_chunk, preferred_element_type=jnp.float32)
+        .astype(jnp.bfloat16)
+        .reshape(vocab_shards, path_count * model_width)
+    )
+    arrived = lax.all_to_all(
+        jnp.concatenate([column_pieces, path_pieces], axis=1),
+        "vocab",
+        split_axis=0,
+        concat_axis=0,
+        tiled=True,
+    )
+    layer_part = arrived[:, : chunk_rows * share_width].reshape(token_rows, share_width)
+    head_rows = (
+        jnp.sum(arrived[:, chunk_rows * share_width :].astype(jnp.float32), axis=0)
+        .reshape(path_count, model_width)
+        .astype(jnp.bfloat16)
+    )
     request_picker = (
         path_index[:, :, None] == jnp.arange(draft_length, dtype=jnp.int32)[None, None, :]
     ).astype(jnp.bfloat16)
@@ -211,15 +245,7 @@
         fresh_values.reshape(local_requests, draft_length, key_local * head_dim),
         preferred_element_type=jnp.float32,
     ).astype(jnp.bfloat16)
-    per_shard = path_length // vocab_shards
-    head_picker = lax.dynamic_slice_in_dim(request_picker, vocab_shard * per_shard, per_shard, 1)
-    head_rows = jnp.einsum(
-        "ytm,ymu->ytu",
-        head_picker,
-        updated.reshape(local_requests, draft_length, model_width),
-        preferred_element_type=jnp.float32,
-    ).astype(jnp.bfloat16)
-    flat_rows = head_rows.reshape(local_requests * per_shard, model_width).astype(jnp.float32)
+    flat_rows = head_rows.astype(jnp.float32)
     mean_square = jnp.mean(flat_rows * flat_rows, axis=1)
     norm_values = jnp.sqrt(mean_square + eps_norm).reshape(local_requests, per_shard)
     head_in = (

time: 118 us -> 118 us (level)
  blocking collectives: 11.3 us -> 0 us
  waiting for transfers between devices: 37.1 us -> 42.5 us
  starting transfers between devices: 30.2 us -> 35 us
    all_to_all x1 -> x0, blocking collectives: 11.3 us -> none  [gather_rows(): lax.all_to_all(copies, axis_name, split_axis=0, concat_axis=0, tiled=True)]
    all_to_all x0 -> x1, starting transfers between devices: none -> 4.72 us  [per_device(): lax.all_to_all(jnp.concatenate([column_pieces, path_pieces], axis=1), 'vo...]
    all_to_all x0 -> x1, waiting for transfers between devices: none -> 4.36 us  [per_device(): lax.all_to_all(jnp.concatenate([column_pieces, path_pieces], axis=1), 'vo...]
    reshape x1, local copies, waits for them, and re-layouts: 1.68 us -> 0.08 us  [gather_rows(): return arrived.reshape(shards * chunk.shape[0], *chunk.shape[1:])]
    dot_general x1, matrix products: 1.07 us -> 2.48 us  [per_device(): jnp.dot(hidden_in, gate_weight, preferred_element_type=jnp.float32)]
  transfers between devices with their start and end apart: 5 -> 6, of which waited for: 5 -> 6; matrix products, arithmetic and copies ran while one was open for 5% -> 5% of each run, Pallas kernels for 0% -> 0%
where the time goes in v4:
time: 118 us; the launch traced here: 117 us
  waiting for transfers between devices  42.5 us (36%)
  starting transfers between devices  35 us (30%)
  matrix products  16.8 us (14%)
  other arithmetic  15.1 us (13%)
  local copies, waits for them, and re-layouts  6.65 us (6%)
    all_to_all x3, waiting for transfers between devices, gather_rows(): lax.all_to_all(copies, axis_name, split_axis=0, concat_axis=0, tiled=True)  25.4 us
    all_to_all x3, starting transfers between devices, gather_rows(): lax.all_to_all(copies, axis_name, split_axis=0, concat_axis=0, tiled=True)  19 us
    all_to_all x2, waiting for transfers between devices, scatter_rows(): lax.all_to_all(pieces, axis_name, split_axis=0, concat_axis=0, tiled=True)  12.7 us
    all_to_all x2, starting transfers between devices, scatter_rows(): lax.all_to_all(pieces, axis_name, split_axis=0, concat_axis=0, tiled=True)  11.3 us
    all_to_all x1, starting transfers between devices, per_device(): lax.all_to_all(jnp.concatenate([column_pieces, path_pieces], axis=1), 'vo...  4.72 us
    all_to_all x1, waiting for transfers between devices, per_device(): lax.all_to_all(jnp.concatenate([column_pieces, path_pieces], axis=1), 'vo...  4.36 us
    dot_general x1, matrix products, per_device(): down_part = jnp.dot(hidden, down_weight, preferred_element_type=jnp.float32)  3.42 us
    dot_general x1, matrix products, per_device(): jnp.dot(hidden_in, gate_weight, preferred_element_type=jnp.float32)  2.48 us
  transfers between devices with their start and end apart: 6, of which 6 were waited for; matrix products, arithmetic and copies ran while one was open for 5% of the time, Pallas kernels for 0%

profile of v4, /device:TPU:2, one launch (start us, length us, event | category | flops | bytes accessed | tf_op | source)
XLA Modules:
  0.0 117.2 jit_solution(11228110063331095156)
XLA Ops:
  0.7 0.9 fusion.44
  1.6 0.7 add.184
  2.4 0.7 convert_element_type.144
  3.1 1.2 multiply_reduce_fusion
  4.3 1.0 convolution_minimum_fusion.5
  6.4 0.7 add_convert_fusion.1
  7.3 1.6 %convolution_bitcast_fusion.1 = f32[2,1,2,64,96]{4,3,2,0,1:T(8,128)S(1)} fusion(bf16[1536,2,96,1]{0,2,1,3:T(8,128)(2,1)} %bitcast.161, bf16[2,64,1536]{2,1,0:T(8,128)(2,1)} %param.18, f32[1536]{0:T(1024)S(1)} %convert_element_type.144, f32[2,64]{1,0:T(2,128)S(1)} %add_rsqrt_fusion), kind=kOutput, calls=%fused_computation.12 | convolution fusion | flops 76283904 | bytes 1088000 | tf_op jit(solution)/shard_map/rim,mkgd->rkgid/dot_general | solution.py:101
  8.9 1.3 %convolution_bitcast_fusion.4 = f32[2,1,64,96]{3,2,0,1:T(8,128)S(1)} fusion(bf16[1536,96]{0,1:T(8,128)(2,1)} %param.29, bf16[2,64,1536]{2,1,0:T(8,128)(2,1)S(1)} %copy-done.1, f32[1536]{0:T(1024)S(1)} %convert_element_type.144, f32[2,64]{1,0:T(2,128)S(1)} %add_rsqrt_fusion), kind=kOutput, calls=%fused_computation.19 | convolution fusion | flops 38535168 | bytes 743936 | tf_op jit(solution)/shard_map/rim,mkd->rkid/dot_general | solution.py:109
  10.6 1.0 fusion.37
  11.7 0.6 select_reduce_fusion
  12.6 0.5 convert_reduce_fusion
  13.2 0.5 convolution_bitcast_fusion.3
  14.1 0.6 copy-done.18
  15.0 1.1 fusion.1
  16.1 6.4 %all-to-all-start = ((bf16[8,16,1536]{2,1,0:T(8,128)(2,1)}), bf16[8,16,1536]{2,1,0:T(8,128)(2,1)}, u32[]{:S(2)}, u32[]{:S(2)}) async-start(bf16[8,16,1536]{2,1,0:T(8,128)(2,1)} %fusion.1), calls=%async_computation | async-start | bytes 786432 | tf_op jit(solution)/shard_map/all_to_all | solution.py:30
  22.4 1.0 bitcast_convert_fusion
  23.4 6.6 %all-to-all-done = bf16[8,16,1536]{2,1,0:T(8,128)(2,1)} async-done(((bf16[8,16,1536]{2,1,0:T(8,128)(2,1)}), bf16[8,16,1536]{2,1,0:T(8,128)(2,1)}, u32[]{:S(2)}, u32[]{:S(2)}) %all-to-all-start) | async-done | bytes 393248 | tf_op jit(solution)/shard_map/all_to_all | solution.py:30
  30.0 1.1 convert_reduce_fusion.1
  31.1 1.0 multiply_reduce_fusion.1
  32.1 0.6 copy-done.2
  32.8 0.8 broadcast_in_dim.117
  33.6 4.8 %all-to-all-start.1 = ((bf16[8,16,1536]{2,1,0:T(8,128)(2,1)}), bf16[8,16,1536]{2,1,0:T(8,128)(2,1)S(1)}, u32[]{:S(2)}, u32[]{:S(2)}) async-start(bf16[8,16,1536]{2,1,0:T(8,128)(2,1)} %broadcast_in_dim.117), calls=%async_computation.1 | async-start | bytes 786432 | tf_op jit(solution)/shard_map/all_to_all | solution.py:36
  38.5 0.6 fusion.54
  39.1 6.8 %all-to-all-done.1 = bf16[8,16,1536]{2,1,0:T(8,128)(2,1)S(1)} async-done(((bf16[8,16,1536]{2,1,0:T(8,128)(2,1)}), bf16[8,16,1536]{2,1,0:T(8,128)(2,1)S(1)}, u32[]{:S(2)}, u32[]{:S(2)}) %all-to-all-start.1) | async-done | bytes 393248 | tf_op jit(solution)/shard_map/all_to_all | solution.py:36
  45.9 2.5 %fusion.56 = f32[128,512]{1,0:T(8,128)} fusion(bf16[128,1536]{1,0:T(8,128)(2,1)S(1)} %bitcast.151, bf16[1536,512]{1,0:T(8,128)(2,1)} %param.32), kind=kOutput, calls=%fused_computation.132 | convolution fusion | flops 201326592 | bytes 2228224 | tf_op jit(solution)/shard_map/dot_general | solution.py:181
  48.4 3.4 %convolution_convert_fusion = bf16[128,1536]{1,0:T(8,128)(2,1)} fusion(bf16[512,1536]{1,0:T(8,128)(2,1)} %param.34, bf16[128,1536]{1,0:T(8,128)(2,1)S(1)} %bitcast.152, bf16[1536,512]{1,0:T(8,128)(2,1)} %param.33, f32[128,512]{1,0:T(8,128)} %fusion.56), kind=kOutput, calls=%fused_computation.4 | convolution fusion | flops 403243008 | bytes 4194304 | tf_op jit(solution)/shard_map/dot_general | solution.py:184
  51.8 4.9 %all-to-all-start.2 = ((bf16[8,16,1536]{2,1,0:T(8,128)(2,1)}), bf16[8,16,1536]{2,1,0:T(8,128)(2,1)S(1)}, u32[]{:S(2)}, u32[]{:S(2)}) async-start(bf16[8,16,1536]{2,1,0:T(8,128)(2,1)} %bitcast.154), calls=%async_computation.2 | async-start | bytes 786432 | tf_op jit(solution)/shard_map/all_to_all | solution.py:30
  56.7 1.3 %fusion.45 = pred[16]{0:T(512)(128)(4,1)S(1)} fusion(s32[]{:T(128)} %bitcast.1, s32[]{:T(128)} %bitcast, s32[]{:T(128)S(6)} %mul.190), kind=kLoop, calls=%fused_computation.114 | loop fusion | flops 784 | bytes 28 | tf_op jit(solution)/shard_map/lt | solution.py:191
  58.1 6.1 %all-to-all-done.2 = bf16[8,16,1536]{2,1,0:T(8,128)(2,1)S(1)} async-done(((bf16[8,16,1536]{2,1,0:T(8,128)(2,1)}), bf16[8,16,1536]{2,1,0:T(8,128)(2,1)S(1)}, u32[]{:S(2)}, u32[]{:S(2)}) %all-to-all-start.2) | async-done | bytes 393248 | tf_op jit(solution)/shard_map/all_to_all | solution.py:30
  64.2 0.7 reduce_sum.103
  64.9 1.0 select_convert_fusion.3
  66.9 0.7 reduce.10
  67.5 0.7 reshape.481
  68.2 4.7 %all-to-all-start.3 = ((bf16[8,2,3072]{2,1,0:T(2,128)(2,1)}), bf16[8,2,3072]{2,1,0:T(2,128)(2,1)S(1)}, u32[]{:S(2)}, u32[]{:S(2)}) async-start(bf16[8,2,3072]{2,1,0:T(2,128)(2,1)} %reshape.481), calls=%async_computation.3 | async-start | bytes 196608 | tf_op jit(solution)/shard_map/all_to_all | solution.py:220
  72.9 4.4 %all-to-all-done.3 = bf16[8,2,3072]{2,1,0:T(2,128)(2,1)S(1)} async-done(((bf16[8,2,3072]{2,1,0:T(2,128)(2,1)}), bf16[8,2,3072]{2,1,0:T(2,128)(2,1)S(1)}, u32[]{:S(2)}, u32[]{:S(2)}) %all-to-all-start.3) | async-done | bytes 98336 | tf_op jit(solution)/shard_map/all_to_all | solution.py:220
  77.4 0.6 slice_reduce_fusion
  78.2 0.5 fusion.47
  78.8 0.8 broadcast_in_dim.119
  79.6 10.1 %all-to-all-start.4 = ((bf16[32,2,1536]{2,1,0:T(2,128)(2,1)}), bf16[32,2,1536]{2,1,0:T(2,128)(2,1)S(1)}, u32[]{:S(2)}, u32[]{:S(2)}) async-start(bf16[32,2,1536]{2,1,0:T(2,128)(2,1)} %broadcast_in_dim.119), calls=%async_computation.4 | async-start | bytes 393216 | tf_op jit(solution)/shard_map/all_to_all | solution.py:36
  89.7 0.8 convolution_convert_fusion.3
  90.5 10.4 %all-to-all-done.4 = bf16[32,2,1536]{2,1,0:T(2,128)(2,1)S(1)} async-done(((bf16[32,2,1536]{2,1,0:T(2,128)(2,1)}), bf16[32,2,1536]{2,1,0:T(2,128)(2,1)S(1)}, u32[]{:S(2)}, u32[]{:S(2)}) %all-to-all-start.4) | async-done | bytes 196640 | tf_op jit(solution)/shard_map/all_to_all | solution.py:36
  100.9 1.1 convolution_reduce_fusion
  102.1 0.6 broadcast_in_dim.120
  102.7 4.1 %all-to-all-start.5 = ((f32[32,1,64]{2,1,0:T(1,128)}), f32[32,1,64]{2,1,0:T(1,128)S(1)}, u32[]{:S(2)}, u32[]{:S(2)}) async-start(f32[32,1,64]{2,1,0:T(1,128)} %broadcast_in_dim.120), calls=%async_computation.5 | async-start | bytes 32768 | tf_op jit(solution)/shard_map/all_to_all | solution.py:36
  106.8 0.8 convolution_convert_fusion.4
  107.6 0.8 reshape_reshape.4
  108.4 8.2 %all-to-all-done.5 = f32[32,1,64]{2,1,0:T(1,128)S(1)} async-done(((f32[32,1,64]{2,1,0:T(1,128)}), f32[32,1,64]{2,1,0:T(1,128)S(1)}, u32[]{:S(2)}, u32[]{:S(2)}) %all-to-all-start.5) | async-done | bytes 8224 | tf_op jit(solution)/shard_map/all_to_all | solution.py:36
  116.6 0.5 reduce_max.39
  (78 shorter events, 4.3 us)
Async XLA Ops:
  0.6 100.3 %copy-start = (bf16[1536,1000]{0,1:T(8,128)(2,1)S(1)}, bf16[1536,1000]{0,1:T(8,128)(2,1)}, u32[]{:S(2)}) copy-start(bf16[1536,1000]{0,1:T(8,128)(2,1)} %param.35) | copy-start | bytes 9216004
  0.6 8.3 %copy-start.1 = (bf16[2,64,1536]{2,1,0:T(8,128)(2,1)S(1)}, bf16[2,64,1536]{2,1,0:T(8,128)(2,1)}, u32[]{:S(2)}) copy-start(bf16[2,64,1536]{2,1,0:T(8,128)(2,1)} %param.18) | copy-start | bytes 1179652
  0.7 9.5 %copy-start.12 = (f32[48]{0:T(128)}, f32[48]{0:T(128)S(1)}, u32[]{:S(2)}) copy-start(f32[48]{0:T(128)S(1)} %multiply_power_fusion) | copy-start | bytes 580
  3.1 7.1 %copy-start.7 = (f32[1536]{0:T(1024)}, f32[1536]{0:T(1024)S(1)}, u32[]{:S(2)}) copy-start(f32[1536]{0:T(1024)S(1)} %convert_element_type.144) | copy-start | bytes 18436
  4.3 5.9 %copy-start.13 = (f32[2,64]{1,0:T(2,128)}, f32[2,64]{1,0:T(2,128)S(1)}, u32[]{:S(2)}) copy-start(f32[2,64]{1,0:T(2,128)S(1)} %add_rsqrt_fusion) | copy-start | bytes 1540
  7.2 3.1 %copy-start.6 = (f32[2,64]{1,0:T(2,128)}, f32[2,64]{1,0:T(2,128)S(1)}, u32[]{:S(2)}) copy-start(f32[2,64]{1,0:T(2,128)S(1)} %add_convert_fusion.1) | copy-start | bytes 1540
  7.3 4.4 %copy-start.4 = (bf16[2048,96]{0,1:T(8,128)(2,1)S(1)}, bf16[2048,96]{0,1:T(8,128)(2,1)}, u32[]{:S(2)}) copy-start(bf16[2048,96]{0,1:T(8,128)(2,1)} %param.23) | copy-start | bytes 1179652
  11.7 1.5 %copy-start.15 = (bf16[2048,96]{0,1:T(8,128)(2,1)S(1)}, bf16[2048,96]{0,1:T(8,128)(2,1)}, u32[]{:S(2)}) copy-start(bf16[2048,96]{0,1:T(8,128)(2,1)} %param.24) | copy-start | bytes 1179652
  12.6 1.2 copy-start.8
  12.6 1.2 copy-start.14
  12.6 1.2 copy-start.16
  13.2 1.8 %copy-start.3 = (bf16[192,1536]{1,0:T(8,128)(2,1)S(1)}, bf16[192,1536]{1,0:T(8,128)(2,1)}, u32[]{:S(2)}) copy-start(bf16[192,1536]{1,0:T(8,128)(2,1)} %param.31) | copy-start | bytes 1769476
  13.7 8.7 %copy-start.10 = (bf16[1536]{0:T(1024)(128)(2,1)S(1)}, bf16[1536]{0:T(1024)(128)(2,1)}, u32[]{:S(2)}) copy-start(bf16[1536]{0:T(1024)(128)(2,1)} %param.26) | copy-start | bytes 9220
  14.1 0.6 copy-start.18
  16.1 22.3 %copy-start.17 = (s32[64]{0:T(128)S(1)}, s32[64]{0:T(128)}, u32[]{:S(2)}) copy-start(s32[64]{0:T(128)} %param.20) | copy-start | bytes 772
  16.1 13.9 %all-to-all-start = ((bf16[8,16,1536]{2,1,0:T(8,128)(2,1)}), bf16[8,16,1536]{2,1,0:T(8,128)(2,1)}, u32[]{:S(2)}, u32[]{:S(2)}) async-start(bf16[8,16,1536]{2,1,0:T(8,128)(2,1)} %fusion.1), calls=%async_computation | async-start | bytes 786432 | tf_op jit(solution)/shard_map/all_to_all | solution.py:30
  32.1 0.6 copy-start.2
  33.6 12.3 %all-to-all-start.1 = ((bf16[8,16,1536]{2,1,0:T(8,128)(2,1)}), bf16[8,16,1536]{2,1,0:T(8,128)(2,1)S(1)}, u32[]{:S(2)}, u32[]{:S(2)}) async-start(bf16[8,16,1536]{2,1,0:T(8,128)(2,1)} %broadcast_in_dim.117), calls=%async_computation.1 | async-start | bytes 786432 | tf_op jit(solution)/shard_map/all_to_all | solution.py:36
  48.4 9.7 %copy-start.9 = (s32[2,8]{1,0:T(2,128)S(1)}, s32[2,8]{1,0:T(2,128)}, u32[]{:S(2)}) copy-start(s32[2,8]{1,0:T(2,128)} %param.21) | copy-start | bytes 196
  51.8 21.1 %copy-start.11 = (bf16[1536]{0:T(1024)(128)(2,1)S(1)}, bf16[1536]{0:T(1024)(128)(2,1)}, u32[]{:S(2)}) copy-start(bf16[1536]{0:T(1024)(128)(2,1)} %param.27) | copy-start | bytes 9220
  51.8 12.4 %all-to-all-start.2 = ((bf16[8,16,1536]{2,1,0:T(8,128)(2,1)}), bf16[8,16,1536]{2,1,0:T(8,128)(2,1)S(1)}, u32[]{:S(2)}, u32[]{:S(2)}) async-start(bf16[8,16,1536]{2,1,0:T(8,128)(2,1)} %bitcast.154), calls=%async_computation.2 | async-start | bytes 786432 | tf_op jit(solution)/shard_map/all_to_all | solution.py:30
  64.9 24.8 %copy-start.19 = (bf16[2,64,96]{2,1,0:T(8,128)(2,1)S(1)}, bf16[2,64,96]{2,1,0:T(8,128)(2,1)}, u32[]{:S(2)}) copy-start(bf16[2,64,96]{2,1,0:T(8,128)(2,1)} %copy-done.18) | copy-start | bytes 73732
  68.2 9.1 %all-to-all-start.3 = ((bf16[8,2,3072]{2,1,0:T(2,128)(2,1)}), bf16[8,2,3072]{2,1,0:T(2,128)(2,1)S(1)}, u32[]{:S(2)}, u32[]{:S(2)}) async-start(bf16[8,2,3072]{2,1,0:T(2,128)(2,1)} %reshape.481), calls=%async_computation.3 | async-start | bytes 196608 | tf_op jit(solution)/shard_map/all_to_all | solution.py:220
  79.6 21.2 %all-to-all-start.4 = ((bf16[32,2,1536]{2,1,0:T(2,128)(2,1)}), bf16[32,2,1536]{2,1,0:T(2,128)(2,1)S(1)}, u32[]{:S(2)}, u32[]{:S(2)}) async-start(bf16[32,2,1536]{2,1,0:T(2,128)(2,1)} %broadcast_in_dim.119), calls=%async_computation.4 | async-start | bytes 393216 | tf_op jit(solution)/shard_map/all_to_all | solution.py:36
  100.9 6.7 %copy-start.5 = (bf16[8,3072]{1,0:T(8,128)(2,1)S(1)}, bf16[8,3072]{1,0:T(8,128)(2,1)}, u32[]{:S(2)}) copy-start(bf16[8,3072]{1,0:T(8,128)(2,1)} %get-tuple-element.10) | copy-start | bytes 147460
  102.7 14.0 %all-to-all-start.5 = ((f32[32,1,64]{2,1,0:T(1,128)}), f32[32,1,64]{2,1,0:T(1,128)S(1)}, u32[]{:S(2)}, u32[]{:S(2)}) async-start(f32[32,1,64]{2,1,0:T(1,128)} %broadcast_in_dim.120), calls=%async_computation.5 | async-start | bytes 32768 | tf_op jit(solution)/shard_map/all_to_all | solution.py:36

commit v5 on v2

--- a/solution.py
+++ b/solution.py
@@ -22,13 +22,6 @@
             jnp.einsum("bij,bjk->bik", reached, reached, precision=lax.Precision.HIGHEST), 1.0
         )
     return reached
-
-
-def scatter_rows(partial, axis_name, shards):
-    rows = partial.shape[0] // shards
-    pieces = partial.reshape(shards, rows, *partial.shape[1:]).astype(jnp.bfloat16)
-    arrived = lax.all_to_all(pieces, axis_name, split_axis=0, concat_axis=0, tiled=True)
-    return jnp.sum(arrived.astype(jnp.float32), axis=0)
 
 
 def gather_rows(chunk, axis_name, shards):
@@ -169,9 +162,38 @@
     fresh_values = fresh_values.transpose(0, 2, 1, 3)
     chunk_rows = token_rows // vocab_shards
     chunk_start = vocab_shard * chunk_rows
-    residual_chunk = lax.dynamic_slice_in_dim(states, chunk_start, chunk_rows, 0) + scatter_rows(
-        attend_part, "vocab", vocab_shards
-    )
+    share_width = model_width // vocab_shards
+    path_length = path_index.shape[1]
+    per_shard = path_length // vocab_shards
+    path_count = local_requests * per_shard
+    path_rows_all = (
+        (
+            path_index.reshape(local_requests, vocab_shards, per_shard)
+            + (jnp.arange(local_requests, dtype=jnp.int32) * draft_length)[:, None, None]
+        )
+        .transpose(1, 0, 2)
+        .reshape(vocab_shards, path_count)
+    )
+    own_path_rows = lax.dynamic_index_in_dim(path_rows_all, vocab_shard, keepdims=False)
+    send_rows = jnp.concatenate(
+        [
+            jnp.arange(token_rows, dtype=jnp.int32).reshape(vocab_shards, chunk_rows),
+            path_rows_all,
+        ],
+        axis=1,
+    ).reshape(-1)
+
+    def scatter_with_path(partial):
+        pieces = jnp.take(partial.astype(jnp.bfloat16), send_rows, axis=0).reshape(
+            vocab_shards, chunk_rows + path_count, model_width
+        )
+        arrived = lax.all_to_all(pieces, "vocab", split_axis=0, concat_axis=0, tiled=True)
+        summed = jnp.sum(arrived.astype(jnp.float32), axis=0)
+        return summed[:chunk_rows], summed[chunk_rows:]
+
+    attn_chunk, attn_path = scatter_with_path(attend_part)
+    residual_chunk = lax.dynamic_slice_in_dim(states, chunk_start, chunk_rows, 0) + attn_chunk
+    residual_path = jnp.take(states, own_path_rows, axis=0) + attn_path
     hidden_chunk = (
         residual_chunk
         * lax.rsqrt(jnp.mean(residual_chunk * residual_chunk, axis=1, keepdims=True) + eps_norm)
@@ -182,7 +204,9 @@
     up_out = jnp.dot(hidden_in, up_weight, preferred_element_type=jnp.float32)
     hidden = (jax.nn.silu(gate_out) * up_out).astype(jnp.bfloat16)
     down_part = jnp.dot(hidden, down_weight, preferred_element_type=jnp.float32)
-    feed_chunk = scatter_rows(down_part, "vocab", vocab_shards).astype(jnp.bfloat16)
+    feed_chunk, feed_path = scatter_with_path(down_part)
+    feed_chunk = feed_chunk.astype(jnp.bfloat16)
+    feed_path = feed_path.astype(jnp.bfloat16)
     local_counts = lax.dynamic_slice_in_dim(
         live_draft_count, request_shard * local_requests, local_requests
     )
@@ -192,10 +216,19 @@
     layer_chunk = jnp.where(
         chunk_live[:, None], residual_chunk + feed_chunk.astype(jnp.float32), 0.0
     ).astype(jnp.bfloat16)
-    updated = gather_rows(layer_chunk, "vocab", vocab_shards)
-    share_width = model_width // vocab_shards
-    layer_part = lax.dynamic_slice_in_dim(updated, vocab_shard * share_width, share_width, 1)
-    path_length = path_index.shape[1]
+    column_pieces = (
+        layer_chunk.reshape(chunk_rows, vocab_shards, share_width)
+        .transpose(1, 0, 2)
+        .reshape(vocab_shards, chunk_rows * share_width)
+    )
+    arrived = lax.all_to_all(column_pieces, "vocab", split_axis=0, concat_axis=0, tiled=True)
+    layer_part = arrived.reshape(token_rows, share_width)
+    path_live = (own_path_rows % draft_length) < jnp.take(
+        local_counts, own_path_rows // draft_length
+    )
+    head_rows = jnp.where(
+        path_live[:, None], residual_path + feed_path.astype(jnp.float32), 0.0
+    ).astype(jnp.bfloat16)
     request_picker = (
         path_index[:, :, None] == jnp.arange(draft_length, dtype=jnp.int32)[None, None, :]
     ).astype(jnp.bfloat16)
@@ -211,15 +244,7 @@
         fresh_values.reshape(local_requests, draft_length, key_local * head_dim),
         preferred_element_type=jnp.float32,
     ).astype(jnp.bfloat16)
-    per_shard = path_length // vocab_shards
-    head_picker = lax.dynamic_slice_in_dim(request_picker, vocab_shard * per_shard, per_shard, 1)
-    head_rows = jnp.einsum(
-        "ytm,ymu->ytu",
-        head_picker,
-        updated.reshape(local_requests, draft_length, model_width),
-        preferred_element_type=jnp.float32,
-    ).astype(jnp.bfloat16)
-    flat_rows = head_rows.reshape(local_requests * per_shard, model_width).astype(jnp.float32)
+    flat_rows = head_rows.astype(jnp.float32)
     mean_square = jnp.mean(flat_rows * flat_rows, axis=1)
     norm_values = jnp.sqrt(mean_square + eps_norm).reshape(local_requests, per_shard)
     head_in = (

time: 118 us -> 129 us (1.093)
  blocking collectives: 11.3 us -> 0 us
  local copies, waits for them, and re-layouts: 6.74 us -> 16.9 us
  other arithmetic: 14 us -> 22.7 us
  starting transfers between devices: 30.2 us -> 35.6 us
  waiting for transfers between devices: 37.1 us -> 33.8 us
    all_to_all x1 -> x0, blocking collectives: 11.3 us -> none  [gather_rows(): lax.all_to_all(copies, axis_name, split_axis=0, concat_axis=0, tiled=True)]
    gather x0 -> x4, local copies, waits for them, and re-layouts: none -> 5.78 us  [the longest x2 3.45 us: scatter_with_path(): jnp.take(partial.astype(jnp.bfloat16), send_rows, axis=0)]
    all_to_all x2 -> x3, starting transfers between devices: 11.2 us -> 16.7 us  [the longest x2 12 us: scatter_with_path(): lax.all_to_all(pieces, 'vocab', split_axis=0, concat_axis=0, tiled=True)]
    select_n x0 -> x5, other arithmetic: none -> 4.05 us  [the longest x3 2.83 us: scatter_with_path(): jnp.take(partial.astype(jnp.bfloat16), send_rows, axis=0)]
    all_to_all x3, waiting for transfers between devices: 25 us -> 22.1 us  [gather_rows(): lax.all_to_all(copies, axis_name, split_axis=0, concat_axis=0, tiled=True)]
    unnamed x39 -> x53, local copies, waits for them, and re-layouts: 1.37 us -> 3.7 us
    reshape x0 -> x6, local copies, waits for them, and re-layouts: none -> 2.24 us  [the longest x2 1.94 us: scatter_with_path(): jnp.take(partial.astype(jnp.bfloat16), send_rows, axis=0)]
    dot_general x1, matrix products: 1.07 us -> 2.49 us  [per_device(): jnp.dot(hidden_in, gate_weight, preferred_element_type=jnp.float32)]
  transfers between devices with their start and end apart: 5 -> 6, of which waited for: 5 -> 6; matrix products, arithmetic and copies ran while one was open for 5% -> 14% of each run, Pallas kernels for 0% -> 0%
where the time goes in v5:
time: 129 us; the launch traced here: 127 us
  starting transfers between devices  35.6 us (28%)
  waiting for transfers between devices  33.8 us (26%)
  other arithmetic  22.7 us (18%)
  local copies, waits for them, and re-layouts  16.9 us (13%)
  matrix products  16.8 us (13%)
    all_to_all x3, waiting for transfers between devices, gather_rows(): lax.all_to_all(copies, axis_name, split_axis=0, concat_axis=0, tiled=True)  22.1 us
    all_to_all x3, starting transfers between devices, gather_rows(): lax.all_to_all(copies, axis_name, split_axis=0, concat_axis=0, tiled=True)  18.9 us
    all_to_all x2, starting transfers between devices, scatter_with_path(): lax.all_to_all(pieces, 'vocab', split_axis=0, concat_axis=0, tiled=True)  12 us
    all_to_all x2, waiting for transfers between devices, scatter_with_path(): lax.all_to_all(pieces, 'vocab', split_axis=0, concat_axis=0, tiled=True)  10.5 us
    all_to_all x1, starting transfers between devices, per_device(): lax.all_to_all(column_pieces, 'vocab', split_axis=0, concat_axis=0, tiled...  4.7 us
    unnamed x53, local copies, waits for them, and re-layouts  3.7 us
    gather x2, local copies, waits for them, and re-layouts, scatter_with_path(): jnp.take(partial.astype(jnp.bfloat16), send_rows, axis=0)  3.45 us
    select_n x3, other arithmetic, scatter_with_path(): jnp.take(partial.astype(jnp.bfloat16), send_rows, axis=0)  2.83 us
  transfers between devices with their start and end apart: 6, of which 6 were waited for; matrix products, arithmetic and copies ran while one was open for 14% of the time, Pallas kernels for 0%

profile of v5, /device:TPU:2, one launch (start us, length us, event | category | flops | bytes accessed | tf_op | source)
XLA Modules:
  0.0 127.1 jit_solution(11506127339526550712)
XLA Ops:
  0.7 0.9 copy.69
  3.1 0.8 fusion.46
  3.8 0.7 add.226
  4.6 0.7 convert_element_type.128
  5.3 1.2 multiply_reduce_fusion
  6.5 1.0 convolution_minimum_fusion.5
  8.6 0.7 add_convert_fusion.1
  9.5 1.6 %convolution_bitcast_fusion.1 = f32[2,1,2,64,96]{4,3,2,0,1:T(8,128)S(1)} fusion(bf16[1536,2,96,1]{0,2,1,3:T(8,128)(2,1)} %bitcast.154, bf16[2,64,1536]{2,1,0:T(8,128)(2,1)} %param.20, f32[1536]{0:T(1024)S(1)} %convert_element_type.128, f32[2,64]{1,0:T(2,128)S(1)} %add_rsqrt_fusion), kind=kOutput, calls=%fused_computation.16 | convolution fusion | flops 76283904 | bytes 1088000 | tf_op jit(solution)/shard_map/rim,mkgd->rkgid/dot_general | solution.py:94
  11.1 1.3 %convolution_bitcast_fusion.4 = f32[2,1,64,96]{3,2,0,1:T(8,128)S(1)} fusion(bf16[1536,96]{0,1:T(8,128)(2,1)} %param.31, bf16[2,64,1536]{2,1,0:T(8,128)(2,1)S(1)} %copy-done.1, f32[1536]{0:T(1024)S(1)} %convert_element_type.128, f32[2,64]{1,0:T(2,128)S(1)} %add_rsqrt_fusion), kind=kOutput, calls=%fused_computation.23 | convolution fusion | flops 38535168 | bytes 743936 | tf_op jit(solution)/shard_map/rim,mkd->rkid/dot_general | solution.py:102
  12.7 1.0 fusion.36
  17.5 1.7 %gather_fusion.2 = bf16[144,1536]{1,0:T(8,128)(2,1)} fusion(bf16[128,1536]{1,0:T(8,128)(2,1)S(1)} %fusion.1, s32[1024]{0:T(1024)S(1)} %pad_clamp_fusion.2), kind=kCustom, calls=%fused_computation.clone | custom fusion | bytes 885312 | tf_op jit(solution)/shard_map/jit(_take)/gather | solution.py:187
  19.2 1.1 broadcast_select_fusion.1
  20.3 1.0 reshape.457
  21.3 6.3 %all-to-all-start = ((bf16[8,18,1536]{2,1,0:T(8,128)(2,1)}), bf16[8,18,1536]{2,1,0:T(8,128)(2,1)}, u32[]{:S(2)}, u32[]{:S(2)}) async-start(bf16[8,18,1536]{2,1,0:T(8,128)(2,1)} %reshape.457), calls=%async_computation | async-start | bytes 1179648 | tf_op jit(solution)/shard_map/all_to_all | solution.py:190
  27.6 0.7 compare_select_fusion.2
  29.4 2.0 %bitcast_convert_fusion = f32[128,1536]{1,0:T(8,128)} fusion(bf16[2,64,1536]{2,1,0:T(8,128)(2,1)} %param.20), kind=kLoop, calls=%fused_computation.155 | loop fusion | flops 196608 | bytes 1179648 | tf_op jit(solution)/shard_map/convert_element_type | solution.py:64
  31.3 6.0 %all-to-all-done = bf16[8,18,1536]{2,1,0:T(8,128)(2,1)} async-done(((bf16[8,18,1536]{2,1,0:T(8,128)(2,1)}), bf16[8,18,1536]{2,1,0:T(8,128)(2,1)}, u32[]{:S(2)}, u32[]{:S(2)}) %all-to-all-start) | async-done | bytes 442400 | tf_op jit(solution)/shard_map/all_to_all | solution.py:190
  37.3 1.2 convert_reduce_fusion.1
  38.5 1.1 multiply_reduce_fusion.1
  40.3 0.8 broadcast_in_dim.152
  41.1 4.8 %all-to-all-start.1 = ((bf16[8,16,1536]{2,1,0:T(8,128)(2,1)}), bf16[8,16,1536]{2,1,0:T(8,128)(2,1)S(1)}, u32[]{:S(2)}, u32[]{:S(2)}) async-start(bf16[8,16,1536]{2,1,0:T(8,128)(2,1)} %broadcast_in_dim.152), calls=%async_computation.1 | async-start | bytes 786432 | tf_op jit(solution)/shard_map/all_to_all | solution.py:29
  47.8 5.6 %all-to-all-done.1 = bf16[8,16,1536]{2,1,0:T(8,128)(2,1)S(1)} async-done(((bf16[8,16,1536]{2,1,0:T(8,128)(2,1)}), bf16[8,16,1536]{2,1,0:T(8,128)(2,1)S(1)}, u32[]{:S(2)}, u32[]{:S(2)}) %all-to-all-start.1) | async-done | bytes 393248 | tf_op jit(solution)/shard_map/all_to_all | solution.py:29
  53.4 0.7 copy-done.2
  54.1 2.5 %fusion.60 = f32[128,512]{1,0:T(8,128)} fusion(bf16[128,1536]{1,0:T(8,128)(2,1)S(1)} %bitcast.145, bf16[1536,512]{1,0:T(8,128)(2,1)} %param.34), kind=kOutput, calls=%fused_computation.156 | convolution fusion | flops 201326592 | bytes 2228224 | tf_op jit(solution)/shard_map/dot_general | solution.py:203
  56.6 2.8 %convolution_convert_fusion = bf16[128,1536]{1,0:T(8,128)(2,1)S(1)} fusion(bf16[512,1536]{1,0:T(8,128)(2,1)} %param.36, bf16[128,1536]{1,0:T(8,128)(2,1)} %bitcast.146, bf16[1536,512]{1,0:T(8,128)(2,1)} %param.35, f32[128,512]{1,0:T(8,128)} %fusion.60), kind=kOutput, calls=%fused_computation.8 | convolution fusion | flops 403243008 | bytes 4194304 | tf_op jit(solution)/shard_map/dot_general | solution.py:206
  59.4 1.7 %gather_fusion.3 = bf16[144,1536]{1,0:T(8,128)(2,1)} fusion(bf16[128,1536]{1,0:T(8,128)(2,1)S(1)} %convolution_convert_fusion, s32[1024]{0:T(1024)S(1)} %pad_clamp_fusion.2), kind=kCustom, calls=%fused_computation.1.clone | custom fusion | bytes 885312 | tf_op jit(solution)/shard_map/jit(_take)/gather | solution.py:187
  61.1 1.1 broadcast_select_fusion
  62.3 1.0 reshape.459
  63.3 5.7 %all-to-all-start.2 = ((bf16[8,18,1536]{2,1,0:T(8,128)(2,1)}), bf16[8,18,1536]{2,1,0:T(8,128)(2,1)}, u32[]{:S(2)}, u32[]{:S(2)}) async-start(bf16[8,18,1536]{2,1,0:T(8,128)(2,1)} %reshape.459), calls=%async_computation.2 | async-start | bytes 1179648 | tf_op jit(solution)/shard_map/all_to_all | solution.py:190
  68.9 0.7 pad_clamp_fusion
  69.6 1.7 %gather_fusion.1 = f32[2,1536]{1,0:T(2,128)S(1)} fusion(f32[128,1536]{1,0:T(8,128)} %bitcast_convert_fusion, s32[1024]{0:T(1024)S(1)} %pad_clamp_fusion), kind=kCustom, calls=%fused_computation.3 | custom fusion | bytes 24584 | tf_op jit(solution)/shard_map/jit(_take)/gather | solution.py:196
  71.3 1.3 %fusion.47 = pred[16]{0:T(512)(128)(4,1)S(1)} fusion(s32[]{:T(128)} %bitcast.1, s32[]{:T(128)} %bitcast, s32[]{:T(128)S(6)} %mul.182), kind=kLoop, calls=%fused_computation.137 | loop fusion | flops 784 | bytes 28 | tf_op jit(solution)/shard_map/lt | solution.py:215
  72.6 1.5 %convolution_convert_fusion.2 = bf16[2,8,96]{2,1,0:T(8,128)(2,1)} fusion(bf16[2,64,96]{2,1,0:T(8,128)(2,1)} %copy-done.24, s32[2,8]{1,0:T(2,128)S(1)} %copy-done.14), kind=kOutput, calls=%fused_computation.32 | convolution fusion | flops 199168 | bytes 27712 | tf_op jit(solution)/shard_map/ytm,ymu->ytu/dot_general | solution.py:241
  74.2 4.4 %all-to-all-done.2 = bf16[8,18,1536]{2,1,0:T(8,128)(2,1)} async-done(((bf16[8,18,1536]{2,1,0:T(8,128)(2,1)}), bf16[8,18,1536]{2,1,0:T(8,128)(2,1)}, u32[]{:S(2)}, u32[]{:S(2)}) %all-to-all-start.2) | async-done | bytes 442400 | tf_op jit(solution)/shard_map/all_to_all | solution.py:190
  78.6 1.2 reduce.8
  79.8 1.0 fusion.38
  81.4 0.8 broadcast_in_dim.159
  82.2 10.0 %all-to-all-start.4 = ((bf16[32,2,1536]{2,1,0:T(2,128)(2,1)}), bf16[32,2,1536]{2,1,0:T(2,128)(2,1)S(1)}, u32[]{:S(2)}, u32[]{:S(2)}) async-start(bf16[32,2,1536]{2,1,0:T(2,128)(2,1)} %broadcast_in_dim.159), calls=%async_computation.4 | async-start | bytes 393216 | tf_op jit(solution)/shard_map/all_to_all | solution.py:29
  93.1 0.9 reduce.10
  94.6 8.5 %all-to-all-done.4 = bf16[32,2,1536]{2,1,0:T(2,128)(2,1)S(1)} async-done(((bf16[32,2,1536]{2,1,0:T(2,128)(2,1)}), bf16[32,2,1536]{2,1,0:T(2,128)(2,1)S(1)}, u32[]{:S(2)}, u32[]{:S(2)}) %all-to-all-start.4) | async-done | bytes 196640 | tf_op jit(solution)/shard_map/all_to_all | solution.py:29
  103.2 4.7 %all-to-all-start.3 = ((bf16[8,2,1536]{2,1,0:T(2,128)(2,1)}), bf16[8,2,1536]{2,1,0:T(2,128)(2,1)S(1)}, u32[]{:S(2)}, u32[]{:S(2)}) async-start(bf16[8,2,1536]{2,1,0:T(2,128)(2,1)} %reshape.531), calls=%async_computation.3 | async-start | bytes 98304 | tf_op jit(solution)/shard_map/all_to_all | solution.py:224
  107.9 0.7 reshape.461
  108.6 2.1 %convolution_reduce_fusion = f32[64]{0:T(128)S(1)} fusion(bf16[64,1536]{1,0:T(8,128)(2,1)} %reshape.461, bf16[1536,1000]{0,1:T(8,128)(2,1)S(1)} %copy-done), kind=kOutput, calls=%fused_computation.15 | convolution fusion | flops 196671936 | bytes 3268864 | tf_op jit(solution)/shard_map/dot_general | solution.py:254
  110.7 1.3 %all-to-all-done.3 = bf16[8,2,1536]{2,1,0:T(2,128)(2,1)S(1)} async-done(((bf16[8,2,1536]{2,1,0:T(2,128)(2,1)}), bf16[8,2,1536]{2,1,0:T(2,128)(2,1)S(1)}, u32[]{:S(2)}, u32[]{:S(2)}) %all-to-all-start.3) | async-done | bytes 49184 | tf_op jit(solution)/shard_map/all_to_all | solution.py:224
  112.6 4.2 %all-to-all-start.5 = ((f32[32,1,64]{2,1,0:T(1,128)}), f32[32,1,64]{2,1,0:T(1,128)S(1)}, u32[]{:S(2)}, u32[]{:S(2)}) async-start(f32[32,1,64]{2,1,0:T(1,128)} %broadcast_in_dim.160), calls=%async_computation.5 | async-start | bytes 32768 | tf_op jit(solution)/shard_map/all_to_all | solution.py:29
  116.8 0.8 convolution_convert_fusion.3
  117.9 0.8 reshape_reshape.3
  118.6 7.9 %all-to-all-done.5 = f32[32,1,64]{2,1,0:T(1,128)S(1)} async-done(((f32[32,1,64]{2,1,0:T(1,128)}), f32[32,1,64]{2,1,0:T(1,128)S(1)}, u32[]{:S(2)}, u32[]{:S(2)}) %all-to-all-start.5) | async-done | bytes 8224 | tf_op jit(solution)/shard_map/all_to_all | solution.py:29
  (106 shorter events, 13.7 us)
Async XLA Ops:
  0.6 108.0 %copy-start = (bf16[1536,1000]{0,1:T(8,128)(2,1)S(1)}, bf16[1536,1000]{0,1:T(8,128)(2,1)}, u32[]{:S(2)}) copy-start(bf16[1536,1000]{0,1:T(8,128)(2,1)} %param.37) | copy-start | bytes 9216004
  0.6 10.4 %copy-start.1 = (bf16[2,64,1536]{2,1,0:T(8,128)(2,1)S(1)}, bf16[2,64,1536]{2,1,0:T(8,128)(2,1)}, u32[]{:S(2)}) copy-start(bf16[2,64,1536]{2,1,0:T(8,128)(2,1)} %param.20) | copy-start | bytes 1179652
  0.7 11.7 %copy-start.18 = (f32[48]{0:T(128)}, f32[48]{0:T(128)S(1)}, u32[]{:S(2)}) copy-start(f32[48]{0:T(128)S(1)} %multiply_power_fusion) | copy-start | bytes 580
  1.7 7.6 %copy-start.10 = (s32[2,8]{0,1:T(8,128)}, s32[2,8]{0,1:T(8,128)S(1)}, u32[]{:S(2)}) copy-start(s32[2,8]{0,1:T(8,128)S(1)} %broadcast_add_fusion) | copy-start | bytes 196
  5.3 7.1 %copy-start.12 = (f32[1536]{0:T(1024)}, f32[1536]{0:T(1024)S(1)}, u32[]{:S(2)}) copy-start(f32[1536]{0:T(1024)S(1)} %convert_element_type.128) | copy-start | bytes 18436
  6.5 5.9 %copy-start.19 = (f32[2,64]{1,0:T(2,128)}, f32[2,64]{1,0:T(2,128)S(1)}, u32[]{:S(2)}) copy-start(f32[2,64]{1,0:T(2,128)S(1)} %add_rsqrt_fusion) | copy-start | bytes 1540
  9.3 3.1 %copy-start.11 = (f32[2,64]{1,0:T(2,128)}, f32[2,64]{1,0:T(2,128)S(1)}, u32[]{:S(2)}) copy-start(f32[2,64]{1,0:T(2,128)S(1)} %add_convert_fusion.1) | copy-start | bytes 1540
  9.4 4.4 %copy-start.7 = (bf16[2048,96]{0,1:T(8,128)(2,1)S(1)}, bf16[2048,96]{0,1:T(8,128)(2,1)}, u32[]{:S(2)}) copy-start(bf16[2048,96]{0,1:T(8,128)(2,1)} %param.25) | copy-start | bytes 1179652
  13.7 1.6 %copy-start.8 = (bf16[2,64,48]{2,1,0:T(8,128)(2,1)}, bf16[2,64,48]{2,1,0:T(8,128)(2,1)S(1)}, u32[]{:S(2)}) copy-start(bf16[2,64,48]{2,1,0:T(8,128)(2,1)S(1)} %get-tuple-element.15) | copy-start | bytes 36868
  13.9 1.5 %copy-start.21 = (bf16[2048,96]{0,1:T(8,128)(2,1)S(1)}, bf16[2048,96]{0,1:T(8,128)(2,1)}, u32[]{:S(2)}) copy-start(bf16[2048,96]{0,1:T(8,128)(2,1)} %param.26) | copy-start | bytes 1179652
  14.8 1.2 copy-start.13
  14.8 1.2 copy-start.20
  14.8 1.2 copy-start.22
  15.3 1.8 %copy-start.17 = (s32[144]{0:T(256)S(1)}, s32[144]{0:T(256)}, u32[]{:S(2)}) copy-start(s32[144]{0:T(256)} %compare_select_fusion) | copy-start | bytes 1732
  15.3 1.8 %copy-start.5 = (bf16[192,1536]{1,0:T(8,128)(2,1)S(1)}, bf16[192,1536]{1,0:T(8,128)(2,1)}, u32[]{:S(2)}) copy-start(bf16[192,1536]{1,0:T(8,128)(2,1)} %param.33) | copy-start | bytes 1769476
  16.3 0.6 copy-start.24
  19.2 10.1 %copy-start.15 = (bf16[1536]{0:T(1024)(128)(2,1)S(1)}, bf16[1536]{0:T(1024)(128)(2,1)}, u32[]{:S(2)}) copy-start(bf16[1536]{0:T(1024)(128)(2,1)} %param.28) | copy-start | bytes 9220
  21.3 16.0 %all-to-all-start = ((bf16[8,18,1536]{2,1,0:T(8,128)(2,1)}), bf16[8,18,1536]{2,1,0:T(8,128)(2,1)}, u32[]{:S(2)}, u32[]{:S(2)}) async-start(bf16[8,18,1536]{2,1,0:T(8,128)(2,1)} %reshape.457), calls=%async_computation | async-start | bytes 1179648 | tf_op jit(solution)/shard_map/all_to_all | solution.py:190
  27.6 18.3 %copy-start.23 = (s32[64]{0:T(128)S(1)}, s32[64]{0:T(128)}, u32[]{:S(2)}) copy-start(s32[64]{0:T(128)} %param.22) | copy-start | bytes 772
  38.5 1.8 %copy-start.6 = (f32[18,1536]{1,0:T(8,128)}, f32[18,1536]{1,0:T(8,128)S(1)}, u32[]{:S(2)}) copy-start(f32[18,1536]{1,0:T(8,128)S(1)} %convert_reduce_fusion.1) | copy-start | bytes 331780
  39.6 0.6 copy-start.3
  41.1 12.3 %all-to-all-start.1 = ((bf16[8,16,1536]{2,1,0:T(8,128)(2,1)}), bf16[8,16,1536]{2,1,0:T(8,128)(2,1)S(1)}, u32[]{:S(2)}, u32[]{:S(2)}) async-start(bf16[8,16,1536]{2,1,0:T(8,128)(2,1)} %broadcast_in_dim.152), calls=%async_computation.1 | async-start | bytes 786432 | tf_op jit(solution)/shard_map/all_to_all | solution.py:29
  53.4 0.7 copy-start.2
  61.1 10.2 %copy-start.16 = (bf16[1536]{0:T(1024)(128)(2,1)S(1)}, bf16[1536]{0:T(1024)(128)(2,1)}, u32[]{:S(2)}) copy-start(bf16[1536]{0:T(1024)(128)(2,1)} %param.29) | copy-start | bytes 9220
  61.1 11.5 %copy-start.14 = (s32[2,8]{1,0:T(2,128)S(1)}, s32[2,8]{1,0:T(2,128)}, u32[]{:S(2)}) copy-start(s32[2,8]{1,0:T(2,128)} %param.23) | copy-start | bytes 196
  63.3 28.9 %copy-start.4 = (f32[16,1536]{1,0:T(8,128)S(1)}, f32[16,1536]{1,0:T(8,128)}, u32[]{:S(2)}) copy-start(f32[16,1536]{1,0:T(8,128)} %copy-done.3) | copy-start | bytes 294916
  63.3 15.4 %all-to-all-start.2 = ((bf16[8,18,1536]{2,1,0:T(8,128)(2,1)}), bf16[8,18,1536]{2,1,0:T(8,128)(2,1)}, u32[]{:S(2)}, u32[]{:S(2)}) async-start(bf16[8,18,1536]{2,1,0:T(8,128)(2,1)} %reshape.459), calls=%async_computation.2 | async-start | bytes 1179648 | tf_op jit(solution)/shard_map/all_to_all | solution.py:190
  82.2 21.0 %all-to-all-start.4 = ((bf16[32,2,1536]{2,1,0:T(2,128)(2,1)}), bf16[32,2,1536]{2,1,0:T(2,128)(2,1)S(1)}, u32[]{:S(2)}, u32[]{:S(2)}) async-start(bf16[32,2,1536]{2,1,0:T(2,128)(2,1)} %broadcast_in_dim.159), calls=%async_computation.4 | async-start | bytes 393216 | tf_op jit(solution)/shard_map/all_to_all | solution.py:29
  92.4 24.3 %copy-start.9 = (bf16[2,64,48]{2,1,0:T(8,128)(2,1)S(1)}, bf16[2,64,48]{2,1,0:T(8,128)(2,1)}, u32[]{:S(2)}) copy-start(bf16[2,64,48]{2,1,0:T(8,128)(2,1)} %copy-done.8) | copy-start | bytes 36868
  103.2 8.8 %all-to-all-start.3 = ((bf16[8,2,1536]{2,1,0:T(2,128)(2,1)}), bf16[8,2,1536]{2,1,0:T(2,128)(2,1)S(1)}, u32[]{:S(2)}, u32[]{:S(2)}) async-start(bf16[8,2,1536]{2,1,0:T(2,128)(2,1)} %reshape.531), calls=%async_computation.3 | async-start | bytes 98304 | tf_op jit(solution)/shard_map/all_to_all | solution.py:224
  112.6 14.0 %all-to-all-start.5 = ((f32[32,1,64]{2,1,0:T(1,128)}), f32[32,1,64]{2,1,0:T(1,128)S(1)}, u32[]{:S(2)}, u32[]{:S(2)}) async-start(f32[32,1,64]{2,1,0:T(1,128)} %broadcast_in_dim.160), calls=%async_computation.5 | async-start | bytes 32768 | tf_op jit(solution)/shard_map/all_to_all | solution.py:29

commit v6 on v4

--- a/solution.py
+++ b/solution.py
@@ -1,6 +1,8 @@
 import jax
 import jax.numpy as jnp
 from jax import lax
+from jax.experimental import pallas as pl
+from jax.experimental.pallas import tpu as pltpu
 from jax.sharding import PartitionSpec as P
 
 HEAD_SIZE = 96
@@ -22,6 +24,49 @@
             jnp.einsum("bij,bjk->bik", reached, reached, precision=lax.Precision.HIGHEST), 1.0
         )
     return reached
+
+
+def feed_forward_kernel(x_ref, gate_ref, up_ref, down_ref, out_ref, acc_ref):
+    step = pl.program_id(0)
+
+    @pl.when(step == 0)
+    def _():
+        acc_ref[...] = jnp.zeros_like(acc_ref)
+
+    x = x_ref[...]
+    gate_out = jnp.dot(x, gate_ref[...], preferred_element_type=jnp.float32)
+    up_out = jnp.dot(x, up_ref[...], preferred_element_type=jnp.float32)
+    hidden = (gate_out / (1.0 + jnp.exp(-gate_out)) * up_out).astype(jnp.bfloat16)
+    acc_ref[...] += jnp.dot(hidden, down_ref[...], preferred_element_type=jnp.float32)
+
+    @pl.when(step == pl.num_programs(0) - 1)
+    def _():
+        out_ref[...] = acc_ref[...].astype(out_ref.dtype)
+
+
+def feed_forward(hidden_in, gate_weight, up_weight, down_weight, block=256):
+    rows, width = hidden_in.shape
+    units = gate_weight.shape[1]
+    block = min(block, units)
+    return pl.pallas_call(
+        feed_forward_kernel,
+        grid=(units // block,),
+        in_specs=[
+            pl.BlockSpec((rows, width), lambda j: (0, 0)),
+            pl.BlockSpec((width, block), lambda j: (0, j)),
+            pl.BlockSpec((width, block), lambda j: (0, j)),
+            pl.BlockSpec((block, width), lambda j: (j, 0)),
+        ],
+        out_specs=pl.BlockSpec((rows, width), lambda j: (0, 0)),
+        out_shape=jax.ShapeDtypeStruct((rows, width), jnp.bfloat16),
+        scratch_shapes=[pltpu.VMEM((rows, width), jnp.float32)],
+        compiler_params=pltpu.CompilerParams(dimension_semantics=("arbitrary",)),
+        cost_estimate=pl.CostEstimate(
+            flops=6 * rows * width * units,
+            transcendentals=rows * units,
+            bytes_accessed=2 * (3 * width * units + 2 * rows * width),
+        ),
+    )(hidden_in, gate_weight, up_weight, down_weight)
 
 
 def scatter_rows(partial, axis_name, shards):
@@ -178,10 +223,7 @@
         * hidden_gain.astype(jnp.float32)
     ).astype(jnp.bfloat16)
     hidden_in = gather_rows(hidden_chunk, "vocab", vocab_shards)
-    gate_out = jnp.dot(hidden_in, gate_weight, preferred_element_type=jnp.float32)
-    up_out = jnp.dot(hidden_in, up_weight, preferred_element_type=jnp.float32)
-    hidden = (jax.nn.silu(gate_out) * up_out).astype(jnp.bfloat16)
-    down_part = jnp.dot(hidden, down_weight, preferred_element_type=jnp.float32)
+    down_part = feed_forward(hidden_in, gate_weight, up_weight, down_weight)
     feed_chunk = scatter_rows(down_part, "vocab", vocab_shards).astype(jnp.bfloat16)
     local_counts = lax.dynamic_slice_in_dim(
         live_draft_count, request_shard * local_requests, local_requests

time: 118 us -> 117 us (level)
  matrix products: 16.8 us -> 10.9 us
  Pallas kernels: 0 us -> 4.04 us
    dot_general x2 -> x0, matrix products: 5.9 us -> none  [the longest x1 3.42 us: per_device(): down_part = jnp.dot(hidden, down_weight, preferred_element_type=jnp.float32)]
    pallas_call x0 -> x1, Pallas kernels: none -> 4.04 us  [feed_forward(): pl.pallas_call(feed_forward_kernel, grid=(units // block,), in_specs=[pl....]
    unnamed x43 -> x45, local copies, waits for them, and re-layouts: 2.11 us -> 2.84 us
where the time goes in v6:
time: 117 us; the launch traced here: 116 us
  waiting for transfers between devices  42.5 us (36%)
  starting transfers between devices  35 us (30%)
  other arithmetic  15.1 us (13%)
  matrix products  10.9 us (9%)
  local copies, waits for them, and re-layouts  7.38 us (6%)
  Pallas kernels  4.04 us (3%)
    all_to_all x3, waiting for transfers between devices, gather_rows(): lax.all_to_all(copies, axis_name, split_axis=0, concat_axis=0, tiled=True)  25.4 us
    all_to_all x3, starting transfers between devices, gather_rows(): lax.all_to_all(copies, axis_name, split_axis=0, concat_axis=0, tiled=True)  19 us
    all_to_all x2, waiting for transfers between devices, scatter_rows(): lax.all_to_all(pieces, axis_name, split_axis=0, concat_axis=0, tiled=True)  12.7 us
    all_to_all x2, starting transfers between devices, scatter_rows(): lax.all_to_all(pieces, axis_name, split_axis=0, concat_axis=0, tiled=True)  11.3 us
    all_to_all x1, starting transfers between devices, per_device(): lax.all_to_all(jnp.concatenate([column_pieces, path_pieces], axis=1), 'vo...  4.72 us
    all_to_all x1, waiting for transfers between devices, per_device(): lax.all_to_all(jnp.concatenate([column_pieces, path_pieces], axis=1), 'vo...  4.36 us
    pallas_call x1, Pallas kernels, feed_forward(): pl.pallas_call(feed_forward_kernel, grid=(units // block,), in_specs=[pl....  4.04 us
    unnamed x45, local copies, waits for them, and re-layouts  2.84 us
  transfers between devices with their start and end apart: 6, of which 6 were waited for; matrix products, arithmetic and copies ran while one was open for 5% of the time, Pallas kernels for 0%

profile of v6, /device:TPU:2, one launch (start us, length us, event | category | flops | bytes accessed | tf_op | source)
XLA Modules:
  0.0 116.0 jit_solution(6512941546044404521)
XLA Ops:
  0.7 0.9 fusion.37
  1.6 0.7 add.180
  2.4 0.7 convert_element_type.135
  3.1 1.2 multiply_reduce_fusion
  4.3 1.0 convolution_minimum_fusion.5
  6.4 0.7 add_convert_fusion.1
  7.3 1.6 %convolution_bitcast_fusion.1 = f32[2,1,2,64,96]{4,3,2,0,1:T(8,128)S(1)} fusion(bf16[1536,2,96,1]{0,2,1,3:T(8,128)(2,1)} %bitcast.155, bf16[2,64,1536]{2,1,0:T(8,128)(2,1)} %param.18, f32[1536]{0:T(1024)S(1)} %convert_element_type.135, f32[2,64]{1,0:T(2,128)S(1)} %add_rsqrt_fusion), kind=kOutput, calls=%fused_computation.9 | convolution fusion | flops 76283904 | bytes 1088000 | tf_op jit(solution)/shard_map/rim,mkgd->rkgid/dot_general | solution.py:146
  8.9 1.3 %convolution_bitcast_fusion.4 = f32[2,1,64,96]{3,2,0,1:T(8,128)S(1)} fusion(bf16[1536,96]{0,1:T(8,128)(2,1)} %param.29, bf16[2,64,1536]{2,1,0:T(8,128)(2,1)S(1)} %copy-done.1, f32[1536]{0:T(1024)S(1)} %convert_element_type.135, f32[2,64]{1,0:T(2,128)S(1)} %add_rsqrt_fusion), kind=kOutput, calls=%fused_computation.16 | convolution fusion | flops 38535168 | bytes 743936 | tf_op jit(solution)/shard_map/rim,mkd->rkid/dot_general | solution.py:154
  10.6 1.0 fusion.30
  11.7 0.6 select_reduce_fusion
  12.6 0.5 convert_reduce_fusion
  13.2 0.5 convolution_bitcast_fusion.3
  14.1 0.6 copy-done.19
  15.0 1.1 fusion.1
  16.1 6.4 %all-to-all-start = ((bf16[8,16,1536]{2,1,0:T(8,128)(2,1)}), bf16[8,16,1536]{2,1,0:T(8,128)(2,1)}, u32[]{:S(2)}, u32[]{:S(2)}) async-start(bf16[8,16,1536]{2,1,0:T(8,128)(2,1)} %fusion.1), calls=%async_computation | async-start | bytes 786432 | tf_op jit(solution)/shard_map/all_to_all | solution.py:75
  22.4 1.0 bitcast_convert_fusion
  23.4 6.6 %all-to-all-done = bf16[8,16,1536]{2,1,0:T(8,128)(2,1)} async-done(((bf16[8,16,1536]{2,1,0:T(8,128)(2,1)}), bf16[8,16,1536]{2,1,0:T(8,128)(2,1)}, u32[]{:S(2)}, u32[]{:S(2)}) %all-to-all-start) | async-done | bytes 393248 | tf_op jit(solution)/shard_map/all_to_all | solution.py:75
  30.0 1.1 convert_reduce_fusion.1
  31.1 1.0 multiply_reduce_fusion.1
  32.1 0.6 copy-done.3
  32.8 0.8 broadcast_in_dim.117
  33.6 4.8 %all-to-all-start.1 = ((bf16[8,16,1536]{2,1,0:T(8,128)(2,1)}), bf16[8,16,1536]{2,1,0:T(8,128)(2,1)S(1)}, u32[]{:S(2)}, u32[]{:S(2)}) async-start(bf16[8,16,1536]{2,1,0:T(8,128)(2,1)} %broadcast_in_dim.117), calls=%async_computation.1 | async-start | bytes 786432 | tf_op jit(solution)/shard_map/all_to_all | solution.py:81
  38.5 0.6 fusion.46
  39.0 6.8 %all-to-all-done.1 = bf16[8,16,1536]{2,1,0:T(8,128)(2,1)S(1)} async-done(((bf16[8,16,1536]{2,1,0:T(8,128)(2,1)}), bf16[8,16,1536]{2,1,0:T(8,128)(2,1)S(1)}, u32[]{:S(2)}, u32[]{:S(2)}) %all-to-all-start.1) | async-done | bytes 393248 | tf_op jit(solution)/shard_map/all_to_all | solution.py:81
  45.9 0.7 copy-done.2
  46.6 4.0 %shard_map.209 = bf16[128,1536]{1,0:T(8,128)(2,1)} custom-call(bf16[128,1536]{1,0:T(8,128)(2,1)} %bitcast.146, bf16[1536,512]{1,0:T(8,128)(2,1)} %gate_ref.1, bf16[1536,512]{1,0:T(8,128)(2,1)} %up_ref.1, bf16[512,1536]{1,0:T(8,128)(2,1)} %down_ref.1), custom_call_target="tpu_custom_call" | custom-call | flops 603979776 | bytes 5505024 | tf_op jit(solution)/shard_map/pallas_call | solution.py:51
  50.7 4.9 %all-to-all-start.2 = ((bf16[8,16,1536]{2,1,0:T(8,128)(2,1)}), bf16[8,16,1536]{2,1,0:T(8,128)(2,1)S(1)}, u32[]{:S(2)}, u32[]{:S(2)}) async-start(bf16[8,16,1536]{2,1,0:T(8,128)(2,1)} %bitcast.147), calls=%async_computation.2 | async-start | bytes 786432 | tf_op jit(solution)/shard_map/all_to_all | solution.py:75
  55.6 1.3 %fusion.38 = pred[16]{0:T(512)(128)(4,1)S(1)} fusion(s32[]{:T(128)} %bitcast.1, s32[]{:T(128)} %bitcast, s32[]{:T(128)S(6)} %mul.183), kind=kLoop, calls=%fused_computation.105 | loop fusion | flops 784 | bytes 28 | tf_op jit(solution)/shard_map/lt | solution.py:233
  57.0 6.1 %all-to-all-done.2 = bf16[8,16,1536]{2,1,0:T(8,128)(2,1)S(1)} async-done(((bf16[8,16,1536]{2,1,0:T(8,128)(2,1)}), bf16[8,16,1536]{2,1,0:T(8,128)(2,1)S(1)}, u32[]{:S(2)}, u32[]{:S(2)}) %all-to-all-start.2) | async-done | bytes 393248 | tf_op jit(solution)/shard_map/all_to_all | solution.py:75
  63.1 0.7 reduce_sum.103
  63.8 1.0 select_convert_fusion.3
  65.7 0.7 reduce.10
  66.4 0.7 reshape.483
  67.1 4.7 %all-to-all-start.3 = ((bf16[8,2,3072]{2,1,0:T(2,128)(2,1)}), bf16[8,2,3072]{2,1,0:T(2,128)(2,1)S(1)}, u32[]{:S(2)}, u32[]{:S(2)}) async-start(bf16[8,2,3072]{2,1,0:T(2,128)(2,1)} %reshape.483), calls=%async_computation.3 | async-start | bytes 196608 | tf_op jit(solution)/shard_map/all_to_all | solution.py:262
  71.8 4.4 %all-to-all-done.3 = bf16[8,2,3072]{2,1,0:T(2,128)(2,1)S(1)} async-done(((bf16[8,2,3072]{2,1,0:T(2,128)(2,1)}), bf16[8,2,3072]{2,1,0:T(2,128)(2,1)S(1)}, u32[]{:S(2)}, u32[]{:S(2)}) %all-to-all-start.3) | async-done | bytes 98336 | tf_op jit(solution)/shard_map/all_to_all | solution.py:262
  76.3 0.6 slice_reduce_fusion
  77.1 0.5 fusion.40
  77.7 0.8 broadcast_in_dim.119
  78.5 10.1 %all-to-all-start.4 = ((bf16[32,2,1536]{2,1,0:T(2,128)(2,1)}), bf16[32,2,1536]{2,1,0:T(2,128)(2,1)S(1)}, u32[]{:S(2)}, u32[]{:S(2)}) async-start(bf16[32,2,1536]{2,1,0:T(2,128)(2,1)} %broadcast_in_dim.119), calls=%async_computation.4 | async-start | bytes 393216 | tf_op jit(solution)/shard_map/all_to_all | solution.py:81
  88.6 0.8 convolution_convert_fusion.2
  89.3 10.4 %all-to-all-done.4 = bf16[32,2,1536]{2,1,0:T(2,128)(2,1)S(1)} async-done(((bf16[32,2,1536]{2,1,0:T(2,128)(2,1)}), bf16[32,2,1536]{2,1,0:T(2,128)(2,1)S(1)}, u32[]{:S(2)}, u32[]{:S(2)}) %all-to-all-start.4) | async-done | bytes 196640 | tf_op jit(solution)/shard_map/all_to_all | solution.py:81
  99.8 1.1 convolution_reduce_fusion
  100.9 0.6 broadcast_in_dim.120
  101.6 4.1 %all-to-all-start.5 = ((f32[32,1,64]{2,1,0:T(1,128)}), f32[32,1,64]{2,1,0:T(1,128)S(1)}, u32[]{:S(2)}, u32[]{:S(2)}) async-start(f32[32,1,64]{2,1,0:T(1,128)} %broadcast_in_dim.120), calls=%async_computation.5 | async-start | bytes 32768 | tf_op jit(solution)/shard_map/all_to_all | solution.py:81
  105.7 0.8 convolution_convert_fusion.3
  106.5 0.8 reshape_reshape.4
  107.3 8.2 %all-to-all-done.5 = f32[32,1,64]{2,1,0:T(1,128)S(1)} async-done(((f32[32,1,64]{2,1,0:T(1,128)}), f32[32,1,64]{2,1,0:T(1,128)S(1)}, u32[]{:S(2)}, u32[]{:S(2)}) %all-to-all-start.5) | async-done | bytes 8224 | tf_op jit(solution)/shard_map/all_to_all | solution.py:81
  115.5 0.5 reduce_max.39
  (79 shorter events, 4.3 us)
Async XLA Ops:
  0.6 99.2 %copy-start = (bf16[1536,1000]{0,1:T(8,128)(2,1)S(1)}, bf16[1536,1000]{0,1:T(8,128)(2,1)}, u32[]{:S(2)}) copy-start(bf16[1536,1000]{0,1:T(8,128)(2,1)} %param.35) | copy-start | bytes 9216004
  0.6 8.3 %copy-start.1 = (bf16[2,64,1536]{2,1,0:T(8,128)(2,1)S(1)}, bf16[2,64,1536]{2,1,0:T(8,128)(2,1)}, u32[]{:S(2)}) copy-start(bf16[2,64,1536]{2,1,0:T(8,128)(2,1)} %param.18) | copy-start | bytes 1179652
  0.7 9.5 %copy-start.13 = (f32[48]{0:T(128)}, f32[48]{0:T(128)S(1)}, u32[]{:S(2)}) copy-start(f32[48]{0:T(128)S(1)} %multiply_power_fusion) | copy-start | bytes 580
  3.1 7.1 %copy-start.8 = (f32[1536]{0:T(1024)}, f32[1536]{0:T(1024)S(1)}, u32[]{:S(2)}) copy-start(f32[1536]{0:T(1024)S(1)} %convert_element_type.135) | copy-start | bytes 18436
  4.3 5.9 %copy-start.14 = (f32[2,64]{1,0:T(2,128)}, f32[2,64]{1,0:T(2,128)S(1)}, u32[]{:S(2)}) copy-start(f32[2,64]{1,0:T(2,128)S(1)} %add_rsqrt_fusion) | copy-start | bytes 1540
  7.2 3.1 %copy-start.7 = (f32[2,64]{1,0:T(2,128)}, f32[2,64]{1,0:T(2,128)S(1)}, u32[]{:S(2)}) copy-start(f32[2,64]{1,0:T(2,128)S(1)} %add_convert_fusion.1) | copy-start | bytes 1540
  7.3 4.4 %copy-start.5 = (bf16[2048,96]{0,1:T(8,128)(2,1)S(1)}, bf16[2048,96]{0,1:T(8,128)(2,1)}, u32[]{:S(2)}) copy-start(bf16[2048,96]{0,1:T(8,128)(2,1)} %param.23) | copy-start | bytes 1179652
  11.7 1.5 %copy-start.16 = (bf16[2048,96]{0,1:T(8,128)(2,1)S(1)}, bf16[2048,96]{0,1:T(8,128)(2,1)}, u32[]{:S(2)}) copy-start(bf16[2048,96]{0,1:T(8,128)(2,1)} %param.24) | copy-start | bytes 1179652
  12.6 1.2 copy-start.9
  12.6 1.2 copy-start.15
  12.6 1.2 copy-start.17
  13.2 1.8 %copy-start.4 = (bf16[192,1536]{1,0:T(8,128)(2,1)S(1)}, bf16[192,1536]{1,0:T(8,128)(2,1)}, u32[]{:S(2)}) copy-start(bf16[192,1536]{1,0:T(8,128)(2,1)} %param.31) | copy-start | bytes 1769476
  13.7 8.7 %copy-start.11 = (bf16[1536]{0:T(1024)(128)(2,1)S(1)}, bf16[1536]{0:T(1024)(128)(2,1)}, u32[]{:S(2)}) copy-start(bf16[1536]{0:T(1024)(128)(2,1)} %param.26) | copy-start | bytes 9220
  14.1 0.6 copy-start.19
  16.1 22.3 %copy-start.18 = (s32[64]{0:T(128)S(1)}, s32[64]{0:T(128)}, u32[]{:S(2)}) copy-start(s32[64]{0:T(128)} %param.20) | copy-start | bytes 772
  16.1 13.9 %all-to-all-start = ((bf16[8,16,1536]{2,1,0:T(8,128)(2,1)}), bf16[8,16,1536]{2,1,0:T(8,128)(2,1)}, u32[]{:S(2)}, u32[]{:S(2)}) async-start(bf16[8,16,1536]{2,1,0:T(8,128)(2,1)} %fusion.1), calls=%async_computation | async-start | bytes 786432 | tf_op jit(solution)/shard_map/all_to_all | solution.py:75
  32.1 0.6 copy-start.3
  33.6 12.3 %all-to-all-start.1 = ((bf16[8,16,1536]{2,1,0:T(8,128)(2,1)}), bf16[8,16,1536]{2,1,0:T(8,128)(2,1)S(1)}, u32[]{:S(2)}, u32[]{:S(2)}) async-start(bf16[8,16,1536]{2,1,0:T(8,128)(2,1)} %broadcast_in_dim.117), calls=%async_computation.1 | async-start | bytes 786432 | tf_op jit(solution)/shard_map/all_to_all | solution.py:81
  45.9 0.7 copy-start.2
  46.6 10.3 %copy-start.10 = (s32[2,8]{1,0:T(2,128)S(1)}, s32[2,8]{1,0:T(2,128)}, u32[]{:S(2)}) copy-start(s32[2,8]{1,0:T(2,128)} %param.21) | copy-start | bytes 196
  50.6 21.1 %copy-start.12 = (bf16[1536]{0:T(1024)(128)(2,1)S(1)}, bf16[1536]{0:T(1024)(128)(2,1)}, u32[]{:S(2)}) copy-start(bf16[1536]{0:T(1024)(128)(2,1)} %param.27) | copy-start | bytes 9220
  50.7 12.4 %all-to-all-start.2 = ((bf16[8,16,1536]{2,1,0:T(8,128)(2,1)}), bf16[8,16,1536]{2,1,0:T(8,128)(2,1)S(1)}, u32[]{:S(2)}, u32[]{:S(2)}) async-start(bf16[8,16,1536]{2,1,0:T(8,128)(2,1)} %bitcast.147), calls=%async_computation.2 | async-start | bytes 786432 | tf_op jit(solution)/shard_map/all_to_all | solution.py:75
  63.8 24.8 %copy-start.20 = (bf16[2,64,96]{2,1,0:T(8,128)(2,1)S(1)}, bf16[2,64,96]{2,1,0:T(8,128)(2,1)}, u32[]{:S(2)}) copy-start(bf16[2,64,96]{2,1,0:T(8,128)(2,1)} %copy-done.19) | copy-start | bytes 73732
  67.1 9.1 %all-to-all-start.3 = ((bf16[8,2,3072]{2,1,0:T(2,128)(2,1)}), bf16[8,2,3072]{2,1,0:T(2,128)(2,1)S(1)}, u32[]{:S(2)}, u32[]{:S(2)}) async-start(bf16[8,2,3072]{2,1,0:T(2,128)(2,1)} %reshape.483), calls=%async_computation.3 | async-start | bytes 196608 | tf_op jit(solution)/shard_map/all_to_all | solution.py:262
  78.5 21.3 %all-to-all-start.4 = ((bf16[32,2,1536]{2,1,0:T(2,128)(2,1)}), bf16[32,2,1536]{2,1,0:T(2,128)(2,1)S(1)}, u32[]{:S(2)}, u32[]{:S(2)}) async-start(bf16[32,2,1536]{2,1,0:T(2,128)(2,1)} %broadcast_in_dim.119), calls=%async_computation.4 | async-start | bytes 393216 | tf_op jit(solution)/shard_map/all_to_all | solution.py:81
  99.8 6.7 %copy-start.6 = (bf16[8,3072]{1,0:T(8,128)(2,1)S(1)}, bf16[8,3072]{1,0:T(8,128)(2,1)}, u32[]{:S(2)}) copy-start(bf16[8,3072]{1,0:T(8,128)(2,1)} %get-tuple-element.10) | copy-start | bytes 147460
  101.6 14.0 %all-to-all-start.5 = ((f32[32,1,64]{2,1,0:T(1,128)}), f32[32,1,64]{2,1,0:T(1,128)S(1)}, u32[]{:S(2)}, u32[]{:S(2)}) async-start(f32[32,1,64]{2,1,0:T(1,128)} %broadcast_in_dim.120), calls=%async_computation.5 | async-start | bytes 32768 | tf_op jit(solution)/shard_map/all_to_all | solution.py:81

commit v7 on v6

--- a/solution.py
+++ b/solution.py
@@ -67,6 +67,50 @@
             bytes_accessed=2 * (3 * width * units + 2 * rows * width),
         ),
     )(hidden_in, gate_weight, up_weight, down_weight)
+
+
+def residual_norm_kernel(chunk_ref, arrived_ref, states_ref, gain_ref, residual_ref, copies_ref):
+    shards = arrived_ref.shape[0]
+    summed = arrived_ref[0].astype(jnp.float32)
+    for source in range(1, shards):
+        summed = summed + arrived_ref[source].astype(jnp.float32)
+    residual = states_ref[...].astype(jnp.float32) + summed
+    mean_square = jnp.mean(residual * residual, axis=1, keepdims=True)
+    hidden = (
+        residual * lax.rsqrt(mean_square + eps_norm) * gain_ref[...].astype(jnp.float32)
+    ).astype(copies_ref.dtype)
+    residual_ref[...] = residual
+    for target in range(shards):
+        copies_ref[target] = hidden
+
+
+def residual_norm(arrived, draft_rows, gain, chunk):
+    shards, rows, width = arrived.shape
+    return pl.pallas_call(
+        residual_norm_kernel,
+        grid_spec=pltpu.PrefetchScalarGridSpec(
+            num_scalar_prefetch=1,
+            grid=(1,),
+            in_specs=[
+                pl.BlockSpec((shards, rows, width), lambda i, c: (0, 0, 0)),
+                pl.BlockSpec((rows, width), lambda i, c: (c[0], 0)),
+                pl.BlockSpec((1, width), lambda i, c: (0, 0)),
+            ],
+            out_specs=[
+                pl.BlockSpec((rows, width), lambda i, c: (0, 0)),
+                pl.BlockSpec((shards, rows, width), lambda i, c: (0, 0, 0)),
+            ],
+        ),
+        out_shape=[
+            jax.ShapeDtypeStruct((rows, width), jnp.float32),
+            jax.ShapeDtypeStruct((shards, rows, width), jnp.bfloat16),
+        ],
+        cost_estimate=pl.CostEstimate(
+            flops=12 * shards * rows * width,
+            transcendentals=rows,
+            bytes_accessed=2 * (2 * shards + 1) * rows * width + 4 * rows * width,
+        ),
+    )(chunk.reshape(1).astype(jnp.int32), arrived, draft_rows, gain.reshape(1, width))
 
 
 def scatter_rows(partial, axis_name, shards):
@@ -214,15 +258,19 @@
     fresh_values = fresh_values.transpose(0, 2, 1, 3)
     chunk_rows = token_rows // vocab_shards
     chunk_start = vocab_shard * chunk_rows
-    residual_chunk = lax.dynamic_slice_in_dim(states, chunk_start, chunk_rows, 0) + scatter_rows(
-        attend_part, "vocab", vocab_shards
-    )
-    hidden_chunk = (
-        residual_chunk
-        * lax.rsqrt(jnp.mean(residual_chunk * residual_chunk, axis=1, keepdims=True) + eps_norm)
-        * hidden_gain.astype(jnp.float32)
-    ).astype(jnp.bfloat16)
-    hidden_in = gather_rows(hidden_chunk, "vocab", vocab_shards)
+    attn_arrived = lax.all_to_all(
+        attend_part.reshape(vocab_shards, chunk_rows, model_width).astype(jnp.bfloat16),
+        "vocab",
+        split_axis=0,
+        concat_axis=0,
+        tiled=True,
+    )
+    residual_chunk, hidden_copies = residual_norm(
+        attn_arrived, draft_states.reshape(token_rows, model_width), hidden_gain, vocab_shard
+    )
+    hidden_in = lax.all_to_all(
+        hidden_copies, "vocab", split_axis=0, concat_axis=0, tiled=True
+    ).reshape(token_rows, model_width)
     down_part = feed_forward(hidden_in, gate_weight, up_weight, down_weight)
     feed_chunk = scatter_rows(down_part, "vocab", vocab_shards).astype(jnp.bfloat16)
     local_counts = lax.dynamic_slice_in_dim(

time: 117 us -> 119 us (1.017)
  Pallas kernels: 4.04 us -> 5.98 us
    all_to_all x0 -> x2, waiting for transfers between devices: none -> 13.7 us  [the longest x1 6.88 us: per_device(): lax.all_to_all(attend_part.reshape(vocab_shards, chunk_rows, model_width)...]
    all_to_all x0 -> x2, starting transfers between devices: none -> 10.4 us  [the longest x1 5.61 us: per_device(): lax.all_to_all(attend_part.reshape(vocab_shards, chunk_rows, model_width)...]
    all_to_all x3 -> x2, waiting for transfers between devices: 25.4 us -> 18.6 us  [gather_rows(): lax.all_to_all(copies, axis_name, split_axis=0, concat_axis=0, tiled=True)]
    all_to_all x2 -> x1, waiting for transfers between devices: 12.7 us -> 6.09 us  [scatter_rows(): lax.all_to_all(pieces, axis_name, split_axis=0, concat_axis=0, tiled=True)]
    all_to_all x2 -> x1, starting transfers between devices: 11.3 us -> 4.94 us  [scatter_rows(): lax.all_to_all(pieces, axis_name, split_axis=0, concat_axis=0, tiled=True)]
    all_to_all x3 -> x2, starting transfers between devices: 19 us -> 14.8 us  [gather_rows(): lax.all_to_all(copies, axis_name, split_axis=0, concat_axis=0, tiled=True)]
    pallas_call x0 -> x1, Pallas kernels: none -> 1.95 us  [residual_norm(): pl.pallas_call(residual_norm_kernel, grid_spec=pltpu.PrefetchScalarGridSp...]
    dot_general x1, matrix products: 1.61 us -> 0.38 us  [per_device(): jnp.einsum('rim,mkgd->rkgid', request_states, query_weight.reshape(model_...]
  transfers between devices with their start and end apart: 6 -> 6, of which waited for: 6 -> 6; matrix products, arithmetic and copies ran while one was open for 5% -> 4% of each run, Pallas kernels for 0% -> 0%
where the time goes in v7:
time: 119 us; the launch traced here: 118 us
  waiting for transfers between devices  42.8 us (36%)
  starting transfers between devices  34.9 us (29%)
  other arithmetic  15.3 us (13%)
  matrix products  10.8 us (9%)
  local copies, waits for them, and re-layouts  7.73 us (6%)
  Pallas kernels  5.98 us (5%)
    all_to_all x2, waiting for transfers between devices, gather_rows(): lax.all_to_all(copies, axis_name, split_axis=0, concat_axis=0, tiled=True)  18.6 us
    all_to_all x2, starting transfers between devices, gather_rows(): lax.all_to_all(copies, axis_name, split_axis=0, concat_axis=0, tiled=True)  14.8 us
    all_to_all x1, waiting for transfers between devices, per_device(): lax.all_to_all(attend_part.reshape(vocab_shards, chunk_rows, model_width)...  6.88 us
    all_to_all x1, waiting for transfers between devices, per_device(): lax.all_to_all(hidden_copies, 'vocab', split_axis=0, concat_axis=0, tiled...  6.82 us
    all_to_all x1, waiting for transfers between devices, scatter_rows(): lax.all_to_all(pieces, axis_name, split_axis=0, concat_axis=0, tiled=True)  6.09 us
    all_to_all x1, starting transfers between devices, per_device(): lax.all_to_all(attend_part.reshape(vocab_shards, chunk_rows, model_width)...  5.61 us
    all_to_all x1, starting transfers between devices, scatter_rows(): lax.all_to_all(pieces, axis_name, split_axis=0, concat_axis=0, tiled=True)  4.94 us
    all_to_all x1, starting transfers between devices, per_device(): lax.all_to_all(hidden_copies, 'vocab', split_axis=0, concat_axis=0, tiled...  4.81 us
  transfers between devices with their start and end apart: 6, of which 6 were waited for; matrix products, arithmetic and copies ran while one was open for 4% of the time, Pallas kernels for 0%

profile of v7, /device:TPU:2, one launch (start us, length us, event | category | flops | bytes accessed | tf_op | source)
XLA Modules:
  0.0 118.5 jit_solution(12157271463267801473)
XLA Ops:
  1.2 0.8 fusion.43
  2.0 0.7 add.165
  2.6 1.2 fusion.7
  3.8 0.6 add_rsqrt_fusion
  4.4 1.3 %convert_element_type.119 = f32[1536]{0:T(1024)} convert(bf16[1536]{0:T(1024)(128)(2,1)} %param.25) | non-fusion elementwise | flops 1536 | bytes 9216 | tf_op jit(solution)/shard_map/convert_element_type | solution.py:164
  5.7 1.0 convolution_minimum_fusion.5
  7.8 1.3 %add_convert_fusion.1 = f32[2,64]{1,0:T(2,128)} fusion(f32[2,64]{1,0:T(2,128)S(1)} %get-tuple-element.21, s32[2]{0:T(128)} %param.22), kind=kLoop, calls=%fused_computation.102 | loop fusion | flops 512 | bytes 1032 | tf_op jit(solution)/shard_map/convert_element_type | solution.py:173
  9.1 0.6 broadcast_compare_fusion
  9.7 0.8 copy.53
  10.6 1.5 %convolution_convert_fusion.1 = bf16[2,64,96]{2,1,0:T(8,128)(2,1)S(1)} fusion(bf16[1536,96]{0,1:T(8,128)(2,1)} %param.30, bf16[2,64,1536]{2,1,0:T(8,128)(2,1)} %param.18, f32[1536]{0:T(1024)} %convert_element_type.119, f32[2,64]{1,0:T(2,128)} %add_rsqrt_fusion), kind=kOutput, calls=%fused_computation.24 | convolution fusion | flops 38547456 | bytes 719360 | tf_op jit(solution)/shard_map/rim,mkd->rkid/dot_general | solution.py:205
  12.1 1.3 %convolution_bitcast_fusion.4 = f32[2,1,64,96]{3,2,0,1:T(8,128)S(1)} fusion(bf16[1536,96]{0,1:T(8,128)(2,1)} %param.29, bf16[2,64,1536]{2,1,0:T(8,128)(2,1)S(1)} %copy-done.1, f32[1536]{0:T(1024)} %convert_element_type.119, f32[2,64]{1,0:T(2,128)} %add_rsqrt_fusion), kind=kOutput, calls=%fused_computation.16 | convolution fusion | flops 38535168 | bytes 743936 | tf_op jit(solution)/shard_map/rim,mkd->rkid/dot_general | solution.py:198
  13.5 1.0 multiply_cosine_fusion.1
  14.5 1.0 fusion.36
  16.0 0.6 select_reduce_fusion
  17.0 0.5 convert_reduce_fusion
  18.6 1.0 fusion.1
  19.6 5.6 %all-to-all-start = ((bf16[8,16,1536]{2,1,0:T(8,128)(2,1)}), bf16[8,16,1536]{2,1,0:T(8,128)(2,1)S(1)}, u32[]{:S(2)}, u32[]{:S(2)}) async-start(bf16[8,16,1536]{2,1,0:T(8,128)(2,1)} %fusion.1), calls=%async_computation | async-start | bytes 786432 | tf_op jit(solution)/shard_map/all_to_all | solution.py:261
  25.2 0.6 reshape.446.gain_ref
  25.8 6.9 %all-to-all-done.arrived_ref = bf16[8,16,1536]{2,1,0:T(8,128)(2,1)S(1)} async-done(((bf16[8,16,1536]{2,1,0:T(8,128)(2,1)}), bf16[8,16,1536]{2,1,0:T(8,128)(2,1)S(1)}, u32[]{:S(2)}, u32[]{:S(2)}) %all-to-all-start) | async-done | bytes 393248 | tf_op jit(solution)/shard_map/all_to_all | solution.py:261
  32.7 0.7 copy-done.2
  33.5 1.9 %shard_map.209 = (f32[16,1536]{1,0:T(8,128)}, bf16[8,16,1536]{2,1,0:T(8,128)(2,1)}) custom-call(s32[1]{0:T(128)} %bitcast.3.chunk_ref, bf16[8,16,1536]{2,1,0:T(8,128)(2,1)} %copy-done.2, bf16[128,1536]{1,0:T(8,128)(2,1)} %bitcast.145, bf16[1,1536]{1,0:T(2,128)(2,1)} %reshape.446.gain_ref), custom_call_target="tpu_custom_call" | custom-call | flops 2359296 | bytes 933888 | tf_op jit(solution)/shard_map/pallas_call | solution.py:89
  35.4 4.8 %all-to-all-start.1 = ((bf16[8,16,1536]{2,1,0:T(8,128)(2,1)}), bf16[8,16,1536]{2,1,0:T(8,128)(2,1)S(1)}, u32[]{:S(2)}, u32[]{:S(2)}) async-start(bf16[8,16,1536]{2,1,0:T(8,128)(2,1)} %get-tuple-element.8), calls=%async_computation.1 | async-start | bytes 786432 | tf_op jit(solution)/shard_map/all_to_all | solution.py:271
  40.3 0.6 fusion.52
  40.9 6.8 %all-to-all-done.1 = bf16[8,16,1536]{2,1,0:T(8,128)(2,1)S(1)} async-done(((bf16[8,16,1536]{2,1,0:T(8,128)(2,1)}), bf16[8,16,1536]{2,1,0:T(8,128)(2,1)S(1)}, u32[]{:S(2)}, u32[]{:S(2)}) %all-to-all-start.1) | async-done | bytes 393248 | tf_op jit(solution)/shard_map/all_to_all | solution.py:271
  47.7 0.7 copy-done.3
  48.4 4.0 %shard_map.210 = bf16[128,1536]{1,0:T(8,128)(2,1)} custom-call(bf16[128,1536]{1,0:T(8,128)(2,1)} %bitcast.146, bf16[1536,512]{1,0:T(8,128)(2,1)} %gate_ref.1, bf16[1536,512]{1,0:T(8,128)(2,1)} %up_ref.1, bf16[512,1536]{1,0:T(8,128)(2,1)} %down_ref.1), custom_call_target="tpu_custom_call" | custom-call | flops 603979776 | bytes 5505024 | tf_op jit(solution)/shard_map/pallas_call | solution.py:51
  52.5 4.9 %all-to-all-start.2 = ((bf16[8,16,1536]{2,1,0:T(8,128)(2,1)}), bf16[8,16,1536]{2,1,0:T(8,128)(2,1)S(1)}, u32[]{:S(2)}, u32[]{:S(2)}) async-start(bf16[8,16,1536]{2,1,0:T(8,128)(2,1)} %bitcast.147), calls=%async_computation.2 | async-start | bytes 786432 | tf_op jit(solution)/shard_map/all_to_all | solution.py:119
  57.4 1.3 %fusion.44 = pred[16]{0:T(512)(128)(4,1)S(1)} fusion(s32[]{:T(128)} %bitcast.1, s32[]{:T(128)} %bitcast, s32[]{:T(128)S(6)} %mul.164), kind=kLoop, calls=%fused_computation.104 | loop fusion | flops 784 | bytes 28 | tf_op jit(solution)/shard_map/lt | solution.py:281
  58.8 6.1 %all-to-all-done.2 = bf16[8,16,1536]{2,1,0:T(8,128)(2,1)S(1)} async-done(((bf16[8,16,1536]{2,1,0:T(8,128)(2,1)}), bf16[8,16,1536]{2,1,0:T(8,128)(2,1)S(1)}, u32[]{:S(2)}, u32[]{:S(2)}) %all-to-all-start.2) | async-done | bytes 393248 | tf_op jit(solution)/shard_map/all_to_all | solution.py:119
  64.9 0.7 reduce_sum.83
  65.6 1.0 select_convert_fusion.3
  67.6 0.7 reduce.10
  68.2 0.7 reshape.482
  68.9 4.7 %all-to-all-start.3 = ((bf16[8,2,3072]{2,1,0:T(2,128)(2,1)}), bf16[8,2,3072]{2,1,0:T(2,128)(2,1)S(1)}, u32[]{:S(2)}, u32[]{:S(2)}) async-start(bf16[8,2,3072]{2,1,0:T(2,128)(2,1)} %reshape.482), calls=%async_computation.3 | async-start | bytes 196608 | tf_op jit(solution)/shard_map/all_to_all | solution.py:310
  73.6 4.4 %all-to-all-done.3 = bf16[8,2,3072]{2,1,0:T(2,128)(2,1)S(1)} async-done(((bf16[8,2,3072]{2,1,0:T(2,128)(2,1)}), bf16[8,2,3072]{2,1,0:T(2,128)(2,1)S(1)}, u32[]{:S(2)}, u32[]{:S(2)}) %all-to-all-start.3) | async-done | bytes 98336 | tf_op jit(solution)/shard_map/all_to_all | solution.py:310
  78.1 0.6 slice_reduce_fusion
  78.9 0.5 fusion.46
  79.5 0.8 broadcast_in_dim.110
  80.3 10.7 %all-to-all-start.4 = ((bf16[32,2,1536]{2,1,0:T(2,128)(2,1)}), bf16[32,2,1536]{2,1,0:T(2,128)(2,1)S(1)}, u32[]{:S(2)}, u32[]{:S(2)}) async-start(bf16[32,2,1536]{2,1,0:T(2,128)(2,1)} %broadcast_in_dim.110), calls=%async_computation.4 | async-start | bytes 393216 | tf_op jit(solution)/shard_map/all_to_all | solution.py:125
  91.0 0.8 convolution_convert_fusion.2
  91.8 10.4 %all-to-all-done.4 = bf16[32,2,1536]{2,1,0:T(2,128)(2,1)S(1)} async-done(((bf16[32,2,1536]{2,1,0:T(2,128)(2,1)}), bf16[32,2,1536]{2,1,0:T(2,128)(2,1)S(1)}, u32[]{:S(2)}, u32[]{:S(2)}) %all-to-all-start.4) | async-done | bytes 196640 | tf_op jit(solution)/shard_map/all_to_all | solution.py:125
  102.3 1.1 convolution_reduce_fusion
  103.4 0.6 broadcast_in_dim.111
  104.0 4.1 %all-to-all-start.5 = ((f32[32,1,64]{2,1,0:T(1,128)}), f32[32,1,64]{2,1,0:T(1,128)S(1)}, u32[]{:S(2)}, u32[]{:S(2)}) async-start(f32[32,1,64]{2,1,0:T(1,128)} %broadcast_in_dim.111), calls=%async_computation.5 | async-start | bytes 32768 | tf_op jit(solution)/shard_map/all_to_all | solution.py:125
  108.2 0.8 convolution_convert_fusion.3
  109.0 0.8 reshape_reshape.4
  109.7 8.2 %all-to-all-done.5 = f32[32,1,64]{2,1,0:T(1,128)S(1)} async-done(((f32[32,1,64]{2,1,0:T(1,128)}), f32[32,1,64]{2,1,0:T(1,128)S(1)}, u32[]{:S(2)}, u32[]{:S(2)}) %all-to-all-start.5) | async-done | bytes 8224 | tf_op jit(solution)/shard_map/all_to_all | solution.py:125
  118.0 0.5 reduce_max.39
  (66 shorter events, 5.1 us)
Async XLA Ops:
  0.6 101.6 %copy-start = (bf16[1536,1000]{0,1:T(8,128)(2,1)S(1)}, bf16[1536,1000]{0,1:T(8,128)(2,1)}, u32[]{:S(2)}) copy-start(bf16[1536,1000]{0,1:T(8,128)(2,1)} %param.35) | copy-start | bytes 9216004
  0.6 11.5 %copy-start.1 = (bf16[2,64,1536]{2,1,0:T(8,128)(2,1)S(1)}, bf16[2,64,1536]{2,1,0:T(8,128)(2,1)}, u32[]{:S(2)}) copy-start(bf16[2,64,1536]{2,1,0:T(8,128)(2,1)} %param.18) | copy-start | bytes 1179652
  10.6 4.9 %copy-start.7 = (f32[1536]{0:T(1024)S(1)}, f32[1536]{0:T(1024)}, u32[]{:S(2)}) copy-start(f32[1536]{0:T(1024)} %convert_element_type.119) | copy-start | bytes 18436
  10.6 4.9 %copy-start.11 = (f32[2,64]{1,0:T(2,128)S(1)}, f32[2,64]{1,0:T(2,128)}, u32[]{:S(2)}) copy-start(f32[2,64]{1,0:T(2,128)} %add_rsqrt_fusion) | copy-start | bytes 1540
  10.6 4.9 %copy-start.12 = (bf16[1536,192]{0,1:T(8,128)(2,1)S(1)}, bf16[1536,192]{0,1:T(8,128)(2,1)}, u32[]{:S(2)}) copy-start(bf16[1536,192]{0,1:T(8,128)(2,1)} %param.28) | copy-start | bytes 1769476
  10.6 5.4 %copy-start.5 = (bf16[2048,96]{0,1:T(8,128)(2,1)S(1)}, bf16[2048,96]{0,1:T(8,128)(2,1)}, u32[]{:S(2)}) copy-start(bf16[2048,96]{0,1:T(8,128)(2,1)} %param.23) | copy-start | bytes 1179652
  12.1 5.9 %copy-start.15 = (bf16[2,64,96]{2,1,0:T(8,128)(2,1)}, bf16[2,64,96]{2,1,0:T(8,128)(2,1)S(1)}, u32[]{:S(2)}) copy-start(bf16[2,64,96]{2,1,0:T(8,128)(2,1)S(1)} %convolution_convert_fusion.1) | copy-start | bytes 73732
  16.0 1.5 %copy-start.13 = (bf16[2048,96]{0,1:T(8,128)(2,1)S(1)}, bf16[2048,96]{0,1:T(8,128)(2,1)}, u32[]{:S(2)}) copy-start(bf16[2048,96]{0,1:T(8,128)(2,1)} %param.24) | copy-start | bytes 1179652
  17.5 1.1 copy-start.4
  18.0 7.2 %copy-start.10 = (bf16[1536]{0:T(1024)(128)(2,1)S(1)}, bf16[1536]{0:T(1024)(128)(2,1)}, u32[]{:S(2)}) copy-start(bf16[1536]{0:T(1024)(128)(2,1)} %param.26) | copy-start | bytes 9220
  18.1 22.2 %copy-start.14 = (s32[64]{0:T(128)S(1)}, s32[64]{0:T(128)}, u32[]{:S(2)}) copy-start(s32[64]{0:T(128)} %param.20) | copy-start | bytes 772
  19.6 13.1 %all-to-all-start = ((bf16[8,16,1536]{2,1,0:T(8,128)(2,1)}), bf16[8,16,1536]{2,1,0:T(8,128)(2,1)S(1)}, u32[]{:S(2)}, u32[]{:S(2)}) async-start(bf16[8,16,1536]{2,1,0:T(8,128)(2,1)} %fusion.1), calls=%async_computation | async-start | bytes 786432 | tf_op jit(solution)/shard_map/all_to_all | solution.py:261
  32.7 0.7 copy-start.2
  35.4 12.3 %all-to-all-start.1 = ((bf16[8,16,1536]{2,1,0:T(8,128)(2,1)}), bf16[8,16,1536]{2,1,0:T(8,128)(2,1)S(1)}, u32[]{:S(2)}, u32[]{:S(2)}) async-start(bf16[8,16,1536]{2,1,0:T(8,128)(2,1)} %get-tuple-element.8), calls=%async_computation.1 | async-start | bytes 786432 | tf_op jit(solution)/shard_map/all_to_all | solution.py:271
  47.7 0.7 copy-start.3
  48.4 10.3 %copy-start.8 = (s32[2,8]{1,0:T(2,128)S(1)}, s32[2,8]{1,0:T(2,128)}, u32[]{:S(2)}) copy-start(s32[2,8]{1,0:T(2,128)} %param.21) | copy-start | bytes 196
  52.5 21.2 %copy-start.9 = (bf16[1536]{0:T(1024)(128)(2,1)S(1)}, bf16[1536]{0:T(1024)(128)(2,1)}, u32[]{:S(2)}) copy-start(bf16[1536]{0:T(1024)(128)(2,1)} %param.27) | copy-start | bytes 9220
  52.5 12.4 %all-to-all-start.2 = ((bf16[8,16,1536]{2,1,0:T(8,128)(2,1)}), bf16[8,16,1536]{2,1,0:T(8,128)(2,1)S(1)}, u32[]{:S(2)}, u32[]{:S(2)}) async-start(bf16[8,16,1536]{2,1,0:T(8,128)(2,1)} %bitcast.147), calls=%async_computation.2 | async-start | bytes 786432 | tf_op jit(solution)/shard_map/all_to_all | solution.py:119
  65.6 25.4 %copy-start.16 = (bf16[2,64,96]{2,1,0:T(8,128)(2,1)S(1)}, bf16[2,64,96]{2,1,0:T(8,128)(2,1)}, u32[]{:S(2)}) copy-start(bf16[2,64,96]{2,1,0:T(8,128)(2,1)} %copy-done.15) | copy-start | bytes 73732
  68.9 9.1 %all-to-all-start.3 = ((bf16[8,2,3072]{2,1,0:T(2,128)(2,1)}), bf16[8,2,3072]{2,1,0:T(2,128)(2,1)S(1)}, u32[]{:S(2)}, u32[]{:S(2)}) async-start(bf16[8,2,3072]{2,1,0:T(2,128)(2,1)} %reshape.482), calls=%async_computation.3 | async-start | bytes 196608 | tf_op jit(solution)/shard_map/all_to_all | solution.py:310
  80.3 21.9 %all-to-all-start.4 = ((bf16[32,2,1536]{2,1,0:T(2,128)(2,1)}), bf16[32,2,1536]{2,1,0:T(2,128)(2,1)S(1)}, u32[]{:S(2)}, u32[]{:S(2)}) async-start(bf16[32,2,1536]{2,1,0:T(2,128)(2,1)} %broadcast_in_dim.110), calls=%async_computation.4 | async-start | bytes 393216 | tf_op jit(solution)/shard_map/all_to_all | solution.py:125
  102.3 6.7 %copy-start.6 = (bf16[8,3072]{1,0:T(8,128)(2,1)S(1)}, bf16[8,3072]{1,0:T(8,128)(2,1)}, u32[]{:S(2)}) copy-start(bf16[8,3072]{1,0:T(8,128)(2,1)} %get-tuple-element.12) | copy-start | bytes 147460
  104.0 13.9 %all-to-all-start.5 = ((f32[32,1,64]{2,1,0:T(1,128)}), f32[32,1,64]{2,1,0:T(1,128)S(1)}, u32[]{:S(2)}, u32[]{:S(2)}) async-start(f32[32,1,64]{2,1,0:T(1,128)} %broadcast_in_dim.111), calls=%async_computation.5 | async-start | bytes 32768 | tf_op jit(solution)/shard_map/all_to_all | solution.py:125

commit v8 on v7

--- a/solution.py
+++ b/solution.py
@@ -108,7 +108,7 @@
         cost_estimate=pl.CostEstimate(
             flops=12 * shards * rows * width,
             transcendentals=rows,
-            bytes_accessed=2 * (2 * shards + 1) * rows * width + 4 * rows * width,
+            bytes_accessed=4 * shards * rows * width + 8 * rows * width,
         ),
     )(chunk.reshape(1).astype(jnp.int32), arrived, draft_rows, gain.reshape(1, width))
 
@@ -266,7 +266,7 @@
         tiled=True,
     )
     residual_chunk, hidden_copies = residual_norm(
-        attn_arrived, draft_states.reshape(token_rows, model_width), hidden_gain, vocab_shard
+        attn_arrived, states, hidden_gain, vocab_shard
     )
     hidden_in = lax.all_to_all(
         hidden_copies, "vocab", split_axis=0, concat_axis=0, tiled=True

time: 119 us -> 119 us (level)
    dot_general x1, matrix products: 0.38 us -> 2.21 us  [per_device(): jnp.einsum('rim,mkgd->rkgid', request_states, query_weight.reshape(model_...]
    dot_general x1, matrix products: 1.51 us -> 0.32 us  [per_device(): jnp.einsum('rim,mkd->rkid', request_states, value_matrix.reshape(model_wi...]
    unnamed x37 -> x35, local copies, waits for them, and re-layouts: 2.64 us -> 2.19 us
  transfers between devices with their start and end apart: 6 -> 6, of which waited for: 6 -> 6; matrix products, arithmetic and copies ran while one was open for 4% -> 5% of each run, Pallas kernels for 0% -> 0%
where the time goes in v8:
time: 119 us; the launch traced here: 118 us
  waiting for transfers between devices  41.9 us (35%)
  starting transfers between devices  35 us (29%)
  other arithmetic  15.5 us (13%)
  matrix products  11.6 us (10%)
  local copies, waits for them, and re-layouts  7.27 us (6%)
  Pallas kernels  6.03 us (5%)
    all_to_all x2, waiting for transfers between devices, gather_rows(): lax.all_to_all(copies, axis_name, split_axis=0, concat_axis=0, tiled=True)  18.6 us
    all_to_all x2, starting transfers between devices, gather_rows(): lax.all_to_all(copies, axis_name, split_axis=0, concat_axis=0, tiled=True)  14.2 us
    all_to_all x1, waiting for transfers between devices, per_device(): lax.all_to_all(hidden_copies, 'vocab', split_axis=0, concat_axis=0, tiled...  6.82 us
    all_to_all x1, starting transfers between devices, per_device(): lax.all_to_all(attend_part.reshape(vocab_shards, chunk_rows, model_width)...  6.36 us
    all_to_all x1, waiting for transfers between devices, scatter_rows(): lax.all_to_all(pieces, axis_name, split_axis=0, concat_axis=0, tiled=True)  6.09 us
    all_to_all x1, waiting for transfers between devices, per_device(): lax.all_to_all(attend_part.reshape(vocab_shards, chunk_rows, model_width)...  6.01 us
    all_to_all x1, starting transfers between devices, scatter_rows(): lax.all_to_all(pieces, axis_name, split_axis=0, concat_axis=0, tiled=True)  4.94 us
    all_to_all x1, starting transfers between devices, per_device(): lax.all_to_all(hidden_copies, 'vocab', split_axis=0, concat_axis=0, tiled...  4.81 us
  transfers between devices with their start and end apart: 6, of which 6 were waited for; matrix products, arithmetic and copies ran while one was open for 5% of the time, Pallas kernels for 0%

profile of v8, /device:TPU:2, one launch (start us, length us, event | category | flops | bytes accessed | tf_op | source)
XLA Modules:
  0.0 118.3 jit_solution(11328522458798042405)
XLA Ops:
  0.7 1.1 convolution_minimum_fusion.5
  2.9 1.3 %fusion.37 = s32[2]{0:T(128)} fusion(s32[2]{0:T(128)} %param.22), kind=kLoop, calls=%fused_computation.97 | loop fusion | flops 10 | bytes 16 | tf_op jit(solution)/shard_map/reduce_sum | solution.py:218
  4.2 0.7 add_convert_fusion.1
  4.9 0.7 convert_element_type.121
  5.6 1.2 multiply_reduce_fusion
  6.8 2.2 %convolution_bitcast_fusion.1 = f32[2,1,2,64,96]{4,3,2,0,1:T(8,128)} fusion(bf16[1536,2,96,1]{0,2,1,3:T(8,128)(2,1)} %bitcast.156, f32[1536]{0:T(1024)S(1)} %convert_element_type.121, f32[2,64]{1,0:T(2,128)S(1)} %add_rsqrt_fusion, bf16[2,64,1536]{2,1,0:T(8,128)(2,1)} %param.18), kind=kOutput, calls=%fused_computation.9 | convolution fusion | flops 76283904 | bytes 1088000 | tf_op jit(solution)/shard_map/rim,mkgd->rkgid/dot_general | solution.py:190
  9.3 1.0 multiply_cosine_fusion.1
  10.6 0.6 broadcast_compare_fusion
  11.2 0.8 copy.53
  12.0 0.7 add.165
  12.7 0.7 compare_and_fusion
  13.5 1.1 fusion.20
  14.6 1.6 %select_reduce_fusion = (f32[2,2,64]{2,1,0:T(2,128)S(1)}, f32[2,1,2,64,2048]{4,3,2,0,1:T(8,128)S(1)}) fusion(pred[2,2048]{1,0:T(4,128)(4,1)S(1)} %compare_and_fusion, bf16[2048,96]{0,1:T(8,128)(2,1)} %param.23, bf16[2,2,64,48]{3,2,1,0:T(8,128)(2,1)S(1)} %get-tuple-element.10, bf16[2,2,64,48]{3,2,1,0:T(8,128)(2,1)S(1)} %get-tuple-element.9), kind=kOutput, calls=%fused_computation.7 | convolution fusion | flops 102334208 | bytes 2544640 | tf_op jit(solution)/shard_map/rkgid,pkd->rkgip/dot_general | solution.py:225
  16.6 0.5 convert_reduce_fusion
  18.0 0.6 copy-done.14
  18.8 1.1 fusion.1
  19.9 6.4 %all-to-all-start = ((bf16[8,16,1536]{2,1,0:T(8,128)(2,1)}), bf16[8,16,1536]{2,1,0:T(8,128)(2,1)}, u32[]{:S(2)}, u32[]{:S(2)}) async-start(bf16[8,16,1536]{2,1,0:T(8,128)(2,1)} %fusion.1), calls=%async_computation | async-start | bytes 786432 | tf_op jit(solution)/shard_map/all_to_all | solution.py:261
  26.3 0.6 reshape.444.gain_ref
  26.9 1.0 bitcast_convert_fusion.states_ref
  27.9 6.0 %all-to-all-done.arrived_ref = bf16[8,16,1536]{2,1,0:T(8,128)(2,1)} async-done(((bf16[8,16,1536]{2,1,0:T(8,128)(2,1)}), bf16[8,16,1536]{2,1,0:T(8,128)(2,1)}, u32[]{:S(2)}, u32[]{:S(2)}) %all-to-all-start) | async-done | bytes 393248 | tf_op jit(solution)/shard_map/all_to_all | solution.py:261
  33.9 2.0 %shard_map.209 = (f32[16,1536]{1,0:T(8,128)}, bf16[8,16,1536]{2,1,0:T(8,128)(2,1)}) custom-call(s32[1]{0:T(128)} %bitcast.3.chunk_ref, bf16[8,16,1536]{2,1,0:T(8,128)(2,1)} %all-to-all-done.arrived_ref, f32[128,1536]{1,0:T(8,128)} %bitcast_convert_fusion.states_ref, bf16[1,1536]{1,0:T(2,128)(2,1)} %reshape.444.gain_ref), custom_call_target="tpu_custom_call" | custom-call | flops 2359296 | bytes 983040 | tf_op jit(solution)/shard_map/pallas_call | solution.py:89
  35.9 4.8 %all-to-all-start.1 = ((bf16[8,16,1536]{2,1,0:T(8,128)(2,1)}), bf16[8,16,1536]{2,1,0:T(8,128)(2,1)S(1)}, u32[]{:S(2)}, u32[]{:S(2)}) async-start(bf16[8,16,1536]{2,1,0:T(8,128)(2,1)} %get-tuple-element.8), calls=%async_computation.1 | async-start | bytes 786432 | tf_op jit(solution)/shard_map/all_to_all | solution.py:271
  40.7 0.6 fusion.46
  41.3 6.8 %all-to-all-done.1 = bf16[8,16,1536]{2,1,0:T(8,128)(2,1)S(1)} async-done(((bf16[8,16,1536]{2,1,0:T(8,128)(2,1)}), bf16[8,16,1536]{2,1,0:T(8,128)(2,1)S(1)}, u32[]{:S(2)}, u32[]{:S(2)}) %all-to-all-start.1) | async-done | bytes 393248 | tf_op jit(solution)/shard_map/all_to_all | solution.py:271
  48.2 0.7 copy-done.2
  48.9 4.0 %shard_map.210 = bf16[128,1536]{1,0:T(8,128)(2,1)} custom-call(bf16[128,1536]{1,0:T(8,128)(2,1)} %bitcast.147, bf16[1536,512]{1,0:T(8,128)(2,1)} %gate_ref.1, bf16[1536,512]{1,0:T(8,128)(2,1)} %up_ref.1, bf16[512,1536]{1,0:T(8,128)(2,1)} %down_ref.1), custom_call_target="tpu_custom_call" | custom-call | flops 603979776 | bytes 5505024 | tf_op jit(solution)/shard_map/pallas_call | solution.py:51
  52.9 4.9 %all-to-all-start.2 = ((bf16[8,16,1536]{2,1,0:T(8,128)(2,1)}), bf16[8,16,1536]{2,1,0:T(8,128)(2,1)S(1)}, u32[]{:S(2)}, u32[]{:S(2)}) async-start(bf16[8,16,1536]{2,1,0:T(8,128)(2,1)} %bitcast.148), calls=%async_computation.2 | async-start | bytes 786432 | tf_op jit(solution)/shard_map/all_to_all | solution.py:119
  57.9 1.3 %fusion.38 = pred[16]{0:T(512)(128)(4,1)S(1)} fusion(s32[]{:T(128)} %bitcast.1, s32[]{:T(128)} %bitcast, s32[]{:T(128)S(6)} %mul.164), kind=kLoop, calls=%fused_computation.101 | loop fusion | flops 784 | bytes 28 | tf_op jit(solution)/shard_map/lt | solution.py:281
  59.3 6.1 %all-to-all-done.2 = bf16[8,16,1536]{2,1,0:T(8,128)(2,1)S(1)} async-done(((bf16[8,16,1536]{2,1,0:T(8,128)(2,1)}), bf16[8,16,1536]{2,1,0:T(8,128)(2,1)S(1)}, u32[]{:S(2)}, u32[]{:S(2)}) %all-to-all-start.2) | async-done | bytes 393248 | tf_op jit(solution)/shard_map/all_to_all | solution.py:119
  65.4 0.7 reduce_sum.83
  66.0 1.0 select_convert_fusion.3
  68.0 0.7 reduce.10
  68.7 0.7 reshape.481
  69.3 4.7 %all-to-all-start.3 = ((bf16[8,2,3072]{2,1,0:T(2,128)(2,1)}), bf16[8,2,3072]{2,1,0:T(2,128)(2,1)S(1)}, u32[]{:S(2)}, u32[]{:S(2)}) async-start(bf16[8,2,3072]{2,1,0:T(2,128)(2,1)} %reshape.481), calls=%async_computation.3 | async-start | bytes 196608 | tf_op jit(solution)/shard_map/all_to_all | solution.py:310
  74.1 4.4 %all-to-all-done.3 = bf16[8,2,3072]{2,1,0:T(2,128)(2,1)S(1)} async-done(((bf16[8,2,3072]{2,1,0:T(2,128)(2,1)}), bf16[8,2,3072]{2,1,0:T(2,128)(2,1)S(1)}, u32[]{:S(2)}, u32[]{:S(2)}) %all-to-all-start.3) | async-done | bytes 98336 | tf_op jit(solution)/shard_map/all_to_all | solution.py:310
  78.6 0.6 slice_reduce_fusion
  79.4 0.5 fusion.40
  80.0 0.8 broadcast_in_dim.110
  80.7 10.1 %all-to-all-start.4 = ((bf16[32,2,1536]{2,1,0:T(2,128)(2,1)}), bf16[32,2,1536]{2,1,0:T(2,128)(2,1)S(1)}, u32[]{:S(2)}, u32[]{:S(2)}) async-start(bf16[32,2,1536]{2,1,0:T(2,128)(2,1)} %broadcast_in_dim.110), calls=%async_computation.4 | async-start | bytes 393216 | tf_op jit(solution)/shard_map/all_to_all | solution.py:125
  90.8 0.8 convolution_convert_fusion.2
  91.6 10.4 %all-to-all-done.4 = bf16[32,2,1536]{2,1,0:T(2,128)(2,1)S(1)} async-done(((bf16[32,2,1536]{2,1,0:T(2,128)(2,1)}), bf16[32,2,1536]{2,1,0:T(2,128)(2,1)S(1)}, u32[]{:S(2)}, u32[]{:S(2)}) %all-to-all-start.4) | async-done | bytes 196640 | tf_op jit(solution)/shard_map/all_to_all | solution.py:125
  102.1 1.1 convolution_reduce_fusion
  103.2 0.6 broadcast_in_dim.111
  103.8 4.1 %all-to-all-start.5 = ((f32[32,1,64]{2,1,0:T(1,128)}), f32[32,1,64]{2,1,0:T(1,128)S(1)}, u32[]{:S(2)}, u32[]{:S(2)}) async-start(f32[32,1,64]{2,1,0:T(1,128)} %broadcast_in_dim.111), calls=%async_computation.5 | async-start | bytes 32768 | tf_op jit(solution)/shard_map/all_to_all | solution.py:125
  108.0 0.8 convolution_convert_fusion.3
  108.8 0.8 reshape_reshape.4
  109.5 8.2 %all-to-all-done.5 = f32[32,1,64]{2,1,0:T(1,128)S(1)} async-done(((f32[32,1,64]{2,1,0:T(1,128)}), f32[32,1,64]{2,1,0:T(1,128)S(1)}, u32[]{:S(2)}, u32[]{:S(2)}) %all-to-all-start.5) | async-done | bytes 8224 | tf_op jit(solution)/shard_map/all_to_all | solution.py:125
  117.8 0.5 reduce_max.39
  (65 shorter events, 4.7 us)
Async XLA Ops:
  0.6 101.4 %copy-start = (bf16[1536,1000]{0,1:T(8,128)(2,1)S(1)}, bf16[1536,1000]{0,1:T(8,128)(2,1)}, u32[]{:S(2)}) copy-start(bf16[1536,1000]{0,1:T(8,128)(2,1)} %param.35) | copy-start | bytes 9216004
  0.6 8.3 %copy-start.1 = (bf16[2,64,1536]{2,1,0:T(8,128)(2,1)S(1)}, bf16[2,64,1536]{2,1,0:T(8,128)(2,1)}, u32[]{:S(2)}) copy-start(bf16[2,64,1536]{2,1,0:T(8,128)(2,1)} %param.18) | copy-start | bytes 1179652
  0.7 8.3 %copy-start.11 = (bf16[1536,96]{0,1:T(8,128)(2,1)S(1)}, bf16[1536,96]{0,1:T(8,128)(2,1)}, u32[]{:S(2)}) copy-start(bf16[1536,96]{0,1:T(8,128)(2,1)} %param.29) | copy-start | bytes 884740
  6.8 3.8 %copy-start.8 = (f32[2,64]{1,0:T(2,128)}, f32[2,64]{1,0:T(2,128)S(1)}, u32[]{:S(2)}) copy-start(f32[2,64]{1,0:T(2,128)S(1)} %add_rsqrt_fusion) | copy-start | bytes 1540
  14.6 2.5 %copy-start.10 = (bf16[2048,96]{0,1:T(8,128)(2,1)S(1)}, bf16[2048,96]{0,1:T(8,128)(2,1)}, u32[]{:S(2)}) copy-start(bf16[2048,96]{0,1:T(8,128)(2,1)} %param.24) | copy-start | bytes 1179652
  16.6 1.1 copy-start.9
  16.6 1.1 copy-start.12
  17.1 1.7 %copy-start.3 = (bf16[192,1536]{1,0:T(8,128)(2,1)S(1)}, bf16[192,1536]{1,0:T(8,128)(2,1)}, u32[]{:S(2)}) copy-start(bf16[192,1536]{1,0:T(8,128)(2,1)} %param.31) | copy-start | bytes 1769476
  18.0 0.6 copy-start.14
  18.0 8.3 %copy-start.7 = (bf16[1536]{0:T(1024)(128)(2,1)S(1)}, bf16[1536]{0:T(1024)(128)(2,1)}, u32[]{:S(2)}) copy-start(bf16[1536]{0:T(1024)(128)(2,1)} %param.26) | copy-start | bytes 9220
  19.9 20.8 %copy-start.13 = (s32[64]{0:T(128)S(1)}, s32[64]{0:T(128)}, u32[]{:S(2)}) copy-start(s32[64]{0:T(128)} %param.20) | copy-start | bytes 772
  19.9 13.9 %all-to-all-start = ((bf16[8,16,1536]{2,1,0:T(8,128)(2,1)}), bf16[8,16,1536]{2,1,0:T(8,128)(2,1)}, u32[]{:S(2)}, u32[]{:S(2)}) async-start(bf16[8,16,1536]{2,1,0:T(8,128)(2,1)} %fusion.1), calls=%async_computation | async-start | bytes 786432 | tf_op jit(solution)/shard_map/all_to_all | solution.py:261
  35.9 12.3 %all-to-all-start.1 = ((bf16[8,16,1536]{2,1,0:T(8,128)(2,1)}), bf16[8,16,1536]{2,1,0:T(8,128)(2,1)S(1)}, u32[]{:S(2)}, u32[]{:S(2)}) async-start(bf16[8,16,1536]{2,1,0:T(8,128)(2,1)} %get-tuple-element.8), calls=%async_computation.1 | async-start | bytes 786432 | tf_op jit(solution)/shard_map/all_to_all | solution.py:271
  48.2 0.7 copy-start.2
  48.9 10.3 %copy-start.5 = (s32[2,8]{1,0:T(2,128)S(1)}, s32[2,8]{1,0:T(2,128)}, u32[]{:S(2)}) copy-start(s32[2,8]{1,0:T(2,128)} %param.21) | copy-start | bytes 196
  52.9 21.1 %copy-start.6 = (bf16[1536]{0:T(1024)(128)(2,1)S(1)}, bf16[1536]{0:T(1024)(128)(2,1)}, u32[]{:S(2)}) copy-start(bf16[1536]{0:T(1024)(128)(2,1)} %param.27) | copy-start | bytes 9220
  52.9 12.4 %all-to-all-start.2 = ((bf16[8,16,1536]{2,1,0:T(8,128)(2,1)}), bf16[8,16,1536]{2,1,0:T(8,128)(2,1)S(1)}, u32[]{:S(2)}, u32[]{:S(2)}) async-start(bf16[8,16,1536]{2,1,0:T(8,128)(2,1)} %bitcast.148), calls=%async_computation.2 | async-start | bytes 786432 | tf_op jit(solution)/shard_map/all_to_all | solution.py:119
  66.0 24.8 %copy-start.15 = (bf16[2,64,96]{2,1,0:T(8,128)(2,1)S(1)}, bf16[2,64,96]{2,1,0:T(8,128)(2,1)}, u32[]{:S(2)}) copy-start(bf16[2,64,96]{2,1,0:T(8,128)(2,1)} %copy-done.14) | copy-start | bytes 73732
  69.3 9.1 %all-to-all-start.3 = ((bf16[8,2,3072]{2,1,0:T(2,128)(2,1)}), bf16[8,2,3072]{2,1,0:T(2,128)(2,1)S(1)}, u32[]{:S(2)}, u32[]{:S(2)}) async-start(bf16[8,2,3072]{2,1,0:T(2,128)(2,1)} %reshape.481), calls=%async_computation.3 | async-start | bytes 196608 | tf_op jit(solution)/shard_map/all_to_all | solution.py:310
  80.7 21.2 %all-to-all-start.4 = ((bf16[32,2,1536]{2,1,0:T(2,128)(2,1)}), bf16[32,2,1536]{2,1,0:T(2,128)(2,1)S(1)}, u32[]{:S(2)}, u32[]{:S(2)}) async-start(bf16[32,2,1536]{2,1,0:T(2,128)(2,1)} %broadcast_in_dim.110), calls=%async_computation.4 | async-start | bytes 393216 | tf_op jit(solution)/shard_map/all_to_all | solution.py:125
  102.1 6.7 %copy-start.4 = (bf16[8,3072]{1,0:T(8,128)(2,1)S(1)}, bf16[8,3072]{1,0:T(8,128)(2,1)}, u32[]{:S(2)}) copy-start(bf16[8,3072]{1,0:T(8,128)(2,1)} %get-tuple-element.12) | copy-start | bytes 147460
  103.8 14.0 %all-to-all-start.5 = ((f32[32,1,64]{2,1,0:T(1,128)}), f32[32,1,64]{2,1,0:T(1,128)S(1)}, u32[]{:S(2)}, u32[]{:S(2)}) async-start(f32[32,1,64]{2,1,0:T(1,128)} %broadcast_in_dim.111), calls=%async_computation.5 | async-start | bytes 32768 | tf_op jit(solution)/shard_map/all_to_all | solution.py:125

commit v9 on v6

--- a/solution.py
+++ b/solution.py
@@ -44,7 +44,7 @@
         out_ref[...] = acc_ref[...].astype(out_ref.dtype)
 
 
-def feed_forward(hidden_in, gate_weight, up_weight, down_weight, block=256):
+def feed_forward(hidden_in, gate_weight, up_weight, down_weight, block=128):
     rows, width = hidden_in.shape
     units = gate_weight.shape[1]
     block = min(block, units)

time: 117 us -> 118 us (level)
  Pallas kernels: 4.04 us -> 5.43 us
    pallas_call x1, Pallas kernels: 4.04 us -> 5.43 us  [feed_forward(): pl.pallas_call(feed_forward_kernel, grid=(units // block,), in_specs=[pl....]
where the time goes in v9:
time: 118 us; the launch traced here: 117 us
  waiting for transfers between devices  42.5 us (36%)
  starting transfers between devices  35 us (30%)
  other arithmetic  15.1 us (13%)
  matrix products  10.9 us (9%)
  local copies, waits for them, and re-layouts  7.38 us (6%)
  Pallas kernels  5.43 us (5%)
    all_to_all x3, waiting for transfers between devices, gather_rows(): lax.all_to_all(copies, axis_name, split_axis=0, concat_axis=0, tiled=True)  25.4 us
    all_to_all x3, starting transfers between devices, gather_rows(): lax.all_to_all(copies, axis_name, split_axis=0, concat_axis=0, tiled=True)  19 us
    all_to_all x2, waiting for transfers between devices, scatter_rows(): lax.all_to_all(pieces, axis_name, split_axis=0, concat_axis=0, tiled=True)  12.7 us
    all_to_all x2, starting transfers between devices, scatter_rows(): lax.all_to_all(pieces, axis_name, split_axis=0, concat_axis=0, tiled=True)  11.3 us
    pallas_call x1, Pallas kernels, feed_forward(): pl.pallas_call(feed_forward_kernel, grid=(units // block,), in_specs=[pl....  5.43 us
    all_to_all x1, starting transfers between devices, per_device(): lax.all_to_all(jnp.concatenate([column_pieces, path_pieces], axis=1), 'vo...  4.72 us
    all_to_all x1, waiting for transfers between devices, per_device(): lax.all_to_all(jnp.concatenate([column_pieces, path_pieces], axis=1), 'vo...  4.36 us
    unnamed x45, local copies, waits for them, and re-layouts  2.84 us
  transfers between devices with their start and end apart: 6, of which 6 were waited for; matrix products, arithmetic and copies ran while one was open for 5% of the time, Pallas kernels for 0%

profile of v9, /device:TPU:2, one launch (start us, length us, event | category | flops | bytes accessed | tf_op | source)
XLA Modules:
  0.0 117.4 jit_solution(865136571194124366)
XLA Ops:
  0.7 0.9 fusion.37
  1.6 0.7 add.180
  2.4 0.7 convert_element_type.135
  3.1 1.2 multiply_reduce_fusion
  4.3 1.0 convolution_minimum_fusion.5
  6.4 0.7 add_convert_fusion.1
  7.3 1.6 %convolution_bitcast_fusion.1 = f32[2,1,2,64,96]{4,3,2,0,1:T(8,128)S(1)} fusion(bf16[1536,2,96,1]{0,2,1,3:T(8,128)(2,1)} %bitcast.155, bf16[2,64,1536]{2,1,0:T(8,128)(2,1)} %param.18, f32[1536]{0:T(1024)S(1)} %convert_element_type.135, f32[2,64]{1,0:T(2,128)S(1)} %add_rsqrt_fusion), kind=kOutput, calls=%fused_computation.9 | convolution fusion | flops 76283904 | bytes 1088000 | tf_op jit(solution)/shard_map/rim,mkgd->rkgid/dot_general | solution.py:146
  8.9 1.3 %convolution_bitcast_fusion.4 = f32[2,1,64,96]{3,2,0,1:T(8,128)S(1)} fusion(bf16[1536,96]{0,1:T(8,128)(2,1)} %param.29, bf16[2,64,1536]{2,1,0:T(8,128)(2,1)S(1)} %copy-done.1, f32[1536]{0:T(1024)S(1)} %convert_element_type.135, f32[2,64]{1,0:T(2,128)S(1)} %add_rsqrt_fusion), kind=kOutput, calls=%fused_computation.16 | convolution fusion | flops 38535168 | bytes 743936 | tf_op jit(solution)/shard_map/rim,mkd->rkid/dot_general | solution.py:154
  10.6 1.0 fusion.30
  11.7 0.6 select_reduce_fusion
  12.6 0.5 convert_reduce_fusion
  13.2 0.5 convolution_bitcast_fusion.3
  14.1 0.6 copy-done.19
  15.0 1.1 fusion.1
  16.1 6.4 %all-to-all-start = ((bf16[8,16,1536]{2,1,0:T(8,128)(2,1)}), bf16[8,16,1536]{2,1,0:T(8,128)(2,1)}, u32[]{:S(2)}, u32[]{:S(2)}) async-start(bf16[8,16,1536]{2,1,0:T(8,128)(2,1)} %fusion.1), calls=%async_computation | async-start | bytes 786432 | tf_op jit(solution)/shard_map/all_to_all | solution.py:75
  22.4 1.0 bitcast_convert_fusion
  23.4 6.6 %all-to-all-done = bf16[8,16,1536]{2,1,0:T(8,128)(2,1)} async-done(((bf16[8,16,1536]{2,1,0:T(8,128)(2,1)}), bf16[8,16,1536]{2,1,0:T(8,128)(2,1)}, u32[]{:S(2)}, u32[]{:S(2)}) %all-to-all-start) | async-done | bytes 393248 | tf_op jit(solution)/shard_map/all_to_all | solution.py:75
  30.0 1.1 convert_reduce_fusion.1
  31.1 1.0 multiply_reduce_fusion.1
  32.1 0.6 copy-done.3
  32.8 0.8 broadcast_in_dim.117
  33.6 4.8 %all-to-all-start.1 = ((bf16[8,16,1536]{2,1,0:T(8,128)(2,1)}), bf16[8,16,1536]{2,1,0:T(8,128)(2,1)S(1)}, u32[]{:S(2)}, u32[]{:S(2)}) async-start(bf16[8,16,1536]{2,1,0:T(8,128)(2,1)} %broadcast_in_dim.117), calls=%async_computation.1 | async-start | bytes 786432 | tf_op jit(solution)/shard_map/all_to_all | solution.py:81
  38.5 0.6 fusion.46
  39.0 6.8 %all-to-all-done.1 = bf16[8,16,1536]{2,1,0:T(8,128)(2,1)S(1)} async-done(((bf16[8,16,1536]{2,1,0:T(8,128)(2,1)}), bf16[8,16,1536]{2,1,0:T(8,128)(2,1)S(1)}, u32[]{:S(2)}, u32[]{:S(2)}) %all-to-all-start.1) | async-done | bytes 393248 | tf_op jit(solution)/shard_map/all_to_all | solution.py:81
  45.9 0.7 copy-done.2
  46.6 5.4 %shard_map.209 = bf16[128,1536]{1,0:T(8,128)(2,1)} custom-call(bf16[128,1536]{1,0:T(8,128)(2,1)} %bitcast.146, bf16[1536,512]{1,0:T(8,128)(2,1)} %gate_ref.1, bf16[1536,512]{1,0:T(8,128)(2,1)} %up_ref.1, bf16[512,1536]{1,0:T(8,128)(2,1)} %down_ref.1), custom_call_target="tpu_custom_call" | custom-call | flops 603979776 | bytes 5505024 | tf_op jit(solution)/shard_map/pallas_call | solution.py:51
  52.0 4.9 %all-to-all-start.2 = ((bf16[8,16,1536]{2,1,0:T(8,128)(2,1)}), bf16[8,16,1536]{2,1,0:T(8,128)(2,1)S(1)}, u32[]{:S(2)}, u32[]{:S(2)}) async-start(bf16[8,16,1536]{2,1,0:T(8,128)(2,1)} %bitcast.147), calls=%async_computation.2 | async-start | bytes 786432 | tf_op jit(solution)/shard_map/all_to_all | solution.py:75
  57.0 1.3 %fusion.38 = pred[16]{0:T(512)(128)(4,1)S(1)} fusion(s32[]{:T(128)} %bitcast.1, s32[]{:T(128)} %bitcast, s32[]{:T(128)S(6)} %mul.183), kind=kLoop, calls=%fused_computation.105 | loop fusion | flops 784 | bytes 28 | tf_op jit(solution)/shard_map/lt | solution.py:233
  58.4 6.1 %all-to-all-done.2 = bf16[8,16,1536]{2,1,0:T(8,128)(2,1)S(1)} async-done(((bf16[8,16,1536]{2,1,0:T(8,128)(2,1)}), bf16[8,16,1536]{2,1,0:T(8,128)(2,1)S(1)}, u32[]{:S(2)}, u32[]{:S(2)}) %all-to-all-start.2) | async-done | bytes 393248 | tf_op jit(solution)/shard_map/all_to_all | solution.py:75
  64.5 0.7 reduce_sum.103
  65.1 1.0 select_convert_fusion.3
  67.1 0.7 reduce.10
  67.8 0.7 reshape.483
  68.5 4.7 %all-to-all-start.3 = ((bf16[8,2,3072]{2,1,0:T(2,128)(2,1)}), bf16[8,2,3072]{2,1,0:T(2,128)(2,1)S(1)}, u32[]{:S(2)}, u32[]{:S(2)}) async-start(bf16[8,2,3072]{2,1,0:T(2,128)(2,1)} %reshape.483), calls=%async_computation.3 | async-start | bytes 196608 | tf_op jit(solution)/shard_map/all_to_all | solution.py:262
  73.2 4.4 %all-to-all-done.3 = bf16[8,2,3072]{2,1,0:T(2,128)(2,1)S(1)} async-done(((bf16[8,2,3072]{2,1,0:T(2,128)(2,1)}), bf16[8,2,3072]{2,1,0:T(2,128)(2,1)S(1)}, u32[]{:S(2)}, u32[]{:S(2)}) %all-to-all-start.3) | async-done | bytes 98336 | tf_op jit(solution)/shard_map/all_to_all | solution.py:262
  77.7 0.6 slice_reduce_fusion
  78.5 0.5 fusion.40
  79.1 0.8 broadcast_in_dim.119
  79.8 10.1 %all-to-all-start.4 = ((bf16[32,2,1536]{2,1,0:T(2,128)(2,1)}), bf16[32,2,1536]{2,1,0:T(2,128)(2,1)S(1)}, u32[]{:S(2)}, u32[]{:S(2)}) async-start(bf16[32,2,1536]{2,1,0:T(2,128)(2,1)} %broadcast_in_dim.119), calls=%async_computation.4 | async-start | bytes 393216 | tf_op jit(solution)/shard_map/all_to_all | solution.py:81
  89.9 0.8 convolution_convert_fusion.2
  90.7 10.4 %all-to-all-done.4 = bf16[32,2,1536]{2,1,0:T(2,128)(2,1)S(1)} async-done(((bf16[32,2,1536]{2,1,0:T(2,128)(2,1)}), bf16[32,2,1536]{2,1,0:T(2,128)(2,1)S(1)}, u32[]{:S(2)}, u32[]{:S(2)}) %all-to-all-start.4) | async-done | bytes 196640 | tf_op jit(solution)/shard_map/all_to_all | solution.py:81
  101.2 1.1 convolution_reduce_fusion
  102.3 0.6 broadcast_in_dim.120
  102.9 4.1 %all-to-all-start.5 = ((f32[32,1,64]{2,1,0:T(1,128)}), f32[32,1,64]{2,1,0:T(1,128)S(1)}, u32[]{:S(2)}, u32[]{:S(2)}) async-start(f32[32,1,64]{2,1,0:T(1,128)} %broadcast_in_dim.120), calls=%async_computation.5 | async-start | bytes 32768 | tf_op jit(solution)/shard_map/all_to_all | solution.py:81
  107.1 0.8 convolution_convert_fusion.3
  107.9 0.8 reshape_reshape.4
  108.7 8.2 %all-to-all-done.5 = f32[32,1,64]{2,1,0:T(1,128)S(1)} async-done(((f32[32,1,64]{2,1,0:T(1,128)}), f32[32,1,64]{2,1,0:T(1,128)S(1)}, u32[]{:S(2)}, u32[]{:S(2)}) %all-to-all-start.5) | async-done | bytes 8224 | tf_op jit(solution)/shard_map/all_to_all | solution.py:81
  116.9 0.5 reduce_max.39
  (79 shorter events, 4.3 us)
Async XLA Ops:
  0.6 100.5 %copy-start = (bf16[1536,1000]{0,1:T(8,128)(2,1)S(1)}, bf16[1536,1000]{0,1:T(8,128)(2,1)}, u32[]{:S(2)}) copy-start(bf16[1536,1000]{0,1:T(8,128)(2,1)} %param.35) | copy-start | bytes 9216004
  0.6 8.3 %copy-start.1 = (bf16[2,64,1536]{2,1,0:T(8,128)(2,1)S(1)}, bf16[2,64,1536]{2,1,0:T(8,128)(2,1)}, u32[]{:S(2)}) copy-start(bf16[2,64,1536]{2,1,0:T(8,128)(2,1)} %param.18) | copy-start | bytes 1179652
  0.7 9.5 %copy-start.13 = (f32[48]{0:T(128)}, f32[48]{0:T(128)S(1)}, u32[]{:S(2)}) copy-start(f32[48]{0:T(128)S(1)} %multiply_power_fusion) | copy-start | bytes 580
  3.1 7.1 %copy-start.8 = (f32[1536]{0:T(1024)}, f32[1536]{0:T(1024)S(1)}, u32[]{:S(2)}) copy-start(f32[1536]{0:T(1024)S(1)} %convert_element_type.135) | copy-start | bytes 18436
  4.3 5.9 %copy-start.14 = (f32[2,64]{1,0:T(2,128)}, f32[2,64]{1,0:T(2,128)S(1)}, u32[]{:S(2)}) copy-start(f32[2,64]{1,0:T(2,128)S(1)} %add_rsqrt_fusion) | copy-start | bytes 1540
  7.2 3.1 %copy-start.7 = (f32[2,64]{1,0:T(2,128)}, f32[2,64]{1,0:T(2,128)S(1)}, u32[]{:S(2)}) copy-start(f32[2,64]{1,0:T(2,128)S(1)} %add_convert_fusion.1) | copy-start | bytes 1540
  7.3 4.4 %copy-start.5 = (bf16[2048,96]{0,1:T(8,128)(2,1)S(1)}, bf16[2048,96]{0,1:T(8,128)(2,1)}, u32[]{:S(2)}) copy-start(bf16[2048,96]{0,1:T(8,128)(2,1)} %param.23) | copy-start | bytes 1179652
  11.7 1.5 %copy-start.16 = (bf16[2048,96]{0,1:T(8,128)(2,1)S(1)}, bf16[2048,96]{0,1:T(8,128)(2,1)}, u32[]{:S(2)}) copy-start(bf16[2048,96]{0,1:T(8,128)(2,1)} %param.24) | copy-start | bytes 1179652
  12.6 1.2 copy-start.9
  12.6 1.2 copy-start.15
  12.6 1.2 copy-start.17
  13.2 1.8 %copy-start.4 = (bf16[192,1536]{1,0:T(8,128)(2,1)S(1)}, bf16[192,1536]{1,0:T(8,128)(2,1)}, u32[]{:S(2)}) copy-start(bf16[192,1536]{1,0:T(8,128)(2,1)} %param.31) | copy-start | bytes 1769476
  13.7 8.7 %copy-start.11 = (bf16[1536]{0:T(1024)(128)(2,1)S(1)}, bf16[1536]{0:T(1024)(128)(2,1)}, u32[]{:S(2)}) copy-start(bf16[1536]{0:T(1024)(128)(2,1)} %param.26) | copy-start | bytes 9220
  14.1 0.6 copy-start.19
  16.1 22.3 %copy-start.18 = (s32[64]{0:T(128)S(1)}, s32[64]{0:T(128)}, u32[]{:S(2)}) copy-start(s32[64]{0:T(128)} %param.20) | copy-start | bytes 772
  16.1 13.9 %all-to-all-start = ((bf16[8,16,1536]{2,1,0:T(8,128)(2,1)}), bf16[8,16,1536]{2,1,0:T(8,128)(2,1)}, u32[]{:S(2)}, u32[]{:S(2)}) async-start(bf16[8,16,1536]{2,1,0:T(8,128)(2,1)} %fusion.1), calls=%async_computation | async-start | bytes 786432 | tf_op jit(solution)/shard_map/all_to_all | solution.py:75
  32.1 0.6 copy-start.3
  33.6 12.3 %all-to-all-start.1 = ((bf16[8,16,1536]{2,1,0:T(8,128)(2,1)}), bf16[8,16,1536]{2,1,0:T(8,128)(2,1)S(1)}, u32[]{:S(2)}, u32[]{:S(2)}) async-start(bf16[8,16,1536]{2,1,0:T(8,128)(2,1)} %broadcast_in_dim.117), calls=%async_computation.1 | async-start | bytes 786432 | tf_op jit(solution)/shard_map/all_to_all | solution.py:81
  45.9 0.7 copy-start.2
  46.6 11.7 %copy-start.10 = (s32[2,8]{1,0:T(2,128)S(1)}, s32[2,8]{1,0:T(2,128)}, u32[]{:S(2)}) copy-start(s32[2,8]{1,0:T(2,128)} %param.21) | copy-start | bytes 196
  52.0 21.1 %copy-start.12 = (bf16[1536]{0:T(1024)(128)(2,1)S(1)}, bf16[1536]{0:T(1024)(128)(2,1)}, u32[]{:S(2)}) copy-start(bf16[1536]{0:T(1024)(128)(2,1)} %param.27) | copy-start | bytes 9220
  52.0 12.4 %all-to-all-start.2 = ((bf16[8,16,1536]{2,1,0:T(8,128)(2,1)}), bf16[8,16,1536]{2,1,0:T(8,128)(2,1)S(1)}, u32[]{:S(2)}, u32[]{:S(2)}) async-start(bf16[8,16,1536]{2,1,0:T(8,128)(2,1)} %bitcast.147), calls=%async_computation.2 | async-start | bytes 786432 | tf_op jit(solution)/shard_map/all_to_all | solution.py:75
  65.1 24.8 %copy-start.20 = (bf16[2,64,96]{2,1,0:T(8,128)(2,1)S(1)}, bf16[2,64,96]{2,1,0:T(8,128)(2,1)}, u32[]{:S(2)}) copy-start(bf16[2,64,96]{2,1,0:T(8,128)(2,1)} %copy-done.19) | copy-start | bytes 73732
  68.5 9.1 %all-to-all-start.3 = ((bf16[8,2,3072]{2,1,0:T(2,128)(2,1)}), bf16[8,2,3072]{2,1,0:T(2,128)(2,1)S(1)}, u32[]{:S(2)}, u32[]{:S(2)}) async-start(bf16[8,2,3072]{2,1,0:T(2,128)(2,1)} %reshape.483), calls=%async_computation.3 | async-start | bytes 196608 | tf_op jit(solution)/shard_map/all_to_all | solution.py:262
  79.8 21.2 %all-to-all-start.4 = ((bf16[32,2,1536]{2,1,0:T(2,128)(2,1)}), bf16[32,2,1536]{2,1,0:T(2,128)(2,1)S(1)}, u32[]{:S(2)}, u32[]{:S(2)}) async-start(bf16[32,2,1536]{2,1,0:T(2,128)(2,1)} %broadcast_in_dim.119), calls=%async_computation.4 | async-start | bytes 393216 | tf_op jit(solution)/shard_map/all_to_all | solution.py:81
  101.2 6.7 %copy-start.6 = (bf16[8,3072]{1,0:T(8,128)(2,1)S(1)}, bf16[8,3072]{1,0:T(8,128)(2,1)}, u32[]{:S(2)}) copy-start(bf16[8,3072]{1,0:T(8,128)(2,1)} %get-tuple-element.10) | copy-start | bytes 147460
  102.9 14.0 %all-to-all-start.5 = ((f32[32,1,64]{2,1,0:T(1,128)}), f32[32,1,64]{2,1,0:T(1,128)S(1)}, u32[]{:S(2)}, u32[]{:S(2)}) async-start(f32[32,1,64]{2,1,0:T(1,128)} %broadcast_in_dim.120), calls=%async_computation.5 | async-start | bytes 32768 | tf_op jit(solution)/shard_map/all_to_all | solution.py:81

commit v10 on v9

--- a/solution.py
+++ b/solution.py
@@ -44,7 +44,7 @@
         out_ref[...] = acc_ref[...].astype(out_ref.dtype)
 
 
-def feed_forward(hidden_in, gate_weight, up_weight, down_weight, block=128):
+def feed_forward(hidden_in, gate_weight, up_weight, down_weight, block=512):
     rows, width = hidden_in.shape
     units = gate_weight.shape[1]
     block = min(block, units)

time: 118 us -> 117 us (level)
  Pallas kernels: 5.43 us -> 4.13 us
    pallas_call x1, Pallas kernels: 5.43 us -> 4.13 us  [feed_forward(): pl.pallas_call(feed_forward_kernel, grid=(units // block,), in_specs=[pl....]
where the time goes in v10:
time: 117 us; the launch traced here: 116 us
  waiting for transfers between devices  42.5 us (36%)
  starting transfers between devices  35 us (30%)
  other arithmetic  15.1 us (13%)
  matrix products  10.9 us (9%)
  local copies, waits for them, and re-layouts  7.38 us (6%)
  Pallas kernels  4.13 us (4%)
    all_to_all x3, waiting for transfers between devices, gather_rows(): lax.all_to_all(copies, axis_name, split_axis=0, concat_axis=0, tiled=True)  25.4 us
    all_to_all x3, starting transfers between devices, gather_rows(): lax.all_to_all(copies, axis_name, split_axis=0, concat_axis=0, tiled=True)  19 us
    all_to_all x2, waiting for transfers between devices, scatter_rows(): lax.all_to_all(pieces, axis_name, split_axis=0, concat_axis=0, tiled=True)  12.7 us
    all_to_all x2, starting transfers between devices, scatter_rows(): lax.all_to_all(pieces, axis_name, split_axis=0, concat_axis=0, tiled=True)  11.3 us
    all_to_all x1, starting transfers between devices, per_device(): lax.all_to_all(jnp.concatenate([column_pieces, path_pieces], axis=1), 'vo...  4.72 us
    all_to_all x1, waiting for transfers between devices, per_device(): lax.all_to_all(jnp.concatenate([column_pieces, path_pieces], axis=1), 'vo...  4.36 us
    pallas_call x1, Pallas kernels, feed_forward(): pl.pallas_call(feed_forward_kernel, grid=(units // block,), in_specs=[pl....  4.13 us
    unnamed x45, local copies, waits for them, and re-layouts  2.84 us
  transfers between devices with their start and end apart: 6, of which 6 were waited for; matrix products, arithmetic and copies ran while one was open for 5% of the time, Pallas kernels for 0%

profile of v10, /device:TPU:2, one launch (start us, length us, event | category | flops | bytes accessed | tf_op | source)
XLA Modules:
  0.0 116.1 jit_solution(10053946182977951298)
XLA Ops:
  0.7 0.9 fusion.37
  1.6 0.7 add.180
  2.4 0.7 convert_element_type.135
  3.1 1.2 multiply_reduce_fusion
  4.3 1.0 convolution_minimum_fusion.5
  6.4 0.7 add_convert_fusion.1
  7.3 1.6 %convolution_bitcast_fusion.1 = f32[2,1,2,64,96]{4,3,2,0,1:T(8,128)S(1)} fusion(bf16[1536,2,96,1]{0,2,1,3:T(8,128)(2,1)} %bitcast.155, bf16[2,64,1536]{2,1,0:T(8,128)(2,1)} %param.18, f32[1536]{0:T(1024)S(1)} %convert_element_type.135, f32[2,64]{1,0:T(2,128)S(1)} %add_rsqrt_fusion), kind=kOutput, calls=%fused_computation.9 | convolution fusion | flops 76283904 | bytes 1088000 | tf_op jit(solution)/shard_map/rim,mkgd->rkgid/dot_general | solution.py:146
  8.9 1.3 %convolution_bitcast_fusion.4 = f32[2,1,64,96]{3,2,0,1:T(8,128)S(1)} fusion(bf16[1536,96]{0,1:T(8,128)(2,1)} %param.29, bf16[2,64,1536]{2,1,0:T(8,128)(2,1)S(1)} %copy-done.1, f32[1536]{0:T(1024)S(1)} %convert_element_type.135, f32[2,64]{1,0:T(2,128)S(1)} %add_rsqrt_fusion), kind=kOutput, calls=%fused_computation.16 | convolution fusion | flops 38535168 | bytes 743936 | tf_op jit(solution)/shard_map/rim,mkd->rkid/dot_general | solution.py:154
  10.6 1.0 fusion.30
  11.7 0.6 select_reduce_fusion
  12.6 0.5 convert_reduce_fusion
  13.2 0.5 convolution_bitcast_fusion.3
  14.1 0.6 copy-done.19
  15.0 1.1 fusion.1
  16.1 6.4 %all-to-all-start = ((bf16[8,16,1536]{2,1,0:T(8,128)(2,1)}), bf16[8,16,1536]{2,1,0:T(8,128)(2,1)}, u32[]{:S(2)}, u32[]{:S(2)}) async-start(bf16[8,16,1536]{2,1,0:T(8,128)(2,1)} %fusion.1), calls=%async_computation | async-start | bytes 786432 | tf_op jit(solution)/shard_map/all_to_all | solution.py:75
  22.4 1.0 bitcast_convert_fusion
  23.4 6.6 %all-to-all-done = bf16[8,16,1536]{2,1,0:T(8,128)(2,1)} async-done(((bf16[8,16,1536]{2,1,0:T(8,128)(2,1)}), bf16[8,16,1536]{2,1,0:T(8,128)(2,1)}, u32[]{:S(2)}, u32[]{:S(2)}) %all-to-all-start) | async-done | bytes 393248 | tf_op jit(solution)/shard_map/all_to_all | solution.py:75
  30.0 1.1 convert_reduce_fusion.1
  31.1 1.0 multiply_reduce_fusion.1
  32.1 0.6 copy-done.3
  32.8 0.8 broadcast_in_dim.117
  33.6 4.8 %all-to-all-start.1 = ((bf16[8,16,1536]{2,1,0:T(8,128)(2,1)}), bf16[8,16,1536]{2,1,0:T(8,128)(2,1)S(1)}, u32[]{:S(2)}, u32[]{:S(2)}) async-start(bf16[8,16,1536]{2,1,0:T(8,128)(2,1)} %broadcast_in_dim.117), calls=%async_computation.1 | async-start | bytes 786432 | tf_op jit(solution)/shard_map/all_to_all | solution.py:81
  38.5 0.6 fusion.46
  39.0 6.8 %all-to-all-done.1 = bf16[8,16,1536]{2,1,0:T(8,128)(2,1)S(1)} async-done(((bf16[8,16,1536]{2,1,0:T(8,128)(2,1)}), bf16[8,16,1536]{2,1,0:T(8,128)(2,1)S(1)}, u32[]{:S(2)}, u32[]{:S(2)}) %all-to-all-start.1) | async-done | bytes 393248 | tf_op jit(solution)/shard_map/all_to_all | solution.py:81
  45.9 0.7 copy-done.2
  46.6 4.1 %shard_map.209 = bf16[128,1536]{1,0:T(8,128)(2,1)} custom-call(bf16[128,1536]{1,0:T(8,128)(2,1)} %bitcast.146, bf16[1536,512]{1,0:T(8,128)(2,1)} %gate_ref.1, bf16[1536,512]{1,0:T(8,128)(2,1)} %up_ref.1, bf16[512,1536]{1,0:T(8,128)(2,1)} %down_ref.1), custom_call_target="tpu_custom_call" | custom-call | flops 603979776 | bytes 5505024 | tf_op jit(solution)/shard_map/pallas_call | solution.py:51
  50.7 4.9 %all-to-all-start.2 = ((bf16[8,16,1536]{2,1,0:T(8,128)(2,1)}), bf16[8,16,1536]{2,1,0:T(8,128)(2,1)S(1)}, u32[]{:S(2)}, u32[]{:S(2)}) async-start(bf16[8,16,1536]{2,1,0:T(8,128)(2,1)} %bitcast.147), calls=%async_computation.2 | async-start | bytes 786432 | tf_op jit(solution)/shard_map/all_to_all | solution.py:75
  55.7 1.3 %fusion.38 = pred[16]{0:T(512)(128)(4,1)S(1)} fusion(s32[]{:T(128)} %bitcast.1, s32[]{:T(128)} %bitcast, s32[]{:T(128)S(6)} %mul.183), kind=kLoop, calls=%fused_computation.105 | loop fusion | flops 784 | bytes 28 | tf_op jit(solution)/shard_map/lt | solution.py:233
  57.1 6.1 %all-to-all-done.2 = bf16[8,16,1536]{2,1,0:T(8,128)(2,1)S(1)} async-done(((bf16[8,16,1536]{2,1,0:T(8,128)(2,1)}), bf16[8,16,1536]{2,1,0:T(8,128)(2,1)S(1)}, u32[]{:S(2)}, u32[]{:S(2)}) %all-to-all-start.2) | async-done | bytes 393248 | tf_op jit(solution)/shard_map/all_to_all | solution.py:75
  63.2 0.7 reduce_sum.103
  63.9 1.0 select_convert_fusion.3
  65.8 0.7 reduce.10
  66.5 0.7 reshape.483
  67.2 4.7 %all-to-all-start.3 = ((bf16[8,2,3072]{2,1,0:T(2,128)(2,1)}), bf16[8,2,3072]{2,1,0:T(2,128)(2,1)S(1)}, u32[]{:S(2)}, u32[]{:S(2)}) async-start(bf16[8,2,3072]{2,1,0:T(2,128)(2,1)} %reshape.483), calls=%async_computation.3 | async-start | bytes 196608 | tf_op jit(solution)/shard_map/all_to_all | solution.py:262
  71.9 4.4 %all-to-all-done.3 = bf16[8,2,3072]{2,1,0:T(2,128)(2,1)S(1)} async-done(((bf16[8,2,3072]{2,1,0:T(2,128)(2,1)}), bf16[8,2,3072]{2,1,0:T(2,128)(2,1)S(1)}, u32[]{:S(2)}, u32[]{:S(2)}) %all-to-all-start.3) | async-done | bytes 98336 | tf_op jit(solution)/shard_map/all_to_all | solution.py:262
  76.4 0.6 slice_reduce_fusion
  77.2 0.5 fusion.40
  77.8 0.8 broadcast_in_dim.119
  78.6 10.1 %all-to-all-start.4 = ((bf16[32,2,1536]{2,1,0:T(2,128)(2,1)}), bf16[32,2,1536]{2,1,0:T(2,128)(2,1)S(1)}, u32[]{:S(2)}, u32[]{:S(2)}) async-start(bf16[32,2,1536]{2,1,0:T(2,128)(2,1)} %broadcast_in_dim.119), calls=%async_computation.4 | async-start | bytes 393216 | tf_op jit(solution)/shard_map/all_to_all | solution.py:81
  88.7 0.8 convolution_convert_fusion.2
  89.4 10.4 %all-to-all-done.4 = bf16[32,2,1536]{2,1,0:T(2,128)(2,1)S(1)} async-done(((bf16[32,2,1536]{2,1,0:T(2,128)(2,1)}), bf16[32,2,1536]{2,1,0:T(2,128)(2,1)S(1)}, u32[]{:S(2)}, u32[]{:S(2)}) %all-to-all-start.4) | async-done | bytes 196640 | tf_op jit(solution)/shard_map/all_to_all | solution.py:81
  99.9 1.1 convolution_reduce_fusion
  101.0 0.6 broadcast_in_dim.120
  101.7 4.1 %all-to-all-start.5 = ((f32[32,1,64]{2,1,0:T(1,128)}), f32[32,1,64]{2,1,0:T(1,128)S(1)}, u32[]{:S(2)}, u32[]{:S(2)}) async-start(f32[32,1,64]{2,1,0:T(1,128)} %broadcast_in_dim.120), calls=%async_computation.5 | async-start | bytes 32768 | tf_op jit(solution)/shard_map/all_to_all | solution.py:81
  105.8 0.8 convolution_convert_fusion.3
  106.6 0.8 reshape_reshape.4
  107.4 8.2 %all-to-all-done.5 = f32[32,1,64]{2,1,0:T(1,128)S(1)} async-done(((f32[32,1,64]{2,1,0:T(1,128)}), f32[32,1,64]{2,1,0:T(1,128)S(1)}, u32[]{:S(2)}, u32[]{:S(2)}) %all-to-all-start.5) | async-done | bytes 8224 | tf_op jit(solution)/shard_map/all_to_all | solution.py:81
  115.6 0.5 reduce_max.39
  (79 shorter events, 4.3 us)
Async XLA Ops:
  0.6 99.3 %copy-start = (bf16[1536,1000]{0,1:T(8,128)(2,1)S(1)}, bf16[1536,1000]{0,1:T(8,128)(2,1)}, u32[]{:S(2)}) copy-start(bf16[1536,1000]{0,1:T(8,128)(2,1)} %param.35) | copy-start | bytes 9216004
  0.6 8.3 %copy-start.1 = (bf16[2,64,1536]{2,1,0:T(8,128)(2,1)S(1)}, bf16[2,64,1536]{2,1,0:T(8,128)(2,1)}, u32[]{:S(2)}) copy-start(bf16[2,64,1536]{2,1,0:T(8,128)(2,1)} %param.18) | copy-start | bytes 1179652
  0.7 9.5 %copy-start.13 = (f32[48]{0:T(128)}, f32[48]{0:T(128)S(1)}, u32[]{:S(2)}) copy-start(f32[48]{0:T(128)S(1)} %multiply_power_fusion) | copy-start | bytes 580
  3.1 7.1 %copy-start.8 = (f32[1536]{0:T(1024)}, f32[1536]{0:T(1024)S(1)}, u32[]{:S(2)}) copy-start(f32[1536]{0:T(1024)S(1)} %convert_element_type.135) | copy-start | bytes 18436
  4.3 5.9 %copy-start.14 = (f32[2,64]{1,0:T(2,128)}, f32[2,64]{1,0:T(2,128)S(1)}, u32[]{:S(2)}) copy-start(f32[2,64]{1,0:T(2,128)S(1)} %add_rsqrt_fusion) | copy-start | bytes 1540
  7.2 3.1 %copy-start.7 = (f32[2,64]{1,0:T(2,128)}, f32[2,64]{1,0:T(2,128)S(1)}, u32[]{:S(2)}) copy-start(f32[2,64]{1,0:T(2,128)S(1)} %add_convert_fusion.1) | copy-start | bytes 1540
  7.3 4.4 %copy-start.5 = (bf16[2048,96]{0,1:T(8,128)(2,1)S(1)}, bf16[2048,96]{0,1:T(8,128)(2,1)}, u32[]{:S(2)}) copy-start(bf16[2048,96]{0,1:T(8,128)(2,1)} %param.23) | copy-start | bytes 1179652
  11.7 1.5 %copy-start.16 = (bf16[2048,96]{0,1:T(8,128)(2,1)S(1)}, bf16[2048,96]{0,1:T(8,128)(2,1)}, u32[]{:S(2)}) copy-start(bf16[2048,96]{0,1:T(8,128)(2,1)} %param.24) | copy-start | bytes 1179652
  12.6 1.2 copy-start.9
  12.6 1.2 copy-start.15
  12.6 1.2 copy-start.17
  13.2 1.8 %copy-start.4 = (bf16[192,1536]{1,0:T(8,128)(2,1)S(1)}, bf16[192,1536]{1,0:T(8,128)(2,1)}, u32[]{:S(2)}) copy-start(bf16[192,1536]{1,0:T(8,128)(2,1)} %param.31) | copy-start | bytes 1769476
  13.7 8.7 %copy-start.11 = (bf16[1536]{0:T(1024)(128)(2,1)S(1)}, bf16[1536]{0:T(1024)(128)(2,1)}, u32[]{:S(2)}) copy-start(bf16[1536]{0:T(1024)(128)(2,1)} %param.26) | copy-start | bytes 9220
  14.1 0.6 copy-start.19
  16.1 22.3 %copy-start.18 = (s32[64]{0:T(128)S(1)}, s32[64]{0:T(128)}, u32[]{:S(2)}) copy-start(s32[64]{0:T(128)} %param.20) | copy-start | bytes 772
  16.1 13.9 %all-to-all-start = ((bf16[8,16,1536]{2,1,0:T(8,128)(2,1)}), bf16[8,16,1536]{2,1,0:T(8,128)(2,1)}, u32[]{:S(2)}, u32[]{:S(2)}) async-start(bf16[8,16,1536]{2,1,0:T(8,128)(2,1)} %fusion.1), calls=%async_computation | async-start | bytes 786432 | tf_op jit(solution)/shard_map/all_to_all | solution.py:75
  32.1 0.6 copy-start.3
  33.6 12.3 %all-to-all-start.1 = ((bf16[8,16,1536]{2,1,0:T(8,128)(2,1)}), bf16[8,16,1536]{2,1,0:T(8,128)(2,1)S(1)}, u32[]{:S(2)}, u32[]{:S(2)}) async-start(bf16[8,16,1536]{2,1,0:T(8,128)(2,1)} %broadcast_in_dim.117), calls=%async_computation.1 | async-start | bytes 786432 | tf_op jit(solution)/shard_map/all_to_all | solution.py:81
  45.9 0.7 copy-start.2
  46.6 10.4 %copy-start.10 = (s32[2,8]{1,0:T(2,128)S(1)}, s32[2,8]{1,0:T(2,128)}, u32[]{:S(2)}) copy-start(s32[2,8]{1,0:T(2,128)} %param.21) | copy-start | bytes 196
  50.7 21.1 %copy-start.12 = (bf16[1536]{0:T(1024)(128)(2,1)S(1)}, bf16[1536]{0:T(1024)(128)(2,1)}, u32[]{:S(2)}) copy-start(bf16[1536]{0:T(1024)(128)(2,1)} %param.27) | copy-start | bytes 9220
  50.7 12.4 %all-to-all-start.2 = ((bf16[8,16,1536]{2,1,0:T(8,128)(2,1)}), bf16[8,16,1536]{2,1,0:T(8,128)(2,1)S(1)}, u32[]{:S(2)}, u32[]{:S(2)}) async-start(bf16[8,16,1536]{2,1,0:T(8,128)(2,1)} %bitcast.147), calls=%async_computation.2 | async-start | bytes 786432 | tf_op jit(solution)/shard_map/all_to_all | solution.py:75
  63.9 24.8 %copy-start.20 = (bf16[2,64,96]{2,1,0:T(8,128)(2,1)S(1)}, bf16[2,64,96]{2,1,0:T(8,128)(2,1)}, u32[]{:S(2)}) copy-start(bf16[2,64,96]{2,1,0:T(8,128)(2,1)} %copy-done.19) | copy-start | bytes 73732
  67.2 9.1 %all-to-all-start.3 = ((bf16[8,2,3072]{2,1,0:T(2,128)(2,1)}), bf16[8,2,3072]{2,1,0:T(2,128)(2,1)S(1)}, u32[]{:S(2)}, u32[]{:S(2)}) async-start(bf16[8,2,3072]{2,1,0:T(2,128)(2,1)} %reshape.483), calls=%async_computation.3 | async-start | bytes 196608 | tf_op jit(solution)/shard_map/all_to_all | solution.py:262
  78.6 21.2 %all-to-all-start.4 = ((bf16[32,2,1536]{2,1,0:T(2,128)(2,1)}), bf16[32,2,1536]{2,1,0:T(2,128)(2,1)S(1)}, u32[]{:S(2)}, u32[]{:S(2)}) async-start(bf16[32,2,1536]{2,1,0:T(2,128)(2,1)} %broadcast_in_dim.119), calls=%async_computation.4 | async-start | bytes 393216 | tf_op jit(solution)/shard_map/all_to_all | solution.py:81
  99.9 6.7 %copy-start.6 = (bf16[8,3072]{1,0:T(8,128)(2,1)S(1)}, bf16[8,3072]{1,0:T(8,128)(2,1)}, u32[]{:S(2)}) copy-start(bf16[8,3072]{1,0:T(8,128)(2,1)} %get-tuple-element.10) | copy-start | bytes 147460
  101.7 14.0 %all-to-all-start.5 = ((f32[32,1,64]{2,1,0:T(1,128)}), f32[32,1,64]{2,1,0:T(1,128)S(1)}, u32[]{:S(2)}, u32[]{:S(2)}) async-start(f32[32,1,64]{2,1,0:T(1,128)} %broadcast_in_dim.120), calls=%async_computation.5 | async-start | bytes 32768 | tf_op jit(solution)/shard_map/all_to_all | solution.py:81

commit v11 on v10

--- a/solution.py
+++ b/solution.py
@@ -1,3 +1,5 @@
+import functools
+
 import jax
 import jax.numpy as jnp
 from jax import lax
@@ -68,6 +70,38 @@
         ),
     )(hidden_in, gate_weight, up_weight, down_weight)
 
+
+def head_prepare_kernel(head_offset, arrived_ref, gain_ref, copies_ref, norm_ref):
+    width = copies_ref.shape[2]
+    rows = []
+    for row in range(norm_ref.shape[0]):
+        start = head_offset + row * width
+        piece = arrived_ref[:, start : start + width].astype(jnp.float32)
+        rows.append(jnp.sum(piece, axis=0, keepdims=True).astype(jnp.bfloat16).astype(jnp.float32))
+    path_rows = jnp.concatenate(rows, axis=0)
+    mean_square = jnp.mean(path_rows * path_rows, axis=1, keepdims=True)
+    norm_ref[...] = jnp.sqrt(mean_square + eps_norm)
+    head_in = (
+        path_rows * lax.rsqrt(mean_square + eps_norm) * gain_ref[...].astype(jnp.float32)
+    ).astype(copies_ref.dtype)
+    for target in range(copies_ref.shape[0]):
+        copies_ref[target] = head_in
+
+
+def head_prepare(arrived, gain, head_offset, path_count, targets):
+    width = gain.shape[0]
+    return pl.pallas_call(
+        functools.partial(head_prepare_kernel, head_offset),
+        out_shape=[
+            jax.ShapeDtypeStruct((targets, path_count, width), jnp.bfloat16),
+            jax.ShapeDtypeStruct((path_count, 1), jnp.float32),
+        ],
+        cost_estimate=pl.CostEstimate(
+            flops=6 * arrived.size,
+            transcendentals=2 * path_count,
+            bytes_accessed=2 * arrived.size + 2 * targets * path_count * width,
+        ),
+    )(arrived, gain.reshape(1, width))
 
 def scatter_rows(partial, axis_name, shards):
     rows = partial.shape[0] // shards
@@ -267,11 +301,6 @@
         tiled=True,
     )
     layer_part = arrived[:, : chunk_rows * share_width].reshape(token_rows, share_width)
-    head_rows = (
-        jnp.sum(arrived[:, chunk_rows * share_width :].astype(jnp.float32), axis=0)
-        .reshape(path_count, model_width)
-        .astype(jnp.bfloat16)
-    )
     request_picker = (
         path_index[:, :, None] == jnp.arange(draft_length, dtype=jnp.int32)[None, None, :]
     ).astype(jnp.bfloat16)
@@ -287,18 +316,15 @@
         fresh_values.reshape(local_requests, draft_length, key_local * head_dim),
         preferred_element_type=jnp.float32,
     ).astype(jnp.bfloat16)
-    flat_rows = head_rows.astype(jnp.float32)
-    mean_square = jnp.mean(flat_rows * flat_rows, axis=1)
-    norm_values = jnp.sqrt(mean_square + eps_norm).reshape(local_requests, per_shard)
-    head_in = (
-        flat_rows * lax.rsqrt(mean_square + eps_norm)[:, None] * final_gain.astype(jnp.float32)
-    ).astype(jnp.bfloat16)
+    head_copies, path_norms = head_prepare(
+        arrived, final_gain, chunk_rows * share_width, path_count, request_shards
+    )
+    norm_values = path_norms.reshape(local_requests, per_shard)
+    gathered_head = lax.all_to_all(
+        head_copies, "req", split_axis=0, concat_axis=0, tiled=True
+    ).reshape(request_shards * path_count, model_width)
     local_max = jnp.max(
-        jnp.dot(
-            gather_rows(head_in, "req", request_shards),
-            head_weight,
-            preferred_element_type=jnp.float32,
-        ),
+        jnp.dot(gathered_head, head_weight, preferred_element_type=jnp.float32),
         axis=1,
     )
     every_max = gather_rows(local_max[None], "req", request_shards)

time: 117 us -> 117 us (level)
  Pallas kernels: 4.13 us -> 5.85 us
  other arithmetic: 15.1 us -> 13.8 us
  waiting for transfers between devices: 42.5 us -> 41.3 us
    all_to_all x3 -> x2, waiting for transfers between devices: 25.4 us -> 14.4 us  [gather_rows(): lax.all_to_all(copies, axis_name, split_axis=0, concat_axis=0, tiled=True)]
    all_to_all x0 -> x1, waiting for transfers between devices: none -> 10.4 us  [per_device(): lax.all_to_all(head_copies, 'req', split_axis=0, concat_axis=0, tiled=True)]
    all_to_all x0 -> x1, starting transfers between devices: none -> 10.1 us  [per_device(): lax.all_to_all(head_copies, 'req', split_axis=0, concat_axis=0, tiled=True)]
    all_to_all x3 -> x2, starting transfers between devices: 19 us -> 8.95 us  [gather_rows(): lax.all_to_all(copies, axis_name, split_axis=0, concat_axis=0, tiled=True)]
    pallas_call x0 -> x1, Pallas kernels: none -> 1.72 us  [head_prepare(): pl.pallas_call(functools.partial(head_prepare_kernel, head_offset), out_s...]
    unnamed x45 -> x48, local copies, waits for them, and re-layouts: 2.84 us -> 4.12 us
  transfers between devices with their start and end apart: 6 -> 6, of which waited for: 6 -> 6; matrix products, arithmetic and copies ran while one was open for 5% -> 6% of each run, Pallas kernels for 0% -> 0%
where the time goes in v11:
time: 117 us; the launch traced here: 116 us
  waiting for transfers between devices  41.3 us (35%)
  starting transfers between devices  35.1 us (30%)
  other arithmetic  13.8 us (12%)
  matrix products  10.9 us (9%)
  local copies, waits for them, and re-layouts  8.48 us (7%)
  Pallas kernels  5.85 us (5%)
    all_to_all x2, waiting for transfers between devices, gather_rows(): lax.all_to_all(copies, axis_name, split_axis=0, concat_axis=0, tiled=True)  14.4 us
    all_to_all x2, waiting for transfers between devices, scatter_rows(): lax.all_to_all(pieces, axis_name, split_axis=0, concat_axis=0, tiled=True)  12.7 us
    all_to_all x2, starting transfers between devices, scatter_rows(): lax.all_to_all(pieces, axis_name, split_axis=0, concat_axis=0, tiled=True)  11.3 us
    all_to_all x1, waiting for transfers between devices, per_device(): lax.all_to_all(head_copies, 'req', split_axis=0, concat_axis=0, tiled=True)  10.4 us
    all_to_all x1, starting transfers between devices, per_device(): lax.all_to_all(head_copies, 'req', split_axis=0, concat_axis=0, tiled=True)  10.1 us
    all_to_all x2, starting transfers between devices, gather_rows(): lax.all_to_all(copies, axis_name, split_axis=0, concat_axis=0, tiled=True)  8.95 us
    all_to_all x1, starting transfers between devices, per_device(): lax.all_to_all(jnp.concatenate([column_pieces, path_pieces], axis=1), 'vo...  4.72 us
    pallas_call x1, Pallas kernels, feed_forward(): pl.pallas_call(feed_forward_kernel, grid=(units // block,), in_specs=[pl....  4.14 us
  transfers between devices with their start and end apart: 6, of which 6 were waited for; matrix products, arithmetic and copies ran while one was open for 6% of the time, Pallas kernels for 0%

profile of v11, /device:TPU:2, one launch (start us, length us, event | category | flops | bytes accessed | tf_op | source)
XLA Modules:
  0.0 116.4 jit_solution(17371912681145923912)
XLA Ops:
  0.7 0.9 fusion.37
  1.6 0.7 add.165
  2.4 0.7 convert_element_type.108
  3.1 1.2 multiply_reduce_fusion
  4.3 1.0 convolution_minimum_fusion.5
  6.4 0.7 add_convert_fusion.1
  7.3 1.6 %convolution_bitcast_fusion.1 = f32[2,1,2,64,96]{4,3,2,0,1:T(8,128)S(1)} fusion(bf16[1536,2,96,1]{0,2,1,3:T(8,128)(2,1)} %bitcast.154, bf16[2,64,1536]{2,1,0:T(8,128)(2,1)} %param.18, f32[1536]{0:T(1024)S(1)} %convert_element_type.108, f32[2,64]{1,0:T(2,128)S(1)} %add_rsqrt_fusion), kind=kOutput, calls=%fused_computation.9 | convolution fusion | flops 76283904 | bytes 1088000 | tf_op jit(solution)/shard_map/rim,mkgd->rkgid/dot_general | solution.py:180
  8.9 1.3 %convolution_bitcast_fusion.4 = f32[2,1,64,96]{3,2,0,1:T(8,128)S(1)} fusion(bf16[1536,96]{0,1:T(8,128)(2,1)} %param.29, bf16[2,64,1536]{2,1,0:T(8,128)(2,1)S(1)} %copy-done.1, f32[1536]{0:T(1024)S(1)} %convert_element_type.108, f32[2,64]{1,0:T(2,128)S(1)} %add_rsqrt_fusion), kind=kOutput, calls=%fused_computation.16 | convolution fusion | flops 38535168 | bytes 743936 | tf_op jit(solution)/shard_map/rim,mkd->rkid/dot_general | solution.py:188
  10.6 1.0 fusion.30
  11.7 0.6 select_reduce_fusion
  12.6 0.5 convert_reduce_fusion
  14.1 0.6 copy-done.20
  15.0 1.1 fusion.1
  16.1 6.4 %all-to-all-start = ((bf16[8,16,1536]{2,1,0:T(8,128)(2,1)}), bf16[8,16,1536]{2,1,0:T(8,128)(2,1)}, u32[]{:S(2)}, u32[]{:S(2)}) async-start(bf16[8,16,1536]{2,1,0:T(8,128)(2,1)} %fusion.1), calls=%async_computation | async-start | bytes 786432 | tf_op jit(solution)/shard_map/all_to_all | solution.py:109
  22.4 1.0 bitcast_convert_fusion
  23.4 6.6 %all-to-all-done = bf16[8,16,1536]{2,1,0:T(8,128)(2,1)} async-done(((bf16[8,16,1536]{2,1,0:T(8,128)(2,1)}), bf16[8,16,1536]{2,1,0:T(8,128)(2,1)}, u32[]{:S(2)}, u32[]{:S(2)}) %all-to-all-start) | async-done | bytes 393248 | tf_op jit(solution)/shard_map/all_to_all | solution.py:109
  30.0 1.1 convert_reduce_fusion.1
  31.1 1.0 multiply_reduce_fusion.1
  32.1 0.6 copy-done.3
  32.8 0.8 broadcast_in_dim.109
  33.6 4.8 %all-to-all-start.1 = ((bf16[8,16,1536]{2,1,0:T(8,128)(2,1)}), bf16[8,16,1536]{2,1,0:T(8,128)(2,1)S(1)}, u32[]{:S(2)}, u32[]{:S(2)}) async-start(bf16[8,16,1536]{2,1,0:T(8,128)(2,1)} %broadcast_in_dim.109), calls=%async_computation.1 | async-start | bytes 786432 | tf_op jit(solution)/shard_map/all_to_all | solution.py:115
  38.5 0.6 fusion.45
  39.1 6.8 %all-to-all-done.1 = bf16[8,16,1536]{2,1,0:T(8,128)(2,1)S(1)} async-done(((bf16[8,16,1536]{2,1,0:T(8,128)(2,1)}), bf16[8,16,1536]{2,1,0:T(8,128)(2,1)S(1)}, u32[]{:S(2)}, u32[]{:S(2)}) %all-to-all-start.1) | async-done | bytes 393248 | tf_op jit(solution)/shard_map/all_to_all | solution.py:115
  45.9 0.7 copy-done.2
  46.6 4.1 %shard_map.209 = bf16[128,1536]{1,0:T(8,128)(2,1)} custom-call(bf16[128,1536]{1,0:T(8,128)(2,1)} %bitcast.144, bf16[1536,512]{1,0:T(8,128)(2,1)} %gate_ref.1, bf16[1536,512]{1,0:T(8,128)(2,1)} %up_ref.1, bf16[512,1536]{1,0:T(8,128)(2,1)} %down_ref.1), custom_call_target="tpu_custom_call" | custom-call | flops 603979776 | bytes 5505024 | tf_op jit(solution)/shard_map/pallas_call | solution.py:53
  50.8 4.9 %all-to-all-start.2 = ((bf16[8,16,1536]{2,1,0:T(8,128)(2,1)}), bf16[8,16,1536]{2,1,0:T(8,128)(2,1)S(1)}, u32[]{:S(2)}, u32[]{:S(2)}) async-start(bf16[8,16,1536]{2,1,0:T(8,128)(2,1)} %bitcast.145), calls=%async_computation.2 | async-start | bytes 786432 | tf_op jit(solution)/shard_map/all_to_all | solution.py:109
  55.7 1.3 %fusion.38 = pred[16]{0:T(512)(128)(4,1)S(1)} fusion(s32[]{:T(128)} %bitcast.1, s32[]{:T(128)} %bitcast, s32[]{:T(128)S(6)} %mul.156), kind=kLoop, calls=%fused_computation.102 | loop fusion | flops 784 | bytes 28 | tf_op jit(solution)/shard_map/lt | solution.py:267
  57.1 6.1 %all-to-all-done.2 = bf16[8,16,1536]{2,1,0:T(8,128)(2,1)S(1)} async-done(((bf16[8,16,1536]{2,1,0:T(8,128)(2,1)}), bf16[8,16,1536]{2,1,0:T(8,128)(2,1)S(1)}, u32[]{:S(2)}, u32[]{:S(2)}) %all-to-all-start.2) | async-done | bytes 393248 | tf_op jit(solution)/shard_map/all_to_all | solution.py:109
  63.2 0.7 reduce_sum.82
  63.9 1.0 select_convert_fusion.3
  65.8 0.7 reduce.9
  66.5 0.7 reshape.424
  67.2 4.7 %all-to-all-start.3 = ((bf16[8,2,3072]{2,1,0:T(2,128)(2,1)}), bf16[8,2,3072]{2,1,0:T(2,128)(2,1)S(1)}, u32[]{:S(2)}, u32[]{:S(2)}) async-start(bf16[8,2,3072]{2,1,0:T(2,128)(2,1)} %reshape.424), calls=%async_computation.3 | async-start | bytes 196608 | tf_op jit(solution)/shard_map/all_to_all | solution.py:296
  71.9 0.6 reshape.393.gain_ref
  72.5 3.8 %all-to-all-done.3 = bf16[8,2,3072]{2,1,0:T(2,128)(2,1)S(1)} async-done(((bf16[8,2,3072]{2,1,0:T(2,128)(2,1)}), bf16[8,2,3072]{2,1,0:T(2,128)(2,1)S(1)}, u32[]{:S(2)}, u32[]{:S(2)}) %all-to-all-start.3) | async-done | bytes 98336 | tf_op jit(solution)/shard_map/all_to_all | solution.py:296
  76.4 0.7 copy.77
  77.1 1.7 %shard_map.210 = (bf16[32,2,1536]{2,1,0:T(2,128)(2,1)}, f32[2,1]{1,0:T(2,128)}) custom-call(bf16[8,6144]{1,0:T(8,128)(2,1)} %bitcast.146, bf16[1,1536]{1,0:T(2,128)(2,1)} %reshape.393.gain_ref), custom_call_target="tpu_custom_call" | custom-call | flops 294912 | bytes 294912 | tf_op jit(solution)/shard_map/pallas_call | solution.py:93
  78.8 10.1 %all-to-all-start.4 = ((bf16[32,2,1536]{2,1,0:T(2,128)(2,1)}), bf16[32,2,1536]{2,1,0:T(2,128)(2,1)S(1)}, u32[]{:S(2)}, u32[]{:S(2)}) async-start(bf16[32,2,1536]{2,1,0:T(2,128)(2,1)} %get-tuple-element.8), calls=%async_computation.4 | async-start | bytes 393216 | tf_op jit(solution)/shard_map/all_to_all | solution.py:323
  88.9 0.8 convolution_convert_fusion.2
  89.7 10.4 %all-to-all-done.4 = bf16[32,2,1536]{2,1,0:T(2,128)(2,1)S(1)} async-done(((bf16[32,2,1536]{2,1,0:T(2,128)(2,1)}), bf16[32,2,1536]{2,1,0:T(2,128)(2,1)S(1)}, u32[]{:S(2)}, u32[]{:S(2)}) %all-to-all-start.4) | async-done | bytes 196640 | tf_op jit(solution)/shard_map/all_to_all | solution.py:323
  100.2 1.1 convolution_reduce_fusion
  101.3 0.6 broadcast_in_dim.111
  101.9 4.1 %all-to-all-start.5 = ((f32[32,1,64]{2,1,0:T(1,128)}), f32[32,1,64]{2,1,0:T(1,128)S(1)}, u32[]{:S(2)}, u32[]{:S(2)}) async-start(f32[32,1,64]{2,1,0:T(1,128)} %broadcast_in_dim.111), calls=%async_computation.5 | async-start | bytes 32768 | tf_op jit(solution)/shard_map/all_to_all | solution.py:115
  106.0 0.8 convolution_convert_fusion.3
  106.8 0.8 reshape_reshape.4
  107.6 0.6 copy.64
  108.2 7.6 %all-to-all-done.5 = f32[32,1,64]{2,1,0:T(1,128)S(1)} async-done(((f32[32,1,64]{2,1,0:T(1,128)}), f32[32,1,64]{2,1,0:T(1,128)S(1)}, u32[]{:S(2)}, u32[]{:S(2)}) %all-to-all-start.5) | async-done | bytes 8224 | tf_op jit(solution)/shard_map/all_to_all | solution.py:115
  115.8 0.5 reduce_max.39
  (78 shorter events, 4.5 us)
Async XLA Ops:
  0.6 99.5 %copy-start = (bf16[1536,1000]{0,1:T(8,128)(2,1)S(1)}, bf16[1536,1000]{0,1:T(8,128)(2,1)}, u32[]{:S(2)}) copy-start(bf16[1536,1000]{0,1:T(8,128)(2,1)} %param.35) | copy-start | bytes 9216004
  0.6 8.3 %copy-start.1 = (bf16[2,64,1536]{2,1,0:T(8,128)(2,1)S(1)}, bf16[2,64,1536]{2,1,0:T(8,128)(2,1)}, u32[]{:S(2)}) copy-start(bf16[2,64,1536]{2,1,0:T(8,128)(2,1)} %param.18) | copy-start | bytes 1179652
  0.7 9.5 %copy-start.13 = (f32[48]{0:T(128)}, f32[48]{0:T(128)S(1)}, u32[]{:S(2)}) copy-start(f32[48]{0:T(128)S(1)} %multiply_power_fusion) | copy-start | bytes 580
  3.1 7.1 %copy-start.8 = (f32[1536]{0:T(1024)}, f32[1536]{0:T(1024)S(1)}, u32[]{:S(2)}) copy-start(f32[1536]{0:T(1024)S(1)} %convert_element_type.108) | copy-start | bytes 18436
  4.3 5.9 %copy-start.14 = (f32[2,64]{1,0:T(2,128)}, f32[2,64]{1,0:T(2,128)S(1)}, u32[]{:S(2)}) copy-start(f32[2,64]{1,0:T(2,128)S(1)} %add_rsqrt_fusion) | copy-start | bytes 1540
  7.2 3.1 %copy-start.7 = (f32[2,64]{1,0:T(2,128)}, f32[2,64]{1,0:T(2,128)S(1)}, u32[]{:S(2)}) copy-start(f32[2,64]{1,0:T(2,128)S(1)} %add_convert_fusion.1) | copy-start | bytes 1540
  7.3 4.4 %copy-start.6 = (bf16[2048,96]{0,1:T(8,128)(2,1)S(1)}, bf16[2048,96]{0,1:T(8,128)(2,1)}, u32[]{:S(2)}) copy-start(bf16[2048,96]{0,1:T(8,128)(2,1)} %param.23) | copy-start | bytes 1179652
  11.7 1.5 %copy-start.16 = (bf16[2048,96]{0,1:T(8,128)(2,1)S(1)}, bf16[2048,96]{0,1:T(8,128)(2,1)}, u32[]{:S(2)}) copy-start(bf16[2048,96]{0,1:T(8,128)(2,1)} %param.24) | copy-start | bytes 1179652
  12.6 1.2 copy-start.9
  12.6 1.2 copy-start.15
  12.6 1.2 copy-start.17
  13.2 1.8 %copy-start.5 = (bf16[192,1536]{1,0:T(8,128)(2,1)S(1)}, bf16[192,1536]{1,0:T(8,128)(2,1)}, u32[]{:S(2)}) copy-start(bf16[192,1536]{1,0:T(8,128)(2,1)} %param.31) | copy-start | bytes 1769476
  13.7 8.7 %copy-start.11 = (bf16[1536]{0:T(1024)(128)(2,1)S(1)}, bf16[1536]{0:T(1024)(128)(2,1)}, u32[]{:S(2)}) copy-start(bf16[1536]{0:T(1024)(128)(2,1)} %param.26) | copy-start | bytes 9220
  14.1 0.6 copy-start.20
  16.1 22.3 %copy-start.19 = (s32[64]{0:T(128)S(1)}, s32[64]{0:T(128)}, u32[]{:S(2)}) copy-start(s32[64]{0:T(128)} %param.20) | copy-start | bytes 772
  16.1 13.9 %all-to-all-start = ((bf16[8,16,1536]{2,1,0:T(8,128)(2,1)}), bf16[8,16,1536]{2,1,0:T(8,128)(2,1)}, u32[]{:S(2)}, u32[]{:S(2)}) async-start(bf16[8,16,1536]{2,1,0:T(8,128)(2,1)} %fusion.1), calls=%async_computation | async-start | bytes 786432 | tf_op jit(solution)/shard_map/all_to_all | solution.py:109
  32.1 0.6 copy-start.3
  33.6 12.3 %all-to-all-start.1 = ((bf16[8,16,1536]{2,1,0:T(8,128)(2,1)}), bf16[8,16,1536]{2,1,0:T(8,128)(2,1)S(1)}, u32[]{:S(2)}, u32[]{:S(2)}) async-start(bf16[8,16,1536]{2,1,0:T(8,128)(2,1)} %broadcast_in_dim.109), calls=%async_computation.1 | async-start | bytes 786432 | tf_op jit(solution)/shard_map/all_to_all | solution.py:115
  45.9 0.7 copy-start.2
  46.6 10.4 %copy-start.10 = (s32[2,8]{1,0:T(2,128)S(1)}, s32[2,8]{1,0:T(2,128)}, u32[]{:S(2)}) copy-start(s32[2,8]{1,0:T(2,128)} %param.21) | copy-start | bytes 196
  50.8 21.2 %copy-start.12 = (bf16[1536]{0:T(1024)(128)(2,1)S(1)}, bf16[1536]{0:T(1024)(128)(2,1)}, u32[]{:S(2)}) copy-start(bf16[1536]{0:T(1024)(128)(2,1)} %param.27) | copy-start | bytes 9220
  50.8 12.4 %all-to-all-start.2 = ((bf16[8,16,1536]{2,1,0:T(8,128)(2,1)}), bf16[8,16,1536]{2,1,0:T(8,128)(2,1)S(1)}, u32[]{:S(2)}, u32[]{:S(2)}) async-start(bf16[8,16,1536]{2,1,0:T(8,128)(2,1)} %bitcast.145), calls=%async_computation.2 | async-start | bytes 786432 | tf_op jit(solution)/shard_map/all_to_all | solution.py:109
  63.9 25.0 %copy-start.21 = (bf16[2,64,96]{2,1,0:T(8,128)(2,1)S(1)}, bf16[2,64,96]{2,1,0:T(8,128)(2,1)}, u32[]{:S(2)}) copy-start(bf16[2,64,96]{2,1,0:T(8,128)(2,1)} %copy-done.20) | copy-start | bytes 73732
  67.2 9.1 %all-to-all-start.3 = ((bf16[8,2,3072]{2,1,0:T(2,128)(2,1)}), bf16[8,2,3072]{2,1,0:T(2,128)(2,1)S(1)}, u32[]{:S(2)}, u32[]{:S(2)}) async-start(bf16[8,2,3072]{2,1,0:T(2,128)(2,1)} %reshape.424), calls=%async_computation.3 | async-start | bytes 196608 | tf_op jit(solution)/shard_map/all_to_all | solution.py:296
  78.8 21.3 %all-to-all-start.4 = ((bf16[32,2,1536]{2,1,0:T(2,128)(2,1)}), bf16[32,2,1536]{2,1,0:T(2,128)(2,1)S(1)}, u32[]{:S(2)}, u32[]{:S(2)}) async-start(bf16[32,2,1536]{2,1,0:T(2,128)(2,1)} %get-tuple-element.8), calls=%async_computation.4 | async-start | bytes 393216 | tf_op jit(solution)/shard_map/all_to_all | solution.py:323
  88.9 18.7 %copy-start.18 = (f32[2,1]{1,0:T(2,128)S(1)}, f32[2,1]{1,0:T(2,128)}, u32[]{:S(2)}) copy-start(f32[2,1]{1,0:T(2,128)} %get-tuple-element.37) | copy-start | bytes 28
  100.1 6.7 %copy-start.4 = (bf16[8,1,6144]{2,0,1:T(8,128)(2,1)S(1)}, bf16[8,1,6144]{2,0,1:T(8,128)(2,1)}, u32[]{:S(2)}) copy-start(bf16[8,1,6144]{2,0,1:T(8,128)(2,1)} %copy.77) | copy-start | bytes 294916
  101.9 14.0 %all-to-all-start.5 = ((f32[32,1,64]{2,1,0:T(1,128)}), f32[32,1,64]{2,1,0:T(1,128)S(1)}, u32[]{:S(2)}, u32[]{:S(2)}) async-start(f32[32,1,64]{2,1,0:T(1,128)} %broadcast_in_dim.111), calls=%async_computation.5 | async-start | bytes 32768 | tf_op jit(solution)/shard_map/all_to_all | solution.py:115

commit v12 on v10

--- a/solution.py
+++ b/solution.py
@@ -73,7 +73,10 @@
     rows = partial.shape[0] // shards
     pieces = partial.reshape(shards, rows, *partial.shape[1:]).astype(jnp.bfloat16)
     arrived = lax.all_to_all(pieces, axis_name, split_axis=0, concat_axis=0, tiled=True)
-    return jnp.sum(arrived.astype(jnp.float32), axis=0)
+    summed = arrived[0].astype(jnp.float32)
+    for source in range(1, shards):
+        summed = summed + arrived[source].astype(jnp.float32)
+    return summed
 
 
 def gather_rows(chunk, axis_name, shards):

time: 117 us -> 116 us (level)
  waiting for transfers between devices: 42.5 us -> 38.9 us
  matrix products: 10.9 us -> 12.3 us
    reduce_sum x2 -> x0, other arithmetic: 1.73 us -> none  [scatter_rows(): return jnp.sum(arrived.astype(jnp.float32), axis=0)]
    all_to_all x2, waiting for transfers between devices: 12.7 us -> 11.1 us  [scatter_rows(): lax.all_to_all(pieces, axis_name, split_axis=0, concat_axis=0, tiled=True)]
    all_to_all x3, waiting for transfers between devices: 25.4 us -> 24.2 us  [gather_rows(): lax.all_to_all(copies, axis_name, split_axis=0, concat_axis=0, tiled=True)]
  transfers between devices with their start and end apart: 6 -> 6, of which waited for: 6 -> 6; matrix products, arithmetic and copies ran while one was open for 5% -> 8% of each run, Pallas kernels for 0% -> 0%
where the time goes in v12:
time: 116 us; the launch traced here: 115 us
  waiting for transfers between devices  38.9 us (34%)
  starting transfers between devices  35 us (30%)
  other arithmetic  16.1 us (14%)
  matrix products  12.3 us (11%)
  local copies, waits for them, and re-layouts  7.42 us (6%)
  Pallas kernels  4.14 us (4%)
    all_to_all x3, waiting for transfers between devices, gather_rows(): lax.all_to_all(copies, axis_name, split_axis=0, concat_axis=0, tiled=True)  24.2 us
    all_to_all x3, starting transfers between devices, gather_rows(): lax.all_to_all(copies, axis_name, split_axis=0, concat_axis=0, tiled=True)  19.8 us
    all_to_all x2, waiting for transfers between devices, scatter_rows(): lax.all_to_all(pieces, axis_name, split_axis=0, concat_axis=0, tiled=True)  11.1 us
    all_to_all x2, starting transfers between devices, scatter_rows(): lax.all_to_all(pieces, axis_name, split_axis=0, concat_axis=0, tiled=True)  10.6 us
    all_to_all x1, starting transfers between devices, per_device(): lax.all_to_all(jnp.concatenate([column_pieces, path_pieces], axis=1), 'vo...  4.72 us
    pallas_call x1, Pallas kernels, feed_forward(): pl.pallas_call(feed_forward_kernel, grid=(units // block,), in_specs=[pl....  4.14 us
    all_to_all x1, waiting for transfers between devices, per_device(): lax.all_to_all(jnp.concatenate([column_pieces, path_pieces], axis=1), 'vo...  3.68 us
    unnamed x45, local copies, waits for them, and re-layouts  2.86 us
  transfers between devices with their start and end apart: 6, of which 6 were waited for; matrix products, arithmetic and copies ran while one was open for 8% of the time, Pallas kernels for 0%

profile of v12, /device:TPU:2, one launch (start us, length us, event | category | flops | bytes accessed | tf_op | source)
XLA Modules:
  0.0 115.0 jit_solution(9719869637943815055)
XLA Ops:
  0.7 0.9 fusion.40
  1.6 0.7 add.232
  2.4 0.7 convert_element_type.213
  3.1 1.2 %multiply_reduce_fusion = f32[2,64]{1,0:T(2,128)S(1)} fusion(bf16[2,64,1536]{2,1,0:T(8,128)(2,1)} %param.18), kind=kLoop, calls=%fused_computation.29 | loop fusion | flops 589696 | bytes 393728 | tf_op jit(solution)/shard_map/reduce_sum | solution.py:122
  4.3 1.0 convolution_minimum_fusion.5
  6.4 0.7 add_convert_fusion.2
  7.3 1.6 %convolution_bitcast_fusion.1 = f32[2,1,2,64,96]{4,3,2,0,1:T(8,128)S(1)} fusion(bf16[1536,2,96,1]{0,2,1,3:T(8,128)(2,1)} %bitcast.163, bf16[2,64,1536]{2,1,0:T(8,128)(2,1)} %param.18, f32[1536]{0:T(1024)S(1)} %convert_element_type.213, f32[2,64]{1,0:T(2,128)S(1)} %add_rsqrt_fusion), kind=kOutput, calls=%fused_computation.9 | convolution fusion | flops 76283904 | bytes 1088000 | tf_op jit(solution)/shard_map/rim,mkgd->rkgid/dot_general | solution.py:149
  8.9 1.3 %convolution_bitcast_fusion.4 = f32[2,1,64,96]{3,2,0,1:T(8,128)S(1)} fusion(bf16[1536,96]{0,1:T(8,128)(2,1)} %param.29, bf16[2,64,1536]{2,1,0:T(8,128)(2,1)S(1)} %copy-done.1, f32[1536]{0:T(1024)S(1)} %convert_element_type.213, f32[2,64]{1,0:T(2,128)S(1)} %add_rsqrt_fusion), kind=kOutput, calls=%fused_computation.16 | convolution fusion | flops 38535168 | bytes 743936 | tf_op jit(solution)/shard_map/rim,mkd->rkid/dot_general | solution.py:157
  10.6 1.0 fusion.33
  11.7 0.6 select_reduce_fusion
  12.7 0.5 convert_reduce_fusion
  14.2 0.6 copy-done.20
  15.0 1.1 fusion.1
  16.1 5.7 %all-to-all-start = ((bf16[8,16,1536]{2,1,0:T(8,128)(2,1)}), bf16[8,16,1536]{2,1,0:T(8,128)(2,1)S(1)}, u32[]{:S(2)}, u32[]{:S(2)}) async-start(bf16[8,16,1536]{2,1,0:T(8,128)(2,1)} %fusion.1), calls=%async_computation | async-start | bytes 786432 | tf_op jit(solution)/shard_map/all_to_all | solution.py:75
  21.8 2.0 %bitcast_convert_fusion = f32[128,1536]{1,0:T(8,128)} fusion(bf16[2,64,1536]{2,1,0:T(8,128)(2,1)} %param.18), kind=kLoop, calls=%fused_computation.124 | loop fusion | flops 196608 | bytes 1179648 | tf_op jit(solution)/shard_map/convert_element_type | solution.py:119
  23.8 5.5 %all-to-all-done = bf16[8,16,1536]{2,1,0:T(8,128)(2,1)S(1)} async-done(((bf16[8,16,1536]{2,1,0:T(8,128)(2,1)}), bf16[8,16,1536]{2,1,0:T(8,128)(2,1)S(1)}, u32[]{:S(2)}, u32[]{:S(2)}) %all-to-all-start) | async-done | bytes 393248 | tf_op jit(solution)/shard_map/all_to_all | solution.py:75
  29.3 1.1 multiply_reduce_fusion.1
  30.4 0.6 copy-done.3
  31.1 0.8 broadcast_in_dim.117
  31.8 4.8 %all-to-all-start.1 = ((bf16[8,16,1536]{2,1,0:T(8,128)(2,1)}), bf16[8,16,1536]{2,1,0:T(8,128)(2,1)S(1)}, u32[]{:S(2)}, u32[]{:S(2)}) async-start(bf16[8,16,1536]{2,1,0:T(8,128)(2,1)} %broadcast_in_dim.117), calls=%async_computation.1 | async-start | bytes 786432 | tf_op jit(solution)/shard_map/all_to_all | solution.py:84
  37.2 0.6 fusion.49
  37.8 6.3 %all-to-all-done.1 = bf16[8,16,1536]{2,1,0:T(8,128)(2,1)S(1)} async-done(((bf16[8,16,1536]{2,1,0:T(8,128)(2,1)}), bf16[8,16,1536]{2,1,0:T(8,128)(2,1)S(1)}, u32[]{:S(2)}, u32[]{:S(2)}) %all-to-all-start.1) | async-done | bytes 393248 | tf_op jit(solution)/shard_map/all_to_all | solution.py:84
  44.1 0.7 copy-done.2
  44.9 4.1 %shard_map.209 = bf16[128,1536]{1,0:T(8,128)(2,1)} custom-call(bf16[128,1536]{1,0:T(8,128)(2,1)} %bitcast.154, bf16[1536,512]{1,0:T(8,128)(2,1)} %gate_ref.1, bf16[1536,512]{1,0:T(8,128)(2,1)} %up_ref.1, bf16[512,1536]{1,0:T(8,128)(2,1)} %down_ref.1), custom_call_target="tpu_custom_call" | custom-call | flops 603979776 | bytes 5505024 | tf_op jit(solution)/shard_map/pallas_call | solution.py:51
  49.0 4.8 %all-to-all-start.2 = ((bf16[8,16,1536]{2,1,0:T(8,128)(2,1)}), bf16[8,16,1536]{2,1,0:T(8,128)(2,1)S(1)}, u32[]{:S(2)}, u32[]{:S(2)}) async-start(bf16[8,16,1536]{2,1,0:T(8,128)(2,1)} %bitcast.155), calls=%async_computation.2 | async-start | bytes 786432 | tf_op jit(solution)/shard_map/all_to_all | solution.py:75
  53.8 1.8 %fusion.41 = pred[16]{0:T(512)(128)(4,1)} fusion(s32[]{:T(128)} %bitcast.1, s32[]{:T(128)} %bitcast, s32[]{:T(128)S(6)} %mul.183), kind=kLoop, calls=%fused_computation.108 | loop fusion | flops 784 | bytes 28 | tf_op jit(solution)/shard_map/lt | solution.py:236
  55.7 5.6 %all-to-all-done.2 = bf16[8,16,1536]{2,1,0:T(8,128)(2,1)S(1)} async-done(((bf16[8,16,1536]{2,1,0:T(8,128)(2,1)}), bf16[8,16,1536]{2,1,0:T(8,128)(2,1)S(1)}, u32[]{:S(2)}, u32[]{:S(2)}) %all-to-all-start.2) | async-done | bytes 393248 | tf_op jit(solution)/shard_map/all_to_all | solution.py:75
  61.3 1.0 fusion.13
  62.6 0.8 convolution_convert_fusion
  63.4 0.5 broadcast.431
  63.9 0.7 reduce.9
  64.6 0.7 reshape.531
  65.3 4.7 %all-to-all-start.3 = ((bf16[8,2,3072]{2,1,0:T(2,128)(2,1)}), bf16[8,2,3072]{2,1,0:T(2,128)(2,1)S(1)}, u32[]{:S(2)}, u32[]{:S(2)}) async-start(bf16[8,2,3072]{2,1,0:T(2,128)(2,1)} %reshape.531), calls=%async_computation.3 | async-start | bytes 196608 | tf_op jit(solution)/shard_map/all_to_all | solution.py:265
  70.0 0.7 convert_element_type.260
  70.7 3.7 %all-to-all-done.3 = bf16[8,2,3072]{2,1,0:T(2,128)(2,1)S(1)} async-done(((bf16[8,2,3072]{2,1,0:T(2,128)(2,1)}), bf16[8,2,3072]{2,1,0:T(2,128)(2,1)S(1)}, u32[]{:S(2)}, u32[]{:S(2)}) %all-to-all-start.3) | async-done | bytes 98336 | tf_op jit(solution)/shard_map/all_to_all | solution.py:265
  74.5 0.6 slice_reduce_fusion
  75.3 0.5 fusion.43
  75.9 0.8 broadcast_in_dim.119
  76.7 10.8 %all-to-all-start.4 = ((bf16[32,2,1536]{2,1,0:T(2,128)(2,1)}), bf16[32,2,1536]{2,1,0:T(2,128)(2,1)S(1)}, u32[]{:S(2)}, u32[]{:S(2)}) async-start(bf16[32,2,1536]{2,1,0:T(2,128)(2,1)} %broadcast_in_dim.119), calls=%async_computation.4 | async-start | bytes 393216 | tf_op jit(solution)/shard_map/all_to_all | solution.py:84
  87.5 1.5 %convolution_convert_fusion.2 = bf16[2,8,96]{2,1,0:T(8,128)(2,1)} fusion(bf16[2,64,96]{2,1,0:T(8,128)(2,1)} %copy-done.20, s32[2,8]{1,0:T(2,128)S(1)} %copy-done.12), kind=kOutput, calls=%fused_computation.25 | convolution fusion | flops 199168 | bytes 27712 | tf_op jit(solution)/shard_map/ytm,ymu->ytu/dot_general | solution.py:287
  89.1 9.6 %all-to-all-done.4 = bf16[32,2,1536]{2,1,0:T(2,128)(2,1)S(1)} async-done(((bf16[32,2,1536]{2,1,0:T(2,128)(2,1)}), bf16[32,2,1536]{2,1,0:T(2,128)(2,1)S(1)}, u32[]{:S(2)}, u32[]{:S(2)}) %all-to-all-start.4) | async-done | bytes 196640 | tf_op jit(solution)/shard_map/all_to_all | solution.py:84
  98.8 1.1 convolution_reduce_fusion
  99.9 0.6 broadcast_in_dim.120
  100.5 4.1 %all-to-all-start.5 = ((f32[32,1,64]{2,1,0:T(1,128)}), f32[32,1,64]{2,1,0:T(1,128)S(1)}, u32[]{:S(2)}, u32[]{:S(2)}) async-start(f32[32,1,64]{2,1,0:T(1,128)} %broadcast_in_dim.120), calls=%async_computation.5 | async-start | bytes 32768 | tf_op jit(solution)/shard_map/all_to_all | solution.py:84
  104.7 0.8 convolution_convert_fusion.3
  105.5 0.8 reshape_reshape.4
  106.3 8.2 %all-to-all-done.5 = f32[32,1,64]{2,1,0:T(1,128)S(1)} async-done(((f32[32,1,64]{2,1,0:T(1,128)}), f32[32,1,64]{2,1,0:T(1,128)S(1)}, u32[]{:S(2)}, u32[]{:S(2)}) %all-to-all-start.5) | async-done | bytes 8224 | tf_op jit(solution)/shard_map/all_to_all | solution.py:84
  114.5 0.5 reduce_max.39
  (77 shorter events, 4.6 us)
Async XLA Ops:
  0.6 98.1 %copy-start = (bf16[1536,1000]{0,1:T(8,128)(2,1)S(1)}, bf16[1536,1000]{0,1:T(8,128)(2,1)}, u32[]{:S(2)}) copy-start(bf16[1536,1000]{0,1:T(8,128)(2,1)} %param.35) | copy-start | bytes 9216004
  0.6 8.3 %copy-start.1 = (bf16[2,64,1536]{2,1,0:T(8,128)(2,1)S(1)}, bf16[2,64,1536]{2,1,0:T(8,128)(2,1)}, u32[]{:S(2)}) copy-start(bf16[2,64,1536]{2,1,0:T(8,128)(2,1)} %param.18) | copy-start | bytes 1179652
  0.7 9.5 %copy-start.14 = (f32[48]{0:T(128)}, f32[48]{0:T(128)S(1)}, u32[]{:S(2)}) copy-start(f32[48]{0:T(128)S(1)} %multiply_power_fusion) | copy-start | bytes 580
  3.1 7.1 %copy-start.10 = (f32[1536]{0:T(1024)}, f32[1536]{0:T(1024)S(1)}, u32[]{:S(2)}) copy-start(f32[1536]{0:T(1024)S(1)} %convert_element_type.213) | copy-start | bytes 18436
  4.3 5.9 %copy-start.15 = (f32[2,64]{1,0:T(2,128)}, f32[2,64]{1,0:T(2,128)S(1)}, u32[]{:S(2)}) copy-start(f32[2,64]{1,0:T(2,128)S(1)} %add_rsqrt_fusion) | copy-start | bytes 1540
  7.2 3.1 %copy-start.9 = (f32[2,64]{1,0:T(2,128)}, f32[2,64]{1,0:T(2,128)S(1)}, u32[]{:S(2)}) copy-start(f32[2,64]{1,0:T(2,128)S(1)} %add_convert_fusion.2) | copy-start | bytes 1540
  7.3 4.4 %copy-start.5 = (bf16[2048,96]{0,1:T(8,128)(2,1)S(1)}, bf16[2048,96]{0,1:T(8,128)(2,1)}, u32[]{:S(2)}) copy-start(bf16[2048,96]{0,1:T(8,128)(2,1)} %param.23) | copy-start | bytes 1179652
  11.6 1.6 %copy-start.6 = (bf16[2,64,48]{2,1,0:T(8,128)(2,1)}, bf16[2,64,48]{2,1,0:T(8,128)(2,1)S(1)}, u32[]{:S(2)}) copy-start(bf16[2,64,48]{2,1,0:T(8,128)(2,1)S(1)} %get-tuple-element.12) | copy-start | bytes 36868
  11.7 1.5 %copy-start.17 = (bf16[2048,96]{0,1:T(8,128)(2,1)S(1)}, bf16[2048,96]{0,1:T(8,128)(2,1)}, u32[]{:S(2)}) copy-start(bf16[2048,96]{0,1:T(8,128)(2,1)} %param.24) | copy-start | bytes 1179652
  12.6 1.2 %copy-start.11 = (f32[1536]{0:T(1024)S(1)}, f32[1536]{0:T(1024)}, u32[]{:S(2)}) copy-start(f32[1536]{0:T(1024)} %copy-done.10) | copy-start | bytes 18436
  12.6 1.2 %copy-start.16 = (f32[2,64]{1,0:T(2,128)S(1)}, f32[2,64]{1,0:T(2,128)}, u32[]{:S(2)}) copy-start(f32[2,64]{1,0:T(2,128)} %copy-done.15) | copy-start | bytes 1540
  12.6 1.2 %copy-start.18 = (bf16[1536,96]{0,1:T(8,128)(2,1)S(1)}, bf16[1536,96]{0,1:T(8,128)(2,1)}, u32[]{:S(2)}) copy-start(bf16[1536,96]{0,1:T(8,128)(2,1)} %param.30) | copy-start | bytes 884740
  13.2 1.8 %copy-start.4 = (bf16[192,1536]{1,0:T(8,128)(2,1)S(1)}, bf16[192,1536]{1,0:T(8,128)(2,1)}, u32[]{:S(2)}) copy-start(bf16[192,1536]{1,0:T(8,128)(2,1)} %param.31) | copy-start | bytes 1769476
  13.7 8.1 %copy-start.13 = (bf16[1536]{0:T(1024)(128)(2,1)S(1)}, bf16[1536]{0:T(1024)(128)(2,1)}, u32[]{:S(2)}) copy-start(bf16[1536]{0:T(1024)(128)(2,1)} %param.26) | copy-start | bytes 9220
  14.1 0.6 copy-start.20
  16.0 20.6 %copy-start.19 = (s32[64]{0:T(128)S(1)}, s32[64]{0:T(128)}, u32[]{:S(2)}) copy-start(s32[64]{0:T(128)} %param.20) | copy-start | bytes 772
  16.1 13.2 %all-to-all-start = ((bf16[8,16,1536]{2,1,0:T(8,128)(2,1)}), bf16[8,16,1536]{2,1,0:T(8,128)(2,1)S(1)}, u32[]{:S(2)}, u32[]{:S(2)}) async-start(bf16[8,16,1536]{2,1,0:T(8,128)(2,1)} %fusion.1), calls=%async_computation | async-start | bytes 786432 | tf_op jit(solution)/shard_map/all_to_all | solution.py:75
  30.3 0.6 copy-start.3
  31.8 12.3 %all-to-all-start.1 = ((bf16[8,16,1536]{2,1,0:T(8,128)(2,1)}), bf16[8,16,1536]{2,1,0:T(8,128)(2,1)S(1)}, u32[]{:S(2)}, u32[]{:S(2)}) async-start(bf16[8,16,1536]{2,1,0:T(8,128)(2,1)} %broadcast_in_dim.117), calls=%async_computation.1 | async-start | bytes 786432 | tf_op jit(solution)/shard_map/all_to_all | solution.py:84
  44.1 0.7 copy-start.2
  44.9 10.8 %copy-start.12 = (s32[2,8]{1,0:T(2,128)S(1)}, s32[2,8]{1,0:T(2,128)}, u32[]{:S(2)}) copy-start(s32[2,8]{1,0:T(2,128)} %param.21) | copy-start | bytes 196
  49.0 12.3 %all-to-all-start.2 = ((bf16[8,16,1536]{2,1,0:T(8,128)(2,1)}), bf16[8,16,1536]{2,1,0:T(8,128)(2,1)S(1)}, u32[]{:S(2)}, u32[]{:S(2)}) async-start(bf16[8,16,1536]{2,1,0:T(8,128)(2,1)} %bitcast.155), calls=%async_computation.2 | async-start | bytes 786432 | tf_op jit(solution)/shard_map/all_to_all | solution.py:75
  65.3 9.1 %all-to-all-start.3 = ((bf16[8,2,3072]{2,1,0:T(2,128)(2,1)}), bf16[8,2,3072]{2,1,0:T(2,128)(2,1)S(1)}, u32[]{:S(2)}, u32[]{:S(2)}) async-start(bf16[8,2,3072]{2,1,0:T(2,128)(2,1)} %reshape.531), calls=%async_computation.3 | async-start | bytes 196608 | tf_op jit(solution)/shard_map/all_to_all | solution.py:265
  76.7 28.0 %copy-start.7 = (bf16[2,64,48]{2,1,0:T(8,128)(2,1)S(1)}, bf16[2,64,48]{2,1,0:T(8,128)(2,1)}, u32[]{:S(2)}) copy-start(bf16[2,64,48]{2,1,0:T(8,128)(2,1)} %copy-done.6) | copy-start | bytes 36868
  76.7 22.0 %all-to-all-start.4 = ((bf16[32,2,1536]{2,1,0:T(2,128)(2,1)}), bf16[32,2,1536]{2,1,0:T(2,128)(2,1)S(1)}, u32[]{:S(2)}, u32[]{:S(2)}) async-start(bf16[32,2,1536]{2,1,0:T(2,128)(2,1)} %broadcast_in_dim.119), calls=%async_computation.4 | async-start | bytes 393216 | tf_op jit(solution)/shard_map/all_to_all | solution.py:84
  98.8 6.7 %copy-start.8 = (bf16[8,3072]{1,0:T(8,128)(2,1)S(1)}, bf16[8,3072]{1,0:T(8,128)(2,1)}, u32[]{:S(2)}) copy-start(bf16[8,3072]{1,0:T(8,128)(2,1)} %get-tuple-element.10) | copy-start | bytes 147460
  100.5 13.9 %all-to-all-start.5 = ((f32[32,1,64]{2,1,0:T(1,128)}), f32[32,1,64]{2,1,0:T(1,128)S(1)}, u32[]{:S(2)}, u32[]{:S(2)}) async-start(f32[32,1,64]{2,1,0:T(1,128)} %broadcast_in_dim.120), calls=%async_computation.5 | async-start | bytes 32768 | tf_op jit(solution)/shard_map/all_to_all | solution.py:84

commit v13 on v12

--- a/solution.py
+++ b/solution.py
@@ -1,3 +1,5 @@
+import functools
+
 import jax
 import jax.numpy as jnp
 from jax import lax
@@ -271,7 +273,10 @@
     )
     layer_part = arrived[:, : chunk_rows * share_width].reshape(token_rows, share_width)
     head_rows = (
-        jnp.sum(arrived[:, chunk_rows * share_width :].astype(jnp.float32), axis=0)
+        functools.reduce(
+            jnp.add,
+            [arrived[source, chunk_rows * share_width :].astype(jnp.float32) for source in range(vocab_shards)],
+        )
         .reshape(path_count, model_width)
         .astype(jnp.bfloat16)
     )
@@ -305,7 +310,9 @@
         axis=1,
     )
     every_max = gather_rows(local_max[None], "req", request_shards)
-    maxima = jnp.max(every_max, axis=0).reshape(request_shards * local_requests, per_shard)
+    maxima = functools.reduce(
+        jnp.maximum, [every_max[source] for source in range(request_shards)]
+    ).reshape(request_shards * local_requests, per_shard)
     return (
         layer_part.reshape(local_requests, draft_length, share_width),
         accepted_keys,

time: 116 us -> 116 us (level)
    unnamed x45 -> x47, local copies, waits for them, and re-layouts: 2.86 us -> 3.5 us
where the time goes in v13:
time: 116 us; the launch traced here: 115 us
  waiting for transfers between devices  38.9 us (34%)
  starting transfers between devices  35 us (30%)
  other arithmetic  15.6 us (13%)
  matrix products  12.3 us (11%)
  local copies, waits for them, and re-layouts  8.05 us (7%)
  Pallas kernels  4.15 us (4%)
    all_to_all x3, waiting for transfers between devices, gather_rows(): lax.all_to_all(copies, axis_name, split_axis=0, concat_axis=0, tiled=True)  24.1 us
    all_to_all x3, starting transfers between devices, gather_rows(): lax.all_to_all(copies, axis_name, split_axis=0, concat_axis=0, tiled=True)  19.8 us
    all_to_all x2, waiting for transfers between devices, scatter_rows(): lax.all_to_all(pieces, axis_name, split_axis=0, concat_axis=0, tiled=True)  11.1 us
    all_to_all x2, starting transfers between devices, scatter_rows(): lax.all_to_all(pieces, axis_name, split_axis=0, concat_axis=0, tiled=True)  10.5 us
    all_to_all x1, starting transfers between devices, per_device(): lax.all_to_all(jnp.concatenate([column_pieces, path_pieces], axis=1), 'vo...  4.72 us
    pallas_call x1, Pallas kernels, feed_forward(): pl.pallas_call(feed_forward_kernel, grid=(units // block,), in_specs=[pl....  4.15 us
    all_to_all x1, waiting for transfers between devices, per_device(): lax.all_to_all(jnp.concatenate([column_pieces, path_pieces], axis=1), 'vo...  3.68 us
    unnamed x47, local copies, waits for them, and re-layouts  3.5 us
  transfers between devices with their start and end apart: 6, of which 6 were waited for; matrix products, arithmetic and copies ran while one was open for 8% of the time, Pallas kernels for 0%

profile of v13, /device:TPU:2, one launch (start us, length us, event | category | flops | bytes accessed | tf_op | source)
XLA Modules:
  0.0 115.1 jit_solution(9141620001075213329)
XLA Ops:
  0.7 0.9 fusion.50
  1.6 0.7 add.321
  2.4 0.7 convert_element_type.330
  3.1 1.2 %multiply_reduce_fusion = f32[2,64]{1,0:T(2,128)S(1)} fusion(bf16[2,64,1536]{2,1,0:T(8,128)(2,1)} %param.18), kind=kLoop, calls=%fused_computation.29 | loop fusion | flops 589696 | bytes 393728 | tf_op jit(solution)/shard_map/reduce_sum | solution.py:124
  4.3 1.0 convolution_minimum_fusion.5
  6.4 0.7 add_convert_fusion.2
  7.3 1.6 %convolution_bitcast_fusion.1 = f32[2,1,2,64,96]{4,3,2,0,1:T(8,128)S(1)} fusion(bf16[1536,2,96,1]{0,2,1,3:T(8,128)(2,1)} %bitcast.252, bf16[2,64,1536]{2,1,0:T(8,128)(2,1)} %param.18, f32[1536]{0:T(1024)S(1)} %convert_element_type.330, f32[2,64]{1,0:T(2,128)S(1)} %add_rsqrt_fusion), kind=kOutput, calls=%fused_computation.9 | convolution fusion | flops 76283904 | bytes 1088000 | tf_op jit(solution)/shard_map/rim,mkgd->rkgid/dot_general | solution.py:151
  8.9 1.3 %convolution_bitcast_fusion.4 = f32[2,1,64,96]{3,2,0,1:T(8,128)S(1)} fusion(bf16[1536,96]{0,1:T(8,128)(2,1)} %param.29, bf16[2,64,1536]{2,1,0:T(8,128)(2,1)S(1)} %copy-done.1, f32[1536]{0:T(1024)S(1)} %convert_element_type.330, f32[2,64]{1,0:T(2,128)S(1)} %add_rsqrt_fusion), kind=kOutput, calls=%fused_computation.16 | convolution fusion | flops 38535168 | bytes 743936 | tf_op jit(solution)/shard_map/rim,mkd->rkid/dot_general | solution.py:159
  10.6 1.0 fusion.33
  11.7 0.6 select_reduce_fusion
  12.7 0.5 convert_reduce_fusion
  14.2 0.6 copy-done.21
  15.0 1.1 fusion.1
  16.1 5.7 %all-to-all-start = ((bf16[8,16,1536]{2,1,0:T(8,128)(2,1)}), bf16[8,16,1536]{2,1,0:T(8,128)(2,1)S(1)}, u32[]{:S(2)}, u32[]{:S(2)}) async-start(bf16[8,16,1536]{2,1,0:T(8,128)(2,1)} %fusion.1), calls=%async_computation | async-start | bytes 786432 | tf_op jit(solution)/shard_map/all_to_all | solution.py:77
  21.8 2.0 %bitcast_convert_fusion = f32[128,1536]{1,0:T(8,128)} fusion(bf16[2,64,1536]{2,1,0:T(8,128)(2,1)} %param.18), kind=kLoop, calls=%fused_computation.188 | loop fusion | flops 196608 | bytes 1179648 | tf_op jit(solution)/shard_map/convert_element_type | solution.py:121
  23.8 5.5 %all-to-all-done = bf16[8,16,1536]{2,1,0:T(8,128)(2,1)S(1)} async-done(((bf16[8,16,1536]{2,1,0:T(8,128)(2,1)}), bf16[8,16,1536]{2,1,0:T(8,128)(2,1)S(1)}, u32[]{:S(2)}, u32[]{:S(2)}) %all-to-all-start) | async-done | bytes 393248 | tf_op jit(solution)/shard_map/all_to_all | solution.py:77
  29.3 1.1 multiply_reduce_fusion.1
  30.4 0.6 copy-done.3
  31.1 0.8 broadcast_in_dim.117
  31.8 4.8 %all-to-all-start.1 = ((bf16[8,16,1536]{2,1,0:T(8,128)(2,1)}), bf16[8,16,1536]{2,1,0:T(8,128)(2,1)S(1)}, u32[]{:S(2)}, u32[]{:S(2)}) async-start(bf16[8,16,1536]{2,1,0:T(8,128)(2,1)} %broadcast_in_dim.117), calls=%async_computation.1 | async-start | bytes 786432 | tf_op jit(solution)/shard_map/all_to_all | solution.py:86
  37.2 0.6 fusion.75
  37.8 6.3 %all-to-all-done.1 = bf16[8,16,1536]{2,1,0:T(8,128)(2,1)S(1)} async-done(((bf16[8,16,1536]{2,1,0:T(8,128)(2,1)}), bf16[8,16,1536]{2,1,0:T(8,128)(2,1)S(1)}, u32[]{:S(2)}, u32[]{:S(2)}) %all-to-all-start.1) | async-done | bytes 393248 | tf_op jit(solution)/shard_map/all_to_all | solution.py:86
  44.1 0.7 copy-done.2
  44.9 4.1 %shard_map.209 = bf16[128,1536]{1,0:T(8,128)(2,1)} custom-call(bf16[128,1536]{1,0:T(8,128)(2,1)} %bitcast.244, bf16[1536,512]{1,0:T(8,128)(2,1)} %gate_ref.1, bf16[1536,512]{1,0:T(8,128)(2,1)} %up_ref.1, bf16[512,1536]{1,0:T(8,128)(2,1)} %down_ref.1), custom_call_target="tpu_custom_call" | custom-call | flops 603979776 | bytes 5505024 | tf_op jit(solution)/shard_map/pallas_call | solution.py:53
  49.0 4.8 %all-to-all-start.2 = ((bf16[8,16,1536]{2,1,0:T(8,128)(2,1)}), bf16[8,16,1536]{2,1,0:T(8,128)(2,1)S(1)}, u32[]{:S(2)}, u32[]{:S(2)}) async-start(bf16[8,16,1536]{2,1,0:T(8,128)(2,1)} %bitcast.245), calls=%async_computation.2 | async-start | bytes 786432 | tf_op jit(solution)/shard_map/all_to_all | solution.py:77
  53.8 1.8 %fusion.51 = pred[16]{0:T(512)(128)(4,1)} fusion(s32[]{:T(128)} %bitcast.1, s32[]{:T(128)} %bitcast, s32[]{:T(128)S(6)} %mul.187), kind=kLoop, calls=%fused_computation.125 | loop fusion | flops 784 | bytes 28 | tf_op jit(solution)/shard_map/lt | solution.py:238
  55.7 5.6 %all-to-all-done.2 = bf16[8,16,1536]{2,1,0:T(8,128)(2,1)S(1)} async-done(((bf16[8,16,1536]{2,1,0:T(8,128)(2,1)}), bf16[8,16,1536]{2,1,0:T(8,128)(2,1)S(1)}, u32[]{:S(2)}, u32[]{:S(2)}) %all-to-all-start.2) | async-done | bytes 393248 | tf_op jit(solution)/shard_map/all_to_all | solution.py:77
  61.3 1.0 fusion.13
  62.6 0.8 convolution_convert_fusion
  63.4 0.5 broadcast.434
  63.9 0.7 reduce.11
  64.6 0.7 reshape.1004
  65.3 4.7 %all-to-all-start.3 = ((bf16[8,2,3072]{2,1,0:T(2,128)(2,1)}), bf16[8,2,3072]{2,1,0:T(2,128)(2,1)S(1)}, u32[]{:S(2)}, u32[]{:S(2)}) async-start(bf16[8,2,3072]{2,1,0:T(2,128)(2,1)} %reshape.1004), calls=%async_computation.3 | async-start | bytes 196608 | tf_op jit(solution)/shard_map/all_to_all | solution.py:267
  70.0 0.7 convert_element_type.389
  70.7 3.7 %all-to-all-done.3 = bf16[8,2,3072]{2,1,0:T(2,128)(2,1)S(1)} async-done(((bf16[8,2,3072]{2,1,0:T(2,128)(2,1)}), bf16[8,2,3072]{2,1,0:T(2,128)(2,1)S(1)}, u32[]{:S(2)}, u32[]{:S(2)}) %all-to-all-start.3) | async-done | bytes 98336 | tf_op jit(solution)/shard_map/all_to_all | solution.py:267
  74.5 0.6 copy-done.4
  75.4 0.5 fusion.69
  76.0 0.8 broadcast_in_dim.119
  76.8 10.8 %all-to-all-start.4 = ((bf16[32,2,1536]{2,1,0:T(2,128)(2,1)}), bf16[32,2,1536]{2,1,0:T(2,128)(2,1)S(1)}, u32[]{:S(2)}, u32[]{:S(2)}) async-start(bf16[32,2,1536]{2,1,0:T(2,128)(2,1)} %broadcast_in_dim.119), calls=%async_computation.4 | async-start | bytes 393216 | tf_op jit(solution)/shard_map/all_to_all | solution.py:86
  87.6 1.5 %convolution_convert_fusion.2 = bf16[2,8,96]{2,1,0:T(8,128)(2,1)} fusion(bf16[2,64,96]{2,1,0:T(8,128)(2,1)} %copy-done.21, s32[2,8]{1,0:T(2,128)S(1)} %copy-done.13), kind=kOutput, calls=%fused_computation.25 | convolution fusion | flops 199168 | bytes 27712 | tf_op jit(solution)/shard_map/ytm,ymu->ytu/dot_general | solution.py:292
  89.2 9.6 %all-to-all-done.4 = bf16[32,2,1536]{2,1,0:T(2,128)(2,1)S(1)} async-done(((bf16[32,2,1536]{2,1,0:T(2,128)(2,1)}), bf16[32,2,1536]{2,1,0:T(2,128)(2,1)S(1)}, u32[]{:S(2)}, u32[]{:S(2)}) %all-to-all-start.4) | async-done | bytes 196640 | tf_op jit(solution)/shard_map/all_to_all | solution.py:86
  98.9 1.1 convolution_reduce_fusion
  100.0 0.6 broadcast_in_dim.120
  100.6 4.1 %all-to-all-start.5 = ((f32[32,1,64]{2,1,0:T(1,128)}), f32[32,1,64]{2,1,0:T(1,128)S(1)}, u32[]{:S(2)}, u32[]{:S(2)}) async-start(f32[32,1,64]{2,1,0:T(1,128)} %broadcast_in_dim.120), calls=%async_computation.5 | async-start | bytes 32768 | tf_op jit(solution)/shard_map/all_to_all | solution.py:86
  104.8 0.8 convolution_convert_fusion.3
  105.6 0.8 reshape_reshape.4
  106.4 8.2 %all-to-all-done.5 = f32[32,1,64]{2,1,0:T(1,128)S(1)} async-done(((f32[32,1,64]{2,1,0:T(1,128)}), f32[32,1,64]{2,1,0:T(1,128)S(1)}, u32[]{:S(2)}, u32[]{:S(2)}) %all-to-all-start.5) | async-done | bytes 8224 | tf_op jit(solution)/shard_map/all_to_all | solution.py:86
  114.6 0.5 fusion.53
  (80 shorter events, 4.7 us)
Async XLA Ops:
  0.6 98.2 %copy-start = (bf16[1536,1000]{0,1:T(8,128)(2,1)S(1)}, bf16[1536,1000]{0,1:T(8,128)(2,1)}, u32[]{:S(2)}) copy-start(bf16[1536,1000]{0,1:T(8,128)(2,1)} %param.35) | copy-start | bytes 9216004
  0.6 8.3 %copy-start.1 = (bf16[2,64,1536]{2,1,0:T(8,128)(2,1)S(1)}, bf16[2,64,1536]{2,1,0:T(8,128)(2,1)}, u32[]{:S(2)}) copy-start(bf16[2,64,1536]{2,1,0:T(8,128)(2,1)} %param.18) | copy-start | bytes 1179652
  0.7 9.5 %copy-start.15 = (f32[48]{0:T(128)}, f32[48]{0:T(128)S(1)}, u32[]{:S(2)}) copy-start(f32[48]{0:T(128)S(1)} %multiply_power_fusion) | copy-start | bytes 580
  3.1 7.1 %copy-start.11 = (f32[1536]{0:T(1024)}, f32[1536]{0:T(1024)S(1)}, u32[]{:S(2)}) copy-start(f32[1536]{0:T(1024)S(1)} %convert_element_type.330) | copy-start | bytes 18436
  4.3 5.9 %copy-start.16 = (f32[2,64]{1,0:T(2,128)}, f32[2,64]{1,0:T(2,128)S(1)}, u32[]{:S(2)}) copy-start(f32[2,64]{1,0:T(2,128)S(1)} %add_rsqrt_fusion) | copy-start | bytes 1540
  7.2 3.1 %copy-start.10 = (f32[2,64]{1,0:T(2,128)}, f32[2,64]{1,0:T(2,128)S(1)}, u32[]{:S(2)}) copy-start(f32[2,64]{1,0:T(2,128)S(1)} %add_convert_fusion.2) | copy-start | bytes 1540
  7.3 4.4 %copy-start.7 = (bf16[2048,96]{0,1:T(8,128)(2,1)S(1)}, bf16[2048,96]{0,1:T(8,128)(2,1)}, u32[]{:S(2)}) copy-start(bf16[2048,96]{0,1:T(8,128)(2,1)} %param.23) | copy-start | bytes 1179652
  11.6 1.6 %copy-start.8 = (bf16[2,64,48]{2,1,0:T(8,128)(2,1)}, bf16[2,64,48]{2,1,0:T(8,128)(2,1)S(1)}, u32[]{:S(2)}) copy-start(bf16[2,64,48]{2,1,0:T(8,128)(2,1)S(1)} %get-tuple-element.10) | copy-start | bytes 36868
  11.7 1.5 %copy-start.18 = (bf16[2048,96]{0,1:T(8,128)(2,1)S(1)}, bf16[2048,96]{0,1:T(8,128)(2,1)}, u32[]{:S(2)}) copy-start(bf16[2048,96]{0,1:T(8,128)(2,1)} %param.24) | copy-start | bytes 1179652
  12.6 1.2 %copy-start.12 = (f32[1536]{0:T(1024)S(1)}, f32[1536]{0:T(1024)}, u32[]{:S(2)}) copy-start(f32[1536]{0:T(1024)} %copy-done.11) | copy-start | bytes 18436
  12.6 1.2 %copy-start.17 = (f32[2,64]{1,0:T(2,128)S(1)}, f32[2,64]{1,0:T(2,128)}, u32[]{:S(2)}) copy-start(f32[2,64]{1,0:T(2,128)} %copy-done.16) | copy-start | bytes 1540
  12.7 1.2 %copy-start.19 = (bf16[1536,96]{0,1:T(8,128)(2,1)S(1)}, bf16[1536,96]{0,1:T(8,128)(2,1)}, u32[]{:S(2)}) copy-start(bf16[1536,96]{0,1:T(8,128)(2,1)} %param.30) | copy-start | bytes 884740
  13.2 1.8 %copy-start.6 = (bf16[192,1536]{1,0:T(8,128)(2,1)S(1)}, bf16[192,1536]{1,0:T(8,128)(2,1)}, u32[]{:S(2)}) copy-start(bf16[192,1536]{1,0:T(8,128)(2,1)} %param.31) | copy-start | bytes 1769476
  13.7 8.1 %copy-start.14 = (bf16[1536]{0:T(1024)(128)(2,1)S(1)}, bf16[1536]{0:T(1024)(128)(2,1)}, u32[]{:S(2)}) copy-start(bf16[1536]{0:T(1024)(128)(2,1)} %param.26) | copy-start | bytes 9220
  14.1 0.6 copy-start.21
  16.1 20.6 %copy-start.20 = (s32[64]{0:T(128)S(1)}, s32[64]{0:T(128)}, u32[]{:S(2)}) copy-start(s32[64]{0:T(128)} %param.20) | copy-start | bytes 772
  16.1 13.2 %all-to-all-start = ((bf16[8,16,1536]{2,1,0:T(8,128)(2,1)}), bf16[8,16,1536]{2,1,0:T(8,128)(2,1)S(1)}, u32[]{:S(2)}, u32[]{:S(2)}) async-start(bf16[8,16,1536]{2,1,0:T(8,128)(2,1)} %fusion.1), calls=%async_computation | async-start | bytes 786432 | tf_op jit(solution)/shard_map/all_to_all | solution.py:77
  30.3 0.6 copy-start.3
  31.8 12.3 %all-to-all-start.1 = ((bf16[8,16,1536]{2,1,0:T(8,128)(2,1)}), bf16[8,16,1536]{2,1,0:T(8,128)(2,1)S(1)}, u32[]{:S(2)}, u32[]{:S(2)}) async-start(bf16[8,16,1536]{2,1,0:T(8,128)(2,1)} %broadcast_in_dim.117), calls=%async_computation.1 | async-start | bytes 786432 | tf_op jit(solution)/shard_map/all_to_all | solution.py:86
  44.1 0.7 copy-start.2
  44.9 10.8 %copy-start.13 = (s32[2,8]{1,0:T(2,128)S(1)}, s32[2,8]{1,0:T(2,128)}, u32[]{:S(2)}) copy-start(s32[2,8]{1,0:T(2,128)} %param.21) | copy-start | bytes 196
  49.0 12.3 %all-to-all-start.2 = ((bf16[8,16,1536]{2,1,0:T(8,128)(2,1)}), bf16[8,16,1536]{2,1,0:T(8,128)(2,1)S(1)}, u32[]{:S(2)}, u32[]{:S(2)}) async-start(bf16[8,16,1536]{2,1,0:T(8,128)(2,1)} %bitcast.245), calls=%async_computation.2 | async-start | bytes 786432 | tf_op jit(solution)/shard_map/all_to_all | solution.py:77
  65.3 9.1 %all-to-all-start.3 = ((bf16[8,2,3072]{2,1,0:T(2,128)(2,1)}), bf16[8,2,3072]{2,1,0:T(2,128)(2,1)S(1)}, u32[]{:S(2)}, u32[]{:S(2)}) async-start(bf16[8,2,3072]{2,1,0:T(2,128)(2,1)} %reshape.1004), calls=%async_computation.3 | async-start | bytes 196608 | tf_op jit(solution)/shard_map/all_to_all | solution.py:267
  74.5 0.6 copy-start.4
  76.8 28.0 %copy-start.9 = (bf16[2,64,48]{2,1,0:T(8,128)(2,1)S(1)}, bf16[2,64,48]{2,1,0:T(8,128)(2,1)}, u32[]{:S(2)}) copy-start(bf16[2,64,48]{2,1,0:T(8,128)(2,1)} %copy-done.8) | copy-start | bytes 36868
  76.8 22.0 %all-to-all-start.4 = ((bf16[32,2,1536]{2,1,0:T(2,128)(2,1)}), bf16[32,2,1536]{2,1,0:T(2,128)(2,1)S(1)}, u32[]{:S(2)}, u32[]{:S(2)}) async-start(bf16[32,2,1536]{2,1,0:T(2,128)(2,1)} %broadcast_in_dim.119), calls=%async_computation.4 | async-start | bytes 393216 | tf_op jit(solution)/shard_map/all_to_all | solution.py:86
  98.9 6.7 %copy-start.5 = (bf16[8,1,6144]{2,0,1:T(8,128)(2,1)S(1)}, bf16[8,1,6144]{2,0,1:T(8,128)(2,1)}, u32[]{:S(2)}) copy-start(bf16[8,1,6144]{2,0,1:T(8,128)(2,1)} %copy-done.4) | copy-start | bytes 294916
  100.6 13.9 %all-to-all-start.5 = ((f32[32,1,64]{2,1,0:T(1,128)}), f32[32,1,64]{2,1,0:T(1,128)S(1)}, u32[]{:S(2)}, u32[]{:S(2)}) async-start(f32[32,1,64]{2,1,0:T(1,128)} %broadcast_in_dim.120), calls=%async_computation.5 | async-start | bytes 32768 | tf_op jit(solution)/shard_map/all_to_all | solution.py:86

commit v14 on v12

--- a/solution.py
+++ b/solution.py
@@ -220,12 +220,14 @@
     residual_chunk = lax.dynamic_slice_in_dim(states, chunk_start, chunk_rows, 0) + scatter_rows(
         attend_part, "vocab", vocab_shards
     )
-    hidden_chunk = (
-        residual_chunk
-        * lax.rsqrt(jnp.mean(residual_chunk * residual_chunk, axis=1, keepdims=True) + eps_norm)
+    hidden_copies = (
+        jnp.broadcast_to(residual_chunk[None], (vocab_shards, chunk_rows, model_width))
+        * lax.rsqrt(jnp.mean(residual_chunk * residual_chunk, axis=1, keepdims=True) + eps_norm)[None]
         * hidden_gain.astype(jnp.float32)
     ).astype(jnp.bfloat16)
-    hidden_in = gather_rows(hidden_chunk, "vocab", vocab_shards)
+    hidden_in = lax.all_to_all(
+        hidden_copies, "vocab", split_axis=0, concat_axis=0, tiled=True
+    ).reshape(token_rows, model_width)
     down_part = feed_forward(hidden_in, gate_weight, up_weight, down_weight)
     feed_chunk = scatter_rows(down_part, "vocab", vocab_shards).astype(jnp.bfloat16)
     local_counts = lax.dynamic_slice_in_dim(

time: 116 us -> 116 us (level)
    all_to_all x3 -> x2, waiting for transfers between devices: 24.2 us -> 17.8 us  [gather_rows(): lax.all_to_all(copies, axis_name, split_axis=0, concat_axis=0, tiled=True)]
    all_to_all x0 -> x1, waiting for transfers between devices: none -> 6.31 us  [per_device(): lax.all_to_all(hidden_copies, 'vocab', split_axis=0, concat_axis=0, tiled...]
    all_to_all x0 -> x1, starting transfers between devices: none -> 4.81 us  [per_device(): lax.all_to_all(hidden_copies, 'vocab', split_axis=0, concat_axis=0, tiled...]
    all_to_all x3 -> x2, starting transfers between devices: 19.8 us -> 15 us  [gather_rows(): lax.all_to_all(copies, axis_name, split_axis=0, concat_axis=0, tiled=True)]
where the time goes in v14:
time: 116 us; the launch traced here: 115 us
  waiting for transfers between devices  38.9 us (34%)
  starting transfers between devices  35.1 us (30%)
  other arithmetic  16.9 us (15%)
  matrix products  12.3 us (11%)
  local copies, waits for them, and re-layouts  6.65 us (6%)
  Pallas kernels  4.14 us (4%)
    all_to_all x2, waiting for transfers between devices, gather_rows(): lax.all_to_all(copies, axis_name, split_axis=0, concat_axis=0, tiled=True)  17.8 us
    all_to_all x2, starting transfers between devices, gather_rows(): lax.all_to_all(copies, axis_name, split_axis=0, concat_axis=0, tiled=True)  15 us
    all_to_all x2, waiting for transfers between devices, scatter_rows(): lax.all_to_all(pieces, axis_name, split_axis=0, concat_axis=0, tiled=True)  11.1 us
    all_to_all x2, starting transfers between devices, scatter_rows(): lax.all_to_all(pieces, axis_name, split_axis=0, concat_axis=0, tiled=True)  10.5 us
    all_to_all x1, waiting for transfers between devices, per_device(): lax.all_to_all(hidden_copies, 'vocab', split_axis=0, concat_axis=0, tiled...  6.31 us
    all_to_all x1, starting transfers between devices, per_device(): lax.all_to_all(hidden_copies, 'vocab', split_axis=0, concat_axis=0, tiled...  4.81 us
    all_to_all x1, starting transfers between devices, per_device(): lax.all_to_all(jnp.concatenate([column_pieces, path_pieces], axis=1), 'vo...  4.72 us
    pallas_call x1, Pallas kernels, feed_forward(): pl.pallas_call(feed_forward_kernel, grid=(units // block,), in_specs=[pl....  4.14 us
  transfers between devices with their start and end apart: 6, of which 6 were waited for; matrix products, arithmetic and copies ran while one was open for 8% of the time, Pallas kernels for 0%

profile of v14, /device:TPU:2, one launch (start us, length us, event | category | flops | bytes accessed | tf_op | source)
XLA Modules:
  0.0 115.0 jit_solution(10638321250967872698)
XLA Ops:
  0.7 0.9 fusion.40
  1.6 0.7 add.233
  2.4 0.7 convert_element_type.213
  3.1 1.2 %multiply_reduce_fusion = f32[2,64]{1,0:T(2,128)S(1)} fusion(bf16[2,64,1536]{2,1,0:T(8,128)(2,1)} %param.18), kind=kLoop, calls=%fused_computation.30 | loop fusion | flops 589696 | bytes 393728 | tf_op jit(solution)/shard_map/reduce_sum | solution.py:122
  4.3 1.0 convolution_minimum_fusion.5
  6.4 0.7 add_convert_fusion.2
  7.3 1.6 %convolution_bitcast_fusion.1 = f32[2,1,2,64,96]{4,3,2,0,1:T(8,128)S(1)} fusion(bf16[1536,2,96,1]{0,2,1,3:T(8,128)(2,1)} %bitcast.163, bf16[2,64,1536]{2,1,0:T(8,128)(2,1)} %param.18, f32[1536]{0:T(1024)S(1)} %convert_element_type.213, f32[2,64]{1,0:T(2,128)S(1)} %add_rsqrt_fusion), kind=kOutput, calls=%fused_computation.9 | convolution fusion | flops 76283904 | bytes 1088000 | tf_op jit(solution)/shard_map/rim,mkgd->rkgid/dot_general | solution.py:149
  8.9 1.3 %convolution_bitcast_fusion.4 = f32[2,1,64,96]{3,2,0,1:T(8,128)S(1)} fusion(bf16[1536,96]{0,1:T(8,128)(2,1)} %param.29, bf16[2,64,1536]{2,1,0:T(8,128)(2,1)S(1)} %copy-done.1, f32[1536]{0:T(1024)S(1)} %convert_element_type.213, f32[2,64]{1,0:T(2,128)S(1)} %add_rsqrt_fusion), kind=kOutput, calls=%fused_computation.16 | convolution fusion | flops 38535168 | bytes 743936 | tf_op jit(solution)/shard_map/rim,mkd->rkid/dot_general | solution.py:157
  10.6 1.0 fusion.33
  11.7 0.6 select_reduce_fusion
  12.7 0.5 convert_reduce_fusion
  14.2 0.6 copy-done.20
  15.0 1.1 fusion.1
  16.1 5.7 %all-to-all-start = ((bf16[8,16,1536]{2,1,0:T(8,128)(2,1)}), bf16[8,16,1536]{2,1,0:T(8,128)(2,1)S(1)}, u32[]{:S(2)}, u32[]{:S(2)}) async-start(bf16[8,16,1536]{2,1,0:T(8,128)(2,1)} %fusion.1), calls=%async_computation | async-start | bytes 786432 | tf_op jit(solution)/shard_map/all_to_all | solution.py:75
  21.8 2.0 %bitcast_convert_fusion = f32[128,1536]{1,0:T(8,128)} fusion(bf16[2,64,1536]{2,1,0:T(8,128)(2,1)} %param.18), kind=kLoop, calls=%fused_computation.124 | loop fusion | flops 196608 | bytes 1179648 | tf_op jit(solution)/shard_map/convert_element_type | solution.py:119
  23.8 5.5 %all-to-all-done = bf16[8,16,1536]{2,1,0:T(8,128)(2,1)S(1)} async-done(((bf16[8,16,1536]{2,1,0:T(8,128)(2,1)}), bf16[8,16,1536]{2,1,0:T(8,128)(2,1)S(1)}, u32[]{:S(2)}, u32[]{:S(2)}) %all-to-all-start) | async-done | bytes 393248 | tf_op jit(solution)/shard_map/all_to_all | solution.py:75
  29.3 1.1 multiply_reduce_fusion.1
  30.4 0.6 copy-done.3
  31.0 0.8 multiply_convert_fusion
  31.8 4.8 %all-to-all-start.1 = ((bf16[8,16,1536]{2,1,0:T(8,128)(2,1)}), bf16[8,16,1536]{2,1,0:T(8,128)(2,1)S(1)}, u32[]{:S(2)}, u32[]{:S(2)}) async-start(bf16[8,16,1536]{2,1,0:T(8,128)(2,1)} %multiply_convert_fusion), calls=%async_computation.1 | async-start | bytes 786432 | tf_op jit(solution)/shard_map/all_to_all | solution.py:228
  37.2 0.6 fusion.49
  37.8 6.3 %all-to-all-done.1 = bf16[8,16,1536]{2,1,0:T(8,128)(2,1)S(1)} async-done(((bf16[8,16,1536]{2,1,0:T(8,128)(2,1)}), bf16[8,16,1536]{2,1,0:T(8,128)(2,1)S(1)}, u32[]{:S(2)}, u32[]{:S(2)}) %all-to-all-start.1) | async-done | bytes 393248 | tf_op jit(solution)/shard_map/all_to_all | solution.py:228
  44.1 0.7 copy-done.2
  44.9 4.1 %shard_map.209 = bf16[128,1536]{1,0:T(8,128)(2,1)} custom-call(bf16[128,1536]{1,0:T(8,128)(2,1)} %bitcast.154, bf16[1536,512]{1,0:T(8,128)(2,1)} %gate_ref.1, bf16[1536,512]{1,0:T(8,128)(2,1)} %up_ref.1, bf16[512,1536]{1,0:T(8,128)(2,1)} %down_ref.1), custom_call_target="tpu_custom_call" | custom-call | flops 603979776 | bytes 5505024 | tf_op jit(solution)/shard_map/pallas_call | solution.py:51
  49.0 4.8 %all-to-all-start.2 = ((bf16[8,16,1536]{2,1,0:T(8,128)(2,1)}), bf16[8,16,1536]{2,1,0:T(8,128)(2,1)S(1)}, u32[]{:S(2)}, u32[]{:S(2)}) async-start(bf16[8,16,1536]{2,1,0:T(8,128)(2,1)} %bitcast.155), calls=%async_computation.2 | async-start | bytes 786432 | tf_op jit(solution)/shard_map/all_to_all | solution.py:75
  53.8 1.8 %fusion.41 = pred[16]{0:T(512)(128)(4,1)} fusion(s32[]{:T(128)} %bitcast.1, s32[]{:T(128)} %bitcast, s32[]{:T(128)S(6)} %mul.183), kind=kLoop, calls=%fused_computation.108 | loop fusion | flops 784 | bytes 28 | tf_op jit(solution)/shard_map/lt | solution.py:238
  55.7 5.6 %all-to-all-done.2 = bf16[8,16,1536]{2,1,0:T(8,128)(2,1)S(1)} async-done(((bf16[8,16,1536]{2,1,0:T(8,128)(2,1)}), bf16[8,16,1536]{2,1,0:T(8,128)(2,1)S(1)}, u32[]{:S(2)}, u32[]{:S(2)}) %all-to-all-start.2) | async-done | bytes 393248 | tf_op jit(solution)/shard_map/all_to_all | solution.py:75
  61.3 1.0 fusion.13
  62.5 0.8 convolution_convert_fusion
  63.4 0.5 broadcast.433
  63.9 0.7 reduce.9
  64.6 0.7 reshape.532
  65.3 4.7 %all-to-all-start.3 = ((bf16[8,2,3072]{2,1,0:T(2,128)(2,1)}), bf16[8,2,3072]{2,1,0:T(2,128)(2,1)S(1)}, u32[]{:S(2)}, u32[]{:S(2)}) async-start(bf16[8,2,3072]{2,1,0:T(2,128)(2,1)} %reshape.532), calls=%async_computation.3 | async-start | bytes 196608 | tf_op jit(solution)/shard_map/all_to_all | solution.py:267
  70.0 0.7 convert_element_type.260
  70.7 3.7 %all-to-all-done.3 = bf16[8,2,3072]{2,1,0:T(2,128)(2,1)S(1)} async-done(((bf16[8,2,3072]{2,1,0:T(2,128)(2,1)}), bf16[8,2,3072]{2,1,0:T(2,128)(2,1)S(1)}, u32[]{:S(2)}, u32[]{:S(2)}) %all-to-all-start.3) | async-done | bytes 98336 | tf_op jit(solution)/shard_map/all_to_all | solution.py:267
  74.5 0.6 slice_reduce_fusion
  75.3 0.5 fusion.43
  75.9 0.8 broadcast_in_dim.120
  76.7 10.8 %all-to-all-start.4 = ((bf16[32,2,1536]{2,1,0:T(2,128)(2,1)}), bf16[32,2,1536]{2,1,0:T(2,128)(2,1)S(1)}, u32[]{:S(2)}, u32[]{:S(2)}) async-start(bf16[32,2,1536]{2,1,0:T(2,128)(2,1)} %broadcast_in_dim.120), calls=%async_computation.4 | async-start | bytes 393216 | tf_op jit(solution)/shard_map/all_to_all | solution.py:84
  87.5 1.5 %convolution_convert_fusion.2 = bf16[2,8,96]{2,1,0:T(8,128)(2,1)} fusion(bf16[2,64,96]{2,1,0:T(8,128)(2,1)} %copy-done.20, s32[2,8]{1,0:T(2,128)S(1)} %copy-done.12), kind=kOutput, calls=%fused_computation.25 | convolution fusion | flops 199168 | bytes 27712 | tf_op jit(solution)/shard_map/ytm,ymu->ytu/dot_general | solution.py:289
  89.1 9.6 %all-to-all-done.4 = bf16[32,2,1536]{2,1,0:T(2,128)(2,1)S(1)} async-done(((bf16[32,2,1536]{2,1,0:T(2,128)(2,1)}), bf16[32,2,1536]{2,1,0:T(2,128)(2,1)S(1)}, u32[]{:S(2)}, u32[]{:S(2)}) %all-to-all-start.4) | async-done | bytes 196640 | tf_op jit(solution)/shard_map/all_to_all | solution.py:84
  98.8 1.1 convolution_reduce_fusion
  99.9 0.6 broadcast_in_dim.121
  100.5 4.1 %all-to-all-start.5 = ((f32[32,1,64]{2,1,0:T(1,128)}), f32[32,1,64]{2,1,0:T(1,128)S(1)}, u32[]{:S(2)}, u32[]{:S(2)}) async-start(f32[32,1,64]{2,1,0:T(1,128)} %broadcast_in_dim.121), calls=%async_computation.5 | async-start | bytes 32768 | tf_op jit(solution)/shard_map/all_to_all | solution.py:84
  104.7 0.8 convolution_convert_fusion.3
  105.5 0.8 reshape_reshape.4
  106.3 8.2 %all-to-all-done.5 = f32[32,1,64]{2,1,0:T(1,128)S(1)} async-done(((f32[32,1,64]{2,1,0:T(1,128)}), f32[32,1,64]{2,1,0:T(1,128)S(1)}, u32[]{:S(2)}, u32[]{:S(2)}) %all-to-all-start.5) | async-done | bytes 8224 | tf_op jit(solution)/shard_map/all_to_all | solution.py:84
  114.5 0.5 reduce_max.39
  (76 shorter events, 4.5 us)
Async XLA Ops:
  0.6 98.1 %copy-start = (bf16[1536,1000]{0,1:T(8,128)(2,1)S(1)}, bf16[1536,1000]{0,1:T(8,128)(2,1)}, u32[]{:S(2)}) copy-start(bf16[1536,1000]{0,1:T(8,128)(2,1)} %param.35) | copy-start | bytes 9216004
  0.6 8.3 %copy-start.1 = (bf16[2,64,1536]{2,1,0:T(8,128)(2,1)S(1)}, bf16[2,64,1536]{2,1,0:T(8,128)(2,1)}, u32[]{:S(2)}) copy-start(bf16[2,64,1536]{2,1,0:T(8,128)(2,1)} %param.18) | copy-start | bytes 1179652
  0.7 9.5 %copy-start.14 = (f32[48]{0:T(128)}, f32[48]{0:T(128)S(1)}, u32[]{:S(2)}) copy-start(f32[48]{0:T(128)S(1)} %multiply_power_fusion) | copy-start | bytes 580
  3.1 7.1 %copy-start.10 = (f32[1536]{0:T(1024)}, f32[1536]{0:T(1024)S(1)}, u32[]{:S(2)}) copy-start(f32[1536]{0:T(1024)S(1)} %convert_element_type.213) | copy-start | bytes 18436
  4.3 5.9 %copy-start.15 = (f32[2,64]{1,0:T(2,128)}, f32[2,64]{1,0:T(2,128)S(1)}, u32[]{:S(2)}) copy-start(f32[2,64]{1,0:T(2,128)S(1)} %add_rsqrt_fusion) | copy-start | bytes 1540
  7.2 3.1 %copy-start.9 = (f32[2,64]{1,0:T(2,128)}, f32[2,64]{1,0:T(2,128)S(1)}, u32[]{:S(2)}) copy-start(f32[2,64]{1,0:T(2,128)S(1)} %add_convert_fusion.2) | copy-start | bytes 1540
  7.3 4.4 %copy-start.5 = (bf16[2048,96]{0,1:T(8,128)(2,1)S(1)}, bf16[2048,96]{0,1:T(8,128)(2,1)}, u32[]{:S(2)}) copy-start(bf16[2048,96]{0,1:T(8,128)(2,1)} %param.23) | copy-start | bytes 1179652
  11.6 1.6 %copy-start.6 = (bf16[2,64,48]{2,1,0:T(8,128)(2,1)}, bf16[2,64,48]{2,1,0:T(8,128)(2,1)S(1)}, u32[]{:S(2)}) copy-start(bf16[2,64,48]{2,1,0:T(8,128)(2,1)S(1)} %get-tuple-element.12) | copy-start | bytes 36868
  11.7 1.5 %copy-start.17 = (bf16[2048,96]{0,1:T(8,128)(2,1)S(1)}, bf16[2048,96]{0,1:T(8,128)(2,1)}, u32[]{:S(2)}) copy-start(bf16[2048,96]{0,1:T(8,128)(2,1)} %param.24) | copy-start | bytes 1179652
  12.6 1.2 %copy-start.11 = (f32[1536]{0:T(1024)S(1)}, f32[1536]{0:T(1024)}, u32[]{:S(2)}) copy-start(f32[1536]{0:T(1024)} %copy-done.10) | copy-start | bytes 18436
  12.6 1.2 %copy-start.16 = (f32[2,64]{1,0:T(2,128)S(1)}, f32[2,64]{1,0:T(2,128)}, u32[]{:S(2)}) copy-start(f32[2,64]{1,0:T(2,128)} %copy-done.15) | copy-start | bytes 1540
  12.6 1.2 %copy-start.18 = (bf16[1536,96]{0,1:T(8,128)(2,1)S(1)}, bf16[1536,96]{0,1:T(8,128)(2,1)}, u32[]{:S(2)}) copy-start(bf16[1536,96]{0,1:T(8,128)(2,1)} %param.30) | copy-start | bytes 884740
  13.2 1.8 %copy-start.4 = (bf16[192,1536]{1,0:T(8,128)(2,1)S(1)}, bf16[192,1536]{1,0:T(8,128)(2,1)}, u32[]{:S(2)}) copy-start(bf16[192,1536]{1,0:T(8,128)(2,1)} %param.31) | copy-start | bytes 1769476
  13.7 8.1 %copy-start.13 = (bf16[1536]{0:T(1024)(128)(2,1)S(1)}, bf16[1536]{0:T(1024)(128)(2,1)}, u32[]{:S(2)}) copy-start(bf16[1536]{0:T(1024)(128)(2,1)} %param.26) | copy-start | bytes 9220
  14.1 0.6 copy-start.20
  16.0 20.6 %copy-start.19 = (s32[64]{0:T(128)S(1)}, s32[64]{0:T(128)}, u32[]{:S(2)}) copy-start(s32[64]{0:T(128)} %param.20) | copy-start | bytes 772
  16.1 13.2 %all-to-all-start = ((bf16[8,16,1536]{2,1,0:T(8,128)(2,1)}), bf16[8,16,1536]{2,1,0:T(8,128)(2,1)S(1)}, u32[]{:S(2)}, u32[]{:S(2)}) async-start(bf16[8,16,1536]{2,1,0:T(8,128)(2,1)} %fusion.1), calls=%async_computation | async-start | bytes 786432 | tf_op jit(solution)/shard_map/all_to_all | solution.py:75
  30.3 0.6 copy-start.3
  31.8 12.3 %all-to-all-start.1 = ((bf16[8,16,1536]{2,1,0:T(8,128)(2,1)}), bf16[8,16,1536]{2,1,0:T(8,128)(2,1)S(1)}, u32[]{:S(2)}, u32[]{:S(2)}) async-start(bf16[8,16,1536]{2,1,0:T(8,128)(2,1)} %multiply_convert_fusion), calls=%async_computation.1 | async-start | bytes 786432 | tf_op jit(solution)/shard_map/all_to_all | solution.py:228
  44.1 0.7 copy-start.2
  44.9 10.8 %copy-start.12 = (s32[2,8]{1,0:T(2,128)S(1)}, s32[2,8]{1,0:T(2,128)}, u32[]{:S(2)}) copy-start(s32[2,8]{1,0:T(2,128)} %param.21) | copy-start | bytes 196
  49.0 12.3 %all-to-all-start.2 = ((bf16[8,16,1536]{2,1,0:T(8,128)(2,1)}), bf16[8,16,1536]{2,1,0:T(8,128)(2,1)S(1)}, u32[]{:S(2)}, u32[]{:S(2)}) async-start(bf16[8,16,1536]{2,1,0:T(8,128)(2,1)} %bitcast.155), calls=%async_computation.2 | async-start | bytes 786432 | tf_op jit(solution)/shard_map/all_to_all | solution.py:75
  65.3 9.1 %all-to-all-start.3 = ((bf16[8,2,3072]{2,1,0:T(2,128)(2,1)}), bf16[8,2,3072]{2,1,0:T(2,128)(2,1)S(1)}, u32[]{:S(2)}, u32[]{:S(2)}) async-start(bf16[8,2,3072]{2,1,0:T(2,128)(2,1)} %reshape.532), calls=%async_computation.3 | async-start | bytes 196608 | tf_op jit(solution)/shard_map/all_to_all | solution.py:267
  76.7 28.0 %copy-start.7 = (bf16[2,64,48]{2,1,0:T(8,128)(2,1)S(1)}, bf16[2,64,48]{2,1,0:T(8,128)(2,1)}, u32[]{:S(2)}) copy-start(bf16[2,64,48]{2,1,0:T(8,128)(2,1)} %copy-done.6) | copy-start | bytes 36868
  76.7 22.0 %all-to-all-start.4 = ((bf16[32,2,1536]{2,1,0:T(2,128)(2,1)}), bf16[32,2,1536]{2,1,0:T(2,128)(2,1)S(1)}, u32[]{:S(2)}, u32[]{:S(2)}) async-start(bf16[32,2,1536]{2,1,0:T(2,128)(2,1)} %broadcast_in_dim.120), calls=%async_computation.4 | async-start | bytes 393216 | tf_op jit(solution)/shard_map/all_to_all | solution.py:84
  98.8 6.7 %copy-start.8 = (bf16[8,3072]{1,0:T(8,128)(2,1)S(1)}, bf16[8,3072]{1,0:T(8,128)(2,1)}, u32[]{:S(2)}) copy-start(bf16[8,3072]{1,0:T(8,128)(2,1)} %get-tuple-element.10) | copy-start | bytes 147460
  100.5 13.9 %all-to-all-start.5 = ((f32[32,1,64]{2,1,0:T(1,128)}), f32[32,1,64]{2,1,0:T(1,128)S(1)}, u32[]{:S(2)}, u32[]{:S(2)}) async-start(f32[32,1,64]{2,1,0:T(1,128)} %broadcast_in_dim.121), calls=%async_computation.5 | async-start | bytes 32768 | tf_op jit(solution)/shard_map/all_to_all | solution.py:84

commit v15 on v14

--- a/solution.py
+++ b/solution.py
@@ -295,15 +295,16 @@
     flat_rows = head_rows.astype(jnp.float32)
     mean_square = jnp.mean(flat_rows * flat_rows, axis=1)
     norm_values = jnp.sqrt(mean_square + eps_norm).reshape(local_requests, per_shard)
-    head_in = (
-        flat_rows * lax.rsqrt(mean_square + eps_norm)[:, None] * final_gain.astype(jnp.float32)
-    ).astype(jnp.bfloat16)
+    head_copies = (
+        jnp.broadcast_to(flat_rows[None], (request_shards, *flat_rows.shape))
+        * lax.rsqrt(mean_square + eps_norm)[None, :, None]
+        * final_gain.astype(jnp.float32)
+    ).astype(jnp.bfloat16)
+    gathered_head = lax.all_to_all(
+        head_copies, "req", split_axis=0, concat_axis=0, tiled=True
+    ).reshape(request_shards * flat_rows.shape[0], model_width)
     local_max = jnp.max(
-        jnp.dot(
-            gather_rows(head_in, "req", request_shards),
-            head_weight,
-            preferred_element_type=jnp.float32,
-        ),
+        jnp.dot(gathered_head, head_weight, preferred_element_type=jnp.float32),
         axis=1,
     )
     every_max = gather_rows(local_max[None], "req", request_shards)

time: 116 us -> 116 us (level)
    all_to_all x0 -> x1, starting transfers between devices: none -> 10.8 us  [per_device(): lax.all_to_all(head_copies, 'req', split_axis=0, concat_axis=0, tiled=True)]
    all_to_all x2 -> x1, starting transfers between devices: 15 us -> 4.14 us  [gather_rows(): lax.all_to_all(copies, axis_name, split_axis=0, concat_axis=0, tiled=True)]
    all_to_all x2 -> x1, waiting for transfers between devices: 17.8 us -> 8.22 us  [gather_rows(): lax.all_to_all(copies, axis_name, split_axis=0, concat_axis=0, tiled=True)]
    all_to_all x0 -> x1, waiting for transfers between devices: none -> 9.62 us  [per_device(): lax.all_to_all(head_copies, 'req', split_axis=0, concat_axis=0, tiled=True)]
where the time goes in v15:
time: 116 us; the launch traced here: 115 us
  waiting for transfers between devices  38.9 us (34%)
  starting transfers between devices  35.1 us (30%)
  other arithmetic  17.7 us (15%)
  matrix products  12.3 us (11%)
  local copies, waits for them, and re-layouts  5.87 us (5%)
  Pallas kernels  4.14 us (4%)
    all_to_all x2, waiting for transfers between devices, scatter_rows(): lax.all_to_all(pieces, axis_name, split_axis=0, concat_axis=0, tiled=True)  11.1 us
    all_to_all x1, starting transfers between devices, per_device(): lax.all_to_all(head_copies, 'req', split_axis=0, concat_axis=0, tiled=True)  10.8 us
    all_to_all x2, starting transfers between devices, scatter_rows(): lax.all_to_all(pieces, axis_name, split_axis=0, concat_axis=0, tiled=True)  10.5 us
    all_to_all x1, waiting for transfers between devices, per_device(): lax.all_to_all(head_copies, 'req', split_axis=0, concat_axis=0, tiled=True)  9.62 us
    all_to_all x1, waiting for transfers between devices, gather_rows(): lax.all_to_all(copies, axis_name, split_axis=0, concat_axis=0, tiled=True)  8.22 us
    all_to_all x1, waiting for transfers between devices, per_device(): lax.all_to_all(hidden_copies, 'vocab', split_axis=0, concat_axis=0, tiled...  6.31 us
    all_to_all x1, starting transfers between devices, per_device(): lax.all_to_all(hidden_copies, 'vocab', split_axis=0, concat_axis=0, tiled...  4.81 us
    all_to_all x1, starting transfers between devices, per_device(): lax.all_to_all(jnp.concatenate([column_pieces, path_pieces], axis=1), 'vo...  4.72 us
  transfers between devices with their start and end apart: 6, of which 6 were waited for; matrix products, arithmetic and copies ran while one was open for 8% of the time, Pallas kernels for 0%

profile of v15, /device:TPU:2, one launch (start us, length us, event | category | flops | bytes accessed | tf_op | source)
XLA Modules:
  0.0 115.0 jit_solution(2293236318383442087)
XLA Ops:
  0.7 0.9 fusion.40
  1.6 0.7 add.234
  2.4 0.7 convert_element_type.209
  3.1 1.2 %multiply_reduce_fusion = f32[2,64]{1,0:T(2,128)S(1)} fusion(bf16[2,64,1536]{2,1,0:T(8,128)(2,1)} %param.18), kind=kLoop, calls=%fused_computation.30 | loop fusion | flops 589696 | bytes 393728 | tf_op jit(solution)/shard_map/reduce_sum | solution.py:122
  4.3 1.0 convolution_minimum_fusion.5
  6.4 0.7 add_convert_fusion.2
  7.3 1.6 %convolution_bitcast_fusion.1 = f32[2,1,2,64,96]{4,3,2,0,1:T(8,128)S(1)} fusion(bf16[1536,2,96,1]{0,2,1,3:T(8,128)(2,1)} %bitcast.163, bf16[2,64,1536]{2,1,0:T(8,128)(2,1)} %param.18, f32[1536]{0:T(1024)S(1)} %convert_element_type.209, f32[2,64]{1,0:T(2,128)S(1)} %add_rsqrt_fusion), kind=kOutput, calls=%fused_computation.9 | convolution fusion | flops 76283904 | bytes 1088000 | tf_op jit(solution)/shard_map/rim,mkgd->rkgid/dot_general | solution.py:149
  8.9 1.3 %convolution_bitcast_fusion.4 = f32[2,1,64,96]{3,2,0,1:T(8,128)S(1)} fusion(bf16[1536,96]{0,1:T(8,128)(2,1)} %param.29, bf16[2,64,1536]{2,1,0:T(8,128)(2,1)S(1)} %copy-done.1, f32[1536]{0:T(1024)S(1)} %convert_element_type.209, f32[2,64]{1,0:T(2,128)S(1)} %add_rsqrt_fusion), kind=kOutput, calls=%fused_computation.16 | convolution fusion | flops 38535168 | bytes 743936 | tf_op jit(solution)/shard_map/rim,mkd->rkid/dot_general | solution.py:157
  10.6 1.0 fusion.33
  11.7 0.6 select_reduce_fusion
  12.7 0.5 convert_reduce_fusion
  14.2 0.6 copy-done.20
  15.0 1.1 fusion.1
  16.1 5.7 %all-to-all-start = ((bf16[8,16,1536]{2,1,0:T(8,128)(2,1)}), bf16[8,16,1536]{2,1,0:T(8,128)(2,1)S(1)}, u32[]{:S(2)}, u32[]{:S(2)}) async-start(bf16[8,16,1536]{2,1,0:T(8,128)(2,1)} %fusion.1), calls=%async_computation | async-start | bytes 786432 | tf_op jit(solution)/shard_map/all_to_all | solution.py:75
  21.8 2.0 %bitcast_convert_fusion = f32[128,1536]{1,0:T(8,128)} fusion(bf16[2,64,1536]{2,1,0:T(8,128)(2,1)} %param.18), kind=kLoop, calls=%fused_computation.124 | loop fusion | flops 196608 | bytes 1179648 | tf_op jit(solution)/shard_map/convert_element_type | solution.py:119
  23.8 5.5 %all-to-all-done = bf16[8,16,1536]{2,1,0:T(8,128)(2,1)S(1)} async-done(((bf16[8,16,1536]{2,1,0:T(8,128)(2,1)}), bf16[8,16,1536]{2,1,0:T(8,128)(2,1)S(1)}, u32[]{:S(2)}, u32[]{:S(2)}) %all-to-all-start) | async-done | bytes 393248 | tf_op jit(solution)/shard_map/all_to_all | solution.py:75
  29.3 1.1 multiply_reduce_fusion.1
  30.4 0.6 copy-done.3
  31.0 0.8 multiply_convert_fusion
  31.8 4.8 %all-to-all-start.1 = ((bf16[8,16,1536]{2,1,0:T(8,128)(2,1)}), bf16[8,16,1536]{2,1,0:T(8,128)(2,1)S(1)}, u32[]{:S(2)}, u32[]{:S(2)}) async-start(bf16[8,16,1536]{2,1,0:T(8,128)(2,1)} %multiply_convert_fusion), calls=%async_computation.1 | async-start | bytes 786432 | tf_op jit(solution)/shard_map/all_to_all | solution.py:228
  37.2 0.6 fusion.49
  37.8 6.3 %all-to-all-done.1 = bf16[8,16,1536]{2,1,0:T(8,128)(2,1)S(1)} async-done(((bf16[8,16,1536]{2,1,0:T(8,128)(2,1)}), bf16[8,16,1536]{2,1,0:T(8,128)(2,1)S(1)}, u32[]{:S(2)}, u32[]{:S(2)}) %all-to-all-start.1) | async-done | bytes 393248 | tf_op jit(solution)/shard_map/all_to_all | solution.py:228
  44.1 0.7 copy-done.2
  44.9 4.1 %shard_map.209 = bf16[128,1536]{1,0:T(8,128)(2,1)} custom-call(bf16[128,1536]{1,0:T(8,128)(2,1)} %bitcast.154, bf16[1536,512]{1,0:T(8,128)(2,1)} %gate_ref.1, bf16[1536,512]{1,0:T(8,128)(2,1)} %up_ref.1, bf16[512,1536]{1,0:T(8,128)(2,1)} %down_ref.1), custom_call_target="tpu_custom_call" | custom-call | flops 603979776 | bytes 5505024 | tf_op jit(solution)/shard_map/pallas_call | solution.py:51
  49.0 4.8 %all-to-all-start.2 = ((bf16[8,16,1536]{2,1,0:T(8,128)(2,1)}), bf16[8,16,1536]{2,1,0:T(8,128)(2,1)S(1)}, u32[]{:S(2)}, u32[]{:S(2)}) async-start(bf16[8,16,1536]{2,1,0:T(8,128)(2,1)} %bitcast.155), calls=%async_computation.2 | async-start | bytes 786432 | tf_op jit(solution)/shard_map/all_to_all | solution.py:75
  53.8 1.8 %fusion.41 = pred[16]{0:T(512)(128)(4,1)} fusion(s32[]{:T(128)} %bitcast.1, s32[]{:T(128)} %bitcast, s32[]{:T(128)S(6)} %mul.175), kind=kLoop, calls=%fused_computation.108 | loop fusion | flops 784 | bytes 28 | tf_op jit(solution)/shard_map/lt | solution.py:238
  55.7 5.6 %all-to-all-done.2 = bf16[8,16,1536]{2,1,0:T(8,128)(2,1)S(1)} async-done(((bf16[8,16,1536]{2,1,0:T(8,128)(2,1)}), bf16[8,16,1536]{2,1,0:T(8,128)(2,1)S(1)}, u32[]{:S(2)}, u32[]{:S(2)}) %all-to-all-start.2) | async-done | bytes 393248 | tf_op jit(solution)/shard_map/all_to_all | solution.py:75
  61.3 1.0 fusion.13
  62.5 0.8 convolution_convert_fusion
  63.4 0.5 broadcast.417
  63.9 0.7 reduce.9
  64.6 0.7 reshape.505
  65.3 4.7 %all-to-all-start.3 = ((bf16[8,2,3072]{2,1,0:T(2,128)(2,1)}), bf16[8,2,3072]{2,1,0:T(2,128)(2,1)S(1)}, u32[]{:S(2)}, u32[]{:S(2)}) async-start(bf16[8,2,3072]{2,1,0:T(2,128)(2,1)} %reshape.505), calls=%async_computation.3 | async-start | bytes 196608 | tf_op jit(solution)/shard_map/all_to_all | solution.py:267
  70.0 0.7 convert_element_type.256
  70.7 3.7 %all-to-all-done.3 = bf16[8,2,3072]{2,1,0:T(2,128)(2,1)S(1)} async-done(((bf16[8,2,3072]{2,1,0:T(2,128)(2,1)}), bf16[8,2,3072]{2,1,0:T(2,128)(2,1)S(1)}, u32[]{:S(2)}, u32[]{:S(2)}) %all-to-all-start.3) | async-done | bytes 98336 | tf_op jit(solution)/shard_map/all_to_all | solution.py:267
  74.5 0.6 slice_reduce_fusion
  75.3 0.5 fusion.43
  75.8 0.8 multiply_convert_fusion.2
  76.7 10.8 %all-to-all-start.4 = ((bf16[32,2,1536]{2,1,0:T(2,128)(2,1)}), bf16[32,2,1536]{2,1,0:T(2,128)(2,1)S(1)}, u32[]{:S(2)}, u32[]{:S(2)}) async-start(bf16[32,2,1536]{2,1,0:T(2,128)(2,1)} %multiply_convert_fusion.2), calls=%async_computation.4 | async-start | bytes 393216 | tf_op jit(solution)/shard_map/all_to_all | solution.py:303
  87.5 1.5 %convolution_convert_fusion.2 = bf16[2,8,96]{2,1,0:T(8,128)(2,1)} fusion(bf16[2,64,96]{2,1,0:T(8,128)(2,1)} %copy-done.20, s32[2,8]{1,0:T(2,128)S(1)} %copy-done.12), kind=kOutput, calls=%fused_computation.25 | convolution fusion | flops 199168 | bytes 27712 | tf_op jit(solution)/shard_map/ytm,ymu->ytu/dot_general | solution.py:289
  89.1 9.6 %all-to-all-done.4 = bf16[32,2,1536]{2,1,0:T(2,128)(2,1)S(1)} async-done(((bf16[32,2,1536]{2,1,0:T(2,128)(2,1)}), bf16[32,2,1536]{2,1,0:T(2,128)(2,1)S(1)}, u32[]{:S(2)}, u32[]{:S(2)}) %all-to-all-start.4) | async-done | bytes 196640 | tf_op jit(solution)/shard_map/all_to_all | solution.py:303
  98.8 1.1 convolution_reduce_fusion
  99.9 0.6 broadcast_in_dim.121
  100.5 4.1 %all-to-all-start.5 = ((f32[32,1,64]{2,1,0:T(1,128)}), f32[32,1,64]{2,1,0:T(1,128)S(1)}, u32[]{:S(2)}, u32[]{:S(2)}) async-start(f32[32,1,64]{2,1,0:T(1,128)} %broadcast_in_dim.121), calls=%async_computation.5 | async-start | bytes 32768 | tf_op jit(solution)/shard_map/all_to_all | solution.py:84
  104.7 0.8 convolution_convert_fusion.3
  105.5 0.8 reshape_reshape.4
  106.2 8.2 %all-to-all-done.5 = f32[32,1,64]{2,1,0:T(1,128)S(1)} async-done(((f32[32,1,64]{2,1,0:T(1,128)}), f32[32,1,64]{2,1,0:T(1,128)S(1)}, u32[]{:S(2)}, u32[]{:S(2)}) %all-to-all-start.5) | async-done | bytes 8224 | tf_op jit(solution)/shard_map/all_to_all | solution.py:84
  114.5 0.5 reduce_max.39
  (75 shorter events, 4.5 us)
Async XLA Ops:
  0.6 98.1 %copy-start = (bf16[1536,1000]{0,1:T(8,128)(2,1)S(1)}, bf16[1536,1000]{0,1:T(8,128)(2,1)}, u32[]{:S(2)}) copy-start(bf16[1536,1000]{0,1:T(8,128)(2,1)} %param.35) | copy-start | bytes 9216004
  0.6 8.3 %copy-start.1 = (bf16[2,64,1536]{2,1,0:T(8,128)(2,1)S(1)}, bf16[2,64,1536]{2,1,0:T(8,128)(2,1)}, u32[]{:S(2)}) copy-start(bf16[2,64,1536]{2,1,0:T(8,128)(2,1)} %param.18) | copy-start | bytes 1179652
  0.7 9.5 %copy-start.14 = (f32[48]{0:T(128)}, f32[48]{0:T(128)S(1)}, u32[]{:S(2)}) copy-start(f32[48]{0:T(128)S(1)} %multiply_power_fusion) | copy-start | bytes 580
  3.1 7.1 %copy-start.10 = (f32[1536]{0:T(1024)}, f32[1536]{0:T(1024)S(1)}, u32[]{:S(2)}) copy-start(f32[1536]{0:T(1024)S(1)} %convert_element_type.209) | copy-start | bytes 18436
  4.3 5.9 %copy-start.15 = (f32[2,64]{1,0:T(2,128)}, f32[2,64]{1,0:T(2,128)S(1)}, u32[]{:S(2)}) copy-start(f32[2,64]{1,0:T(2,128)S(1)} %add_rsqrt_fusion) | copy-start | bytes 1540
  7.2 3.1 %copy-start.9 = (f32[2,64]{1,0:T(2,128)}, f32[2,64]{1,0:T(2,128)S(1)}, u32[]{:S(2)}) copy-start(f32[2,64]{1,0:T(2,128)S(1)} %add_convert_fusion.2) | copy-start | bytes 1540
  7.3 4.4 %copy-start.5 = (bf16[2048,96]{0,1:T(8,128)(2,1)S(1)}, bf16[2048,96]{0,1:T(8,128)(2,1)}, u32[]{:S(2)}) copy-start(bf16[2048,96]{0,1:T(8,128)(2,1)} %param.23) | copy-start | bytes 1179652
  11.6 1.6 %copy-start.6 = (bf16[2,64,48]{2,1,0:T(8,128)(2,1)}, bf16[2,64,48]{2,1,0:T(8,128)(2,1)S(1)}, u32[]{:S(2)}) copy-start(bf16[2,64,48]{2,1,0:T(8,128)(2,1)S(1)} %get-tuple-element.12) | copy-start | bytes 36868
  11.7 1.5 %copy-start.17 = (bf16[2048,96]{0,1:T(8,128)(2,1)S(1)}, bf16[2048,96]{0,1:T(8,128)(2,1)}, u32[]{:S(2)}) copy-start(bf16[2048,96]{0,1:T(8,128)(2,1)} %param.24) | copy-start | bytes 1179652
  12.6 1.2 %copy-start.11 = (f32[1536]{0:T(1024)S(1)}, f32[1536]{0:T(1024)}, u32[]{:S(2)}) copy-start(f32[1536]{0:T(1024)} %copy-done.10) | copy-start | bytes 18436
  12.6 1.2 %copy-start.16 = (f32[2,64]{1,0:T(2,128)S(1)}, f32[2,64]{1,0:T(2,128)}, u32[]{:S(2)}) copy-start(f32[2,64]{1,0:T(2,128)} %copy-done.15) | copy-start | bytes 1540
  12.6 1.2 %copy-start.18 = (bf16[1536,96]{0,1:T(8,128)(2,1)S(1)}, bf16[1536,96]{0,1:T(8,128)(2,1)}, u32[]{:S(2)}) copy-start(bf16[1536,96]{0,1:T(8,128)(2,1)} %param.30) | copy-start | bytes 884740
  13.2 1.8 %copy-start.4 = (bf16[192,1536]{1,0:T(8,128)(2,1)S(1)}, bf16[192,1536]{1,0:T(8,128)(2,1)}, u32[]{:S(2)}) copy-start(bf16[192,1536]{1,0:T(8,128)(2,1)} %param.31) | copy-start | bytes 1769476
  13.7 8.1 %copy-start.13 = (bf16[1536]{0:T(1024)(128)(2,1)S(1)}, bf16[1536]{0:T(1024)(128)(2,1)}, u32[]{:S(2)}) copy-start(bf16[1536]{0:T(1024)(128)(2,1)} %param.26) | copy-start | bytes 9220
  14.1 0.6 copy-start.20
  16.0 20.6 %copy-start.19 = (s32[64]{0:T(128)S(1)}, s32[64]{0:T(128)}, u32[]{:S(2)}) copy-start(s32[64]{0:T(128)} %param.20) | copy-start | bytes 772
  16.1 13.2 %all-to-all-start = ((bf16[8,16,1536]{2,1,0:T(8,128)(2,1)}), bf16[8,16,1536]{2,1,0:T(8,128)(2,1)S(1)}, u32[]{:S(2)}, u32[]{:S(2)}) async-start(bf16[8,16,1536]{2,1,0:T(8,128)(2,1)} %fusion.1), calls=%async_computation | async-start | bytes 786432 | tf_op jit(solution)/shard_map/all_to_all | solution.py:75
  30.3 0.6 copy-start.3
  31.8 12.3 %all-to-all-start.1 = ((bf16[8,16,1536]{2,1,0:T(8,128)(2,1)}), bf16[8,16,1536]{2,1,0:T(8,128)(2,1)S(1)}, u32[]{:S(2)}, u32[]{:S(2)}) async-start(bf16[8,16,1536]{2,1,0:T(8,128)(2,1)} %multiply_convert_fusion), calls=%async_computation.1 | async-start | bytes 786432 | tf_op jit(solution)/shard_map/all_to_all | solution.py:228
  44.1 0.7 copy-start.2
  44.9 10.8 %copy-start.12 = (s32[2,8]{1,0:T(2,128)S(1)}, s32[2,8]{1,0:T(2,128)}, u32[]{:S(2)}) copy-start(s32[2,8]{1,0:T(2,128)} %param.21) | copy-start | bytes 196
  49.0 12.3 %all-to-all-start.2 = ((bf16[8,16,1536]{2,1,0:T(8,128)(2,1)}), bf16[8,16,1536]{2,1,0:T(8,128)(2,1)S(1)}, u32[]{:S(2)}, u32[]{:S(2)}) async-start(bf16[8,16,1536]{2,1,0:T(8,128)(2,1)} %bitcast.155), calls=%async_computation.2 | async-start | bytes 786432 | tf_op jit(solution)/shard_map/all_to_all | solution.py:75
  65.3 9.1 %all-to-all-start.3 = ((bf16[8,2,3072]{2,1,0:T(2,128)(2,1)}), bf16[8,2,3072]{2,1,0:T(2,128)(2,1)S(1)}, u32[]{:S(2)}, u32[]{:S(2)}) async-start(bf16[8,2,3072]{2,1,0:T(2,128)(2,1)} %reshape.505), calls=%async_computation.3 | async-start | bytes 196608 | tf_op jit(solution)/shard_map/all_to_all | solution.py:267
  76.7 28.0 %copy-start.7 = (bf16[2,64,48]{2,1,0:T(8,128)(2,1)S(1)}, bf16[2,64,48]{2,1,0:T(8,128)(2,1)}, u32[]{:S(2)}) copy-start(bf16[2,64,48]{2,1,0:T(8,128)(2,1)} %copy-done.6) | copy-start | bytes 36868
  76.7 22.0 %all-to-all-start.4 = ((bf16[32,2,1536]{2,1,0:T(2,128)(2,1)}), bf16[32,2,1536]{2,1,0:T(2,128)(2,1)S(1)}, u32[]{:S(2)}, u32[]{:S(2)}) async-start(bf16[32,2,1536]{2,1,0:T(2,128)(2,1)} %multiply_convert_fusion.2), calls=%async_computation.4 | async-start | bytes 393216 | tf_op jit(solution)/shard_map/all_to_all | solution.py:303
  98.8 6.7 %copy-start.8 = (bf16[8,3072]{1,0:T(8,128)(2,1)S(1)}, bf16[8,3072]{1,0:T(8,128)(2,1)}, u32[]{:S(2)}) copy-start(bf16[8,3072]{1,0:T(8,128)(2,1)} %get-tuple-element.10) | copy-start | bytes 147460
  100.5 13.9 %all-to-all-start.5 = ((f32[32,1,64]{2,1,0:T(1,128)}), f32[32,1,64]{2,1,0:T(1,128)S(1)}, u32[]{:S(2)}, u32[]{:S(2)}) async-start(f32[32,1,64]{2,1,0:T(1,128)} %broadcast_in_dim.121), calls=%async_computation.5 | async-start | bytes 32768 | tf_op jit(solution)/shard_map/all_to_all | solution.py:84
